TPU v7x, 128 devices: a whole 4x4x4 slice. The times are simulated.
128 devices in a mesh: mx: 16 (over y, z_lo, core), my: 8 (over z_hi, x).
Axes of the slice: x: 4, y: 4, z: 4 (z_hi: 2, z_lo: 2; z = z_hi * 2 + z_lo), core: 2. Of those that a mesh axis runs over, the one named last changes fastest.
Arguments:
- documents: bfloat16 [131072, 768], P(('mx', 'my')), may hold values from -12 to 12
- owner_tile: int32 [131072, 1], P(('mx', 'my')), may hold values from 0 to 127; in each aligned block of 1024 rows (0 to 1023, 1024 to 2047, ...) at most 16 rows name the same one
- unit_in_tile: int32 [131072], P(('mx', 'my')), may hold values from 0 to 4095
- codebook: bfloat16 [1024, 512, 768], P('mx', 'my'), may hold values from -6 to 6
Outputs:
- new_codebook: bfloat16 [1024, 512, 768], P('mx', 'my')
Inputs may be any that keep to these rules, and one draw needn't show every extreme that they name: `owner_tile`: among the rows of one device no tile is named by more than 16 documents, and in every draw some tile is named by exactly 16 rows of some device.
All inputs are finite; a program needn't handle non-finite values.
Results may differ from a plain program's by a relative error of at most 0.001.
Values may be sent and summed in bfloat16 or wider, within the bound.
No kernel may reach another device: no remote copies, remote signals or barrier semaphores. Data moves between devices by JAX's collectives and lax.ppermute only.
A program may use at most 256 MiB of HBM per device.

v0:
```python
import math

import jax
import jax.numpy as jnp
import numpy as np
from jax import lax
from jax.experimental import pallas as pl
from jax.sharding import PartitionSpec as P

RADIUS = 8
HI = lax.Precision.HIGH


def band_matrix(out_len):
    ext = out_len + 2 * RADIUS
    mat = np.zeros((out_len, ext), np.float32)
    for r in range(out_len):
        for k in range(-RADIUS, RADIUS + 1):
            mat[r, r + k + RADIUS] = math.exp(-2.0 * k * k / RADIUS**2)
    return mat


def accumulate_kernel(ids_ref, docs_ref, num_ref, hits_ref):
    block, rows = num_ref.shape[0], ids_ref.shape[1]
    feature = num_ref.shape[1]
    first = pl.program_id(0) * block
    units = first + lax.broadcasted_iota(jnp.int32, (block, rows), 0)
    one_hot = (units == ids_ref[...]).astype(jnp.bfloat16)
    sums = jnp.dot(one_hot, docs_ref[...], preferred_element_type=jnp.float32)
    num_ref[...] = sums[:, :feature]
    hits_ref[...] = sums[:, feature:]


def accumulate(ids, docs, unit_total, feature):
    rows, width = docs.shape
    block = 512
    return pl.pallas_call(
        accumulate_kernel,
        grid=(unit_total // block,),
        in_specs=[
            pl.BlockSpec((1, rows), lambda j: (0, 0)),
            pl.BlockSpec((rows, width), lambda j: (0, 0)),
        ],
        out_specs=[
            pl.BlockSpec((block, feature), lambda j: (j, 0)),
            pl.BlockSpec((block, width - feature), lambda j: (j, 0)),
        ],
        out_shape=[
            jax.ShapeDtypeStruct((unit_total, feature), jnp.float32),
            jax.ShapeDtypeStruct((unit_total, width - feature), jnp.float32),
        ],
    )(ids.reshape(1, rows), docs)


def halo(x, axis, dim):
    devices, length = lax.axis_size(axis), x.shape[dim]
    up = [(i, i + 1) for i in range(devices - 1)]
    down = [(j, i) for i, j in up]
    last = lax.slice_in_dim(x, length - RADIUS, length, axis=dim)
    leading = lax.slice_in_dim(x, 0, RADIUS, axis=dim)
    before = lax.ppermute(last, axis, up)
    after = lax.ppermute(leading, axis, down)
    return jnp.concatenate([before, x, after], axis=dim)


def on_device(documents, owner_tile, unit_in_tile, codebook):
    rows_mx = lax.axis_size("mx")
    cols_my = lax.axis_size("my")
    tile_total = rows_mx * cols_my
    rows_tile, cols_tile, feature = codebook.shape
    doc_count = documents.shape[0]
    capacity = max(2, 2 * doc_count // tile_total)
    target = owner_tile[:, 0]
    tile_hits = (target[:, None] == jnp.arange(tile_total, dtype=jnp.int32)[None, :]).astype(
        jnp.int32
    )
    earlier = jnp.cumsum(tile_hits, axis=0) - tile_hits
    slot_pos = jnp.sum(earlier * tile_hits, axis=1)
    unit_row = unit_in_tile // cols_tile
    unit_col = unit_in_tile % cols_tile
    extra = jnp.zeros((doc_count, 128), jnp.bfloat16)
    extra = extra.at[:, 0].set(unit_row.astype(jnp.bfloat16))
    extra = extra.at[:, 1].set(unit_col.astype(jnp.bfloat16))
    extra = extra.at[:, 2].set(1.0)
    rows_out = jnp.concatenate([documents, extra], axis=1)
    width = feature + 128
    send_place = target * capacity + slot_pos
    outgoing = jnp.zeros((tile_total * capacity, width), jnp.bfloat16).at[send_place].set(rows_out)
    got = lax.all_to_all(
        outgoing.reshape(tile_total, capacity, width),
        ("mx", "my"),
        split_axis=0,
        concat_axis=0,
        tiled=True,
    ).reshape(-1, width)
    mark_row = got[:, feature].astype(jnp.int32)
    mark_col = got[:, feature + 1].astype(jnp.int32)
    unit_ids = jnp.where(got[:, feature + 2] > 0.5, mark_col * rows_tile + mark_row, -1)
    unit_total = rows_tile * cols_tile
    numerator, counter = accumulate(unit_ids, got, unit_total, feature)
    num_cm = numerator.reshape(cols_tile, rows_tile, feature)
    hits_cm = counter[:, 2].reshape(cols_tile, rows_tile)

    g_rows = jnp.asarray(band_matrix(rows_tile))
    g_cols = jnp.asarray(band_matrix(cols_tile))
    ext_num = halo(num_cm, "mx", 1)
    ext_hits = halo(hits_cm, "mx", 1)
    row_num = jnp.einsum("rk,cke->cre", g_rows, ext_num, precision=HI)
    row_hits = jnp.einsum("rk,ck->cr", g_rows, ext_hits, precision=HI)
    ext_num = halo(row_num, "my", 0)
    ext_hits = halo(row_hits, "my", 0)
    smooth_num = jnp.einsum("ck,kre->rce", g_cols, ext_num, precision=HI)
    smooth_hits = jnp.einsum("ck,kr->rc", g_cols, ext_hits, precision=HI)
    updated = (smooth_num + 8.0 * codebook.astype(jnp.float32)) / (smooth_hits[:, :, None] + 8.0)
    return updated.astype(jnp.bfloat16)


def solution(mesh):
    return jax.shard_map(
        on_device,
        mesh=mesh,
        in_specs=(
            P(("mx", "my"), None),
            P(("mx", "my"), None),
            P(("mx", "my")),
            P("mx", "my", None),
        ),
        out_specs=P("mx", "my", None),
        check_vma=False,
    )
```

profile of v0, /device:TPU:32, one launch (start us, length us, event | category | flops | bytes accessed | tf_op | source)
XLA Modules:
  0.0 236.9 jit_solution(13572348682326996633)
XLA Ops:
  0.0 0.0 copy-start.2
  0.0 0.6 compare_reduce_fusion.2
  0.6 0.6 compare_reduce_fusion.1
  1.3 0.7 compare_reduce_fusion
  1.9 1.9 fusion.32
  3.9 0.8 copy.9
  4.7 0.1 scatter.19
  4.8 0.6 broadcast_select_fusion
  5.4 0.1 scatter.24
  5.5 0.2 copy.11
  5.7 0.2 fusion.25
  6.0 0.1 copy.10
  6.1 1.0 fusion.24
  7.1 0.0 copy-done.6
  7.2 0.0 copy-done.2
  7.2 7.6 %scatter_custom_fusion = bf16[2048,896]{1,0:T(8,128)(2,1)} fusion(s32[1024]{0:T(1024)S(1)} %bitcast.51, bf16[1024,128]{1,0:T(8,128)(2,1)S(1)} %copy.11, bf16[]{:T(256)} %constant.141, bf16[1024,768]{1,0:T(8,128)(2,1)S(1)} %copy-done.2, bf16[]{:T(256)} %constant.115.clone.1), kind=kCustom, calls=%fused_computation.15 | custom fusion | flops 3670016 | bytes 5505028 | tf_op jit(solution)/shard_map/scatter | solution.py:88
  14.8 56.7 %all_to_all.5 = bf16[128,16,896]{2,1,0:T(8,128)(2,1)S(1)} all-to-all(bf16[128,16,896]{2,1,0:T(8,128)(2,1)} %bitcast.46), channel_id=1, replica_groups=mesh['mx'=16,'my'=8] {'mx','my'}, dimensions={0} | all-to-all | bytes 7340032 | tf_op jit(solution)/shard_map/all_to_all | solution.py:89
  71.6 0.0 copy-start
  71.6 1.8 copy-done
  73.4 1.3 select_reduce_fusion
  74.7 22.0 %shard_map.64 = (f32[4096,768]{1,0:T(8,128)}, f32[4096,128]{1,0:T(8,128)}) custom-call(s32[1,2048]{1,0:T(1,128)} %bitcast.49, bf16[2048,896]{1,0:T(8,128)(2,1)} %bitcast.43), custom_call_target="tpu_custom_call" | custom-call | tf_op jit(solution)/shard_map/pallas_call | solution.py:37
  96.7 0.0 copy-start.1
  96.7 2.2 fusion.36
  98.9 1.9 collective-permute-start
  100.8 3.6 %collective-permute-start.1 = (f32[64,8,768]{2,1,0:T(8,128)S(1)}, f32[64,8,768]{2,1,0:T(8,128)}, u32[]{:S(2)}, u32[]{:S(2)}) collective-permute-start(f32[64,8,768]{2,1,0:T(8,128)S(1)} %get-tuple-element.48), channel_id=1, source_target_pairs={{8,0},{16,8},{24,16},{32,24},{40,32},{48,40},{56,48},{64,56},{72,6... | collective-permute-start | bytes 4718600 | tf_op jit(solution)/shard_map/ppermute | solution.py:62
  104.5 0.0 copy-done.1
  104.5 1.2 slice_reduce_fusion
  105.7 0.1 reshape_squeeze.3
  105.8 0.1 fusion.38
  105.8 2.9 %collective-permute-start.5 = (f32[64,8]{1,0:T(8,128)S(1)}, f32[64,8]{1,0:T(8,128)S(1)}, u32[]{:S(2)}, u32[]{:S(2)}) collective-permute-start(f32[64,8]{1,0:T(8,128)S(1)} %get-tuple-element.52), channel_id=1, source_target_pairs={{8,0},{16,8},{24,16},{32,24},{40,32},{48,40},{56,48},{64,56},{72,6... | collective-permute-start | bytes 6152 | tf_op jit(solution)/shard_map/ppermute | solution.py:62
  108.7 63.1 %collective-permute-done = f32[64,8,768]{2,1,0:T(8,128)} collective-permute-done((f32[64,8,768]{2,1,0:T(8,128)S(1)}, f32[64,8,768]{2,1,0:T(8,128)}, u32[]{:S(2)}, u32[]{:S(2)}) %collective-permute-start) | collective-permute-done | bytes 1572896 | tf_op jit(solution)/shard_map/ppermute | solution.py:61
  171.8 0.0 collective-permute-done.1
  171.8 0.0 copy-done.7
  171.8 9.4 %fusion.12 = f32[64,64,768]{2,1,0:T(8,128)S(1)} fusion(f32[64,80,1]{1,0,2:T(8,128)S(1)} %copy-done.7, f32[64,8,768]{2,1,0:T(8,128)} %collective-permute-done.1, f32[64,64,768]{2,1,0:T(8,128)} %bitcast.45, f32[64,8,768]{2,1,0:T(8,128)} %collective-permute-done), kind=kOutput, calls=%fused_computation.13 | convolution fusion | flops 1517813760 | bytes 28332032 | tf_op jit(solution)/shard_map/rk,cke->cre/dot_general | solution.py:108
  181.1 0.0 copy-start.3
  181.2 0.0 copy-start.4
  181.2 0.0 copy-start.5
  181.2 0.3 fusion.35
  181.5 1.4 collective-permute-start.2
  182.9 1.3 collective-permute-start.3
  184.2 0.0 copy-done.3
  184.2 0.2 fusion.39
  184.4 1.9 collective-permute-start.4
  186.3 0.0 collective-permute-done.5
  186.3 0.0 copy-done.4
  186.3 0.2 fusion.40
  186.5 3.1 %collective-permute-done.4 = f32[64,8]{1,0:T(8,128)S(1)} collective-permute-done((f32[64,8]{1,0:T(8,128)S(1)}, f32[64,8]{1,0:T(8,128)S(1)}, u32[]{:S(2)}, u32[]{:S(2)}) %collective-permute-start.4) | collective-permute-done | bytes 2080 | tf_op jit(solution)/shard_map/ppermute | solution.py:61
  189.6 0.0 copy-done.5
  189.6 0.2 fusion.22
  189.8 1.3 collective-permute-start.7
  191.1 0.2 fusion.41
  191.3 5.2 %collective-permute-start.6 = (f32[8,64]{1,0:T(8,128)S(1)}, f32[8,64]{1,0:T(8,128)S(1)}, u32[]{:S(2)}, u32[]{:S(2)}) collective-permute-start(f32[8,64]{1,0:T(8,128)S(1)} %get-tuple-element.49), channel_id=1, source_target_pairs={{0,1},{1,2},{2,3},{3,4},{4,5},{5,6},{6,7},{8,9},{9,10},{10,11},{11... | collective-permute-start | bytes 6152 | tf_op jit(solution)/shard_map/ppermute | solution.py:61
  196.5 8.8 %collective-permute-done.7 = f32[8,64]{1,0:T(8,128)S(1)} collective-permute-done((f32[8,64]{1,0:T(8,128)S(1)}, f32[8,64]{1,0:T(8,128)S(1)}, u32[]{:S(2)}, u32[]{:S(2)}) %collective-permute-start.7) | collective-permute-done | bytes 2080 | tf_op jit(solution)/shard_map/ppermute | solution.py:62
  205.3 0.2 fusion.42
  205.5 0.0 collective-permute-done.6
  205.5 0.0 slice-start
  205.5 0.2 fusion.21
  205.8 0.0 slice-start.1
  205.8 0.0 collective-permute-done.2
  205.8 0.0 collective-permute-done.3
  205.8 6.8 %pad_maximum_fusion = f32[80,64,768]{2,1,0:T(8,128)} fusion(f32[8,64,768]{2,1,0:T(8,128)S(1)} %collective-permute-done.3, f32[64,64,768]{2,1,0:T(8,128)S(1)} %fusion.12, f32[8,64,768]{2,1,0:T(8,128)S(1)} %collective-permute-done.2), kind=kLoop, calls=%fused_computation.7 | loop fusion | flops 7864320 | bytes 31457280 | tf_op jit(solution)/shard_map/concatenate | solution.py:63
  212.6 0.0 slice-done
  212.6 0.0 slice-done.1
  212.6 24.3 %fusion.9 = bf16[64,64,768]{2,1,0:T(8,128)(2,1)} fusion(bf16[64,64,768]{2,1,0:T(8,128)(2,1)S(1)} %bitcast.53, f32[64,64]{1,0:T(8,128)S(1)} %fusion.21, f32[64,80,1]{1,0,2:T(8,128)S(1)} %copy-done.7, f32[80,64,768]{2,1,0:T(8,128)} %pad_maximum_fusion), kind=kOutput, calls=%fused_computation.12 | convolution fusion | flops 1525678080 | bytes 28348416 | tf_op jit(solution)/shard_map/ck,kre->rce/dot_general | solution.py:112
  (12 shorter events, 0.1 us)
Async XLA Ops:
  0.0 7.1 %copy-start.6 = (s32[1024,1]{0,1:T(1,128)S(1)}, s32[1024,1]{0,1:T(1,128)}, u32[]{:S(2)}) copy-start(s32[1024,1]{0,1:T(1,128)} %param.13) | copy-start | bytes 12292
  0.0 7.2 %copy-start.2 = (bf16[1024,768]{1,0:T(8,128)(2,1)S(1)}, bf16[1024,768]{1,0:T(8,128)(2,1)}, u32[]{:S(2)}) copy-start(bf16[1024,768]{1,0:T(8,128)(2,1)} %param.12) | copy-start | bytes 4718596
  71.6 1.8 copy-start
  96.7 7.8 %copy-start.1 = (f32[4096,128]{1,0:T(8,128)S(1)}, f32[4096,128]{1,0:T(8,128)}, u32[]{:S(2)}) copy-start(f32[4096,128]{1,0:T(8,128)} %get-tuple-element.44) | copy-start | bytes 6291460
  96.7 75.1 %copy-start.7 = (f32[64,80,1]{1,0,2:T(8,128)S(1)}, f32[64,80,1]{1,0,2:T(8,128)}, u32[]{:S(2)}) copy-start(f32[64,80,1]{1,0,2:T(8,128)} %constant.136) | copy-start | bytes 61444
  98.9 72.8 %collective-permute-start = (f32[64,8,768]{2,1,0:T(8,128)S(1)}, f32[64,8,768]{2,1,0:T(8,128)}, u32[]{:S(2)}, u32[]{:S(2)}) collective-permute-start(f32[64,8,768]{2,1,0:T(8,128)S(1)} %get-tuple-element.47), channel_id=1, source_target_pairs={{0,8},{8,16},{16,24},{24,32},{32,40},{40,48},{48,56},{56,64},{64,7... | collective-permute-start | bytes 4718600 | tf_op jit(solution)/shard_map/ppermute | solution.py:61
  100.8 70.9 %collective-permute-start.1 = (f32[64,8,768]{2,1,0:T(8,128)S(1)}, f32[64,8,768]{2,1,0:T(8,128)}, u32[]{:S(2)}, u32[]{:S(2)}) collective-permute-start(f32[64,8,768]{2,1,0:T(8,128)S(1)} %get-tuple-element.48), channel_id=1, source_target_pairs={{8,0},{16,8},{24,16},{32,24},{40,32},{48,40},{56,48},{64,56},{72,6... | collective-permute-start | bytes 4718600 | tf_op jit(solution)/shard_map/ppermute | solution.py:62
  105.8 80.5 %collective-permute-start.5 = (f32[64,8]{1,0:T(8,128)S(1)}, f32[64,8]{1,0:T(8,128)S(1)}, u32[]{:S(2)}, u32[]{:S(2)}) collective-permute-start(f32[64,8]{1,0:T(8,128)S(1)} %get-tuple-element.52), channel_id=1, source_target_pairs={{8,0},{16,8},{24,16},{32,24},{40,32},{48,40},{56,48},{64,56},{72,6... | collective-permute-start | bytes 6152 | tf_op jit(solution)/shard_map/ppermute | solution.py:62
  181.1 3.0 %copy-start.3 = (f32[64,64]{1,0:T(8,128)S(1)}, f32[64,64]{1,0:T(8,128)}, u32[]{:S(2)}) copy-start(f32[64,64]{1,0:T(8,128)} %constant.134) | copy-start | bytes 49156
  181.2 5.2 %copy-start.4 = (f32[64,8]{1,0:T(8,128)S(1)}, f32[64,8]{1,0:T(8,128)}, u32[]{:S(2)}) copy-start(f32[64,8]{1,0:T(8,128)} %constant.135) | copy-start | bytes 6148
  181.2 8.4 %copy-start.5 = (f32[64,8]{1,0:T(8,128)S(1)}, f32[64,8]{1,0:T(8,128)}, u32[]{:S(2)}) copy-start(f32[64,8]{1,0:T(8,128)} %constant.133) | copy-start | bytes 6148
  181.5 24.3 %collective-permute-start.2 = (f32[8,64,768]{2,1,0:T(8,128)S(1)}, f32[8,64,768]{2,1,0:T(8,128)S(1)}, u32[]{:S(2)}, u32[]{:S(2)}) collective-permute-start(f32[8,64,768]{2,1,0:T(8,128)S(1)} %get-tuple-element.45), channel_id=1, source_target_pairs={{0,1},{1,2},{2,3},{3,4},{4,5},{5,6},{6,7},{8,9},{9,10},{10,11},{11... | collective-permute-start | bytes 4718600 | tf_op jit(solution)/shard_map/ppermute | solution.py:61
  182.9 22.9 %collective-permute-start.3 = (f32[8,64,768]{2,1,0:T(8,128)S(1)}, f32[8,64,768]{2,1,0:T(8,128)S(1)}, u32[]{:S(2)}, u32[]{:S(2)}) collective-permute-start(f32[8,64,768]{2,1,0:T(8,128)S(1)} %get-tuple-element.46), channel_id=1, source_target_pairs={{1,0},{2,1},{3,2},{4,3},{5,4},{6,5},{7,6},{9,8},{10,9},{11,10},{12... | collective-permute-start | bytes 4718600 | tf_op jit(solution)/shard_map/ppermute | solution.py:62
  184.4 5.2 %collective-permute-start.4 = (f32[64,8]{1,0:T(8,128)S(1)}, f32[64,8]{1,0:T(8,128)S(1)}, u32[]{:S(2)}, u32[]{:S(2)}) collective-permute-start(f32[64,8]{1,0:T(8,128)S(1)} %get-tuple-element.51), channel_id=1, source_target_pairs={{0,8},{8,16},{16,24},{24,32},{32,40},{40,48},{48,56},{56,64},{64,7... | collective-permute-start | bytes 6152 | tf_op jit(solution)/shard_map/ppermute | solution.py:61
  189.8 15.5 %collective-permute-start.7 = (f32[8,64]{1,0:T(8,128)S(1)}, f32[8,64]{1,0:T(8,128)S(1)}, u32[]{:S(2)}, u32[]{:S(2)}) collective-permute-start(f32[8,64]{1,0:T(8,128)S(1)} %get-tuple-element.50), channel_id=1, source_target_pairs={{1,0},{2,1},{3,2},{4,3},{5,4},{6,5},{7,6},{9,8},{10,9},{11,10},{12... | collective-permute-start | bytes 6152 | tf_op jit(solution)/shard_map/ppermute | solution.py:62
  191.3 14.2 %collective-permute-start.6 = (f32[8,64]{1,0:T(8,128)S(1)}, f32[8,64]{1,0:T(8,128)S(1)}, u32[]{:S(2)}, u32[]{:S(2)}) collective-permute-start(f32[8,64]{1,0:T(8,128)S(1)} %get-tuple-element.49), channel_id=1, source_target_pairs={{0,1},{1,2},{2,3},{3,4},{4,5},{5,6},{6,7},{8,9},{9,10},{10,11},{11... | collective-permute-start | bytes 6152 | tf_op jit(solution)/shard_map/ppermute | solution.py:61
  205.5 7.1 %slice-start = ((s8[6291456]{0:T(1024)(128)(4,1)}), s8[2097152]{0:T(1024)(128)(4,1)S(1)}, s32[]{:S(2)}) async-start(s8[6291456]{0:T(1024)(128)(4,1)} %bitcast.52), calls=%async_computation.1 | async-start | bytes 4194304
  205.8 6.8 %slice-start.1 = ((s8[6291456]{0:T(1024)(128)(4,1)}), s8[4194304]{0:T(1024)(128)(4,1)S(1)}, s32[]{:S(2)}) async-start(s8[6291456]{0:T(1024)(128)(4,1)} %bitcast.52), calls=%async_computation.2 | async-start | bytes 8388608
where the time goes:
time: 237 us
  waiting for transfers between devices  75 us (32%)
  blocking collectives  56.7 us (24%)
  matrix products  34.8 us (15%)
  Pallas kernels  22 us (9%)
  other arithmetic  21.6 us (9%)
  starting transfers between devices  19.5 us (8%)
  local copies, waits for them, and re-layouts  6.98 us (3%)
    ppermute x4, waiting for transfers between devices, halo(): before = lax.ppermute(last, axis, up)  66.2 us
    all_to_all x1, blocking collectives, on_device(): lax.all_to_all(outgoing.reshape(tile_total, capacity, width), ('mx', 'my'...  56.7 us
    dot_general x1, matrix products, on_device(): smooth_num = jnp.einsum('ck,kre->rce', g_cols, ext_num, precision=HI)  24.3 us
    pallas_call x1, Pallas kernels, accumulate(): pl.pallas_call(accumulate_kernel, grid=(unit_total // block,), in_specs=[...  22 us
    ppermute x4, starting transfers between devices, halo(): before = lax.ppermute(last, axis, up)  10.4 us
    dot_general x1, matrix products, on_device(): row_num = jnp.einsum('rk,cke->cre', g_rows, ext_num, precision=HI)  9.37 us
    ppermute x4, starting transfers between devices, halo(): after = lax.ppermute(leading, axis, down)  9.08 us
    ppermute x4, waiting for transfers between devices, halo(): after = lax.ppermute(leading, axis, down)  8.8 us
  transfers between devices with their start and end apart: 8, of which 3 were waited for; matrix products, arithmetic and copies ran while one was open for 5% of the time, Pallas kernels for 0%

commit v1 on v0

--- a/solution.py
+++ b/solution.py
@@ -20,23 +20,21 @@
     return mat
 
 
-def accumulate_kernel(ids_ref, docs_ref, num_ref, hits_ref):
-    block, rows = num_ref.shape[0], ids_ref.shape[1]
-    feature = num_ref.shape[1]
-    first = pl.program_id(0) * block
-    units = first + lax.broadcasted_iota(jnp.int32, (block, rows), 0)
-    one_hot = (units == ids_ref[...]).astype(jnp.bfloat16)
-    sums = jnp.dot(one_hot, docs_ref[...], preferred_element_type=jnp.float32)
-    num_ref[...] = sums[:, :feature]
-    hits_ref[...] = sums[:, feature:]
-
-
-def accumulate(ids, docs, unit_total, feature):
+def accumulate(ids, docs, unit_of, blocks, feature):
     rows, width = docs.shape
     block = 512
+
+    def kernel(ids_ref, docs_ref, num_ref, hits_ref):
+        place = pl.program_id(0) * block + lax.broadcasted_iota(jnp.int32, (block, rows), 0)
+        units = unit_of(place)
+        one_hot = (units == ids_ref[...]).astype(jnp.bfloat16)
+        sums = jnp.dot(one_hot, docs_ref[...], preferred_element_type=jnp.float32)
+        num_ref[...] = sums[:, :feature]
+        hits_ref[...] = sums[:, feature:]
+
     return pl.pallas_call(
-        accumulate_kernel,
-        grid=(unit_total // block,),
+        kernel,
+        grid=(blocks,),
         in_specs=[
             pl.BlockSpec((1, rows), lambda j: (0, 0)),
             pl.BlockSpec((rows, width), lambda j: (0, 0)),
@@ -46,21 +44,17 @@
             pl.BlockSpec((block, width - feature), lambda j: (j, 0)),
         ],
         out_shape=[
-            jax.ShapeDtypeStruct((unit_total, feature), jnp.float32),
-            jax.ShapeDtypeStruct((unit_total, width - feature), jnp.float32),
+            jax.ShapeDtypeStruct((blocks * block, feature), jnp.float32),
+            jax.ShapeDtypeStruct((blocks * block, width - feature), jnp.float32),
         ],
     )(ids.reshape(1, rows), docs)
 
 
-def halo(x, axis, dim):
-    devices, length = lax.axis_size(axis), x.shape[dim]
+def exchange(lead, last, axis):
+    devices = lax.axis_size(axis)
     up = [(i, i + 1) for i in range(devices - 1)]
     down = [(j, i) for i, j in up]
-    last = lax.slice_in_dim(x, length - RADIUS, length, axis=dim)
-    leading = lax.slice_in_dim(x, 0, RADIUS, axis=dim)
-    before = lax.ppermute(last, axis, up)
-    after = lax.ppermute(leading, axis, down)
-    return jnp.concatenate([before, x, after], axis=dim)
+    return lax.ppermute(last, axis, up), lax.ppermute(lead, axis, down)
 
 
 def on_device(documents, owner_tile, unit_in_tile, codebook):
@@ -95,22 +89,40 @@
     ).reshape(-1, width)
     mark_row = got[:, feature].astype(jnp.int32)
     mark_col = got[:, feature + 1].astype(jnp.int32)
-    unit_ids = jnp.where(got[:, feature + 2] > 0.5, mark_col * rows_tile + mark_row, -1)
-    unit_total = rows_tile * cols_tile
-    numerator, counter = accumulate(unit_ids, got, unit_total, feature)
-    num_cm = numerator.reshape(cols_tile, rows_tile, feature)
-    hits_cm = counter[:, 2].reshape(cols_tile, rows_tile)
+    unit_ids = jnp.where(got[:, feature + 2] > 0.5, mark_row * cols_tile + mark_col, -1)
+    inner = cols_tile - 2 * RADIUS
+    band_blocks = RADIUS * rows_tile // 512
+    inner_blocks = inner * rows_tile // 512
+
+    def band_unit(offset):
+        return lambda m: (m // RADIUS) * cols_tile + offset + m % RADIUS
+
+    num_l, cnt_l = accumulate(unit_ids, got, band_unit(0), band_blocks, feature)
+    num_r, cnt_r = accumulate(unit_ids, got, band_unit(cols_tile - RADIUS), band_blocks, feature)
+    band_shape = (rows_tile, RADIUS, feature)
+    num_l, num_r = num_l.reshape(band_shape), num_r.reshape(band_shape)
+    hits_l = cnt_l[:, 2].reshape(rows_tile, RADIUS)
+    hits_r = cnt_r[:, 2].reshape(rows_tile, RADIUS)
+    from_left, from_right = exchange(num_l, num_r, "my")
+    hits_from_left, hits_from_right = exchange(hits_l, hits_r, "my")
+    num_i, cnt_i = accumulate(
+        unit_ids, got, lambda m: (m // inner) * cols_tile + RADIUS + m % inner, inner_blocks, feature
+    )
+    num_i = num_i.reshape(rows_tile, inner, feature)
+    hits_i = cnt_i[:, 2].reshape(rows_tile, inner)
 
     g_rows = jnp.asarray(band_matrix(rows_tile))
     g_cols = jnp.asarray(band_matrix(cols_tile))
-    ext_num = halo(num_cm, "mx", 1)
-    ext_hits = halo(hits_cm, "mx", 1)
-    row_num = jnp.einsum("rk,cke->cre", g_rows, ext_num, precision=HI)
-    row_hits = jnp.einsum("rk,ck->cr", g_rows, ext_hits, precision=HI)
-    ext_num = halo(row_num, "my", 0)
-    ext_hits = halo(row_hits, "my", 0)
-    smooth_num = jnp.einsum("ck,kre->rce", g_cols, ext_num, precision=HI)
-    smooth_hits = jnp.einsum("ck,kr->rc", g_cols, ext_hits, precision=HI)
+    ext_num = jnp.concatenate([from_left, num_l, num_i, num_r, from_right], axis=1)
+    ext_hits = jnp.concatenate([hits_from_left, hits_l, hits_i, hits_r, hits_from_right], axis=1)
+    col_num = jnp.einsum("ck,rke->rce", g_cols, ext_num, precision=HI)
+    col_hits = jnp.einsum("ck,rk->rc", g_cols, ext_hits, precision=HI)
+    above, below = exchange(col_num[:RADIUS], col_num[rows_tile - RADIUS :], "mx")
+    hits_above, hits_below = exchange(col_hits[:RADIUS], col_hits[rows_tile - RADIUS :], "mx")
+    ext_num = jnp.concatenate([above, col_num, below], axis=0)
+    ext_hits = jnp.concatenate([hits_above, col_hits, hits_below], axis=0)
+    smooth_num = jnp.einsum("rk,kce->rce", g_rows, ext_num, precision=HI)
+    smooth_hits = jnp.einsum("rk,kc->rc", g_rows, ext_hits, precision=HI)
     updated = (smooth_num + 8.0 * codebook.astype(jnp.float32)) / (smooth_hits[:, :, None] + 8.0)
     return updated.astype(jnp.bfloat16)
 

time: 237 us -> 243 us (1.025)
  the two profiles are of different devices: /device:TPU:32 before, /device:TPU:15 now
where the time goes in v1:
time: 243 us; the launch traced here: 242 us
  blocking collectives  54.9 us (23%)
  matrix products  39.4 us (16%)
  waiting for transfers between devices  38.3 us (16%)
  Pallas kernels  29.5 us (12%)
  starting transfers between devices  29.2 us (12%)
  local copies, waits for them, and re-layouts  28.2 us (12%)
  other arithmetic  22.1 us (9%)
    all_to_all x1, blocking collectives, on_device(): lax.all_to_all(outgoing.reshape(tile_total, capacity, width), ('mx', 'my'...  54.9 us
    ppermute x8, waiting for transfers between devices, exchange(): return (lax.ppermute(last, axis, up), lax.ppermute(lead, axis, down))  38.3 us
    pallas_call x3, Pallas kernels, accumulate(): pl.pallas_call(kernel, grid=(blocks,), in_specs=[pl.BlockSpec((1, rows),...  29.5 us
    ppermute x8, starting transfers between devices, exchange(): return (lax.ppermute(last, axis, up), lax.ppermute(lead, axis, down))  29.2 us
    dot_general x1, matrix products, on_device(): smooth_num = jnp.einsum('rk,kce->rce', g_rows, ext_num, precision=HI)  29 us
    unnamed x26, local copies, waits for them, and re-layouts  15.2 us
    dot_general x1, matrix products, on_device(): col_num = jnp.einsum('ck,rke->rce', g_cols, ext_num, precision=HI)  9.01 us
    scatter x1, other arithmetic, on_device(): jnp.zeros((tile_total * capacity, width), jnp.bfloat16).at[send_place]  8.23 us
  transfers between devices with their start and end apart: 8, of which 2 were waited for; matrix products, arithmetic and copies ran while one was open for 12% of the time, Pallas kernels for 10%

profile of v1, /device:TPU:15, one launch (start us, length us, event | category | flops | bytes accessed | tf_op | source)
XLA Modules:
  0.0 242.1 jit_solution(15348038847589239242)
XLA Ops:
  0.0 0.6 compare_reduce_fusion.1
  0.6 0.7 compare_reduce_fusion.2
  1.4 0.6 compare_reduce_fusion
  2.0 0.8 copy.11
  2.8 0.2 fusion.15
  3.1 0.1 copy.12
  3.2 1.0 fusion.14
  4.2 0.7 compare_select_fusion
  4.9 2.0 fusion.22
  7.0 0.1 scatter.19
  7.1 0.6 broadcast_select_fusion
  7.7 0.1 scatter.24
  7.8 0.2 copy.13
  7.9 8.2 %scatter_custom_fusion = bf16[2048,896]{1,0:T(8,128)(2,1)} fusion(s32[1024]{0:T(1024)S(1)} %bitcast.60, bf16[1024,128]{1,0:T(8,128)(2,1)S(1)} %copy.13, bf16[]{:T(256)} %constant.150, bf16[1024,768]{1,0:T(8,128)(2,1)} %param.12, bf16[]{:T(256)} %constant.115.clone.1), kind=kCustom, calls=%fused_computation.6 | custom fusion | flops 3670016 | bytes 5505028 | tf_op jit(solution)/shard_map/scatter | solution.py:82
  16.2 54.9 %all_to_all.5 = bf16[128,16,896]{2,1,0:T(8,128)(2,1)S(1)} all-to-all(bf16[128,16,896]{2,1,0:T(8,128)(2,1)} %bitcast.50), channel_id=1, replica_groups=mesh['mx'=16,'my'=8] {'mx','my'}, dimensions={0} | all-to-all | bytes 7340032 | tf_op jit(solution)/shard_map/all_to_all | solution.py:83
  71.0 1.8 copy-done
  72.9 1.4 select_reduce_fusion
  74.3 5.7 %shard_map.64 = (f32[512,768]{1,0:T(8,128)}, f32[512,128]{1,0:T(8,128)}) custom-call(s32[1,2048]{1,0:T(1,128)} %bitcast.54, bf16[2048,896]{1,0:T(8,128)(2,1)} %bitcast.47), custom_call_target="tpu_custom_call" | custom-call | tf_op jit(solution)/shard_map/pallas_call | solution.py:35
  80.0 5.1 %collective-permute-start = (f32[64,8,768]{2,1,0:T(8,128)}, f32[64,8,768]{2,1,0:T(8,128)}, u32[]{:S(2)}, u32[]{:S(2)}) collective-permute-start(f32[64,8,768]{2,1,0:T(8,128)} %bitcast.52), channel_id=1, source_target_pairs={{0,1},{1,2},{2,3},{3,4},{4,5},{5,6},{6,7},{8,9},{9,10},{10,11},{11... | collective-permute-start | bytes 4718600 | tf_op jit(solution)/shard_map/ppermute | solution.py:57
  85.2 18.2 %shard_map.66 = (f32[3072,768]{1,0:T(8,128)}, f32[3072,128]{1,0:T(8,128)}) custom-call(s32[1,2048]{1,0:T(1,128)} %bitcast.55, bf16[2048,896]{1,0:T(8,128)(2,1)} %bitcast.48), custom_call_target="tpu_custom_call" | custom-call | tf_op jit(solution)/shard_map/pallas_call | solution.py:35
  103.3 5.6 %shard_map.65 = (f32[512,768]{1,0:T(8,128)}, f32[512,128]{1,0:T(8,128)}) custom-call(s32[1,2048]{1,0:T(1,128)} %bitcast.56, bf16[2048,896]{1,0:T(8,128)(2,1)} %bitcast.49), custom_call_target="tpu_custom_call" | custom-call | tf_op jit(solution)/shard_map/pallas_call | solution.py:35
  109.0 2.2 collective-permute-start.1
  111.2 1.2 slice_reduce_fusion.1
  112.4 2.3 slice_reduce_fusion
  114.7 0.2 slice_reduce_fusion.2
  114.9 0.1 reshape_squeeze.11
  115.0 0.1 reshape_squeeze.10
  115.1 0.1 reshape_squeeze.9
  115.2 7.0 %collective-permute-start.4 = (f32[64,8]{1,0:T(8,128)S(1)}, f32[64,8]{1,0:T(8,128)S(1)}, u32[]{:S(2)}, u32[]{:S(2)}) collective-permute-start(f32[64,8]{1,0:T(8,128)S(1)} %reshape_squeeze.9), channel_id=1, source_target_pairs={{0,1},{1,2},{2,3},{3,4},{4,5},{5,6},{6,7},{8,9},{9,10},{10,11},{11... | collective-permute-start | bytes 6152 | tf_op jit(solution)/shard_map/ppermute | solution.py:57
  122.2 1.9 collective-permute-start.5
  124.1 0.2 fusion.26
  124.3 0.2 fusion.27
  124.5 0.0 collective-permute-done
  124.5 2.7 %constant_dynamic-update-slice_fusion.4 = f32[64,80,768]{2,1,0:T(8,128)} fusion(f32[64,8,768]{2,1,0:T(8,128)} %collective-permute-done), kind=kLoop, calls=%fused_computation.37 | loop fusion | bytes 3145728
  127.2 1.3 constant_dynamic-update-slice_fusion.3
  128.5 8.0 %constant_dynamic-update-slice_fusion.2 = f32[64,80,768]{2,1,0:T(8,128)} fusion(f32[64,80,768]{2,1,0:T(8,128)} %constant_dynamic-update-slice_fusion.3, f32[64,48,768]{2,1,0:T(8,128)} %bitcast.51), kind=kLoop, calls=%fused_computation.35 | loop fusion | bytes 18874368
  136.4 1.4 constant_dynamic-update-slice_fusion.1
  137.8 11.6 %collective-permute-done.1 = f32[64,8,768]{2,1,0:T(8,128)S(1)} collective-permute-done((f32[64,8,768]{2,1,0:T(8,128)}, f32[64,8,768]{2,1,0:T(8,128)S(1)}, u32[]{:S(2)}, u32[]{:S(2)}) %collective-permute-start.1) | collective-permute-done | bytes 1572896 | tf_op jit(solution)/shard_map/ppermute | solution.py:57
  149.4 1.3 constant_dynamic-update-slice_fusion
  150.7 9.0 %convolution_bitcast_fusion = f32[64,64,768]{2,1,0:T(8,128)S(1)} fusion(f32[64,80,768]{2,1,0:T(8,128)} %constant_dynamic-update-slice_fusion, f32[64,80,1]{1,0,2:T(8,128)S(1)} %copy-done.10), kind=kOutput, calls=%fused_computation.5 | convolution fusion | flops 1509949440 | bytes 28332032 | tf_op jit(solution)/shard_map/ck,rke->rce/dot_general | solution.py:118
  159.7 0.0 copy-start.4
  159.7 0.0 copy-start.9
  159.7 0.0 copy-start.5
  159.7 0.0 copy-start.6
  159.8 0.3 fusion.24
  160.1 4.4 %collective-permute-start.3 = (f32[8,64,768]{2,1,0:T(8,128)S(1)}, f32[8,64,768]{2,1,0:T(8,128)S(1)}, u32[]{:S(2)}, u32[]{:S(2)}) collective-permute-start(f32[8,64,768]{2,1,0:T(8,128)S(1)} %get-tuple-element.54), channel_id=1, source_target_pairs={{8,0},{16,8},{24,16},{32,24},{40,32},{48,40},{56,48},{64,56},{72,6... | collective-permute-start | bytes 4718600 | tf_op jit(solution)/shard_map/ppermute | solution.py:57
  164.5 2.9 %collective-permute-start.2 = (f32[8,64,768]{2,1,0:T(8,128)S(1)}, f32[8,64,768]{2,1,0:T(8,128)S(1)}, u32[]{:S(2)}, u32[]{:S(2)}) collective-permute-start(f32[8,64,768]{2,1,0:T(8,128)S(1)} %get-tuple-element.53), channel_id=1, source_target_pairs={{0,8},{8,16},{16,24},{24,32},{32,40},{40,48},{48,56},{56,64},{64,7... | collective-permute-start | bytes 4718600 | tf_op jit(solution)/shard_map/ppermute | solution.py:57
  167.4 0.0 collective-permute-done.4
  167.5 0.2 fusion.12
  167.7 0.2 convolution_add_fusion.2
  167.8 0.0 collective-permute-done.5
  167.8 0.2 convolution_add_fusion.1
  168.0 1.9 collective-permute-start.7
  170.0 0.2 fusion.28
  170.2 3.6 %collective-permute-start.6 = (f32[8,64]{1,0:T(8,128)S(1)}, f32[8,64]{1,0:T(8,128)S(1)}, u32[]{:S(2)}, u32[]{:S(2)}) collective-permute-start(f32[8,64]{1,0:T(8,128)S(1)} %get-tuple-element.55), channel_id=1, source_target_pairs={{0,8},{8,16},{16,24},{24,32},{32,40},{40,48},{48,56},{56,64},{64,7... | collective-permute-start | bytes 6152 | tf_op jit(solution)/shard_map/ppermute | solution.py:57
  173.8 26.7 %collective-permute-done.7 = f32[8,64]{1,0:T(8,128)S(1)} collective-permute-done((f32[8,64]{1,0:T(8,128)S(1)}, f32[8,64]{1,0:T(8,128)S(1)}, u32[]{:S(2)}, u32[]{:S(2)}) %collective-permute-start.7) | collective-permute-done | bytes 2080 | tf_op jit(solution)/shard_map/ppermute | solution.py:57
  200.5 0.2 fusion.29
  200.8 0.0 collective-permute-done.6
  200.8 0.2 fusion.11
  201.0 0.0 collective-permute-done.3
  201.0 0.0 collective-permute-done.2
  201.0 5.9 %pad_maximum_fusion = f32[80,64,768]{2,1,0:T(8,128)} fusion(f32[8,64,768]{2,1,0:T(8,128)S(1)} %collective-permute-done.3, f32[64,64,768]{2,1,0:T(8,128)S(1)} %convolution_bitcast_fusion, f32[8,64,768]{2,1,0:T(8,128)S(1)} %collective-permute-done.2), kind=kLoop, calls=%fused_computation.1 | loop fusion | flops 7864320 | bytes 31457280 | tf_op jit(solution)/shard_map/concatenate | solution.py:122
  206.9 29.0 %divide_convert_fusion = bf16[64,64,768]{2,0,1:T(8,128)(2,1)S(1)} fusion(bf16[64,64,768]{2,1,0:T(8,128)(2,1)} %param.15, f32[64,64]{0,1:T(8,128)S(1)} %fusion.11, f32[64,80,1]{1,0,2:T(8,128)S(1)} %copy-done.10, f32[80,64,768]{2,1,0:T(8,128)} %pad_maximum_fusion), kind=kOutput, calls=%fused_computation.4 | convolution fusion | flops 1525678080 | bytes 28348416 | tf_op jit(solution)/shard_map/rk,kce->rce/dot_general | solution.py:124
  235.9 6.2 %copy.16 = bf16[64,64,768]{2,1,0:T(8,128)(2,1)} copy(bf16[64,64,768]{2,0,1:T(8,128)(2,1)S(1)} %divide_convert_fusion) | data formatting | bytes 12582912 | tf_op jit(solution)/shard_map/convert_element_type | solution.py:127
  (25 shorter events, 0.1 us)
Async XLA Ops:
  71.0 1.8 copy-start
  74.3 49.8 %copy-start.8 = (f32[64,8]{1,0:T(8,128)S(1)}, f32[64,8]{1,0:T(8,128)}, u32[]{:S(2)}) copy-start(f32[64,8]{1,0:T(8,128)} %constant.134) | copy-start | bytes 6148
  74.3 50.0 %copy-start.7 = (f32[64,48]{1,0:T(8,128)S(1)}, f32[64,48]{1,0:T(8,128)}, u32[]{:S(2)}) copy-start(f32[64,48]{1,0:T(8,128)} %constant.135) | copy-start | bytes 36868
  80.0 34.7 %copy-start.3 = (f32[512,128]{1,0:T(8,128)S(1)}, f32[512,128]{1,0:T(8,128)}, u32[]{:S(2)}) copy-start(f32[512,128]{1,0:T(8,128)} %get-tuple-element.50) | copy-start | bytes 786436
  80.0 44.4 %collective-permute-start = (f32[64,8,768]{2,1,0:T(8,128)}, f32[64,8,768]{2,1,0:T(8,128)}, u32[]{:S(2)}, u32[]{:S(2)}) collective-permute-start(f32[64,8,768]{2,1,0:T(8,128)} %bitcast.52), channel_id=1, source_target_pairs={{0,1},{1,2},{2,3},{3,4},{4,5},{5,6},{6,7},{8,9},{9,10},{10,11},{11... | collective-permute-start | bytes 4718600 | tf_op jit(solution)/shard_map/ppermute | solution.py:57
  109.0 18.2 %copy-start.2 = (f32[512,768]{1,0:T(8,128)S(1)}, f32[512,768]{1,0:T(8,128)}, u32[]{:S(2)}) copy-start(f32[512,768]{1,0:T(8,128)} %get-tuple-element.48) | copy-start | bytes 4718596
  109.0 40.5 %collective-permute-start.1 = (f32[64,8,768]{2,1,0:T(8,128)}, f32[64,8,768]{2,1,0:T(8,128)S(1)}, u32[]{:S(2)}, u32[]{:S(2)}) collective-permute-start(f32[64,8,768]{2,1,0:T(8,128)} %bitcast.53), channel_id=1, source_target_pairs={{1,0},{2,1},{3,2},{4,3},{5,4},{6,5},{7,6},{9,8},{10,9},{11,10},{12... | collective-permute-start | bytes 4718600 | tf_op jit(solution)/shard_map/ppermute | solution.py:57
  115.2 52.3 %collective-permute-start.4 = (f32[64,8]{1,0:T(8,128)S(1)}, f32[64,8]{1,0:T(8,128)S(1)}, u32[]{:S(2)}, u32[]{:S(2)}) collective-permute-start(f32[64,8]{1,0:T(8,128)S(1)} %reshape_squeeze.9), channel_id=1, source_target_pairs={{0,1},{1,2},{2,3},{3,4},{4,5},{5,6},{6,7},{8,9},{9,10},{10,11},{11... | collective-permute-start | bytes 6152 | tf_op jit(solution)/shard_map/ppermute | solution.py:57
  122.2 45.7 %collective-permute-start.5 = (f32[64,8]{1,0:T(8,128)S(1)}, f32[64,8]{1,0:T(8,128)S(1)}, u32[]{:S(2)}, u32[]{:S(2)}) collective-permute-start(f32[64,8]{1,0:T(8,128)S(1)} %reshape_squeeze.10), channel_id=1, source_target_pairs={{1,0},{2,1},{3,2},{4,3},{5,4},{6,5},{7,6},{9,8},{10,9},{11,10},{12... | collective-permute-start | bytes 6152 | tf_op jit(solution)/shard_map/ppermute | solution.py:57
  128.5 8.0 %copy-start.1 = (f32[512,768]{1,0:T(8,128)S(1)}, f32[512,768]{1,0:T(8,128)}, u32[]{:S(2)}) copy-start(f32[512,768]{1,0:T(8,128)} %get-tuple-element.47) | copy-start | bytes 4718596
  136.4 14.3 %copy-start.10 = (f32[64,80,1]{1,0,2:T(8,128)S(1)}, f32[64,80,1]{1,0,2:T(8,128)}, u32[]{:S(2)}) copy-start(f32[64,80,1]{1,0,2:T(8,128)} %constant.139) | copy-start | bytes 61444
  159.7 7.7 %copy-start.4 = (f32[64,8]{1,0:T(8,128)S(1)}, f32[64,8]{1,0:T(8,128)}, u32[]{:S(2)}) copy-start(f32[64,8]{1,0:T(8,128)} %constant.133) | copy-start | bytes 6148
  159.7 7.9 %copy-start.9 = (f32[64,8]{1,0:T(8,128)S(1)}, f32[64,8]{1,0:T(8,128)}, u32[]{:S(2)}) copy-start(f32[64,8]{1,0:T(8,128)} %constant.136) | copy-start | bytes 6148
  159.7 8.1 %copy-start.5 = (f32[64,8]{1,0:T(8,128)S(1)}, f32[64,8]{1,0:T(8,128)}, u32[]{:S(2)}) copy-start(f32[64,8]{1,0:T(8,128)} %constant.137) | copy-start | bytes 6148
  159.7 10.2 %copy-start.6 = (f32[64,64]{1,0:T(8,128)S(1)}, f32[64,64]{1,0:T(8,128)}, u32[]{:S(2)}) copy-start(f32[64,64]{1,0:T(8,128)} %constant.138) | copy-start | bytes 49156
  160.1 40.9 %collective-permute-start.3 = (f32[8,64,768]{2,1,0:T(8,128)S(1)}, f32[8,64,768]{2,1,0:T(8,128)S(1)}, u32[]{:S(2)}, u32[]{:S(2)}) collective-permute-start(f32[8,64,768]{2,1,0:T(8,128)S(1)} %get-tuple-element.54), channel_id=1, source_target_pairs={{8,0},{16,8},{24,16},{32,24},{40,32},{48,40},{56,48},{64,56},{72,6... | collective-permute-start | bytes 4718600 | tf_op jit(solution)/shard_map/ppermute | solution.py:57
  164.5 36.5 %collective-permute-start.2 = (f32[8,64,768]{2,1,0:T(8,128)S(1)}, f32[8,64,768]{2,1,0:T(8,128)S(1)}, u32[]{:S(2)}, u32[]{:S(2)}) collective-permute-start(f32[8,64,768]{2,1,0:T(8,128)S(1)} %get-tuple-element.53), channel_id=1, source_target_pairs={{0,8},{8,16},{16,24},{24,32},{32,40},{40,48},{48,56},{56,64},{64,7... | collective-permute-start | bytes 4718600 | tf_op jit(solution)/shard_map/ppermute | solution.py:57
  168.0 32.5 %collective-permute-start.7 = (f32[8,64]{1,0:T(8,128)S(1)}, f32[8,64]{1,0:T(8,128)S(1)}, u32[]{:S(2)}, u32[]{:S(2)}) collective-permute-start(f32[8,64]{1,0:T(8,128)S(1)} %get-tuple-element.56), channel_id=1, source_target_pairs={{8,0},{16,8},{24,16},{32,24},{40,32},{48,40},{56,48},{64,56},{72,6... | collective-permute-start | bytes 6152 | tf_op jit(solution)/shard_map/ppermute | solution.py:57
  170.2 30.6 %collective-permute-start.6 = (f32[8,64]{1,0:T(8,128)S(1)}, f32[8,64]{1,0:T(8,128)S(1)}, u32[]{:S(2)}, u32[]{:S(2)}) collective-permute-start(f32[8,64]{1,0:T(8,128)S(1)} %get-tuple-element.55), channel_id=1, source_target_pairs={{0,8},{8,16},{16,24},{24,32},{32,40},{40,48},{48,56},{56,64},{64,7... | collective-permute-start | bytes 6152 | tf_op jit(solution)/shard_map/ppermute | solution.py:57

commit v2 on v1

--- a/solution.py
+++ b/solution.py
@@ -5,6 +5,7 @@
 import numpy as np
 from jax import lax
 from jax.experimental import pallas as pl
+from jax.experimental.pallas import tpu as pltpu
 from jax.sharding import PartitionSpec as P
 
 RADIUS = 8
@@ -50,6 +51,45 @@
     )(ids.reshape(1, rows), docs)
 
 
+def finish(above, middle, below, codebook, inv):
+    rows, cols, feature = middle.shape
+    lanes = 128
+    taps = [math.exp(-2.0 * k * k / RADIUS**2) for k in range(RADIUS + 1)]
+
+    def kernel(above_ref, mid_ref, below_ref, cb_ref, inv_ref, out_ref, ext_ref):
+        ext_ref[0:RADIUS] = above_ref[...]
+        ext_ref[RADIUS : RADIUS + rows] = mid_ref[...]
+        ext_ref[RADIUS + rows :] = below_ref[...]
+
+        def body(r, carry):
+            centre = r + RADIUS
+            acc = taps[0] * ext_ref[centre]
+            for k in range(1, RADIUS + 1):
+                acc = acc + taps[k] * (ext_ref[centre - k] + ext_ref[centre + k])
+            upd = (acc + 8.0 * cb_ref[r].astype(jnp.float32)) * inv_ref[r]
+            out_ref[r] = upd.astype(out_ref.dtype)
+            return carry
+
+        lax.fori_loop(0, rows, body, 0, unroll=2)
+
+    halo_spec = pl.BlockSpec((RADIUS, cols, lanes), lambda j: (0, 0, j))
+    slab_spec = pl.BlockSpec((rows, cols, lanes), lambda j: (0, 0, j))
+    return pl.pallas_call(
+        kernel,
+        grid=(feature // lanes,),
+        in_specs=[
+            halo_spec,
+            slab_spec,
+            halo_spec,
+            slab_spec,
+            pl.BlockSpec((rows, cols, 1), lambda j: (0, 0, 0)),
+        ],
+        out_specs=slab_spec,
+        out_shape=jax.ShapeDtypeStruct(codebook.shape, codebook.dtype),
+        scratch_shapes=[pltpu.VMEM((rows + 2 * RADIUS, cols, lanes), jnp.float32)],
+    )(above, middle, below, codebook, inv)
+
+
 def exchange(lead, last, axis):
     devices = lax.axis_size(axis)
     up = [(i, i + 1) for i in range(devices - 1)]
@@ -90,41 +130,28 @@
     mark_row = got[:, feature].astype(jnp.int32)
     mark_col = got[:, feature + 1].astype(jnp.int32)
     unit_ids = jnp.where(got[:, feature + 2] > 0.5, mark_row * cols_tile + mark_col, -1)
-    inner = cols_tile - 2 * RADIUS
-    band_blocks = RADIUS * rows_tile // 512
-    inner_blocks = inner * rows_tile // 512
-
-    def band_unit(offset):
-        return lambda m: (m // RADIUS) * cols_tile + offset + m % RADIUS
-
-    num_l, cnt_l = accumulate(unit_ids, got, band_unit(0), band_blocks, feature)
-    num_r, cnt_r = accumulate(unit_ids, got, band_unit(cols_tile - RADIUS), band_blocks, feature)
-    band_shape = (rows_tile, RADIUS, feature)
-    num_l, num_r = num_l.reshape(band_shape), num_r.reshape(band_shape)
-    hits_l = cnt_l[:, 2].reshape(rows_tile, RADIUS)
-    hits_r = cnt_r[:, 2].reshape(rows_tile, RADIUS)
-    from_left, from_right = exchange(num_l, num_r, "my")
-    hits_from_left, hits_from_right = exchange(hits_l, hits_r, "my")
-    num_i, cnt_i = accumulate(
-        unit_ids, got, lambda m: (m // inner) * cols_tile + RADIUS + m % inner, inner_blocks, feature
+    numerator, counter = accumulate(
+        unit_ids, got, lambda m: m, rows_tile * cols_tile // 512, feature
     )
-    num_i = num_i.reshape(rows_tile, inner, feature)
-    hits_i = cnt_i[:, 2].reshape(rows_tile, inner)
+    numerator = numerator.reshape(rows_tile, cols_tile, feature)
+    counter = counter[:, 2].reshape(rows_tile, cols_tile)
 
     g_rows = jnp.asarray(band_matrix(rows_tile))
     g_cols = jnp.asarray(band_matrix(cols_tile))
-    ext_num = jnp.concatenate([from_left, num_l, num_i, num_r, from_right], axis=1)
-    ext_hits = jnp.concatenate([hits_from_left, hits_l, hits_i, hits_r, hits_from_right], axis=1)
+    last = cols_tile - RADIUS
+    from_left, from_right = exchange(numerator[:, :RADIUS], numerator[:, last:], "my")
+    hits_left, hits_right = exchange(counter[:, :RADIUS], counter[:, last:], "my")
+    ext_num = jnp.concatenate([from_left, numerator, from_right], axis=1)
+    ext_hits = jnp.concatenate([hits_left, counter, hits_right], axis=1)
     col_num = jnp.einsum("ck,rke->rce", g_cols, ext_num, precision=HI)
     col_hits = jnp.einsum("ck,rk->rc", g_cols, ext_hits, precision=HI)
-    above, below = exchange(col_num[:RADIUS], col_num[rows_tile - RADIUS :], "mx")
-    hits_above, hits_below = exchange(col_hits[:RADIUS], col_hits[rows_tile - RADIUS :], "mx")
-    ext_num = jnp.concatenate([above, col_num, below], axis=0)
+    last = rows_tile - RADIUS
+    above, below = exchange(col_num[:RADIUS], col_num[last:], "mx")
+    hits_above, hits_below = exchange(col_hits[:RADIUS], col_hits[last:], "mx")
     ext_hits = jnp.concatenate([hits_above, col_hits, hits_below], axis=0)
-    smooth_num = jnp.einsum("rk,kce->rce", g_rows, ext_num, precision=HI)
     smooth_hits = jnp.einsum("rk,kc->rc", g_rows, ext_hits, precision=HI)
-    updated = (smooth_num + 8.0 * codebook.astype(jnp.float32)) / (smooth_hits[:, :, None] + 8.0)
-    return updated.astype(jnp.bfloat16)
+    inv = (1.0 / (smooth_hits + 8.0))[:, :, None]
+    return finish(above, col_num, below, codebook, inv)
 
 
 def solution(mesh):

time: 243 us -> 223 us (0.918)
  matrix products: 39.4 us -> 10.5 us
  waiting for transfers between devices: 38.3 us -> 54.7 us
  Pallas kernels: 29.5 us -> 44.2 us
  local copies, waits for them, and re-layouts: 28.2 us -> 14.4 us
  other arithmetic: 22.1 us -> 14.3 us
    dot_general x1 -> x0, matrix products: 29 us -> none  [on_device(): smooth_num = jnp.einsum('rk,kce->rce', g_rows, ext_num, precision=HI)]
    pallas_call x0 -> x1, Pallas kernels: none -> 22.3 us  [finish(): pl.pallas_call(kernel, grid=(feature // lanes,), in_specs=[halo_spec, sla...]
    ppermute x8, waiting for transfers between devices: 38.3 us -> 54.7 us  [exchange(): return (lax.ppermute(last, axis, up), lax.ppermute(lead, axis, down))]
    unnamed x26 -> x18, local copies, waits for them, and re-layouts: 15.2 us -> 6.43 us
    pallas_call x3 -> x1, Pallas kernels: 29.5 us -> 21.9 us  [accumulate(): pl.pallas_call(kernel, grid=(blocks,), in_specs=[pl.BlockSpec((1, rows),...]
    convert_element_type x1 -> x0, local copies, waits for them, and re-layouts: 6.22 us -> none  [on_device(): return updated.astype(jnp.bfloat16)]
    concatenate x1 -> x0, other arithmetic: 5.87 us -> none  [on_device(): ext_num = jnp.concatenate([above, col_num, below], axis=0)]
    broadcast_in_dim x0 -> x1, local copies, waits for them, and re-layouts: none -> 2.93 us  [on_device(): inv = (1.0 / (smooth_hits + 8.0))[:, :, None]]
  transfers between devices with their start and end apart: 8 -> 8, of which waited for: 2 -> 4; matrix products, arithmetic and copies ran while one was open for 12% -> 2% of each run, Pallas kernels for 10% -> 0%
where the time goes in v2:
time: 223 us; the launch traced here: 222 us
  blocking collectives  54.9 us (25%)
  waiting for transfers between devices  54.7 us (25%)
  Pallas kernels  44.2 us (20%)
  starting transfers between devices  28.5 us (13%)
  local copies, waits for them, and re-layouts  14.4 us (6%)
  other arithmetic  14.3 us (6%)
  matrix products  10.5 us (5%)
    all_to_all x1, blocking collectives, on_device(): lax.all_to_all(outgoing.reshape(tile_total, capacity, width), ('mx', 'my'...  54.9 us
    ppermute x8, waiting for transfers between devices, exchange(): return (lax.ppermute(last, axis, up), lax.ppermute(lead, axis, down))  54.7 us
    ppermute x8, starting transfers between devices, exchange(): return (lax.ppermute(last, axis, up), lax.ppermute(lead, axis, down))  28.5 us
    pallas_call x1, Pallas kernels, finish(): pl.pallas_call(kernel, grid=(feature // lanes,), in_specs=[halo_spec, sla...  22.3 us
    pallas_call x1, Pallas kernels, accumulate(): pl.pallas_call(kernel, grid=(blocks,), in_specs=[pl.BlockSpec((1, rows),...  21.9 us
    dot_general x1, matrix products, on_device(): col_num = jnp.einsum('ck,rke->rce', g_cols, ext_num, precision=HI)  9.33 us
    scatter x1, other arithmetic, on_device(): jnp.zeros((tile_total * capacity, width), jnp.bfloat16).at[send_place]  7.65 us
    unnamed x18, local copies, waits for them, and re-layouts  6.43 us
  transfers between devices with their start and end apart: 8, of which 4 were waited for; matrix products, arithmetic and copies ran while one was open for 2% of the time, Pallas kernels for 0%

profile of v2, /device:TPU:15, one launch (start us, length us, event | category | flops | bytes accessed | tf_op | source)
XLA Modules:
  0.0 221.9 jit_solution(4810189552455840887)
XLA Ops:
  0.0 0.0 copy-start.7
  0.0 0.0 copy-start.3
  0.0 0.7 compare_reduce_fusion.2
  0.7 0.6 compare_reduce_fusion.1
  1.4 0.6 compare_reduce_fusion
  2.0 2.0 fusion.28
  4.1 0.8 copy.11
  4.9 0.1 scatter.19
  4.9 0.6 broadcast_select_fusion
  5.5 0.1 scatter.24
  5.6 0.2 copy.13
  5.8 0.2 fusion.21
  6.1 0.1 copy.12
  6.2 0.0 copy-done.7
  6.2 0.4 fusion.20
  6.6 0.0 copy-done.3
  6.6 7.6 %scatter_custom_fusion = bf16[2048,896]{1,0:T(8,128)(2,1)} fusion(s32[1024]{0:T(1024)S(1)} %bitcast.48, bf16[1024,128]{1,0:T(8,128)(2,1)S(1)} %copy.13, bf16[]{:T(256)} %constant.141, bf16[1024,768]{1,0:T(8,128)(2,1)S(1)} %copy-done.3, bf16[]{:T(256)} %constant.115.clone.1), kind=kCustom, calls=%fused_computation.9 | custom fusion | flops 3670016 | bytes 5505028 | tf_op jit(solution)/shard_map/scatter | solution.py:122
  14.2 54.9 %all_to_all.5 = bf16[128,16,896]{2,1,0:T(8,128)(2,1)S(1)} all-to-all(bf16[128,16,896]{2,1,0:T(8,128)(2,1)} %bitcast.43), channel_id=1, replica_groups=mesh['mx'=16,'my'=8] {'mx','my'}, dimensions={0} | all-to-all | bytes 7340032 | tf_op jit(solution)/shard_map/all_to_all | solution.py:123
  69.1 0.0 copy-start.1
  69.1 1.8 copy-done.1
  71.0 1.4 select_reduce_fusion
  72.3 21.9 %shard_map.64 = (f32[4096,768]{1,0:T(8,128)}, f32[4096,128]{1,0:T(8,128)}) custom-call(s32[1,2048]{1,0:T(1,128)} %bitcast.46, bf16[2048,896]{1,0:T(8,128)(2,1)} %bitcast.40), custom_call_target="tpu_custom_call" | custom-call | tf_op jit(solution)/shard_map/pallas_call | solution.py:36
  94.3 0.0 copy-start.2
  94.3 2.2 %fusion.32 = (f32[64,8,768]{2,1,0:T(8,128)S(1)}, f32[64,8,768]{2,1,0:T(8,128)S(1)}) fusion(f32[64,64,768]{2,1,0:T(8,128)} %bitcast.41), kind=kLoop, calls=%fused_computation.52 | loop fusion | bytes 6291456 | tf_op jit(solution)/shard_map/slice | solution.py:142
  96.5 0.0 copy-start.8
  96.5 5.0 %collective-permute-start = (f32[64,8,768]{2,1,0:T(8,128)S(1)}, f32[64,8,768]{2,1,0:T(8,128)}, u32[]{:S(2)}, u32[]{:S(2)}) collective-permute-start(f32[64,8,768]{2,1,0:T(8,128)S(1)} %get-tuple-element.47), channel_id=1, source_target_pairs={{0,1},{1,2},{2,3},{3,4},{4,5},{5,6},{6,7},{8,9},{9,10},{10,11},{11... | collective-permute-start | bytes 4718600 | tf_op jit(solution)/shard_map/ppermute | solution.py:97
  101.6 2.1 collective-permute-start.1
  103.7 0.0 copy-done.2
  103.7 1.2 slice_reduce_fusion
  104.9 0.1 reshape_squeeze.3
  104.9 29.4 %collective-permute-done = f32[64,8,768]{2,1,0:T(8,128)} collective-permute-done((f32[64,8,768]{2,1,0:T(8,128)S(1)}, f32[64,8,768]{2,1,0:T(8,128)}, u32[]{:S(2)}, u32[]{:S(2)}) %collective-permute-start) | collective-permute-done | bytes 1572896 | tf_op jit(solution)/shard_map/ppermute | solution.py:97
  134.3 7.5 %collective-permute-done.1 = f32[64,8,768]{2,1,0:T(8,128)} collective-permute-done((f32[64,8,768]{2,1,0:T(8,128)S(1)}, f32[64,8,768]{2,1,0:T(8,128)}, u32[]{:S(2)}, u32[]{:S(2)}) %collective-permute-start.1) | collective-permute-done | bytes 1572896 | tf_op jit(solution)/shard_map/ppermute | solution.py:97
  141.9 0.0 copy-done.8
  141.9 9.3 %fusion.6.mid_ref = f32[64,64,768]{2,1,0:T(8,128)S(1)} fusion(f32[64,80,1]{1,0,2:T(8,128)S(1)} %copy-done.8, f32[64,8,768]{2,1,0:T(8,128)} %collective-permute-done.1, f32[64,64,768]{2,1,0:T(8,128)} %bitcast.42, f32[64,8,768]{2,1,0:T(8,128)} %collective-permute-done), kind=kOutput, calls=%fused_computation.7 | convolution fusion | flops 1517813760 | bytes 28332032 | tf_op jit(solution)/shard_map/ck,rke->rce/dot_general | solution.py:146
  151.2 0.0 copy-start
  151.2 4.6 %copy-done = f32[64,64,768]{2,1,0:T(8,128)} copy-done((f32[64,64,768]{2,1,0:T(8,128)}, f32[64,64,768]{2,1,0:T(8,128)S(1)}, u32[]{:S(2)}) %copy-start) | copy-done | bytes 12582936
  155.8 0.0 copy-start.4
  155.8 0.0 copy-start.5
  155.8 0.0 copy-start.6
  155.8 0.3 fusion.31
  156.1 4.0 %collective-permute-start.3 = (f32[8,64,768]{2,1,0:T(8,128)S(1)}, f32[8,64,768]{2,1,0:T(8,128)}, u32[]{:S(2)}, u32[]{:S(2)}) collective-permute-start(f32[8,64,768]{2,1,0:T(8,128)S(1)} %get-tuple-element.45), channel_id=1, source_target_pairs={{8,0},{16,8},{24,16},{32,24},{40,32},{48,40},{56,48},{64,56},{72,6... | collective-permute-start | bytes 4718600 | tf_op jit(solution)/shard_map/ppermute | solution.py:97
  160.1 2.9 %collective-permute-start.2 = (f32[8,64,768]{2,1,0:T(8,128)S(1)}, f32[8,64,768]{2,1,0:T(8,128)}, u32[]{:S(2)}, u32[]{:S(2)}) collective-permute-start(f32[8,64,768]{2,1,0:T(8,128)S(1)} %get-tuple-element.46), channel_id=1, source_target_pairs={{0,8},{8,16},{16,24},{24,32},{32,40},{40,48},{48,56},{56,64},{64,7... | collective-permute-start | bytes 4718600 | tf_op jit(solution)/shard_map/ppermute | solution.py:97
  163.0 0.1 fusion.34
  163.1 1.9 collective-permute-start.5
  165.0 0.0 copy-done.4
  165.0 0.2 fusion.35
  165.2 7.0 %collective-permute-start.4 = (f32[64,8]{1,0:T(8,128)S(1)}, f32[64,8]{1,0:T(8,128)S(1)}, u32[]{:S(2)}, u32[]{:S(2)}) collective-permute-start(f32[64,8]{1,0:T(8,128)S(1)} %get-tuple-element.51), channel_id=1, source_target_pairs={{0,1},{1,2},{2,3},{3,4},{4,5},{5,6},{6,7},{8,9},{9,10},{10,11},{11... | collective-permute-start | bytes 6152 | tf_op jit(solution)/shard_map/ppermute | solution.py:97
  172.2 0.0 collective-permute-done.5
  172.2 0.0 copy-done.5
  172.2 0.2 fusion.36
  172.4 0.8 collective-permute-done.4
  173.2 0.0 copy-done.6
  173.2 0.2 fusion.18
  173.4 2.8 %collective-permute-start.7 = (f32[8,64]{1,0:T(8,128)S(1)}, f32[8,64]{1,0:T(8,128)S(1)}, u32[]{:S(2)}, u32[]{:S(2)}) collective-permute-start(f32[8,64]{1,0:T(8,128)S(1)} %get-tuple-element.50), channel_id=1, source_target_pairs={{8,0},{16,8},{24,16},{32,24},{40,32},{48,40},{56,48},{64,56},{72,6... | collective-permute-start | bytes 6152 | tf_op jit(solution)/shard_map/ppermute | solution.py:97
  176.1 0.2 fusion.37
  176.3 2.8 %collective-permute-start.6 = (f32[8,64]{1,0:T(8,128)S(1)}, f32[8,64]{1,0:T(8,128)S(1)}, u32[]{:S(2)}, u32[]{:S(2)}) collective-permute-start(f32[8,64]{1,0:T(8,128)S(1)} %get-tuple-element.49), channel_id=1, source_target_pairs={{0,8},{8,16},{16,24},{24,32},{32,40},{40,48},{48,56},{56,64},{64,7... | collective-permute-start | bytes 6152 | tf_op jit(solution)/shard_map/ppermute | solution.py:97
  179.2 17.0 %collective-permute-done.7 = f32[8,64]{1,0:T(8,128)S(1)} collective-permute-done((f32[8,64]{1,0:T(8,128)S(1)}, f32[8,64]{1,0:T(8,128)S(1)}, u32[]{:S(2)}, u32[]{:S(2)}) %collective-permute-start.7) | collective-permute-done | bytes 2080 | tf_op jit(solution)/shard_map/ppermute | solution.py:97
  196.2 0.2 fusion.38
  196.4 0.0 collective-permute-done.6
  196.4 0.2 fusion.17
  196.6 2.9 %copy.15.inv_ref = f32[64,64,1]{2,1,0:T(8,128)} copy(f32[64,64,1]{0,1,2:T(8,128)S(1)} %fusion.17) | data formatting | bytes 32768 | tf_op jit(solution)/shard_map/broadcast_in_dim | solution.py:153
  199.6 0.0 collective-permute-done.3.below_ref
  199.6 0.0 collective-permute-done.2.above_ref
  199.6 22.3 %shard_map.65 = bf16[64,64,768]{2,1,0:T(8,128)(2,1)} custom-call(f32[8,64,768]{2,1,0:T(8,128)} %collective-permute-done.2.above_ref, f32[64,64,768]{2,1,0:T(8,128)} %copy-done, f32[8,64,768]{2,1,0:T(8,128)} %collective-permute-done.3.below_ref, bf16[64,64,768]{2,1,0:T(8,128)(2,1)} %cb_ref.1, f32[64,64,1]{2,1,0:T(8,128)} %copy.15.inv_ref), custom_call_target="tpu_custom_call" | custom-call | tf_op jit(solution)/shard_map/pallas_call | solution.py:77
  (9 shorter events, 0.1 us)
Async XLA Ops:
  0.0 6.2 %copy-start.7 = (s32[1024,1]{0,1:T(1,128)S(1)}, s32[1024,1]{0,1:T(1,128)}, u32[]{:S(2)}) copy-start(s32[1024,1]{0,1:T(1,128)} %param.13) | copy-start | bytes 12292
  0.0 6.6 %copy-start.3 = (bf16[1024,768]{1,0:T(8,128)(2,1)S(1)}, bf16[1024,768]{1,0:T(8,128)(2,1)}, u32[]{:S(2)}) copy-start(bf16[1024,768]{1,0:T(8,128)(2,1)} %param.12) | copy-start | bytes 4718596
  69.1 1.8 copy-start.1
  94.3 9.4 %copy-start.2 = (f32[4096,128]{1,0:T(8,128)S(1)}, f32[4096,128]{1,0:T(8,128)}, u32[]{:S(2)}) copy-start(f32[4096,128]{1,0:T(8,128)} %get-tuple-element.44) | copy-start | bytes 6291460
  96.5 45.3 %copy-start.8 = (f32[64,80,1]{1,0,2:T(8,128)S(1)}, f32[64,80,1]{1,0,2:T(8,128)}, u32[]{:S(2)}) copy-start(f32[64,80,1]{1,0,2:T(8,128)} %constant.137) | copy-start | bytes 61444
  96.5 37.8 %collective-permute-start = (f32[64,8,768]{2,1,0:T(8,128)S(1)}, f32[64,8,768]{2,1,0:T(8,128)}, u32[]{:S(2)}, u32[]{:S(2)}) collective-permute-start(f32[64,8,768]{2,1,0:T(8,128)S(1)} %get-tuple-element.47), channel_id=1, source_target_pairs={{0,1},{1,2},{2,3},{3,4},{4,5},{5,6},{6,7},{8,9},{9,10},{10,11},{11... | collective-permute-start | bytes 4718600 | tf_op jit(solution)/shard_map/ppermute | solution.py:97
  101.6 40.3 %collective-permute-start.1 = (f32[64,8,768]{2,1,0:T(8,128)S(1)}, f32[64,8,768]{2,1,0:T(8,128)}, u32[]{:S(2)}, u32[]{:S(2)}) collective-permute-start(f32[64,8,768]{2,1,0:T(8,128)S(1)} %get-tuple-element.48), channel_id=1, source_target_pairs={{1,0},{2,1},{3,2},{4,3},{5,4},{6,5},{7,6},{9,8},{10,9},{11,10},{12... | collective-permute-start | bytes 4718600 | tf_op jit(solution)/shard_map/ppermute | solution.py:97
  151.2 4.6 %copy-start = (f32[64,64,768]{2,1,0:T(8,128)}, f32[64,64,768]{2,1,0:T(8,128)S(1)}, u32[]{:S(2)}) copy-start(f32[64,64,768]{2,1,0:T(8,128)S(1)} %fusion.6.mid_ref) | copy-start | bytes 37748740
  155.8 9.2 %copy-start.4 = (f32[64,64]{1,0:T(8,128)S(1)}, f32[64,64]{1,0:T(8,128)}, u32[]{:S(2)}) copy-start(f32[64,64]{1,0:T(8,128)} %constant.135) | copy-start | bytes 49156
  155.8 16.4 %copy-start.5 = (f32[64,8]{1,0:T(8,128)S(1)}, f32[64,8]{1,0:T(8,128)}, u32[]{:S(2)}) copy-start(f32[64,8]{1,0:T(8,128)} %constant.136) | copy-start | bytes 6148
  155.8 17.4 %copy-start.6 = (f32[64,8]{1,0:T(8,128)S(1)}, f32[64,8]{1,0:T(8,128)}, u32[]{:S(2)}) copy-start(f32[64,8]{1,0:T(8,128)} %constant.134) | copy-start | bytes 6148
  156.1 43.5 %collective-permute-start.3 = (f32[8,64,768]{2,1,0:T(8,128)S(1)}, f32[8,64,768]{2,1,0:T(8,128)}, u32[]{:S(2)}, u32[]{:S(2)}) collective-permute-start(f32[8,64,768]{2,1,0:T(8,128)S(1)} %get-tuple-element.45), channel_id=1, source_target_pairs={{8,0},{16,8},{24,16},{32,24},{40,32},{48,40},{56,48},{64,56},{72,6... | collective-permute-start | bytes 4718600 | tf_op jit(solution)/shard_map/ppermute | solution.py:97
  160.1 39.4 %collective-permute-start.2 = (f32[8,64,768]{2,1,0:T(8,128)S(1)}, f32[8,64,768]{2,1,0:T(8,128)}, u32[]{:S(2)}, u32[]{:S(2)}) collective-permute-start(f32[8,64,768]{2,1,0:T(8,128)S(1)} %get-tuple-element.46), channel_id=1, source_target_pairs={{0,8},{8,16},{16,24},{24,32},{32,40},{40,48},{48,56},{56,64},{64,7... | collective-permute-start | bytes 4718600 | tf_op jit(solution)/shard_map/ppermute | solution.py:97
  163.1 9.1 %collective-permute-start.5 = (f32[64,8]{1,0:T(8,128)S(1)}, f32[64,8]{1,0:T(8,128)S(1)}, u32[]{:S(2)}, u32[]{:S(2)}) collective-permute-start(f32[64,8]{1,0:T(8,128)S(1)} %get-tuple-element.52), channel_id=1, source_target_pairs={{1,0},{2,1},{3,2},{4,3},{5,4},{6,5},{7,6},{9,8},{10,9},{11,10},{12... | collective-permute-start | bytes 6152 | tf_op jit(solution)/shard_map/ppermute | solution.py:97
  165.2 8.0 %collective-permute-start.4 = (f32[64,8]{1,0:T(8,128)S(1)}, f32[64,8]{1,0:T(8,128)S(1)}, u32[]{:S(2)}, u32[]{:S(2)}) collective-permute-start(f32[64,8]{1,0:T(8,128)S(1)} %get-tuple-element.51), channel_id=1, source_target_pairs={{0,1},{1,2},{2,3},{3,4},{4,5},{5,6},{6,7},{8,9},{9,10},{10,11},{11... | collective-permute-start | bytes 6152 | tf_op jit(solution)/shard_map/ppermute | solution.py:97
  173.4 22.8 %collective-permute-start.7 = (f32[8,64]{1,0:T(8,128)S(1)}, f32[8,64]{1,0:T(8,128)S(1)}, u32[]{:S(2)}, u32[]{:S(2)}) collective-permute-start(f32[8,64]{1,0:T(8,128)S(1)} %get-tuple-element.50), channel_id=1, source_target_pairs={{8,0},{16,8},{24,16},{32,24},{40,32},{48,40},{56,48},{64,56},{72,6... | collective-permute-start | bytes 6152 | tf_op jit(solution)/shard_map/ppermute | solution.py:97
  176.3 20.1 %collective-permute-start.6 = (f32[8,64]{1,0:T(8,128)S(1)}, f32[8,64]{1,0:T(8,128)S(1)}, u32[]{:S(2)}, u32[]{:S(2)}) collective-permute-start(f32[8,64]{1,0:T(8,128)S(1)} %get-tuple-element.49), channel_id=1, source_target_pairs={{0,8},{8,16},{16,24},{24,32},{32,40},{40,48},{48,56},{56,64},{64,7... | collective-permute-start | bytes 6152 | tf_op jit(solution)/shard_map/ppermute | solution.py:97

commit v3 on v2

--- a/solution.py
+++ b/solution.py
@@ -51,15 +51,54 @@
     )(ids.reshape(1, rows), docs)
 
 
-def finish(above, middle, below, codebook, inv):
+def finish_inner(middle, codebook, inv):
     rows, cols, feature = middle.shape
     lanes = 128
+
+    def kernel(mid_ref, cb_ref, inv_ref, out_ref):
+        ext = mid_ref
+        taps = [math.exp(-2.0 * k * k / RADIUS**2) for k in range(RADIUS + 1)]
+
+        def body(r, carry):
+            acc = taps[0] * ext[r]
+            for k in range(1, RADIUS + 1):
+                acc = acc + taps[k] * (ext[r - k] + ext[r + k])
+            upd = (acc + 8.0 * cb_ref[r].astype(jnp.float32)) * inv_ref[r]
+            out_ref[r] = upd.astype(out_ref.dtype)
+            return carry
+
+        lax.fori_loop(RADIUS, rows - RADIUS, body, 0, unroll=2)
+
+    slab_spec = pl.BlockSpec((rows, cols, lanes), lambda j: (0, 0, j))
+    return pl.pallas_call(
+        kernel,
+        grid=(feature // lanes,),
+        in_specs=[slab_spec, slab_spec, pl.BlockSpec((rows, cols, 1), lambda j: (0, 0, 0))],
+        out_specs=slab_spec,
+        out_shape=jax.ShapeDtypeStruct(codebook.shape, codebook.dtype),
+    )(middle, codebook, inv)
+
+
+def finish_edges(above, middle, below, codebook, inv, partial):
+    rows, cols, feature = middle.shape
+    lanes = 128
+    near = 2 * RADIUS
+    last_edge = rows // RADIUS - 1
     taps = [math.exp(-2.0 * k * k / RADIUS**2) for k in range(RADIUS + 1)]
 
-    def kernel(above_ref, mid_ref, below_ref, cb_ref, inv_ref, out_ref, ext_ref):
-        ext_ref[0:RADIUS] = above_ref[...]
-        ext_ref[RADIUS : RADIUS + rows] = mid_ref[...]
-        ext_ref[RADIUS + rows :] = below_ref[...]
+    def kernel(above_ref, mid_ref, below_ref, cb_ref, inv_ref, prev_ref, out_ref, ext_ref):
+        del prev_ref
+        side = pl.program_id(0)
+
+        @pl.when(side == 0)
+        def _():
+            ext_ref[0:RADIUS] = above_ref[...]
+            ext_ref[RADIUS:] = mid_ref[...]
+
+        @pl.when(side == 1)
+        def _():
+            ext_ref[0:near] = mid_ref[...]
+            ext_ref[near:] = below_ref[...]
 
         def body(r, carry):
             centre = r + RADIUS
@@ -70,24 +109,26 @@
             out_ref[r] = upd.astype(out_ref.dtype)
             return carry
 
-        lax.fori_loop(0, rows, body, 0, unroll=2)
-
-    halo_spec = pl.BlockSpec((RADIUS, cols, lanes), lambda j: (0, 0, j))
-    slab_spec = pl.BlockSpec((rows, cols, lanes), lambda j: (0, 0, j))
+        lax.fori_loop(0, RADIUS, body, 0, unroll=2)
+
+    halo_spec = pl.BlockSpec((RADIUS, cols, lanes), lambda i, j: (0, 0, j))
+    edge_spec = pl.BlockSpec((RADIUS, cols, lanes), lambda i, j: (i * last_edge, 0, j))
     return pl.pallas_call(
         kernel,
-        grid=(feature // lanes,),
+        grid=(2, feature // lanes),
         in_specs=[
             halo_spec,
-            slab_spec,
+            pl.BlockSpec((near, cols, lanes), lambda i, j: (i * (rows // near - 1), 0, j)),
             halo_spec,
-            slab_spec,
-            pl.BlockSpec((rows, cols, 1), lambda j: (0, 0, 0)),
-        ],
-        out_specs=slab_spec,
+            edge_spec,
+            pl.BlockSpec((RADIUS, cols, 1), lambda i, j: (i * last_edge, 0, 0)),
+            pl.BlockSpec(memory_space=pl.ANY),
+        ],
+        out_specs=edge_spec,
         out_shape=jax.ShapeDtypeStruct(codebook.shape, codebook.dtype),
-        scratch_shapes=[pltpu.VMEM((rows + 2 * RADIUS, cols, lanes), jnp.float32)],
-    )(above, middle, below, codebook, inv)
+        scratch_shapes=[pltpu.VMEM((near + RADIUS, cols, lanes), jnp.float32)],
+        input_output_aliases={5: 0},
+    )(above, middle, below, codebook, inv, partial)
 
 
 def exchange(lead, last, axis):
@@ -151,7 +192,8 @@
     ext_hits = jnp.concatenate([hits_above, col_hits, hits_below], axis=0)
     smooth_hits = jnp.einsum("rk,kc->rc", g_rows, ext_hits, precision=HI)
     inv = (1.0 / (smooth_hits + 8.0))[:, :, None]
-    return finish(above, col_num, below, codebook, inv)
+    partial = finish_inner(col_num, codebook, inv)
+    return finish_edges(above, col_num, below, codebook, inv, partial)
 
 
 def solution(mesh):

time: 223 us -> 233 us (1.045)
  Pallas kernels: 44.2 us -> 51 us
  waiting for transfers between devices: 54.7 us -> 59.9 us
  starting transfers between devices: 28.5 us -> 23.8 us
  local copies, waits for them, and re-layouts: 14.4 us -> 17.6 us
    pallas_call x1 -> x2, Pallas kernels: 22.3 us -> 29 us  [the longest x1 17.1 us: finish_inner(): pl.pallas_call(kernel, grid=(feature // lanes,), in_specs=[slab_spec, sla...]
    ppermute x8, waiting for transfers between devices: 54.7 us -> 59.9 us  [exchange(): return (lax.ppermute(last, axis, up), lax.ppermute(lead, axis, down))]
    ppermute x8, starting transfers between devices: 28.5 us -> 23.8 us  [exchange(): return (lax.ppermute(last, axis, up), lax.ppermute(lead, axis, down))]
    unnamed x18 -> x22, local copies, waits for them, and re-layouts: 6.43 us -> 8.74 us
  transfers between devices with their start and end apart: 8 -> 8, of which waited for: 4 -> 4; matrix products, arithmetic and copies ran while one was open for 2% -> 7% of each run, Pallas kernels for 0% -> 7%
where the time goes in v3:
time: 233 us; the launch traced here: 232 us
  waiting for transfers between devices  59.9 us (26%)
  blocking collectives  54.9 us (24%)
  Pallas kernels  51 us (22%)
  starting transfers between devices  23.8 us (10%)
  local copies, waits for them, and re-layouts  17.6 us (8%)
  other arithmetic  14.3 us (6%)
  matrix products  10.5 us (5%)
    ppermute x8, waiting for transfers between devices, exchange(): return (lax.ppermute(last, axis, up), lax.ppermute(lead, axis, down))  59.9 us
    all_to_all x1, blocking collectives, on_device(): lax.all_to_all(outgoing.reshape(tile_total, capacity, width), ('mx', 'my'...  54.9 us
    ppermute x8, starting transfers between devices, exchange(): return (lax.ppermute(last, axis, up), lax.ppermute(lead, axis, down))  23.8 us
    pallas_call x1, Pallas kernels, accumulate(): pl.pallas_call(kernel, grid=(blocks,), in_specs=[pl.BlockSpec((1, rows),...  21.9 us
    pallas_call x1, Pallas kernels, finish_inner(): pl.pallas_call(kernel, grid=(feature // lanes,), in_specs=[slab_spec, sla...  17.1 us
    pallas_call x1, Pallas kernels, finish_edges(): pl.pallas_call(kernel, grid=(2, feature // lanes), in_specs=[halo_spec, p...  12 us
    dot_general x1, matrix products, on_device(): col_num = jnp.einsum('ck,rke->rce', g_cols, ext_num, precision=HI)  9.33 us
    unnamed x22, local copies, waits for them, and re-layouts  8.74 us
  transfers between devices with their start and end apart: 8, of which 4 were waited for; matrix products, arithmetic and copies ran while one was open for 7% of the time, Pallas kernels for 7%

profile of v3, /device:TPU:15, one launch (start us, length us, event | category | flops | bytes accessed | tf_op | source)
XLA Modules:
  0.0 232.3 jit_solution(16840008111881073695)
XLA Ops:
  0.0 0.0 copy-start.9
  0.0 0.0 copy-start.5
  0.0 0.7 compare_reduce_fusion.2
  0.7 0.6 compare_reduce_fusion.1
  1.4 0.6 compare_reduce_fusion
  2.0 2.0 fusion.28
  4.1 0.8 copy.12
  4.9 0.1 scatter.19
  4.9 0.6 broadcast_select_fusion
  5.5 0.1 scatter.24
  5.6 0.2 copy.14
  5.8 0.2 fusion.21
  6.1 0.1 copy.13
  6.2 0.0 copy-done.9
  6.2 0.4 fusion.20
  6.6 0.0 copy-done.5
  6.6 7.6 %scatter_custom_fusion = bf16[2048,896]{1,0:T(8,128)(2,1)} fusion(s32[1024]{0:T(1024)S(1)} %bitcast.48, bf16[1024,128]{1,0:T(8,128)(2,1)S(1)} %copy.14, bf16[]{:T(256)} %constant.141, bf16[1024,768]{1,0:T(8,128)(2,1)S(1)} %copy-done.5, bf16[]{:T(256)} %constant.115.clone.1), kind=kCustom, calls=%fused_computation.9 | custom fusion | flops 3670016 | bytes 5505028 | tf_op jit(solution)/shard_map/scatter | solution.py:163
  14.2 54.9 %all_to_all.5 = bf16[128,16,896]{2,1,0:T(8,128)(2,1)S(1)} all-to-all(bf16[128,16,896]{2,1,0:T(8,128)(2,1)} %bitcast.42), channel_id=1, replica_groups=mesh['mx'=16,'my'=8] {'mx','my'}, dimensions={0} | all-to-all | bytes 7340032 | tf_op jit(solution)/shard_map/all_to_all | solution.py:164
  69.1 0.0 copy-start.1
  69.1 1.8 copy-done.1
  71.0 1.4 select_reduce_fusion
  72.3 21.9 %shard_map.64 = (f32[4096,768]{1,0:T(8,128)}, f32[4096,128]{1,0:T(8,128)}) custom-call(s32[1,2048]{1,0:T(1,128)} %bitcast.46, bf16[2048,896]{1,0:T(8,128)(2,1)} %bitcast.39), custom_call_target="tpu_custom_call" | custom-call | tf_op jit(solution)/shard_map/pallas_call | solution.py:36
  94.3 2.2 fusion.32
  96.5 0.0 copy-start.10
  96.5 5.0 %collective-permute-start = (f32[64,8,768]{2,1,0:T(8,128)S(1)}, f32[64,8,768]{2,1,0:T(8,128)}, u32[]{:S(2)}, u32[]{:S(2)}) collective-permute-start(f32[64,8,768]{2,1,0:T(8,128)S(1)} %get-tuple-element.47), channel_id=1, source_target_pairs={{0,1},{1,2},{2,3},{3,4},{4,5},{5,6},{6,7},{8,9},{9,10},{10,11},{11... | collective-permute-start | bytes 4718600 | tf_op jit(solution)/shard_map/ppermute | solution.py:138
  101.6 1.9 collective-permute-start.1
  103.5 0.0 copy-done.2
  103.5 1.2 slice_reduce_fusion
  104.7 0.1 reshape_squeeze.3
  104.8 0.1 fusion.34
  104.8 2.1 collective-permute-start.5
  106.9 27.4 %collective-permute-done = f32[64,8,768]{2,1,0:T(8,128)} collective-permute-done((f32[64,8,768]{2,1,0:T(8,128)S(1)}, f32[64,8,768]{2,1,0:T(8,128)}, u32[]{:S(2)}, u32[]{:S(2)}) %collective-permute-start) | collective-permute-done | bytes 1572896 | tf_op jit(solution)/shard_map/ppermute | solution.py:138
  134.3 7.5 %collective-permute-done.1 = f32[64,8,768]{2,1,0:T(8,128)} collective-permute-done((f32[64,8,768]{2,1,0:T(8,128)S(1)}, f32[64,8,768]{2,1,0:T(8,128)}, u32[]{:S(2)}, u32[]{:S(2)}) %collective-permute-start.1) | collective-permute-done | bytes 1572896 | tf_op jit(solution)/shard_map/ppermute | solution.py:138
  141.9 0.0 copy-done.10
  141.9 9.3 %fusion.6.mid_ref = f32[64,64,768]{2,1,0:T(8,128)S(1)} fusion(f32[64,80,1]{1,0,2:T(8,128)S(1)} %copy-done.10, f32[64,8,768]{2,1,0:T(8,128)} %collective-permute-done.1, f32[64,64,768]{2,1,0:T(8,128)} %bitcast.41, f32[64,8,768]{2,1,0:T(8,128)} %collective-permute-done), kind=kOutput, calls=%fused_computation.7 | convolution fusion | flops 1517813760 | bytes 28332032 | tf_op jit(solution)/shard_map/ck,rke->rce/dot_general | solution.py:187
  151.2 0.0 copy-start
  151.2 4.6 %copy-done = f32[64,64,768]{2,1,0:T(8,128)} copy-done((f32[64,64,768]{2,1,0:T(8,128)}, f32[64,64,768]{2,1,0:T(8,128)S(1)}, u32[]{:S(2)}) %copy-start) | copy-done | bytes 12582936
  155.8 1.9 fusion.31
  157.7 4.4 %collective-permute-start.3 = (f32[8,64,768]{2,1,0:T(8,128)}, f32[8,64,768]{2,1,0:T(8,128)S(1)}, u32[]{:S(2)}, u32[]{:S(2)}) collective-permute-start(f32[8,64,768]{2,1,0:T(8,128)} %get-tuple-element.45), channel_id=1, source_target_pairs={{8,0},{16,8},{24,16},{32,24},{40,32},{48,40},{56,48},{64,56},{72,6... | collective-permute-start | bytes 4718600 | tf_op jit(solution)/shard_map/ppermute | solution.py:138
  162.1 2.9 %collective-permute-start.2 = (f32[8,64,768]{2,1,0:T(8,128)}, f32[8,64,768]{2,1,0:T(8,128)S(1)}, u32[]{:S(2)}, u32[]{:S(2)}) collective-permute-start(f32[8,64,768]{2,1,0:T(8,128)} %get-tuple-element.46), channel_id=1, source_target_pairs={{0,8},{8,16},{16,24},{24,32},{32,40},{40,48},{48,56},{56,64},{64,7... | collective-permute-start | bytes 4718600 | tf_op jit(solution)/shard_map/ppermute | solution.py:138
  165.0 0.0 copy-done.6
  165.0 0.2 fusion.35
  165.2 1.9 collective-permute-start.4
  167.1 0.0 collective-permute-done.5
  167.1 0.0 copy-done.7
  167.1 0.2 fusion.36
  167.3 3.2 %collective-permute-done.4 = f32[64,8]{1,0:T(8,128)S(1)} collective-permute-done((f32[64,8]{1,0:T(8,128)S(1)}, f32[64,8]{1,0:T(8,128)S(1)}, u32[]{:S(2)}, u32[]{:S(2)}) %collective-permute-start.4) | collective-permute-done | bytes 2080 | tf_op jit(solution)/shard_map/ppermute | solution.py:138
  170.5 0.0 copy-done.8
  170.5 0.2 fusion.18
  170.7 2.3 collective-permute-start.7
  173.0 0.2 fusion.37
  173.2 3.2 %collective-permute-start.6 = (f32[8,64]{1,0:T(8,128)S(1)}, f32[8,64]{1,0:T(8,128)S(1)}, u32[]{:S(2)}, u32[]{:S(2)}) collective-permute-start(f32[8,64]{1,0:T(8,128)S(1)} %get-tuple-element.49), channel_id=1, source_target_pairs={{0,8},{8,16},{16,24},{24,32},{32,40},{40,48},{48,56},{56,64},{64,7... | collective-permute-start | bytes 6152 | tf_op jit(solution)/shard_map/ppermute | solution.py:138
  176.5 21.9 %collective-permute-done.7 = f32[8,64]{1,0:T(8,128)S(1)} collective-permute-done((f32[8,64]{1,0:T(8,128)S(1)}, f32[8,64]{1,0:T(8,128)S(1)}, u32[]{:S(2)}, u32[]{:S(2)}) %collective-permute-start.7) | collective-permute-done | bytes 2080 | tf_op jit(solution)/shard_map/ppermute | solution.py:138
  198.3 0.2 fusion.38
  198.5 0.0 collective-permute-done.6
  198.5 0.2 fusion.17
  198.8 0.1 copy.15
  198.8 2.1 copy.17.inv_ref
  200.9 17.1 %shard_map.65.prev_ref = bf16[64,64,768]{2,1,0:T(8,128)(2,1)} custom-call(f32[64,64,768]{2,1,0:T(8,128)} %copy-done, bf16[64,64,768]{2,1,0:T(8,128)(2,1)} %cb_ref.3, f32[64,64,1]{2,1,0:T(8,128)} %copy.17.inv_ref), custom_call_target="tpu_custom_call" | custom-call | tf_op jit(solution)/shard_map/pallas_call | solution.py:73
  218.0 0.0 collective-permute-done.3.below_ref
  218.0 0.0 collective-permute-done.2.above_ref
  218.0 1.2 copy-done.3
  219.2 1.2 copy-done.4
  220.3 12.0 %shard_map.66 = bf16[64,64,768]{2,1,0:T(8,128)(2,1)} custom-call(f32[8,64,768]{2,1,0:T(8,128)} %copy-done.4, f32[64,64,768]{2,1,0:T(8,128)} %copy-done, f32[8,64,768]{2,1,0:T(8,128)} %copy-done.3, bf16[64,64,768]{2,1,0:T(8,128)(2,1)} %cb_ref.3, f32[64,64,1]{2,1,0:T(8,128)} %copy.17.inv_ref, ...), custom_call_target="tpu_custom_call", output_to_operand_aliasing={{}: (5, {})} | custom-call | tf_op jit(solution)/shard_map/pallas_call | solution.py:116
  (15 shorter events, 0.1 us)
Async XLA Ops:
  0.0 6.2 %copy-start.9 = (s32[1024,1]{0,1:T(1,128)S(1)}, s32[1024,1]{0,1:T(1,128)}, u32[]{:S(2)}) copy-start(s32[1024,1]{0,1:T(1,128)} %param.13) | copy-start | bytes 12292
  0.0 6.6 %copy-start.5 = (bf16[1024,768]{1,0:T(8,128)(2,1)S(1)}, bf16[1024,768]{1,0:T(8,128)(2,1)}, u32[]{:S(2)}) copy-start(bf16[1024,768]{1,0:T(8,128)(2,1)} %param.12) | copy-start | bytes 4718596
  69.1 1.8 copy-start.1
  94.3 9.2 %copy-start.2 = (f32[4096,128]{1,0:T(8,128)S(1)}, f32[4096,128]{1,0:T(8,128)}, u32[]{:S(2)}) copy-start(f32[4096,128]{1,0:T(8,128)} %get-tuple-element.44) | copy-start | bytes 6291460
  96.5 45.3 %copy-start.10 = (f32[64,80,1]{1,0,2:T(8,128)S(1)}, f32[64,80,1]{1,0,2:T(8,128)}, u32[]{:S(2)}) copy-start(f32[64,80,1]{1,0,2:T(8,128)} %constant.137) | copy-start | bytes 61444
  96.5 37.8 %collective-permute-start = (f32[64,8,768]{2,1,0:T(8,128)S(1)}, f32[64,8,768]{2,1,0:T(8,128)}, u32[]{:S(2)}, u32[]{:S(2)}) collective-permute-start(f32[64,8,768]{2,1,0:T(8,128)S(1)} %get-tuple-element.47), channel_id=1, source_target_pairs={{0,1},{1,2},{2,3},{3,4},{4,5},{5,6},{6,7},{8,9},{9,10},{10,11},{11... | collective-permute-start | bytes 4718600 | tf_op jit(solution)/shard_map/ppermute | solution.py:138
  101.6 40.3 %collective-permute-start.1 = (f32[64,8,768]{2,1,0:T(8,128)S(1)}, f32[64,8,768]{2,1,0:T(8,128)}, u32[]{:S(2)}, u32[]{:S(2)}) collective-permute-start(f32[64,8,768]{2,1,0:T(8,128)S(1)} %get-tuple-element.48), channel_id=1, source_target_pairs={{1,0},{2,1},{3,2},{4,3},{5,4},{6,5},{7,6},{9,8},{10,9},{11,10},{12... | collective-permute-start | bytes 4718600 | tf_op jit(solution)/shard_map/ppermute | solution.py:138
  104.8 62.3 %collective-permute-start.5 = (f32[64,8]{1,0:T(8,128)S(1)}, f32[64,8]{1,0:T(8,128)S(1)}, u32[]{:S(2)}, u32[]{:S(2)}) collective-permute-start(f32[64,8]{1,0:T(8,128)S(1)} %get-tuple-element.52), channel_id=1, source_target_pairs={{1,0},{2,1},{3,2},{4,3},{5,4},{6,5},{7,6},{9,8},{10,9},{11,10},{12... | collective-permute-start | bytes 6152 | tf_op jit(solution)/shard_map/ppermute | solution.py:138
  151.2 4.6 %copy-start = (f32[64,64,768]{2,1,0:T(8,128)}, f32[64,64,768]{2,1,0:T(8,128)S(1)}, u32[]{:S(2)}) copy-start(f32[64,64,768]{2,1,0:T(8,128)S(1)} %fusion.6.mid_ref) | copy-start | bytes 37748740
  155.8 9.2 %copy-start.6 = (f32[64,64]{1,0:T(8,128)S(1)}, f32[64,64]{1,0:T(8,128)}, u32[]{:S(2)}) copy-start(f32[64,64]{1,0:T(8,128)} %constant.135) | copy-start | bytes 49156
  155.8 11.3 %copy-start.7 = (f32[64,8]{1,0:T(8,128)S(1)}, f32[64,8]{1,0:T(8,128)}, u32[]{:S(2)}) copy-start(f32[64,8]{1,0:T(8,128)} %constant.136) | copy-start | bytes 6148
  155.8 14.7 %copy-start.8 = (f32[64,8]{1,0:T(8,128)S(1)}, f32[64,8]{1,0:T(8,128)}, u32[]{:S(2)}) copy-start(f32[64,8]{1,0:T(8,128)} %constant.134) | copy-start | bytes 6148
  157.7 60.2 %collective-permute-start.3 = (f32[8,64,768]{2,1,0:T(8,128)}, f32[8,64,768]{2,1,0:T(8,128)S(1)}, u32[]{:S(2)}, u32[]{:S(2)}) collective-permute-start(f32[8,64,768]{2,1,0:T(8,128)} %get-tuple-element.45), channel_id=1, source_target_pairs={{8,0},{16,8},{24,16},{32,24},{40,32},{48,40},{56,48},{64,56},{72,6... | collective-permute-start | bytes 4718600 | tf_op jit(solution)/shard_map/ppermute | solution.py:138
  162.1 55.9 %collective-permute-start.2 = (f32[8,64,768]{2,1,0:T(8,128)}, f32[8,64,768]{2,1,0:T(8,128)S(1)}, u32[]{:S(2)}, u32[]{:S(2)}) collective-permute-start(f32[8,64,768]{2,1,0:T(8,128)} %get-tuple-element.46), channel_id=1, source_target_pairs={{0,8},{8,16},{16,24},{24,32},{32,40},{40,48},{48,56},{56,64},{64,7... | collective-permute-start | bytes 4718600 | tf_op jit(solution)/shard_map/ppermute | solution.py:138
  165.2 5.3 %collective-permute-start.4 = (f32[64,8]{1,0:T(8,128)S(1)}, f32[64,8]{1,0:T(8,128)S(1)}, u32[]{:S(2)}, u32[]{:S(2)}) collective-permute-start(f32[64,8]{1,0:T(8,128)S(1)} %get-tuple-element.51), channel_id=1, source_target_pairs={{0,1},{1,2},{2,3},{3,4},{4,5},{5,6},{6,7},{8,9},{9,10},{10,11},{11... | collective-permute-start | bytes 6152 | tf_op jit(solution)/shard_map/ppermute | solution.py:138
  170.7 27.7 %collective-permute-start.7 = (f32[8,64]{1,0:T(8,128)S(1)}, f32[8,64]{1,0:T(8,128)S(1)}, u32[]{:S(2)}, u32[]{:S(2)}) collective-permute-start(f32[8,64]{1,0:T(8,128)S(1)} %get-tuple-element.50), channel_id=1, source_target_pairs={{8,0},{16,8},{24,16},{32,24},{40,32},{48,40},{56,48},{64,56},{72,6... | collective-permute-start | bytes 6152 | tf_op jit(solution)/shard_map/ppermute | solution.py:138
  173.2 25.3 %collective-permute-start.6 = (f32[8,64]{1,0:T(8,128)S(1)}, f32[8,64]{1,0:T(8,128)S(1)}, u32[]{:S(2)}, u32[]{:S(2)}) collective-permute-start(f32[8,64]{1,0:T(8,128)S(1)} %get-tuple-element.49), channel_id=1, source_target_pairs={{0,8},{8,16},{16,24},{24,32},{32,40},{40,48},{48,56},{56,64},{64,7... | collective-permute-start | bytes 6152 | tf_op jit(solution)/shard_map/ppermute | solution.py:138
  218.0 1.2 copy-start.3
  219.1 1.2 copy-start.4

commit v4 on v3

--- a/solution.py
+++ b/solution.py
@@ -102,31 +102,34 @@
 
         def body(r, carry):
             centre = r + RADIUS
-            acc = taps[0] * ext_ref[centre]
-            for k in range(1, RADIUS + 1):
-                acc = acc + taps[k] * (ext_ref[centre - k] + ext_ref[centre + k])
-            upd = (acc + 8.0 * cb_ref[r].astype(jnp.float32)) * inv_ref[r]
-            out_ref[r] = upd.astype(out_ref.dtype)
+            scale = inv_ref[r]
+            for lane in range(0, feature, lanes):
+                part = pl.ds(lane, lanes)
+                acc = taps[0] * ext_ref[centre, :, part]
+                for k in range(1, RADIUS + 1):
+                    acc = acc + taps[k] * (ext_ref[centre - k, :, part] + ext_ref[centre + k, :, part])
+                upd = (acc + 8.0 * cb_ref[r, :, part].astype(jnp.float32)) * scale
+                out_ref[r, :, part] = upd.astype(out_ref.dtype)
             return carry
 
-        lax.fori_loop(0, RADIUS, body, 0, unroll=2)
-
-    halo_spec = pl.BlockSpec((RADIUS, cols, lanes), lambda i, j: (0, 0, j))
-    edge_spec = pl.BlockSpec((RADIUS, cols, lanes), lambda i, j: (i * last_edge, 0, j))
+        lax.fori_loop(0, RADIUS, body, 0)
+
+    halo_spec = pl.BlockSpec((RADIUS, cols, feature), lambda i: (0, 0, 0))
+    edge_spec = pl.BlockSpec((RADIUS, cols, feature), lambda i: (i * last_edge, 0, 0))
     return pl.pallas_call(
         kernel,
-        grid=(2, feature // lanes),
+        grid=(2,),
         in_specs=[
             halo_spec,
-            pl.BlockSpec((near, cols, lanes), lambda i, j: (i * (rows // near - 1), 0, j)),
+            pl.BlockSpec((near, cols, feature), lambda i: (i * (rows // near - 1), 0, 0)),
             halo_spec,
             edge_spec,
-            pl.BlockSpec((RADIUS, cols, 1), lambda i, j: (i * last_edge, 0, 0)),
+            pl.BlockSpec((RADIUS, cols, 1), lambda i: (i, 0, 0)),
             pl.BlockSpec(memory_space=pl.ANY),
         ],
         out_specs=edge_spec,
         out_shape=jax.ShapeDtypeStruct(codebook.shape, codebook.dtype),
-        scratch_shapes=[pltpu.VMEM((near + RADIUS, cols, lanes), jnp.float32)],
+        scratch_shapes=[pltpu.VMEM((near + RADIUS, cols, feature), jnp.float32)],
         input_output_aliases={5: 0},
     )(above, middle, below, codebook, inv, partial)
 
@@ -189,11 +192,18 @@
     last = rows_tile - RADIUS
     above, below = exchange(col_num[:RADIUS], col_num[last:], "mx")
     hits_above, hits_below = exchange(col_hits[:RADIUS], col_hits[last:], "mx")
-    ext_hits = jnp.concatenate([hits_above, col_hits, hits_below], axis=0)
-    smooth_hits = jnp.einsum("rk,kc->rc", g_rows, ext_hits, precision=HI)
-    inv = (1.0 / (smooth_hits + 8.0))[:, :, None]
+    inner_hits = jnp.einsum("rk,kc->rc", g_rows[RADIUS:last, RADIUS : RADIUS + rows_tile], col_hits, precision=HI)
+    inv_inner = 1.0 / (inner_hits + 8.0)
+    inv = jnp.concatenate([jnp.zeros_like(inv_inner[:RADIUS]), inv_inner, jnp.zeros_like(inv_inner[:RADIUS])])
+    inv = inv[:, :, None]
+    edge_top = jnp.concatenate([hits_above, col_hits[: 2 * RADIUS]], axis=0)
+    edge_bottom = jnp.concatenate([col_hits[last - RADIUS :], hits_below], axis=0)
+    g_edge = g_rows[:RADIUS, : 3 * RADIUS]
+    top_hits = jnp.einsum("rk,kc->rc", g_edge, edge_top, precision=HI)
+    bottom_hits = jnp.einsum("rk,kc->rc", g_edge, edge_bottom, precision=HI)
+    inv_edges = (1.0 / (jnp.concatenate([top_hits, bottom_hits], axis=0) + 8.0))[:, :, None]
     partial = finish_inner(col_num, codebook, inv)
-    return finish_edges(above, col_num, below, codebook, inv, partial)
+    return finish_edges(above, col_num, below, codebook, inv_edges, partial)
 
 
 def solution(mesh):

time: 233 us -> 227 us (0.974); the launches traced: 232 us -> 224 us
  waiting for transfers between devices: 59.9 us -> 48.6 us
  starting transfers between devices: 23.8 us -> 30.8 us
  Pallas kernels: 51 us -> 47.7 us
    ppermute x8, waiting for transfers between devices: 59.9 us -> 48.6 us  [exchange(): return (lax.ppermute(last, axis, up), lax.ppermute(lead, axis, down))]
    ppermute x8, starting transfers between devices: 23.8 us -> 30.8 us  [exchange(): return (lax.ppermute(last, axis, up), lax.ppermute(lead, axis, down))]
    pallas_call x1, Pallas kernels: 12 us -> 8.7 us  [finish_edges(): pl.pallas_call(kernel, grid=(2,), in_specs=[halo_spec, pl.BlockSpec((near...]
    unnamed x22 -> x32, local copies, waits for them, and re-layouts: 8.74 us -> 7.62 us
  transfers between devices with their start and end apart: 8 -> 8, of which waited for: 4 -> 3; matrix products, arithmetic and copies ran while one was open for 7% -> 3% of each run, Pallas kernels for 7% -> 8%
where the time goes in v4:
time: 227 us; the launch traced here: 224 us
  blocking collectives  54.9 us (24%)
  waiting for transfers between devices  48.6 us (21%)
  Pallas kernels  47.7 us (21%)
  starting transfers between devices  30.8 us (14%)
  local copies, waits for them, and re-layouts  16.7 us (7%)
  other arithmetic  14.4 us (6%)
  matrix products  10.4 us (5%)
    all_to_all x1, blocking collectives, on_device(): lax.all_to_all(outgoing.reshape(tile_total, capacity, width), ('mx', 'my'...  54.9 us
    ppermute x8, waiting for transfers between devices, exchange(): return (lax.ppermute(last, axis, up), lax.ppermute(lead, axis, down))  48.6 us
    ppermute x8, starting transfers between devices, exchange(): return (lax.ppermute(last, axis, up), lax.ppermute(lead, axis, down))  30.8 us
    pallas_call x1, Pallas kernels, accumulate(): pl.pallas_call(kernel, grid=(blocks,), in_specs=[pl.BlockSpec((1, rows),...  21.9 us
    pallas_call x1, Pallas kernels, finish_inner(): pl.pallas_call(kernel, grid=(feature // lanes,), in_specs=[slab_spec, sla...  17 us
    dot_general x1, matrix products, on_device(): col_num = jnp.einsum('ck,rke->rce', g_cols, ext_num, precision=HI)  9.28 us
    pallas_call x1, Pallas kernels, finish_edges(): pl.pallas_call(kernel, grid=(2,), in_specs=[halo_spec, pl.BlockSpec((near...  8.7 us
    scatter x1, other arithmetic, on_device(): jnp.zeros((tile_total * capacity, width), jnp.bfloat16).at[send_place]  7.65 us
  transfers between devices with their start and end apart: 8, of which 3 were waited for; matrix products, arithmetic and copies ran while one was open for 3% of the time, Pallas kernels for 8%

profile of v4, /device:TPU:15, one launch (start us, length us, event | category | flops | bytes accessed | tf_op | source)
XLA Modules:
  0.0 223.8 jit_solution(9393389296701232436)
XLA Ops:
  0.0 0.6 compare_reduce_fusion.1
  0.6 0.6 compare_reduce_fusion.2
  1.3 0.6 compare_reduce_fusion
  1.9 0.8 copy.21
  2.7 0.2 fusion.21
  3.0 0.1 copy.22
  3.1 0.0 copy-done.5
  3.1 0.4 fusion.20
  3.5 0.0 copy-done.10
  3.5 1.3 fusion.32
  4.9 0.1 scatter.19
  4.9 0.6 broadcast_select_fusion
  5.5 0.1 scatter.24
  5.6 0.2 copy.23
  5.8 0.0 copy-done.4
  5.8 7.6 %scatter_custom_fusion = bf16[2048,896]{1,0:T(8,128)(2,1)} fusion(s32[1024]{0:T(1024)S(1)} %bitcast.53, bf16[1024,128]{1,0:T(8,128)(2,1)S(1)} %copy.23, bf16[]{:T(256)} %constant.153, bf16[1024,768]{1,0:T(8,128)(2,1)S(1)} %copy-done.4, bf16[]{:T(256)} %constant.118.clone.1), kind=kCustom, calls=%fused_computation.9 | custom fusion | flops 3670016 | bytes 5505028 | tf_op jit(solution)/shard_map/scatter | solution.py:166
  13.4 54.9 %all_to_all.5 = bf16[128,16,896]{2,1,0:T(8,128)(2,1)S(1)} all-to-all(bf16[128,16,896]{2,1,0:T(8,128)(2,1)} %bitcast.48), channel_id=1, replica_groups=mesh['mx'=16,'my'=8] {'mx','my'}, dimensions={0} | all-to-all | bytes 7340032 | tf_op jit(solution)/shard_map/all_to_all | solution.py:167
  68.3 1.8 copy-done.1
  70.1 1.4 select_reduce_fusion
  71.5 21.9 %shard_map.64 = (f32[4096,768]{1,0:T(8,128)}, f32[4096,128]{1,0:T(8,128)}) custom-call(s32[1,2048]{1,0:T(1,128)} %bitcast.51, bf16[2048,896]{1,0:T(8,128)(2,1)} %bitcast.45), custom_call_target="tpu_custom_call" | custom-call | tf_op jit(solution)/shard_map/pallas_call | solution.py:36
  93.5 2.2 %fusion.36 = (f32[64,8,768]{2,1,0:T(8,128)S(1)}, f32[64,8,768]{2,1,0:T(8,128)S(1)}) fusion(f32[64,64,768]{2,1,0:T(8,128)} %bitcast.46), kind=kLoop, calls=%fused_computation.61 | loop fusion | bytes 6291456 | tf_op jit(solution)/shard_map/slice | solution.py:186
  95.7 0.0 copy-start.8
  95.7 0.0 copy-start.7
  95.8 0.0 copy-start.6
  95.8 0.0 copy-start.9
  95.8 2.8 %collective-permute-start.1 = (f32[64,8,768]{2,1,0:T(8,128)S(1)}, f32[64,8,768]{2,1,0:T(8,128)}, u32[]{:S(2)}, u32[]{:S(2)}) collective-permute-start(f32[64,8,768]{2,1,0:T(8,128)S(1)} %get-tuple-element.48), channel_id=1, source_target_pairs={{1,0},{2,1},{3,2},{4,3},{5,4},{6,5},{7,6},{9,8},{10,9},{11,10},{12... | collective-permute-start | bytes 4718600 | tf_op jit(solution)/shard_map/ppermute | solution.py:141
  98.6 6.2 %collective-permute-start = (f32[64,8,768]{2,1,0:T(8,128)S(1)}, f32[64,8,768]{2,1,0:T(8,128)}, u32[]{:S(2)}, u32[]{:S(2)}) collective-permute-start(f32[64,8,768]{2,1,0:T(8,128)S(1)} %get-tuple-element.47), channel_id=1, source_target_pairs={{0,1},{1,2},{2,3},{3,4},{4,5},{5,6},{6,7},{8,9},{9,10},{10,11},{11... | collective-permute-start | bytes 4718600 | tf_op jit(solution)/shard_map/ppermute | solution.py:141
  104.8 0.0 copy-done.2
  104.8 1.2 slice_reduce_fusion
  106.0 0.1 reshape_squeeze.3
  106.1 0.1 fusion.38
  106.2 1.9 collective-permute-start.5
  108.1 0.2 fusion.39
  108.3 7.2 %collective-permute-start.4 = (f32[64,8]{1,0:T(8,128)S(1)}, f32[64,8]{1,0:T(8,128)S(1)}, u32[]{:S(2)}, u32[]{:S(2)}) collective-permute-start(f32[64,8]{1,0:T(8,128)S(1)} %get-tuple-element.51), channel_id=1, source_target_pairs={{0,1},{1,2},{2,3},{3,4},{4,5},{5,6},{6,7},{8,9},{9,10},{10,11},{11... | collective-permute-start | bytes 6152 | tf_op jit(solution)/shard_map/ppermute | solution.py:141
  115.4 22.3 %collective-permute-done.5 = f32[64,8]{1,0:T(8,128)S(1)} collective-permute-done((f32[64,8]{1,0:T(8,128)S(1)}, f32[64,8]{1,0:T(8,128)S(1)}, u32[]{:S(2)}, u32[]{:S(2)}) %collective-permute-start.5) | collective-permute-done | bytes 2080 | tf_op jit(solution)/shard_map/ppermute | solution.py:141
  137.7 0.2 fusion.40
  137.9 0.6 collective-permute-done.4
  138.5 0.2 fusion.14
  138.7 0.0 collective-permute-done.1
  138.7 0.0 collective-permute-done
  138.7 9.3 %fusion.6.mid_ref = f32[64,64,768]{2,1,0:T(8,128)S(1)} fusion(f32[64,80,1]{1,0,2:T(8,128)S(1)} %copy-done.9, f32[64,8,768]{2,1,0:T(8,128)} %collective-permute-done.1, f32[64,64,768]{2,1,0:T(8,128)} %bitcast.47, f32[64,8,768]{2,1,0:T(8,128)} %collective-permute-done), kind=kOutput, calls=%fused_computation.7 | convolution fusion | flops 1517813760 | bytes 28332032 | tf_op jit(solution)/shard_map/ck,rke->rce/dot_general | solution.py:190
  148.0 4.5 %copy-done = f32[64,64,768]{2,1,0:T(8,128)} copy-done((f32[64,64,768]{2,1,0:T(8,128)}, f32[64,64,768]{2,1,0:T(8,128)S(1)}, u32[]{:S(2)}) %copy-start) | copy-done | bytes 12582936
  152.6 2.0 fusion.35
  154.5 5.2 %collective-permute-start.2 = (f32[8,64,768]{2,1,0:T(8,128)}, f32[8,64,768]{2,1,0:T(8,128)S(1)}, u32[]{:S(2)}, u32[]{:S(2)}) collective-permute-start(f32[8,64,768]{2,1,0:T(8,128)} %get-tuple-element.46), channel_id=1, source_target_pairs={{0,8},{8,16},{16,24},{24,32},{32,40},{40,48},{48,56},{56,64},{64,7... | collective-permute-start | bytes 4718600 | tf_op jit(solution)/shard_map/ppermute | solution.py:141
  159.8 1.9 collective-permute-start.3
  161.7 3.0 %collective-permute-start.7 = (f32[8,64]{1,0:T(8,128)S(1)}, f32[8,64]{1,0:T(8,128)S(1)}, u32[]{:S(2)}, u32[]{:S(2)}) collective-permute-start(f32[8,64]{1,0:T(8,128)S(1)} %get-tuple-element.50), channel_id=1, source_target_pairs={{8,0},{16,8},{24,16},{32,24},{40,32},{48,40},{56,48},{64,56},{72,6... | collective-permute-start | bytes 6152 | tf_op jit(solution)/shard_map/ppermute | solution.py:141
  164.7 2.6 %collective-permute-start.6 = (f32[8,64]{1,0:T(8,128)S(1)}, f32[8,64]{1,0:T(8,128)S(1)}, u32[]{:S(2)}, u32[]{:S(2)}) collective-permute-start(f32[8,64]{1,0:T(8,128)S(1)} %get-tuple-element.49), channel_id=1, source_target_pairs={{0,8},{8,16},{16,24},{24,32},{32,40},{40,48},{48,56},{56,64},{64,7... | collective-permute-start | bytes 6152 | tf_op jit(solution)/shard_map/ppermute | solution.py:141
  167.3 0.1 fusion.24
  167.4 0.1 fusion.26
  167.5 0.2 fusion.16
  167.7 2.0 copy.26.inv_ref
  169.8 25.7 %collective-permute-done.7 = f32[8,64]{1,0:T(8,128)S(1)} collective-permute-done((f32[8,64]{1,0:T(8,128)S(1)}, f32[8,64]{1,0:T(8,128)S(1)}, u32[]{:S(2)}, u32[]{:S(2)}) %collective-permute-start.7) | collective-permute-done | bytes 2080 | tf_op jit(solution)/shard_map/ppermute | solution.py:141
  195.4 0.0 copy-done.12
  195.4 0.1 fusion.17
  195.5 0.0 collective-permute-done.6
  195.5 0.0 copy-done.11
  195.6 0.1 fusion.18
  195.7 0.3 copy.25
  195.9 0.9 broadcast_divide_fusion.inv_ref
  196.8 17.0 %shard_map.65.prev_ref = bf16[64,64,768]{2,1,0:T(8,128)(2,1)} custom-call(f32[64,64,768]{2,1,0:T(8,128)} %copy-done, bf16[64,64,768]{2,1,0:T(8,128)(2,1)} %cb_ref.3, f32[64,64,1]{2,1,0:T(8,128)} %copy.26.inv_ref), custom_call_target="tpu_custom_call" | custom-call | tf_op jit(solution)/shard_map/pallas_call | solution.py:73
  213.9 0.0 collective-permute-done.2.above_ref
  213.9 0.0 collective-permute-done.3.below_ref
  213.9 1.2 copy-done.3
  215.1 8.7 %shard_map.66 = bf16[64,64,768]{2,1,0:T(8,128)(2,1)} custom-call(f32[8,64,768]{2,1,0:T(8,128)} %copy-done.3, f32[64,64,768]{2,1,0:T(8,128)} %copy-done, f32[8,64,768]{2,1,0:T(8,128)} %collective-permute-done.3.below_ref, bf16[64,64,768]{2,1,0:T(8,128)(2,1)} %cb_ref.3, f32[16,64,1]{2,1,0:T(8,128)} %broadcast_divide_fusion.inv_ref, ...), custom_call_target="tpu_custom_call", output_to_operand_aliasing={{}: (5, {})} | custom-call | tf_op jit(solution)/shard_map/pallas_call | solution.py:119
  (31 shorter events, 0.2 us)
Async XLA Ops:
  0.0 3.1 %copy-start.5 = (s32[1024,1]{0,1:T(1,128)S(1)}, s32[1024,1]{0,1:T(1,128)}, u32[]{:S(2)}) copy-start(s32[1024,1]{0,1:T(1,128)} %param.13) | copy-start | bytes 12292
  0.0 3.5 %copy-start.10 = (s32[1024]{0:T(1024)S(1)}, s32[1024]{0:T(1024)}, u32[]{:S(2)}) copy-start(s32[1024]{0:T(1024)} %param.14) | copy-start | bytes 12292
  0.0 5.8 %copy-start.4 = (bf16[1024,768]{1,0:T(8,128)(2,1)S(1)}, bf16[1024,768]{1,0:T(8,128)(2,1)}, u32[]{:S(2)}) copy-start(bf16[1024,768]{1,0:T(8,128)(2,1)} %param.12) | copy-start | bytes 4718596
  68.3 1.8 copy-start.1
  93.5 11.3 %copy-start.2 = (f32[4096,128]{1,0:T(8,128)S(1)}, f32[4096,128]{1,0:T(8,128)}, u32[]{:S(2)}) copy-start(f32[4096,128]{1,0:T(8,128)} %get-tuple-element.44) | copy-start | bytes 6291460
  95.7 12.4 %copy-start.8 = (f32[64,64]{1,0:T(8,128)S(1)}, f32[64,64]{1,0:T(8,128)}, u32[]{:S(2)}) copy-start(f32[64,64]{1,0:T(8,128)} %constant.140) | copy-start | bytes 49156
  95.7 42.0 %copy-start.7 = (f32[64,8]{1,0:T(8,128)S(1)}, f32[64,8]{1,0:T(8,128)}, u32[]{:S(2)}) copy-start(f32[64,8]{1,0:T(8,128)} %constant.141) | copy-start | bytes 6148
  95.8 42.8 %copy-start.6 = (f32[64,8]{1,0:T(8,128)S(1)}, f32[64,8]{1,0:T(8,128)}, u32[]{:S(2)}) copy-start(f32[64,8]{1,0:T(8,128)} %constant.139) | copy-start | bytes 6148
  95.8 42.9 %copy-start.9 = (f32[64,80,1]{1,0,2:T(8,128)S(1)}, f32[64,80,1]{1,0,2:T(8,128)}, u32[]{:S(2)}) copy-start(f32[64,80,1]{1,0,2:T(8,128)} %constant.147) | copy-start | bytes 61444
  95.8 42.9 %collective-permute-start.1 = (f32[64,8,768]{2,1,0:T(8,128)S(1)}, f32[64,8,768]{2,1,0:T(8,128)}, u32[]{:S(2)}, u32[]{:S(2)}) collective-permute-start(f32[64,8,768]{2,1,0:T(8,128)S(1)} %get-tuple-element.48), channel_id=1, source_target_pairs={{1,0},{2,1},{3,2},{4,3},{5,4},{6,5},{7,6},{9,8},{10,9},{11,10},{12... | collective-permute-start | bytes 4718600 | tf_op jit(solution)/shard_map/ppermute | solution.py:141
  98.6 40.1 %collective-permute-start = (f32[64,8,768]{2,1,0:T(8,128)S(1)}, f32[64,8,768]{2,1,0:T(8,128)}, u32[]{:S(2)}, u32[]{:S(2)}) collective-permute-start(f32[64,8,768]{2,1,0:T(8,128)S(1)} %get-tuple-element.47), channel_id=1, source_target_pairs={{0,1},{1,2},{2,3},{3,4},{4,5},{5,6},{6,7},{8,9},{9,10},{10,11},{11... | collective-permute-start | bytes 4718600 | tf_op jit(solution)/shard_map/ppermute | solution.py:141
  106.2 31.6 %collective-permute-start.5 = (f32[64,8]{1,0:T(8,128)S(1)}, f32[64,8]{1,0:T(8,128)S(1)}, u32[]{:S(2)}, u32[]{:S(2)}) collective-permute-start(f32[64,8]{1,0:T(8,128)S(1)} %get-tuple-element.52), channel_id=1, source_target_pairs={{1,0},{2,1},{3,2},{4,3},{5,4},{6,5},{7,6},{9,8},{10,9},{11,10},{12... | collective-permute-start | bytes 6152 | tf_op jit(solution)/shard_map/ppermute | solution.py:141
  108.3 30.2 %collective-permute-start.4 = (f32[64,8]{1,0:T(8,128)S(1)}, f32[64,8]{1,0:T(8,128)S(1)}, u32[]{:S(2)}, u32[]{:S(2)}) collective-permute-start(f32[64,8]{1,0:T(8,128)S(1)} %get-tuple-element.51), channel_id=1, source_target_pairs={{0,1},{1,2},{2,3},{3,4},{4,5},{5,6},{6,7},{8,9},{9,10},{10,11},{11... | collective-permute-start | bytes 6152 | tf_op jit(solution)/shard_map/ppermute | solution.py:141
  148.0 4.5 %copy-start = (f32[64,64,768]{2,1,0:T(8,128)}, f32[64,64,768]{2,1,0:T(8,128)S(1)}, u32[]{:S(2)}) copy-start(f32[64,64,768]{2,1,0:T(8,128)S(1)} %fusion.6.mid_ref) | copy-start | bytes 37748740
  152.6 14.7 %copy-start.14 = (f32[8,16]{1,0:T(8,128)S(1)}, f32[8,16]{1,0:T(8,128)}, u32[]{:S(2)}) copy-start(f32[8,16]{1,0:T(8,128)} %constant.145) | copy-start | bytes 1540
  152.6 14.9 %copy-start.13 = (f32[8,16]{1,0:T(8,128)S(1)}, f32[8,16]{1,0:T(8,128)}, u32[]{:S(2)}) copy-start(f32[8,16]{1,0:T(8,128)} %constant.144) | copy-start | bytes 1540
  152.6 15.0 %copy-start.15 = (f32[48,64]{1,0:T(8,128)S(1)}, f32[48,64]{1,0:T(8,128)}, u32[]{:S(2)}) copy-start(f32[48,64]{1,0:T(8,128)} %constant.142) | copy-start | bytes 36868
  154.5 40.9 %copy-start.12 = (f32[8,8]{1,0:T(8,128)S(1)}, f32[8,8]{1,0:T(8,128)}, u32[]{:S(2)}) copy-start(f32[8,8]{1,0:T(8,128)} %constant.146) | copy-start | bytes 772
  154.5 41.0 %copy-start.11 = (f32[8,8]{1,0:T(8,128)S(1)}, f32[8,8]{1,0:T(8,128)}, u32[]{:S(2)}) copy-start(f32[8,8]{1,0:T(8,128)} %constant.143) | copy-start | bytes 772
  154.5 59.3 %collective-permute-start.2 = (f32[8,64,768]{2,1,0:T(8,128)}, f32[8,64,768]{2,1,0:T(8,128)S(1)}, u32[]{:S(2)}, u32[]{:S(2)}) collective-permute-start(f32[8,64,768]{2,1,0:T(8,128)} %get-tuple-element.46), channel_id=1, source_target_pairs={{0,8},{8,16},{16,24},{24,32},{32,40},{40,48},{48,56},{56,64},{64,7... | collective-permute-start | bytes 4718600 | tf_op jit(solution)/shard_map/ppermute | solution.py:141
  159.8 54.1 %collective-permute-start.3 = (f32[8,64,768]{2,1,0:T(8,128)}, f32[8,64,768]{2,1,0:T(8,128)}, u32[]{:S(2)}, u32[]{:S(2)}) collective-permute-start(f32[8,64,768]{2,1,0:T(8,128)} %get-tuple-element.45), channel_id=1, source_target_pairs={{8,0},{16,8},{24,16},{32,24},{40,32},{48,40},{56,48},{64,56},{72,6... | collective-permute-start | bytes 4718600 | tf_op jit(solution)/shard_map/ppermute | solution.py:141
  161.7 33.7 %collective-permute-start.7 = (f32[8,64]{1,0:T(8,128)S(1)}, f32[8,64]{1,0:T(8,128)S(1)}, u32[]{:S(2)}, u32[]{:S(2)}) collective-permute-start(f32[8,64]{1,0:T(8,128)S(1)} %get-tuple-element.50), channel_id=1, source_target_pairs={{8,0},{16,8},{24,16},{32,24},{40,32},{48,40},{56,48},{64,56},{72,6... | collective-permute-start | bytes 6152 | tf_op jit(solution)/shard_map/ppermute | solution.py:141
  164.7 30.9 %collective-permute-start.6 = (f32[8,64]{1,0:T(8,128)S(1)}, f32[8,64]{1,0:T(8,128)S(1)}, u32[]{:S(2)}, u32[]{:S(2)}) collective-permute-start(f32[8,64]{1,0:T(8,128)S(1)} %get-tuple-element.49), channel_id=1, source_target_pairs={{0,8},{8,16},{16,24},{24,32},{32,40},{40,48},{48,56},{56,64},{64,7... | collective-permute-start | bytes 6152 | tf_op jit(solution)/shard_map/ppermute | solution.py:141
  213.9 1.2 copy-start.3

commit v5 on v4

--- a/solution.py
+++ b/solution.py
@@ -183,7 +183,9 @@
     g_rows = jnp.asarray(band_matrix(rows_tile))
     g_cols = jnp.asarray(band_matrix(cols_tile))
     last = cols_tile - RADIUS
-    from_left, from_right = exchange(numerator[:, :RADIUS], numerator[:, last:], "my")
+    lead = numerator[:, :RADIUS].astype(jnp.bfloat16)
+    from_left, from_right = exchange(lead, numerator[:, last:].astype(jnp.bfloat16), "my")
+    from_left, from_right = from_left.astype(jnp.float32), from_right.astype(jnp.float32)
     hits_left, hits_right = exchange(counter[:, :RADIUS], counter[:, last:], "my")
     ext_num = jnp.concatenate([from_left, numerator, from_right], axis=1)
     ext_hits = jnp.concatenate([hits_left, counter, hits_right], axis=1)

time: 227 us -> 216 us (0.952)
  waiting for transfers between devices: 48.6 us -> 31.9 us
  other arithmetic: 14.4 us -> 22.3 us
    ppermute x8, waiting for transfers between devices: 48.6 us -> 31.9 us  [exchange(): return (lax.ppermute(last, axis, up), lax.ppermute(lead, axis, down))]
    another operation x8 -> x9, other arithmetic: 4.03 us -> 10.4 us
    unnamed x32 -> x28, local copies, waits for them, and re-layouts: 7.62 us -> 7.63 us
where the time goes in v5:
time: 216 us; the launch traced here: 213 us
  blocking collectives  54.9 us (25%)
  Pallas kernels  47.6 us (22%)
  waiting for transfers between devices  31.9 us (15%)
  starting transfers between devices  30.5 us (14%)
  other arithmetic  22.3 us (10%)
  local copies, waits for them, and re-layouts  15.7 us (7%)
  matrix products  9.72 us (5%)
    all_to_all x1, blocking collectives, on_device(): lax.all_to_all(outgoing.reshape(tile_total, capacity, width), ('mx', 'my'...  54.9 us
    ppermute x8, waiting for transfers between devices, exchange(): return (lax.ppermute(last, axis, up), lax.ppermute(lead, axis, down))  31.9 us
    ppermute x8, starting transfers between devices, exchange(): return (lax.ppermute(last, axis, up), lax.ppermute(lead, axis, down))  30.5 us
    pallas_call x1, Pallas kernels, accumulate(): pl.pallas_call(kernel, grid=(blocks,), in_specs=[pl.BlockSpec((1, rows),...  21.9 us
    pallas_call x1, Pallas kernels, finish_inner(): pl.pallas_call(kernel, grid=(feature // lanes,), in_specs=[slab_spec, sla...  17 us
    another operation x9, other arithmetic  10.4 us
    pallas_call x1, Pallas kernels, finish_edges(): pl.pallas_call(kernel, grid=(2,), in_specs=[halo_spec, pl.BlockSpec((near...  8.7 us
    dot_general x1, matrix products, on_device(): col_num = jnp.einsum('ck,rke->rce', g_cols, ext_num, precision=HI)  8.6 us
  transfers between devices with their start and end apart: 8, of which 3 were waited for; matrix products, arithmetic and copies ran while one was open for 3% of the time, Pallas kernels for 8%

profile of v5, /device:TPU:15, one launch (start us, length us, event | category | flops | bytes accessed | tf_op | source)
XLA Modules:
  0.0 213.1 jit_solution(17846057173887224518)
XLA Ops:
  0.0 0.6 compare_reduce_fusion.1
  0.6 0.7 compare_reduce_fusion.2
  1.3 0.7 compare_reduce_fusion
  2.0 0.8 copy.21
  2.8 0.2 fusion.21
  3.1 0.1 copy.22
  3.2 1.0 fusion.20
  4.3 0.7 compare_select_fusion
  5.0 2.0 fusion.32
  7.0 0.1 scatter.19
  7.1 0.6 broadcast_select_fusion
  7.7 0.1 scatter.24
  7.8 0.2 copy.23
  8.0 7.6 %scatter_custom_fusion = bf16[2048,896]{1,0:T(8,128)(2,1)} fusion(s32[1024]{0:T(1024)S(1)} %bitcast.53, bf16[1024,128]{1,0:T(8,128)(2,1)S(1)} %copy.23, bf16[]{:T(256)} %constant.153, bf16[1024,768]{1,0:T(8,128)(2,1)S(1)} %copy-done.4, bf16[]{:T(256)} %constant.118.clone.1), kind=kCustom, calls=%fused_computation.9 | custom fusion | flops 3670016 | bytes 5505028 | tf_op jit(solution)/shard_map/scatter | solution.py:166
  15.6 54.9 %all_to_all.5 = bf16[128,16,896]{2,1,0:T(8,128)(2,1)S(1)} all-to-all(bf16[128,16,896]{2,1,0:T(8,128)(2,1)} %bitcast.48), channel_id=1, replica_groups=mesh['mx'=16,'my'=8] {'mx','my'}, dimensions={0} | all-to-all | bytes 7340032 | tf_op jit(solution)/shard_map/all_to_all | solution.py:167
  70.5 1.8 copy-done.1
  72.3 1.4 select_reduce_fusion
  73.7 21.9 %shard_map.64 = (f32[4096,768]{1,0:T(8,128)}, f32[4096,128]{1,0:T(8,128)}) custom-call(s32[1,2048]{1,0:T(1,128)} %bitcast.51, bf16[2048,896]{1,0:T(8,128)(2,1)} %bitcast.47), custom_call_target="tpu_custom_call" | custom-call | tf_op jit(solution)/shard_map/pallas_call | solution.py:36
  95.6 5.5 %convert.4 = bf16[64,64,768]{2,1,0:T(8,128)(2,1)S(1)} convert(f32[64,64,768]{2,1,0:T(8,128)} %bitcast.44) | non-fusion elementwise | flops 3145728 | bytes 18874368 | tf_op jit(solution)/shard_map/convert.1
  101.2 0.0 copy-start.7
  101.2 0.0 copy-start.6
  101.2 0.0 copy-start.5
  101.2 1.3 fusion.36
  102.5 2.7 %collective-permute-start.1 = (bf16[64,8,768]{2,1,0:T(8,128)(2,1)}, bf16[64,8,768]{2,1,0:T(8,128)(2,1)S(1)}, u32[]{:S(2)}, u32[]{:S(2)}) collective-permute-start(bf16[64,8,768]{2,1,0:T(8,128)(2,1)} %get-tuple-element.48), channel_id=1, source_target_pairs={{1,0},{2,1},{3,2},{4,3},{5,4},{6,5},{7,6},{9,8},{10,9},{11,10},{12... | collective-permute-start | bytes 2359304 | tf_op jit(solution)/shard_map/ppermute | solution.py:141
  105.2 6.2 %collective-permute-start = (bf16[64,8,768]{2,1,0:T(8,128)(2,1)}, bf16[64,8,768]{2,1,0:T(8,128)(2,1)S(1)}, u32[]{:S(2)}, u32[]{:S(2)}) collective-permute-start(bf16[64,8,768]{2,1,0:T(8,128)(2,1)} %get-tuple-element.47), channel_id=1, source_target_pairs={{0,1},{1,2},{2,3},{3,4},{4,5},{5,6},{6,7},{8,9},{9,10},{10,11},{11... | collective-permute-start | bytes 2359304 | tf_op jit(solution)/shard_map/ppermute | solution.py:141
  111.4 0.0 copy-start.8
  111.4 1.2 slice_reduce_fusion
  112.6 0.1 reshape_squeeze.3
  112.6 0.1 fusion.38
  112.7 1.9 collective-permute-start.5
  114.7 0.2 fusion.39
  114.8 7.2 %collective-permute-start.4 = (f32[64,8]{1,0:T(8,128)S(1)}, f32[64,8]{1,0:T(8,128)S(1)}, u32[]{:S(2)}, u32[]{:S(2)}) collective-permute-start(f32[64,8]{1,0:T(8,128)S(1)} %get-tuple-element.51), channel_id=1, source_target_pairs={{0,1},{1,2},{2,3},{3,4},{4,5},{5,6},{6,7},{8,9},{9,10},{10,11},{11... | collective-permute-start | bytes 6152 | tf_op jit(solution)/shard_map/ppermute | solution.py:141
  122.0 5.5 %collective-permute-done.5 = f32[64,8]{1,0:T(8,128)S(1)} collective-permute-done((f32[64,8]{1,0:T(8,128)S(1)}, f32[64,8]{1,0:T(8,128)S(1)}, u32[]{:S(2)}, u32[]{:S(2)}) %collective-permute-start.5) | collective-permute-done | bytes 2080 | tf_op jit(solution)/shard_map/ppermute | solution.py:141
  127.5 0.2 fusion.40
  127.7 0.7 collective-permute-done.4
  128.4 0.2 fusion.14
  128.6 0.0 collective-permute-done.1
  128.6 0.1 convert_element_type.50
  128.7 0.0 collective-permute-done
  128.7 0.1 convert_element_type.49
  128.8 8.6 %fusion.6.mid_ref = f32[64,64,768]{2,1,0:T(8,128)S(1)} fusion(f32[64,80,1]{1,0,2:T(8,128)S(1)} %copy-done.8, f32[64,8,768]{2,1,0:T(8,128)S(1)} %convert_element_type.50, f32[64,64,768]{2,1,0:T(8,128)} %bitcast.45, f32[64,8,768]{2,1,0:T(8,128)S(1)} %convert_element_type.49), kind=kOutput, calls=%fused_computation.7 | convolution fusion | flops 1517813760 | bytes 28332032 | tf_op jit(solution)/shard_map/ck,rke->rce/dot_general | solution.py:192
  137.5 4.5 %copy-done = f32[64,64,768]{2,1,0:T(8,128)} copy-done((f32[64,64,768]{2,1,0:T(8,128)}, f32[64,64,768]{2,1,0:T(8,128)S(1)}, u32[]{:S(2)}) %copy-start) | copy-done | bytes 12582936
  142.0 0.0 copy-start.9
  142.0 2.0 fusion.35
  144.0 5.1 %collective-permute-start.2 = (f32[8,64,768]{2,1,0:T(8,128)}, f32[8,64,768]{2,1,0:T(8,128)S(1)}, u32[]{:S(2)}, u32[]{:S(2)}) collective-permute-start(f32[8,64,768]{2,1,0:T(8,128)} %get-tuple-element.46), channel_id=1, source_target_pairs={{0,8},{8,16},{16,24},{24,32},{32,40},{40,48},{48,56},{56,64},{64,7... | collective-permute-start | bytes 4718600 | tf_op jit(solution)/shard_map/ppermute | solution.py:141
  149.1 1.9 collective-permute-start.3
  151.1 3.0 %collective-permute-start.7 = (f32[8,64]{1,0:T(8,128)S(1)}, f32[8,64]{1,0:T(8,128)S(1)}, u32[]{:S(2)}, u32[]{:S(2)}) collective-permute-start(f32[8,64]{1,0:T(8,128)S(1)} %get-tuple-element.50), channel_id=1, source_target_pairs={{8,0},{16,8},{24,16},{32,24},{40,32},{48,40},{56,48},{64,56},{72,6... | collective-permute-start | bytes 6152 | tf_op jit(solution)/shard_map/ppermute | solution.py:141
  154.0 2.6 %collective-permute-start.6 = (f32[8,64]{1,0:T(8,128)S(1)}, f32[8,64]{1,0:T(8,128)S(1)}, u32[]{:S(2)}, u32[]{:S(2)}) collective-permute-start(f32[8,64]{1,0:T(8,128)S(1)} %get-tuple-element.49), channel_id=1, source_target_pairs={{0,8},{8,16},{16,24},{24,32},{32,40},{40,48},{48,56},{56,64},{64,7... | collective-permute-start | bytes 6152 | tf_op jit(solution)/shard_map/ppermute | solution.py:141
  156.6 0.1 fusion.24
  156.8 0.1 fusion.26
  156.9 0.2 fusion.16
  157.1 2.0 copy.26.inv_ref
  159.1 25.7 %collective-permute-done.7 = f32[8,64]{1,0:T(8,128)S(1)} collective-permute-done((f32[8,64]{1,0:T(8,128)S(1)}, f32[8,64]{1,0:T(8,128)S(1)}, u32[]{:S(2)}, u32[]{:S(2)}) %collective-permute-start.7) | collective-permute-done | bytes 2080 | tf_op jit(solution)/shard_map/ppermute | solution.py:141
  184.8 0.1 fusion.17
  184.9 0.0 collective-permute-done.6
  184.9 0.0 copy-done.9
  184.9 0.1 fusion.18
  185.0 0.3 copy.25
  185.3 0.9 broadcast_divide_fusion.inv_ref
  186.2 17.0 %shard_map.65.prev_ref = bf16[64,64,768]{2,1,0:T(8,128)(2,1)} custom-call(f32[64,64,768]{2,1,0:T(8,128)} %copy-done, bf16[64,64,768]{2,1,0:T(8,128)(2,1)} %cb_ref.3, f32[64,64,1]{2,1,0:T(8,128)} %copy.26.inv_ref), custom_call_target="tpu_custom_call" | custom-call | tf_op jit(solution)/shard_map/pallas_call | solution.py:73
  203.2 0.0 collective-permute-done.2.above_ref
  203.2 0.0 collective-permute-done.3.below_ref
  203.2 1.2 copy-done.3
  204.4 8.7 %shard_map.66 = bf16[64,64,768]{2,1,0:T(8,128)(2,1)} custom-call(f32[8,64,768]{2,1,0:T(8,128)} %copy-done.3, f32[64,64,768]{2,1,0:T(8,128)} %copy-done, f32[8,64,768]{2,1,0:T(8,128)} %collective-permute-done.3.below_ref, bf16[64,64,768]{2,1,0:T(8,128)(2,1)} %cb_ref.3, f32[16,64,1]{2,1,0:T(8,128)} %broadcast_divide_fusion.inv_ref, ...), custom_call_target="tpu_custom_call", output_to_operand_aliasing={{}: (5, {})} | custom-call | tf_op jit(solution)/shard_map/pallas_call | solution.py:119
  (30 shorter events, 0.2 us)
Async XLA Ops:
  0.0 7.9 %copy-start.4 = (bf16[1024,768]{1,0:T(8,128)(2,1)S(1)}, bf16[1024,768]{1,0:T(8,128)(2,1)}, u32[]{:S(2)}) copy-start(bf16[1024,768]{1,0:T(8,128)(2,1)} %param.12) | copy-start | bytes 4718596
  70.5 1.8 copy-start.1
  101.2 10.2 %copy-start.2 = (f32[4096,128]{1,0:T(8,128)S(1)}, f32[4096,128]{1,0:T(8,128)}, u32[]{:S(2)}) copy-start(f32[4096,128]{1,0:T(8,128)} %get-tuple-element.44) | copy-start | bytes 6291460
  101.2 13.5 %copy-start.7 = (f32[64,64]{1,0:T(8,128)S(1)}, f32[64,64]{1,0:T(8,128)}, u32[]{:S(2)}) copy-start(f32[64,64]{1,0:T(8,128)} %constant.140) | copy-start | bytes 49156
  101.2 26.4 %copy-start.6 = (f32[64,8]{1,0:T(8,128)S(1)}, f32[64,8]{1,0:T(8,128)}, u32[]{:S(2)}) copy-start(f32[64,8]{1,0:T(8,128)} %constant.141) | copy-start | bytes 6148
  101.2 27.2 %copy-start.5 = (f32[64,8]{1,0:T(8,128)S(1)}, f32[64,8]{1,0:T(8,128)}, u32[]{:S(2)}) copy-start(f32[64,8]{1,0:T(8,128)} %constant.139) | copy-start | bytes 6148
  102.5 26.1 %collective-permute-start.1 = (bf16[64,8,768]{2,1,0:T(8,128)(2,1)}, bf16[64,8,768]{2,1,0:T(8,128)(2,1)S(1)}, u32[]{:S(2)}, u32[]{:S(2)}) collective-permute-start(bf16[64,8,768]{2,1,0:T(8,128)(2,1)} %get-tuple-element.48), channel_id=1, source_target_pairs={{1,0},{2,1},{3,2},{4,3},{5,4},{6,5},{7,6},{9,8},{10,9},{11,10},{12... | collective-permute-start | bytes 2359304 | tf_op jit(solution)/shard_map/ppermute | solution.py:141
  105.2 23.5 %collective-permute-start = (bf16[64,8,768]{2,1,0:T(8,128)(2,1)}, bf16[64,8,768]{2,1,0:T(8,128)(2,1)S(1)}, u32[]{:S(2)}, u32[]{:S(2)}) collective-permute-start(bf16[64,8,768]{2,1,0:T(8,128)(2,1)} %get-tuple-element.47), channel_id=1, source_target_pairs={{0,1},{1,2},{2,3},{3,4},{4,5},{5,6},{6,7},{8,9},{9,10},{10,11},{11... | collective-permute-start | bytes 2359304 | tf_op jit(solution)/shard_map/ppermute | solution.py:141
  111.4 17.4 %copy-start.8 = (f32[64,80,1]{1,0,2:T(8,128)S(1)}, f32[64,80,1]{1,0,2:T(8,128)}, u32[]{:S(2)}) copy-start(f32[64,80,1]{1,0,2:T(8,128)} %constant.147) | copy-start | bytes 61444
  112.7 14.8 %collective-permute-start.5 = (f32[64,8]{1,0:T(8,128)S(1)}, f32[64,8]{1,0:T(8,128)S(1)}, u32[]{:S(2)}, u32[]{:S(2)}) collective-permute-start(f32[64,8]{1,0:T(8,128)S(1)} %get-tuple-element.52), channel_id=1, source_target_pairs={{1,0},{2,1},{3,2},{4,3},{5,4},{6,5},{7,6},{9,8},{10,9},{11,10},{12... | collective-permute-start | bytes 6152 | tf_op jit(solution)/shard_map/ppermute | solution.py:141
  114.8 13.6 %collective-permute-start.4 = (f32[64,8]{1,0:T(8,128)S(1)}, f32[64,8]{1,0:T(8,128)S(1)}, u32[]{:S(2)}, u32[]{:S(2)}) collective-permute-start(f32[64,8]{1,0:T(8,128)S(1)} %get-tuple-element.51), channel_id=1, source_target_pairs={{0,1},{1,2},{2,3},{3,4},{4,5},{5,6},{6,7},{8,9},{9,10},{10,11},{11... | collective-permute-start | bytes 6152 | tf_op jit(solution)/shard_map/ppermute | solution.py:141
  137.4 4.6 %copy-start = (f32[64,64,768]{2,1,0:T(8,128)}, f32[64,64,768]{2,1,0:T(8,128)S(1)}, u32[]{:S(2)}) copy-start(f32[64,64,768]{2,1,0:T(8,128)S(1)} %fusion.6.mid_ref) | copy-start | bytes 37748740
  142.0 14.6 %copy-start.12 = (f32[8,16]{1,0:T(8,128)S(1)}, f32[8,16]{1,0:T(8,128)}, u32[]{:S(2)}) copy-start(f32[8,16]{1,0:T(8,128)} %constant.145) | copy-start | bytes 1540
  142.0 14.8 %copy-start.11 = (f32[8,16]{1,0:T(8,128)S(1)}, f32[8,16]{1,0:T(8,128)}, u32[]{:S(2)}) copy-start(f32[8,16]{1,0:T(8,128)} %constant.144) | copy-start | bytes 1540
  142.0 14.9 %copy-start.13 = (f32[48,64]{1,0:T(8,128)S(1)}, f32[48,64]{1,0:T(8,128)}, u32[]{:S(2)}) copy-start(f32[48,64]{1,0:T(8,128)} %constant.142) | copy-start | bytes 36868
  142.0 42.8 %copy-start.10 = (f32[8,8]{1,0:T(8,128)S(1)}, f32[8,8]{1,0:T(8,128)}, u32[]{:S(2)}) copy-start(f32[8,8]{1,0:T(8,128)} %constant.146) | copy-start | bytes 772
  142.0 42.9 %copy-start.9 = (f32[8,8]{1,0:T(8,128)S(1)}, f32[8,8]{1,0:T(8,128)}, u32[]{:S(2)}) copy-start(f32[8,8]{1,0:T(8,128)} %constant.143) | copy-start | bytes 772
  144.0 59.2 %collective-permute-start.2 = (f32[8,64,768]{2,1,0:T(8,128)}, f32[8,64,768]{2,1,0:T(8,128)S(1)}, u32[]{:S(2)}, u32[]{:S(2)}) collective-permute-start(f32[8,64,768]{2,1,0:T(8,128)} %get-tuple-element.46), channel_id=1, source_target_pairs={{0,8},{8,16},{16,24},{24,32},{32,40},{40,48},{48,56},{56,64},{64,7... | collective-permute-start | bytes 4718600 | tf_op jit(solution)/shard_map/ppermute | solution.py:141
  149.1 54.1 %collective-permute-start.3 = (f32[8,64,768]{2,1,0:T(8,128)}, f32[8,64,768]{2,1,0:T(8,128)}, u32[]{:S(2)}, u32[]{:S(2)}) collective-permute-start(f32[8,64,768]{2,1,0:T(8,128)} %get-tuple-element.45), channel_id=1, source_target_pairs={{8,0},{16,8},{24,16},{32,24},{40,32},{48,40},{56,48},{64,56},{72,6... | collective-permute-start | bytes 4718600 | tf_op jit(solution)/shard_map/ppermute | solution.py:141
  151.1 33.7 %collective-permute-start.7 = (f32[8,64]{1,0:T(8,128)S(1)}, f32[8,64]{1,0:T(8,128)S(1)}, u32[]{:S(2)}, u32[]{:S(2)}) collective-permute-start(f32[8,64]{1,0:T(8,128)S(1)} %get-tuple-element.50), channel_id=1, source_target_pairs={{8,0},{16,8},{24,16},{32,24},{40,32},{48,40},{56,48},{64,56},{72,6... | collective-permute-start | bytes 6152 | tf_op jit(solution)/shard_map/ppermute | solution.py:141
  154.0 30.9 %collective-permute-start.6 = (f32[8,64]{1,0:T(8,128)S(1)}, f32[8,64]{1,0:T(8,128)S(1)}, u32[]{:S(2)}, u32[]{:S(2)}) collective-permute-start(f32[8,64]{1,0:T(8,128)S(1)} %get-tuple-element.49), channel_id=1, source_target_pairs={{0,8},{8,16},{16,24},{24,32},{32,40},{40,48},{48,56},{56,64},{64,7... | collective-permute-start | bytes 6152 | tf_op jit(solution)/shard_map/ppermute | solution.py:141
  203.2 1.2 copy-start.3

commit v6 on v4

--- a/solution.py
+++ b/solution.py
@@ -21,34 +21,49 @@
     return mat
 
 
-def accumulate(ids, docs, unit_of, blocks, feature):
+def accumulate(ids, docs, rows_tile, cols_tile, feature, col_blocks, prior=None):
     rows, width = docs.shape
-    block = 512
-
-    def kernel(ids_ref, docs_ref, num_ref, hits_ref):
-        place = pl.program_id(0) * block + lax.broadcasted_iota(jnp.int32, (block, rows), 0)
-        units = unit_of(place)
+    band = rows_tile * RADIUS
+    picks = jnp.asarray(col_blocks, jnp.int32)
+
+    def kernel(picks_ref, ids_ref, docs_ref, *refs):
+        num_ref, hits_ref = refs[-2:]
+        place = lax.broadcasted_iota(jnp.int32, (band, rows), 0)
+        first_col = picks_ref[pl.program_id(0)] * RADIUS
+        units = (place // RADIUS) * cols_tile + first_col + place % RADIUS
         one_hot = (units == ids_ref[...]).astype(jnp.bfloat16)
         sums = jnp.dot(one_hot, docs_ref[...], preferred_element_type=jnp.float32)
-        num_ref[...] = sums[:, :feature]
-        hits_ref[...] = sums[:, feature:]
-
+        num_ref[...] = sums[:, :feature].reshape(rows_tile, RADIUS, feature)
+        hits_ref[...] = sums[:, feature:].reshape(rows_tile, RADIUS, width - feature)
+
+    out_specs = [
+        pl.BlockSpec((rows_tile, RADIUS, feature), lambda j, p: (0, p[j], 0)),
+        pl.BlockSpec((rows_tile, RADIUS, width - feature), lambda j, p: (0, p[j], 0)),
+    ]
+    in_specs = [
+        pl.BlockSpec((1, rows), lambda j, p: (0, 0)),
+        pl.BlockSpec((rows, width), lambda j, p: (0, 0)),
+    ]
+    operands = [ids.reshape(1, rows), docs]
+    aliases = {}
+    if prior is not None:
+        in_specs += [pl.BlockSpec(memory_space=pl.ANY)] * 2
+        operands += list(prior)
+        aliases = {3: 0, 4: 1}
     return pl.pallas_call(
         kernel,
-        grid=(blocks,),
-        in_specs=[
-            pl.BlockSpec((1, rows), lambda j: (0, 0)),
-            pl.BlockSpec((rows, width), lambda j: (0, 0)),
+        grid_spec=pltpu.PrefetchScalarGridSpec(
+            num_scalar_prefetch=1,
+            grid=(len(col_blocks),),
+            in_specs=in_specs,
+            out_specs=out_specs,
+        ),
+        out_shape=[
+            jax.ShapeDtypeStruct((rows_tile, cols_tile, feature), jnp.float32),
+            jax.ShapeDtypeStruct((rows_tile, cols_tile, width - feature), jnp.float32),
         ],
-        out_specs=[
-            pl.BlockSpec((block, feature), lambda j: (j, 0)),
-            pl.BlockSpec((block, width - feature), lambda j: (j, 0)),
-        ],
-        out_shape=[
-            jax.ShapeDtypeStruct((blocks * block, feature), jnp.float32),
-            jax.ShapeDtypeStruct((blocks * block, width - feature), jnp.float32),
-        ],
-    )(ids.reshape(1, rows), docs)
+        input_output_aliases=aliases,
+    )(picks, *operands)
 
 
 def finish_inner(middle, codebook, inv):
@@ -174,17 +189,19 @@
     mark_row = got[:, feature].astype(jnp.int32)
     mark_col = got[:, feature + 1].astype(jnp.int32)
     unit_ids = jnp.where(got[:, feature + 2] > 0.5, mark_row * cols_tile + mark_col, -1)
-    numerator, counter = accumulate(
-        unit_ids, got, lambda m: m, rows_tile * cols_tile // 512, feature
-    )
-    numerator = numerator.reshape(rows_tile, cols_tile, feature)
-    counter = counter[:, 2].reshape(rows_tile, cols_tile)
+    col_total = cols_tile // RADIUS
+    bands = accumulate(unit_ids, got, rows_tile, cols_tile, feature, [0, col_total - 1])
+    last = cols_tile - RADIUS
+    lead, tail = bands[0][:, :RADIUS], bands[0][:, last:]
+    hits_lead, hits_tail = bands[1][:, :RADIUS, 2], bands[1][:, last:, 2]
+    from_left, from_right = exchange(lead, tail, "my")
+    hits_left, hits_right = exchange(hits_lead, hits_tail, "my")
+    inner = list(range(1, col_total - 1))
+    numerator, counter = accumulate(unit_ids, got, rows_tile, cols_tile, feature, inner, bands)
+    counter = counter[:, :, 2]
 
     g_rows = jnp.asarray(band_matrix(rows_tile))
     g_cols = jnp.asarray(band_matrix(cols_tile))
-    last = cols_tile - RADIUS
-    from_left, from_right = exchange(numerator[:, :RADIUS], numerator[:, last:], "my")
-    hits_left, hits_right = exchange(counter[:, :RADIUS], counter[:, last:], "my")
     ext_num = jnp.concatenate([from_left, numerator, from_right], axis=1)
     ext_hits = jnp.concatenate([hits_left, counter, hits_right], axis=1)
     col_num = jnp.einsum("ck,rke->rce", g_cols, ext_num, precision=HI)

time: 227 us -> 215 us (0.947)
  blocking collectives: 54.9 us -> 0 us
  waiting for transfers between devices: 48.6 us -> 74.7 us
  starting transfers between devices: 30.8 us -> 38.5 us
  Pallas kernels: 47.7 us -> 52.5 us
  other arithmetic: 14.4 us -> 17.4 us
  local copies, waits for them, and re-layouts: 16.7 us -> 19.3 us
    all_to_all x1 -> x0, blocking collectives: 54.9 us -> none  [on_device(): lax.all_to_all(outgoing.reshape(tile_total, capacity, width), ('mx', 'my'...]
    all_to_all x0 -> x1, waiting for transfers between devices: none -> 43.3 us  [on_device(): lax.all_to_all(outgoing.reshape(tile_total, capacity, width), ('mx', 'my'...]
    ppermute x8, waiting for transfers between devices: 48.6 us -> 31.4 us  [exchange(): return (lax.ppermute(last, axis, up), lax.ppermute(lead, axis, down))]
    all_to_all x0 -> x1, starting transfers between devices: none -> 11.1 us  [on_device(): lax.all_to_all(outgoing.reshape(tile_total, capacity, width), ('mx', 'my'...]
    pallas_call x1 -> x2, Pallas kernels: 21.9 us -> 26.8 us  [accumulate(): pl.pallas_call(kernel, grid_spec=pltpu.PrefetchScalarGridSpec(num_scalar_...]
    slice x3 -> x5, local copies, waits for them, and re-layouts: 3.49 us -> 8.04 us  [the longest x3 3.15 us: on_device(): hits_lead, hits_tail = (bands[1][:, :RADIUS, 2], bands[1][:, last:, 2])]
    ppermute x8, starting transfers between devices: 30.8 us -> 27.4 us  [exchange(): return (lax.ppermute(last, axis, up), lax.ppermute(lead, axis, down))]
    unnamed x32 -> x26, local copies, waits for them, and re-layouts: 7.62 us -> 5.76 us
  transfers between devices with their start and end apart: 8 -> 9, of which waited for: 3 -> 4; matrix products, arithmetic and copies ran while one was open for 3% -> 5% of each run, Pallas kernels for 8% -> 16%
where the time goes in v6:
time: 215 us; the launch traced here: 213 us
  waiting for transfers between devices  74.7 us (35%)
  Pallas kernels  52.5 us (24%)
  starting transfers between devices  38.5 us (18%)
  local copies, waits for them, and re-layouts  19.3 us (9%)
  other arithmetic  17.4 us (8%)
  matrix products  10.5 us (5%)
    all_to_all x1, waiting for transfers between devices, on_device(): lax.all_to_all(outgoing.reshape(tile_total, capacity, width), ('mx', 'my'...  43.3 us
    ppermute x8, waiting for transfers between devices, exchange(): return (lax.ppermute(last, axis, up), lax.ppermute(lead, axis, down))  31.4 us
    ppermute x8, starting transfers between devices, exchange(): return (lax.ppermute(last, axis, up), lax.ppermute(lead, axis, down))  27.4 us
    pallas_call x2, Pallas kernels, accumulate(): pl.pallas_call(kernel, grid_spec=pltpu.PrefetchScalarGridSpec(num_scalar_...  26.8 us
    pallas_call x1, Pallas kernels, finish_inner(): pl.pallas_call(kernel, grid=(feature // lanes,), in_specs=[slab_spec, sla...  17 us
    all_to_all x1, starting transfers between devices, on_device(): lax.all_to_all(outgoing.reshape(tile_total, capacity, width), ('mx', 'my'...  11.1 us
    dot_general x1, matrix products, on_device(): col_num = jnp.einsum('ck,rke->rce', g_cols, ext_num, precision=HI)  9.31 us
    pallas_call x1, Pallas kernels, finish_edges(): pl.pallas_call(kernel, grid=(2,), in_specs=[halo_spec, pl.BlockSpec((near...  8.7 us
  transfers between devices with their start and end apart: 9, of which 4 were waited for; matrix products, arithmetic and copies ran while one was open for 5% of the time, Pallas kernels for 16%

profile of v6, /device:TPU:15, one launch (start us, length us, event | category | flops | bytes accessed | tf_op | source)
XLA Modules:
  0.0 213.3 jit_solution(7966981582559935745)
XLA Ops:
  0.0 0.6 compare_reduce_fusion.2
  0.7 0.6 compare_reduce_fusion.1
  1.3 0.6 compare_reduce_fusion
  1.9 2.0 fusion.32
  3.9 0.8 copy.29
  4.7 0.1 scatter.19
  4.8 0.6 broadcast_select_fusion
  5.4 0.1 scatter.24
  5.5 0.2 copy.31
  5.6 0.2 fusion.21
  5.9 0.1 copy.30
  6.0 0.0 copy-done.3
  6.1 0.4 fusion.20
  6.4 0.0 copy-done.2
  6.4 7.6 %scatter_custom_fusion = bf16[2048,896]{1,0:T(8,128)(2,1)} fusion(s32[1024]{0:T(1024)S(1)} %bitcast.54, bf16[1024,128]{1,0:T(8,128)(2,1)S(1)} %copy.31, bf16[]{:T(256)} %constant.160, bf16[1024,768]{1,0:T(8,128)(2,1)S(1)} %copy-done.2, bf16[]{:T(256)} %constant.123.clone.1), kind=kCustom, calls=%fused_computation.9 | custom fusion | flops 3670016 | bytes 5505028 | tf_op jit(solution)/shard_map/scatter | solution.py:181
  14.1 11.1 %all-to-all-start = ((bf16[128,16,896]{2,1,0:T(8,128)(2,1)}), bf16[128,16,896]{2,1,0:T(8,128)(2,1)}, u32[]{:S(2)}, u32[]{:S(2)}) async-start(bf16[128,16,896]{2,1,0:T(8,128)(2,1)} %bitcast.46), calls=%async_computation | async-start | bytes 7340032 | tf_op jit(solution)/shard_map/all_to_all | solution.py:182
  25.2 0.6 iota_multiply_fusion.1.picks_ref
  25.8 43.3 %all-to-all-done = bf16[128,16,896]{2,1,0:T(8,128)(2,1)} async-done(((bf16[128,16,896]{2,1,0:T(8,128)(2,1)}), bf16[128,16,896]{2,1,0:T(8,128)(2,1)}, u32[]{:S(2)}, u32[]{:S(2)}) %all-to-all-start) | async-done | bytes 3670048 | tf_op jit(solution)/shard_map/all_to_all | solution.py:182
  69.1 3.2 %select_reduce_fusion = s32[2048]{0:T(1024)} fusion(bf16[2048,896]{1,0:T(8,128)(2,1)} %bitcast.8.docs_ref), kind=kLoop, calls=%fused_computation.23 | loop fusion | flops 12288 | bytes 20480 | tf_op jit(solution)/shard_map/jit(_where)/select_n | solution.py:191
  72.2 8.7 %shard_map.82 = (f32[64,64,768]{2,1,0:T(8,128)}, f32[64,64,128]{2,1,0:T(8,128)}) custom-call(s32[2]{0:T(128)} %iota_multiply_fusion.1.picks_ref, s32[1,2048]{1,0:T(1,128)} %bitcast.47, bf16[2048,896]{1,0:T(8,128)(2,1)} %bitcast.8.docs_ref), custom_call_target="tpu_custom_call" | custom-call | tf_op jit(solution)/shard_map/pallas_call | solution.py:53
  80.9 2.1 fusion.36
  83.0 5.0 %collective-permute-start = (f32[64,8,768]{2,1,0:T(8,128)S(1)}, f32[64,8,768]{2,1,0:T(8,128)}, u32[]{:S(2)}, u32[]{:S(2)}) collective-permute-start(f32[64,8,768]{2,1,0:T(8,128)S(1)} %get-tuple-element.51), channel_id=1, source_target_pairs={{0,1},{1,2},{2,3},{3,4},{4,5},{5,6},{6,7},{8,9},{9,10},{10,11},{11... | collective-permute-start | bytes 4718600 | tf_op jit(solution)/shard_map/ppermute | solution.py:156
  88.1 1.9 collective-permute-start.1
  90.0 1.9 fusion.37
  92.0 1.1 copy.32
  93.0 0.1 copy.33
  93.2 1.9 collective-permute-start.5
  95.1 7.2 %collective-permute-start.4 = (f32[64,8]{0,1:T(8,128)S(1)}, f32[64,8]{0,1:T(8,128)S(1)}, u32[]{:S(2)}, u32[]{:S(2)}) collective-permute-start(f32[64,8]{0,1:T(8,128)S(1)} %bitcast.52), channel_id=1, source_target_pairs={{0,1},{1,2},{2,3},{3,4},{4,5},{5,6},{6,7},{8,9},{9,10},{10,11},{11... | collective-permute-start | bytes 6152 | tf_op jit(solution)/shard_map/ppermute | solution.py:156
  102.3 18.1 %shard_map.83 = (f32[64,64,768]{2,1,0:T(8,128)}, f32[64,64,128]{2,1,0:T(8,128)}) custom-call(s32[6]{0:T(128)} %constant.141.clone.picks_ref, s32[1,2048]{1,0:T(1,128)} %bitcast.48, bf16[2048,896]{1,0:T(8,128)(2,1)} %bitcast.8.docs_ref, f32[64,64,768]{2,1,0:T(8,128)} %get-tuple-element.45.refs_0_, ...), custom_call_target="tpu_custom_call", output_to_operand_aliasing={{0}: (3, {}), {1}: (4, {})} | custom-call | tf_op jit(solution)/shard_map/pallas_call | solution.py:53
  120.4 0.0 copy-start.7
  120.4 2.8 %slice_reduce_fusion = f32[64,64]{1,0:T(8,128)S(1)} fusion(f32[64,64,128]{2,1,0:T(8,128)} %get-tuple-element.48), kind=kLoop, calls=%fused_computation.8 | loop fusion | bytes 32768 | tf_op jit(solution)/shard_map/slice | solution.py:201
  123.2 0.0 copy-done.4
  123.2 0.2 fusion.39
  123.4 5.0 %collective-permute-done.5 = f32[64,8]{0,1:T(8,128)S(1)} collective-permute-done((f32[64,8]{0,1:T(8,128)S(1)}, f32[64,8]{0,1:T(8,128)S(1)}, u32[]{:S(2)}, u32[]{:S(2)}) %collective-permute-start.5) | collective-permute-done | bytes 2080 | tf_op jit(solution)/shard_map/ppermute | solution.py:156
  128.4 0.0 copy-done.5
  128.4 0.2 fusion.40
  128.6 0.0 collective-permute-done.4
  128.7 0.0 copy-done.6
  128.7 0.2 fusion.14
  128.9 0.0 collective-permute-done
  128.9 0.0 collective-permute-done.1
  128.9 9.3 %fusion.6.mid_ref = f32[64,64,768]{2,1,0:T(8,128)S(1)} fusion(f32[64,80,1]{1,0,2:T(8,128)S(1)} %copy-done.7, f32[64,8,768]{2,1,0:T(8,128)} %collective-permute-done.1, f32[64,64,768]{2,1,0:T(8,128)} %get-tuple-element.47, f32[64,8,768]{2,1,0:T(8,128)} %collective-permute-done), kind=kOutput, calls=%fused_computation.7 | convolution fusion | flops 1517813760 | bytes 28332032 | tf_op jit(solution)/shard_map/ck,rke->rce/dot_general | solution.py:207
  138.2 0.0 copy-start
  138.2 4.5 %copy-done = f32[64,64,768]{2,1,0:T(8,128)} copy-done((f32[64,64,768]{2,1,0:T(8,128)}, f32[64,64,768]{2,1,0:T(8,128)S(1)}, u32[]{:S(2)}) %copy-start) | copy-done | bytes 12582936
  142.8 2.0 fusion.35
  144.7 4.2 %collective-permute-start.3 = (f32[8,64,768]{2,1,0:T(8,128)}, f32[8,64,768]{2,1,0:T(8,128)S(1)}, u32[]{:S(2)}, u32[]{:S(2)}) collective-permute-start(f32[8,64,768]{2,1,0:T(8,128)} %get-tuple-element.49), channel_id=1, source_target_pairs={{8,0},{16,8},{24,16},{32,24},{40,32},{48,40},{56,48},{64,56},{72,6... | collective-permute-start | bytes 4718600 | tf_op jit(solution)/shard_map/ppermute | solution.py:156
  148.9 2.9 %collective-permute-start.2 = (f32[8,64,768]{2,1,0:T(8,128)}, f32[8,64,768]{2,1,0:T(8,128)}, u32[]{:S(2)}, u32[]{:S(2)}) collective-permute-start(f32[8,64,768]{2,1,0:T(8,128)} %get-tuple-element.50), channel_id=1, source_target_pairs={{0,8},{8,16},{16,24},{24,32},{32,40},{40,48},{48,56},{56,64},{64,7... | collective-permute-start | bytes 4718600 | tf_op jit(solution)/shard_map/ppermute | solution.py:156
  151.8 2.4 %collective-permute-start.6 = (f32[8,64]{1,0:T(8,128)S(1)}, f32[8,64]{1,0:T(8,128)S(1)}, u32[]{:S(2)}, u32[]{:S(2)}) collective-permute-start(f32[8,64]{1,0:T(8,128)S(1)} %get-tuple-element.55), channel_id=1, source_target_pairs={{0,8},{8,16},{16,24},{24,32},{32,40},{40,48},{48,56},{56,64},{64,7... | collective-permute-start | bytes 6152 | tf_op jit(solution)/shard_map/ppermute | solution.py:156
  154.2 1.9 collective-permute-start.7
  156.2 0.1 fusion.24
  156.3 0.1 fusion.26
  156.4 0.2 fusion.16
  156.6 2.0 copy.36.inv_ref
  158.6 25.5 %collective-permute-done.6 = f32[8,64]{1,0:T(8,128)S(1)} collective-permute-done((f32[8,64]{1,0:T(8,128)S(1)}, f32[8,64]{1,0:T(8,128)S(1)}, u32[]{:S(2)}, u32[]{:S(2)}) %collective-permute-start.6) | collective-permute-done | bytes 2080 | tf_op jit(solution)/shard_map/ppermute | solution.py:156
  184.1 0.1 fusion.18
  184.2 0.9 collective-permute-done.7
  185.1 0.1 fusion.17
  185.2 0.3 copy.35
  185.5 0.9 broadcast_divide_fusion.inv_ref
  186.4 17.0 %shard_map.84.prev_ref = bf16[64,64,768]{2,1,0:T(8,128)(2,1)} custom-call(f32[64,64,768]{2,1,0:T(8,128)} %copy-done, bf16[64,64,768]{2,1,0:T(8,128)(2,1)} %cb_ref.3, f32[64,64,1]{2,1,0:T(8,128)} %copy.36.inv_ref), custom_call_target="tpu_custom_call" | custom-call | tf_op jit(solution)/shard_map/pallas_call | solution.py:88
  203.4 0.0 collective-permute-done.3.below_ref
  203.4 0.0 collective-permute-done.2.above_ref
  203.4 1.2 copy-done.1
  204.6 8.7 %shard_map.85 = bf16[64,64,768]{2,1,0:T(8,128)(2,1)} custom-call(f32[8,64,768]{2,1,0:T(8,128)} %collective-permute-done.2.above_ref, f32[64,64,768]{2,1,0:T(8,128)} %copy-done, f32[8,64,768]{2,1,0:T(8,128)} %copy-done.1, bf16[64,64,768]{2,1,0:T(8,128)(2,1)} %cb_ref.3, f32[16,64,1]{2,1,0:T(8,128)} %broadcast_divide_fusion.inv_ref, ...), custom_call_target="tpu_custom_call", output_to_operand_aliasing={{}: (5, {})} | custom-call | tf_op jit(solution)/shard_map/pallas_call | solution.py:134
  (29 shorter events, 0.2 us)
Async XLA Ops:
  0.0 6.0 %copy-start.3 = (s32[1024,1]{0,1:T(1,128)S(1)}, s32[1024,1]{0,1:T(1,128)}, u32[]{:S(2)}) copy-start(s32[1024,1]{0,1:T(1,128)} %param.15) | copy-start | bytes 12292
  0.0 6.4 %copy-start.2 = (bf16[1024,768]{1,0:T(8,128)(2,1)S(1)}, bf16[1024,768]{1,0:T(8,128)(2,1)}, u32[]{:S(2)}) copy-start(bf16[1024,768]{1,0:T(8,128)(2,1)} %param.14) | copy-start | bytes 4718596
  14.1 55.0 %all-to-all-start = ((bf16[128,16,896]{2,1,0:T(8,128)(2,1)}), bf16[128,16,896]{2,1,0:T(8,128)(2,1)}, u32[]{:S(2)}, u32[]{:S(2)}) async-start(bf16[128,16,896]{2,1,0:T(8,128)(2,1)} %bitcast.46), calls=%async_computation | async-start | bytes 7340032 | tf_op jit(solution)/shard_map/all_to_all | solution.py:182
  83.0 45.9 %collective-permute-start = (f32[64,8,768]{2,1,0:T(8,128)S(1)}, f32[64,8,768]{2,1,0:T(8,128)}, u32[]{:S(2)}, u32[]{:S(2)}) collective-permute-start(f32[64,8,768]{2,1,0:T(8,128)S(1)} %get-tuple-element.51), channel_id=1, source_target_pairs={{0,1},{1,2},{2,3},{3,4},{4,5},{5,6},{6,7},{8,9},{9,10},{10,11},{11... | collective-permute-start | bytes 4718600 | tf_op jit(solution)/shard_map/ppermute | solution.py:156
  88.1 40.8 %collective-permute-start.1 = (f32[64,8,768]{2,1,0:T(8,128)S(1)}, f32[64,8,768]{2,1,0:T(8,128)}, u32[]{:S(2)}, u32[]{:S(2)}) collective-permute-start(f32[64,8,768]{2,1,0:T(8,128)S(1)} %get-tuple-element.52), channel_id=1, source_target_pairs={{1,0},{2,1},{3,2},{4,3},{5,4},{6,5},{7,6},{9,8},{10,9},{11,10},{12... | collective-permute-start | bytes 4718600 | tf_op jit(solution)/shard_map/ppermute | solution.py:156
  93.2 35.2 %collective-permute-start.5 = (f32[64,8]{0,1:T(8,128)S(1)}, f32[64,8]{0,1:T(8,128)S(1)}, u32[]{:S(2)}, u32[]{:S(2)}) collective-permute-start(f32[64,8]{0,1:T(8,128)S(1)} %bitcast.53), channel_id=1, source_target_pairs={{1,0},{2,1},{3,2},{4,3},{5,4},{6,5},{7,6},{9,8},{10,9},{11,10},{12... | collective-permute-start | bytes 6152 | tf_op jit(solution)/shard_map/ppermute | solution.py:156
  95.1 33.5 %collective-permute-start.4 = (f32[64,8]{0,1:T(8,128)S(1)}, f32[64,8]{0,1:T(8,128)S(1)}, u32[]{:S(2)}, u32[]{:S(2)}) collective-permute-start(f32[64,8]{0,1:T(8,128)S(1)} %bitcast.52), channel_id=1, source_target_pairs={{0,1},{1,2},{2,3},{3,4},{4,5},{5,6},{6,7},{8,9},{9,10},{10,11},{11... | collective-permute-start | bytes 6152 | tf_op jit(solution)/shard_map/ppermute | solution.py:156
  120.4 2.8 %copy-start.4 = (f32[64,64]{1,0:T(8,128)S(1)}, f32[64,64]{1,0:T(8,128)}, u32[]{:S(2)}) copy-start(f32[64,64]{1,0:T(8,128)} %constant.147) | copy-start | bytes 49156
  120.4 8.0 %copy-start.5 = (f32[64,8]{1,0:T(8,128)S(1)}, f32[64,8]{1,0:T(8,128)}, u32[]{:S(2)}) copy-start(f32[64,8]{1,0:T(8,128)} %constant.148) | copy-start | bytes 6148
  120.4 8.3 %copy-start.6 = (f32[64,8]{1,0:T(8,128)S(1)}, f32[64,8]{1,0:T(8,128)}, u32[]{:S(2)}) copy-start(f32[64,8]{1,0:T(8,128)} %constant.146) | copy-start | bytes 6148
  120.4 8.5 %copy-start.7 = (f32[64,80,1]{1,0,2:T(8,128)S(1)}, f32[64,80,1]{1,0,2:T(8,128)}, u32[]{:S(2)}) copy-start(f32[64,80,1]{1,0,2:T(8,128)} %constant.154) | copy-start | bytes 61444
  138.2 4.5 %copy-start = (f32[64,64,768]{2,1,0:T(8,128)}, f32[64,64,768]{2,1,0:T(8,128)S(1)}, u32[]{:S(2)}) copy-start(f32[64,64,768]{2,1,0:T(8,128)S(1)} %fusion.6.mid_ref) | copy-start | bytes 37748740
  142.8 13.4 %copy-start.11 = (f32[8,16]{1,0:T(8,128)S(1)}, f32[8,16]{1,0:T(8,128)}, u32[]{:S(2)}) copy-start(f32[8,16]{1,0:T(8,128)} %constant.152) | copy-start | bytes 1540
  142.8 13.5 %copy-start.10 = (f32[8,16]{1,0:T(8,128)S(1)}, f32[8,16]{1,0:T(8,128)}, u32[]{:S(2)}) copy-start(f32[8,16]{1,0:T(8,128)} %constant.151) | copy-start | bytes 1540
  142.8 13.6 %copy-start.12 = (f32[48,64]{1,0:T(8,128)S(1)}, f32[48,64]{1,0:T(8,128)}, u32[]{:S(2)}) copy-start(f32[48,64]{1,0:T(8,128)} %constant.149) | copy-start | bytes 36868
  144.7 39.4 %copy-start.9 = (f32[8,8]{1,0:T(8,128)S(1)}, f32[8,8]{1,0:T(8,128)}, u32[]{:S(2)}) copy-start(f32[8,8]{1,0:T(8,128)} %constant.150) | copy-start | bytes 772
  144.7 40.4 %copy-start.8 = (f32[8,8]{1,0:T(8,128)S(1)}, f32[8,8]{1,0:T(8,128)}, u32[]{:S(2)}) copy-start(f32[8,8]{1,0:T(8,128)} %constant.153) | copy-start | bytes 772
  144.7 58.7 %collective-permute-start.3 = (f32[8,64,768]{2,1,0:T(8,128)}, f32[8,64,768]{2,1,0:T(8,128)S(1)}, u32[]{:S(2)}, u32[]{:S(2)}) collective-permute-start(f32[8,64,768]{2,1,0:T(8,128)} %get-tuple-element.49), channel_id=1, source_target_pairs={{8,0},{16,8},{24,16},{32,24},{40,32},{48,40},{56,48},{64,56},{72,6... | collective-permute-start | bytes 4718600 | tf_op jit(solution)/shard_map/ppermute | solution.py:156
  148.9 54.5 %collective-permute-start.2 = (f32[8,64,768]{2,1,0:T(8,128)}, f32[8,64,768]{2,1,0:T(8,128)}, u32[]{:S(2)}, u32[]{:S(2)}) collective-permute-start(f32[8,64,768]{2,1,0:T(8,128)} %get-tuple-element.50), channel_id=1, source_target_pairs={{0,8},{8,16},{16,24},{24,32},{32,40},{40,48},{48,56},{56,64},{64,7... | collective-permute-start | bytes 4718600 | tf_op jit(solution)/shard_map/ppermute | solution.py:156
  151.8 32.3 %collective-permute-start.6 = (f32[8,64]{1,0:T(8,128)S(1)}, f32[8,64]{1,0:T(8,128)S(1)}, u32[]{:S(2)}, u32[]{:S(2)}) collective-permute-start(f32[8,64]{1,0:T(8,128)S(1)} %get-tuple-element.55), channel_id=1, source_target_pairs={{0,8},{8,16},{16,24},{24,32},{32,40},{40,48},{48,56},{56,64},{64,7... | collective-permute-start | bytes 6152 | tf_op jit(solution)/shard_map/ppermute | solution.py:156
  154.2 30.9 %collective-permute-start.7 = (f32[8,64]{1,0:T(8,128)S(1)}, f32[8,64]{1,0:T(8,128)S(1)}, u32[]{:S(2)}, u32[]{:S(2)}) collective-permute-start(f32[8,64]{1,0:T(8,128)S(1)} %get-tuple-element.56), channel_id=1, source_target_pairs={{8,0},{16,8},{24,16},{32,24},{40,32},{48,40},{56,48},{64,56},{72,6... | collective-permute-start | bytes 6152 | tf_op jit(solution)/shard_map/ppermute | solution.py:156
  203.4 1.2 copy-start.1

commit v7 on v6

--- a/solution.py
+++ b/solution.py
@@ -192,10 +192,11 @@
     col_total = cols_tile // RADIUS
     bands = accumulate(unit_ids, got, rows_tile, cols_tile, feature, [0, col_total - 1])
     last = cols_tile - RADIUS
-    lead, tail = bands[0][:, :RADIUS], bands[0][:, last:]
-    hits_lead, hits_tail = bands[1][:, :RADIUS, 2], bands[1][:, last:, 2]
+    lead = jnp.concatenate([bands[0][:, :RADIUS], bands[1][:, :RADIUS]], axis=2)
+    tail = jnp.concatenate([bands[0][:, last:], bands[1][:, last:]], axis=2)
     from_left, from_right = exchange(lead, tail, "my")
-    hits_left, hits_right = exchange(hits_lead, hits_tail, "my")
+    hits_left, hits_right = from_left[:, :, feature + 2], from_right[:, :, feature + 2]
+    from_left, from_right = from_left[:, :, :feature], from_right[:, :, :feature]
     inner = list(range(1, col_total - 1))
     numerator, counter = accumulate(unit_ids, got, rows_tile, cols_tile, feature, inner, bands)
     counter = counter[:, :, 2]
@@ -207,8 +208,12 @@
     col_num = jnp.einsum("ck,rke->rce", g_cols, ext_num, precision=HI)
     col_hits = jnp.einsum("ck,rk->rc", g_cols, ext_hits, precision=HI)
     last = rows_tile - RADIUS
-    above, below = exchange(col_num[:RADIUS], col_num[last:], "mx")
-    hits_above, hits_below = exchange(col_hits[:RADIUS], col_hits[last:], "mx")
+    def with_hits(rows):
+        hit_lanes = jnp.pad(col_hits[rows][:, :, None], ((0, 0), (0, 0), (0, 127)))
+        return jnp.concatenate([col_num[rows], hit_lanes], axis=2)
+
+    above, below = exchange(with_hits(slice(0, RADIUS)), with_hits(slice(last, rows_tile)), "mx")
+    hits_above, hits_below = above[:, :, feature], below[:, :, feature]
     inner_hits = jnp.einsum("rk,kc->rc", g_rows[RADIUS:last, RADIUS : RADIUS + rows_tile], col_hits, precision=HI)
     inv_inner = 1.0 / (inner_hits + 8.0)
     inv = jnp.concatenate([jnp.zeros_like(inv_inner[:RADIUS]), inv_inner, jnp.zeros_like(inv_inner[:RADIUS])])

time: 215 us -> 216 us (level)
  starting transfers between devices: 38.5 us -> 25.1 us
  waiting for transfers between devices: 74.7 us -> 82.7 us
  other arithmetic: 17.4 us -> 23.7 us
    ppermute x8 -> x4, starting transfers between devices: 27.4 us -> 14.1 us  [exchange(): return (lax.ppermute(last, axis, up), lax.ppermute(lead, axis, down))]
    ppermute x8 -> x4, waiting for transfers between devices: 31.4 us -> 39.4 us  [exchange(): return (lax.ppermute(last, axis, up), lax.ppermute(lead, axis, down))]
    concatenate x0 -> x4, other arithmetic: none -> 6.46 us  [the longest x2 3.74 us: with_hits(): return jnp.concatenate([col_num[rows], hit_lanes], axis=2)]
    slice x6 -> x11, local copies, waits for them, and re-layouts: 7.2 us -> 7.79 us  [the longest x2 3.16 us: on_device(): tail = jnp.concatenate([bands[0][:, last:], bands[1][:, last:]], axis=2)]
  transfers between devices with their start and end apart: 9 -> 5, of which waited for: 4 -> 5; matrix products, arithmetic and copies ran while one was open for 5% -> 5% of each run, Pallas kernels for 16% -> 16%
where the time goes in v7:
time: 216 us; the launch traced here: 215 us
  waiting for transfers between devices  82.7 us (38%)
  Pallas kernels  52.7 us (24%)
  starting transfers between devices  25.1 us (12%)
  other arithmetic  23.7 us (11%)
  local copies, waits for them, and re-layouts  20.3 us (9%)
  matrix products  9.81 us (5%)
    all_to_all x1, waiting for transfers between devices, on_device(): lax.all_to_all(outgoing.reshape(tile_total, capacity, width), ('mx', 'my'...  43.4 us
    ppermute x4, waiting for transfers between devices, exchange(): return (lax.ppermute(last, axis, up), lax.ppermute(lead, axis, down))  39.4 us
    pallas_call x2, Pallas kernels, accumulate(): pl.pallas_call(kernel, grid_spec=pltpu.PrefetchScalarGridSpec(num_scalar_...  26.9 us
    pallas_call x1, Pallas kernels, finish_inner(): pl.pallas_call(kernel, grid=(feature // lanes,), in_specs=[slab_spec, sla...  17.1 us
    ppermute x4, starting transfers between devices, exchange(): return (lax.ppermute(last, axis, up), lax.ppermute(lead, axis, down))  14.1 us
    all_to_all x1, starting transfers between devices, on_device(): lax.all_to_all(outgoing.reshape(tile_total, capacity, width), ('mx', 'my'...  11.1 us
    pallas_call x1, Pallas kernels, finish_edges(): pl.pallas_call(kernel, grid=(2,), in_specs=[halo_spec, pl.BlockSpec((near...  8.71 us
    dot_general x1, matrix products, on_device(): col_num = jnp.einsum('ck,rke->rce', g_cols, ext_num, precision=HI)  8.6 us
  transfers between devices with their start and end apart: 5, of which 5 were waited for; matrix products, arithmetic and copies ran while one was open for 5% of the time, Pallas kernels for 16%

profile of v7, /device:TPU:15, one launch (start us, length us, event | category | flops | bytes accessed | tf_op | source)
XLA Modules:
  0.0 214.8 jit_solution(4259398648536034152)
XLA Ops:
  0.0 0.6 compare_reduce_fusion.1
  0.6 0.7 compare_reduce_fusion.2
  1.4 0.6 compare_reduce_fusion
  2.0 2.0 fusion.35
  4.1 0.1 scatter.19
  4.2 0.6 broadcast_select_fusion
  4.7 0.1 scatter.24
  4.8 0.0 copy-start.2
  4.8 0.2 copy.45
  5.0 0.9 copy.43
  5.9 0.2 fusion.21
  6.2 0.1 copy.44
  6.3 0.4 fusion.20
  6.7 7.6 %scatter_custom_fusion = bf16[2048,896]{1,0:T(8,128)(2,1)} fusion(s32[1024]{0:T(1024)S(1)} %bitcast.57, bf16[1024,128]{1,0:T(8,128)(2,1)S(1)} %copy.45, bf16[]{:T(256)} %constant.171, bf16[1024,768]{1,0:T(8,128)(2,1)S(1)} %copy-done.2, bf16[]{:T(256)} %constant.124.clone.1), kind=kCustom, calls=%fused_computation.12 | custom fusion | flops 3670016 | bytes 5505028 | tf_op jit(solution)/shard_map/scatter | solution.py:181
  14.3 11.1 %all-to-all-start = ((bf16[128,16,896]{2,1,0:T(8,128)(2,1)}), bf16[128,16,896]{2,1,0:T(8,128)(2,1)}, u32[]{:S(2)}, u32[]{:S(2)}) async-start(bf16[128,16,896]{2,1,0:T(8,128)(2,1)} %bitcast.51), calls=%async_computation | async-start | bytes 7340032 | tf_op jit(solution)/shard_map/all_to_all | solution.py:182
  25.4 0.5 iota_multiply_fusion.1.picks_ref
  26.0 43.4 %all-to-all-done = bf16[128,16,896]{2,1,0:T(8,128)(2,1)} async-done(((bf16[128,16,896]{2,1,0:T(8,128)(2,1)}), bf16[128,16,896]{2,1,0:T(8,128)(2,1)}, u32[]{:S(2)}, u32[]{:S(2)}) %all-to-all-start) | async-done | bytes 3670048 | tf_op jit(solution)/shard_map/all_to_all | solution.py:182
  69.3 2.9 %select_reduce_fusion = s32[2048]{0:T(1024)} fusion(bf16[2048,896]{1,0:T(8,128)(2,1)} %bitcast.8.docs_ref), kind=kLoop, calls=%fused_computation.28 | loop fusion | flops 12288 | bytes 20480 | tf_op jit(solution)/shard_map/jit(_where)/select_n | solution.py:191
  72.3 8.7 %shard_map.82 = (f32[64,64,768]{2,1,0:T(8,128)}, f32[64,64,128]{2,1,0:T(8,128)}) custom-call(s32[2]{0:T(128)} %iota_multiply_fusion.1.picks_ref, s32[1,2048]{1,0:T(1,128)} %bitcast.52, bf16[2048,896]{1,0:T(8,128)(2,1)} %bitcast.8.docs_ref), custom_call_target="tpu_custom_call" | custom-call | tf_op jit(solution)/shard_map/pallas_call | solution.py:53
  81.0 2.1 fusion.39
  83.1 1.1 fusion.40
  84.1 1.4 pad_maximum_fusion
  85.5 5.0 %collective-permute-start = (f32[64,8,896]{2,1,0:T(8,128)}, f32[64,8,896]{2,1,0:T(8,128)S(1)}, u32[]{:S(2)}, u32[]{:S(2)}) collective-permute-start(f32[64,8,896]{2,1,0:T(8,128)} %pad_maximum_fusion), channel_id=1, source_target_pairs={{0,1},{1,2},{2,3},{3,4},{4,5},{5,6},{6,7},{8,9},{9,10},{10,11},{11... | collective-permute-start | bytes 5505032 | tf_op jit(solution)/shard_map/ppermute | solution.py:156
  90.6 1.3 pad_maximum_fusion.1
  91.9 2.1 collective-permute-start.1
  94.0 18.2 %shard_map.83 = (f32[64,64,768]{2,1,0:T(8,128)}, f32[64,64,128]{2,1,0:T(8,128)}) custom-call(s32[6]{0:T(128)} %constant.142.clone.picks_ref, s32[1,2048]{1,0:T(1,128)} %bitcast.53, bf16[2048,896]{1,0:T(8,128)(2,1)} %bitcast.8.docs_ref, f32[64,64,768]{2,1,0:T(8,128)} %get-tuple-element.45.refs_0_, ...), custom_call_target="tpu_custom_call", output_to_operand_aliasing={{0}: (3, {}), {1}: (4, {})} | custom-call | tf_op jit(solution)/shard_map/pallas_call | solution.py:53
  112.2 2.8 %slice_reduce_fusion = f32[64,64]{1,0:T(8,128)S(1)} fusion(f32[64,64,128]{2,1,0:T(8,128)} %get-tuple-element.48), kind=kLoop, calls=%fused_computation.8 | loop fusion | bytes 32768 | tf_op jit(solution)/shard_map/slice | solution.py:202
  115.0 0.2 fusion.41
  115.2 14.0 %collective-permute-done = f32[64,8,896]{2,1,0:T(8,128)S(1)} collective-permute-done((f32[64,8,896]{2,1,0:T(8,128)}, f32[64,8,896]{2,1,0:T(8,128)S(1)}, u32[]{:S(2)}, u32[]{:S(2)}) %collective-permute-start) | collective-permute-done | bytes 1835040 | tf_op jit(solution)/shard_map/ppermute | solution.py:156
  129.2 0.1 slice.159
  129.3 0.1 copy.46
  129.5 8.5 %collective-permute-done.1 = f32[64,8,896]{2,1,0:T(8,128)} collective-permute-done((f32[64,8,896]{2,1,0:T(8,128)}, f32[64,8,896]{2,1,0:T(8,128)}, u32[]{:S(2)}, u32[]{:S(2)}) %collective-permute-start.1) | collective-permute-done | bytes 1835040 | tf_op jit(solution)/shard_map/ppermute | solution.py:156
  138.0 1.1 slice.160
  139.0 0.1 copy.47
  139.2 0.1 slice.156
  139.3 0.0 copy-start.7
  139.3 1.5 slice.157
  140.9 8.6 %fusion.6.mid_ref = f32[64,64,768]{2,1,0:T(8,128)S(1)} fusion(f32[64,80,1]{1,0,2:T(8,128)S(1)} %copy-done.7, f32[64,8,768]{2,1,0:T(8,128)S(1)} %slice.157, f32[64,64,768]{2,1,0:T(8,128)} %get-tuple-element.47, f32[64,8,768]{2,1,0:T(8,128)S(1)} %slice.156), kind=kOutput, calls=%fused_computation.7 | convolution fusion | flops 1517813760 | bytes 28332032 | tf_op jit(solution)/shard_map/ck,rke->rce/dot_general | solution.py:208
  149.5 4.6 %copy-done = f32[64,64,768]{2,1,0:T(8,128)} copy-done((f32[64,64,768]{2,1,0:T(8,128)}, f32[64,64,768]{2,1,0:T(8,128)S(1)}, u32[]{:S(2)}) %copy-start) | copy-done | bytes 12582936
  154.0 0.3 fusion.38
  154.3 0.5 copy-done.5
  154.8 0.2 fusion.30
  155.0 0.2 fusion.14
  155.3 0.1 copy.48
  155.4 1.4 select_maximum_fusion.1
  156.8 5.0 %collective-permute-start.2 = (f32[8,64,896]{2,1,0:T(8,128)}, f32[8,64,896]{2,1,0:T(8,128)S(1)}, u32[]{:S(2)}, u32[]{:S(2)}) collective-permute-start(f32[8,64,896]{2,1,0:T(8,128)} %select_maximum_fusion.1), channel_id=1, source_target_pairs={{0,8},{8,16},{16,24},{24,32},{32,40},{40,48},{48,56},{56,64},{64,7... | collective-permute-start | bytes 5505032 | tf_op jit(solution)/shard_map/ppermute | solution.py:156
  161.9 0.9 copy.49
  162.7 2.4 %select_maximum_fusion = f32[8,64,896]{2,1,0:T(8,128)} fusion(f32[8,64,1]{2,1,0:T(8,128)} %copy.49, f32[8,64,768]{2,1,0:T(8,128)S(1)} %get-tuple-element.49), kind=kLoop, calls=%fused_computation.9 | loop fusion | flops 1376256 | bytes 3409920 | tf_op jit(solution)/shard_map/concatenate | solution.py:213
  165.1 1.9 collective-permute-start.3
  167.0 0.1 fusion.16
  167.2 2.1 copy.52.inv_ref
  169.2 17.1 %shard_map.84.prev_ref = bf16[64,64,768]{2,1,0:T(8,128)(2,1)} custom-call(f32[64,64,768]{2,1,0:T(8,128)} %copy-done, bf16[64,64,768]{2,1,0:T(8,128)(2,1)} %cb_ref.3, f32[64,64,1]{2,1,0:T(8,128)} %copy.52.inv_ref), custom_call_target="tpu_custom_call" | custom-call | tf_op jit(solution)/shard_map/pallas_call | solution.py:88
  186.3 0.0 copy-done.11
  186.3 0.1 fusion.26
  186.4 0.1 fusion.24
  186.6 15.4 %collective-permute-done.2.above_ref = f32[8,64,896]{2,1,0:T(8,128)S(1)} collective-permute-done((f32[8,64,896]{2,1,0:T(8,128)}, f32[8,64,896]{2,1,0:T(8,128)S(1)}, u32[]{:S(2)}, u32[]{:S(2)}) %collective-permute-start.2) | collective-permute-done | bytes 1835040 | tf_op jit(solution)/shard_map/ppermute | solution.py:156
  202.0 0.1 slice_reduce_fusion.2
  202.1 0.1 fusion.18
  202.3 1.5 collective-permute-done.3.below_ref
  203.7 1.1 slice_reduce_fusion.1
  204.8 0.1 fusion.17
  204.9 0.2 copy.51
  205.2 0.9 broadcast_divide_fusion.inv_ref
  206.1 8.7 %shard_map.85 = bf16[64,64,768]{2,1,0:T(8,128)(2,1)} custom-call(f32[8,64,896]{2,1,0:T(8,128)} %copy-done.1, f32[64,64,768]{2,1,0:T(8,128)} %copy-done, f32[8,64,896]{2,1,0:T(8,128)} %collective-permute-done.3.below_ref, bf16[64,64,768]{2,1,0:T(8,128)(2,1)} %cb_ref.3, f32[16,64,1]{2,1,0:T(8,128)} %broadcast_divide_fusion.inv_ref, ...), custom_call_target="tpu_custom_call", output_to_operand_aliasing={{}: (5, {})} | custom-call | tf_op jit(solution)/shard_map/pallas_call | solution.py:134
  (33 shorter events, 0.2 us)
Async XLA Ops:
  0.0 6.3 %copy-start.3 = (s32[1024,1]{0,1:T(1,128)S(1)}, s32[1024,1]{0,1:T(1,128)}, u32[]{:S(2)}) copy-start(s32[1024,1]{0,1:T(1,128)} %param.15) | copy-start | bytes 12292
  4.8 1.9 copy-start.2
  14.3 55.0 %all-to-all-start = ((bf16[128,16,896]{2,1,0:T(8,128)(2,1)}), bf16[128,16,896]{2,1,0:T(8,128)(2,1)}, u32[]{:S(2)}, u32[]{:S(2)}) async-start(bf16[128,16,896]{2,1,0:T(8,128)(2,1)} %bitcast.51), calls=%async_computation | async-start | bytes 7340032 | tf_op jit(solution)/shard_map/all_to_all | solution.py:182
  85.5 43.7 %collective-permute-start = (f32[64,8,896]{2,1,0:T(8,128)}, f32[64,8,896]{2,1,0:T(8,128)S(1)}, u32[]{:S(2)}, u32[]{:S(2)}) collective-permute-start(f32[64,8,896]{2,1,0:T(8,128)} %pad_maximum_fusion), channel_id=1, source_target_pairs={{0,1},{1,2},{2,3},{3,4},{4,5},{5,6},{6,7},{8,9},{9,10},{10,11},{11... | collective-permute-start | bytes 5505032 | tf_op jit(solution)/shard_map/ppermute | solution.py:156
  91.9 46.1 %collective-permute-start.1 = (f32[64,8,896]{2,1,0:T(8,128)}, f32[64,8,896]{2,1,0:T(8,128)}, u32[]{:S(2)}, u32[]{:S(2)}) collective-permute-start(f32[64,8,896]{2,1,0:T(8,128)} %pad_maximum_fusion.1), channel_id=1, source_target_pairs={{1,0},{2,1},{3,2},{4,3},{5,4},{6,5},{7,6},{9,8},{10,9},{11,10},{12... | collective-permute-start | bytes 5505032 | tf_op jit(solution)/shard_map/ppermute | solution.py:156
  112.2 2.8 %copy-start.4 = (f32[64,64]{1,0:T(8,128)S(1)}, f32[64,64]{1,0:T(8,128)}, u32[]{:S(2)}) copy-start(f32[64,64]{1,0:T(8,128)} %constant.151) | copy-start | bytes 49156
  139.3 1.5 copy-start.7
  149.5 4.6 %copy-start = (f32[64,64,768]{2,1,0:T(8,128)}, f32[64,64,768]{2,1,0:T(8,128)S(1)}, u32[]{:S(2)}) copy-start(f32[64,64,768]{2,1,0:T(8,128)S(1)} %fusion.6.mid_ref) | copy-start | bytes 37748740
  154.0 0.8 copy-start.5
  154.0 1.0 copy-start.6
  156.8 45.2 %collective-permute-start.2 = (f32[8,64,896]{2,1,0:T(8,128)}, f32[8,64,896]{2,1,0:T(8,128)S(1)}, u32[]{:S(2)}, u32[]{:S(2)}) collective-permute-start(f32[8,64,896]{2,1,0:T(8,128)} %select_maximum_fusion.1), channel_id=1, source_target_pairs={{0,8},{8,16},{16,24},{24,32},{32,40},{40,48},{48,56},{56,64},{64,7... | collective-permute-start | bytes 5505032 | tf_op jit(solution)/shard_map/ppermute | solution.py:156
  162.7 4.3 %copy-start.12 = (f32[48,64]{1,0:T(8,128)S(1)}, f32[48,64]{1,0:T(8,128)}, u32[]{:S(2)}) copy-start(f32[48,64]{1,0:T(8,128)} %constant.154) | copy-start | bytes 36868
  165.1 38.6 %collective-permute-start.3 = (f32[8,64,896]{2,1,0:T(8,128)}, f32[8,64,896]{2,1,0:T(8,128)}, u32[]{:S(2)}, u32[]{:S(2)}) collective-permute-start(f32[8,64,896]{2,1,0:T(8,128)} %select_maximum_fusion), channel_id=1, source_target_pairs={{8,0},{16,8},{24,16},{32,24},{40,32},{48,40},{56,48},{64,56},{72,6... | collective-permute-start | bytes 5505032 | tf_op jit(solution)/shard_map/ppermute | solution.py:156
  169.2 17.1 %copy-start.11 = (f32[8,16]{1,0:T(8,128)S(1)}, f32[8,16]{1,0:T(8,128)}, u32[]{:S(2)}) copy-start(f32[8,16]{1,0:T(8,128)} %constant.156) | copy-start | bytes 1540
  169.2 17.2 %copy-start.10 = (f32[8,16]{1,0:T(8,128)S(1)}, f32[8,16]{1,0:T(8,128)}, u32[]{:S(2)}) copy-start(f32[8,16]{1,0:T(8,128)} %constant.157) | copy-start | bytes 1540
  169.2 32.9 %copy-start.9 = (f32[8,8]{1,0:T(8,128)S(1)}, f32[8,8]{1,0:T(8,128)}, u32[]{:S(2)}) copy-start(f32[8,8]{1,0:T(8,128)} %constant.155) | copy-start | bytes 772
  169.2 35.6 %copy-start.8 = (f32[8,8]{1,0:T(8,128)S(1)}, f32[8,8]{1,0:T(8,128)}, u32[]{:S(2)}) copy-start(f32[8,8]{1,0:T(8,128)} %constant.158) | copy-start | bytes 772
  202.0 4.1 %copy-start.1 = (f32[8,64,896]{2,1,0:T(8,128)}, f32[8,64,896]{2,1,0:T(8,128)S(1)}, u32[]{:S(2)}) copy-start(f32[8,64,896]{2,1,0:T(8,128)S(1)} %collective-permute-done.2.above_ref) | copy-start | bytes 5505028

commit v8 on v7

--- a/solution.py
+++ b/solution.py
@@ -66,23 +66,39 @@
     )(picks, *operands)
 
 
+TAPS = [math.exp(-2.0 * k * k / RADIUS**2) for k in range(RADIUS + 1)]
+GROUP = 4
+
+
+def row_group(read, cb_ref, inv_ref, out_ref, first, cols, lanes):
+    for c0 in range(0, cols, 8):
+        window = [read(j, c0, lanes) for j in range(GROUP + 2 * RADIUS)]
+        for q in range(GROUP):
+            centre = q + RADIUS
+            acc = TAPS[0] * window[centre]
+            for k in range(1, RADIUS + 1):
+                acc = acc + TAPS[k] * (window[centre - k] + window[centre + k])
+            r = first + q
+            base = cb_ref[r, pl.ds(c0, 8), lanes].astype(jnp.float32)
+            upd = (acc + 8.0 * base) * inv_ref[r, pl.ds(c0, 8), :]
+            out_ref[r, pl.ds(c0, 8), lanes] = upd.astype(out_ref.dtype)
+
+
 def finish_inner(middle, codebook, inv):
     rows, cols, feature = middle.shape
     lanes = 128
 
     def kernel(mid_ref, cb_ref, inv_ref, out_ref):
-        ext = mid_ref
-        taps = [math.exp(-2.0 * k * k / RADIUS**2) for k in range(RADIUS + 1)]
-
-        def body(r, carry):
-            acc = taps[0] * ext[r]
-            for k in range(1, RADIUS + 1):
-                acc = acc + taps[k] * (ext[r - k] + ext[r + k])
-            upd = (acc + 8.0 * cb_ref[r].astype(jnp.float32)) * inv_ref[r]
-            out_ref[r] = upd.astype(out_ref.dtype)
+        def body(i, carry):
+            first = RADIUS + i * GROUP
+
+            def read(j, c0, part):
+                return mid_ref[first + j - RADIUS, pl.ds(c0, 8), part]
+
+            row_group(read, cb_ref, inv_ref, out_ref, first, cols, slice(None))
             return carry
 
-        lax.fori_loop(RADIUS, rows - RADIUS, body, 0, unroll=2)
+        lax.fori_loop(0, (rows - 2 * RADIUS) // GROUP, body, 0)
 
     slab_spec = pl.BlockSpec((rows, cols, lanes), lambda j: (0, 0, j))
     return pl.pallas_call(
@@ -99,7 +115,6 @@
     lanes = 128
     near = 2 * RADIUS
     last_edge = rows // RADIUS - 1
-    taps = [math.exp(-2.0 * k * k / RADIUS**2) for k in range(RADIUS + 1)]
 
     def kernel(above_ref, mid_ref, below_ref, cb_ref, inv_ref, prev_ref, out_ref, ext_ref):
         del prev_ref
@@ -115,19 +130,17 @@
             ext_ref[0:near] = mid_ref[...]
             ext_ref[near:] = below_ref[...]
 
-        def body(r, carry):
-            centre = r + RADIUS
-            scale = inv_ref[r]
+        def body(i, carry):
+            first = i * GROUP
+
+            def read(j, c0, part):
+                return ext_ref[first + j, pl.ds(c0, 8), part]
+
             for lane in range(0, feature, lanes):
-                part = pl.ds(lane, lanes)
-                acc = taps[0] * ext_ref[centre, :, part]
-                for k in range(1, RADIUS + 1):
-                    acc = acc + taps[k] * (ext_ref[centre - k, :, part] + ext_ref[centre + k, :, part])
-                upd = (acc + 8.0 * cb_ref[r, :, part].astype(jnp.float32)) * scale
-                out_ref[r, :, part] = upd.astype(out_ref.dtype)
+                row_group(read, cb_ref, inv_ref, out_ref, first, cols, pl.ds(lane, lanes))
             return carry
 
-        lax.fori_loop(0, RADIUS, body, 0)
+        lax.fori_loop(0, RADIUS // GROUP, body, 0)
 
     halo_spec = pl.BlockSpec((RADIUS, cols, feature), lambda i: (0, 0, 0))
     edge_spec = pl.BlockSpec((RADIUS, cols, feature), lambda i: (i * last_edge, 0, 0))

time: 216 us -> 215 us (level)
  Pallas kernels: 52.7 us -> 50.5 us
where the time goes in v8:
time: 215 us; the launch traced here: 214 us
  waiting for transfers between devices  84.2 us (39%)
  Pallas kernels  50.5 us (23%)
  starting transfers between devices  25.1 us (12%)
  other arithmetic  23.7 us (11%)
  local copies, waits for them, and re-layouts  20.3 us (9%)
  matrix products  9.81 us (5%)
    all_to_all x1, waiting for transfers between devices, on_device(): lax.all_to_all(outgoing.reshape(tile_total, capacity, width), ('mx', 'my'...  43.4 us
    ppermute x4, waiting for transfers between devices, exchange(): return (lax.ppermute(last, axis, up), lax.ppermute(lead, axis, down))  40.8 us
    pallas_call x2, Pallas kernels, accumulate(): pl.pallas_call(kernel, grid_spec=pltpu.PrefetchScalarGridSpec(num_scalar_...  26.9 us
    pallas_call x1, Pallas kernels, finish_inner(): pl.pallas_call(kernel, grid=(feature // lanes,), in_specs=[slab_spec, sla...  15.6 us
    ppermute x4, starting transfers between devices, exchange(): return (lax.ppermute(last, axis, up), lax.ppermute(lead, axis, down))  14.1 us
    all_to_all x1, starting transfers between devices, on_device(): lax.all_to_all(outgoing.reshape(tile_total, capacity, width), ('mx', 'my'...  11.1 us
    dot_general x1, matrix products, on_device(): col_num = jnp.einsum('ck,rke->rce', g_cols, ext_num, precision=HI)  8.6 us
    pallas_call x1, Pallas kernels, finish_edges(): pl.pallas_call(kernel, grid=(2,), in_specs=[halo_spec, pl.BlockSpec((near...  7.93 us
  transfers between devices with their start and end apart: 5, of which 5 were waited for; matrix products, arithmetic and copies ran while one was open for 5% of the time, Pallas kernels for 16%

profile of v8, /device:TPU:15, one launch (start us, length us, event | category | flops | bytes accessed | tf_op | source)
XLA Modules:
  0.0 214.0 jit_solution(7329885297230283061)
XLA Ops:
  0.0 0.6 compare_reduce_fusion.1
  0.6 0.7 compare_reduce_fusion.2
  1.4 0.6 compare_reduce_fusion
  2.0 2.0 fusion.35
  4.1 0.1 scatter.19
  4.2 0.6 broadcast_select_fusion
  4.7 0.1 scatter.24
  4.8 0.0 copy-start.2
  4.8 0.2 copy.45
  5.0 0.9 copy.43
  5.9 0.2 fusion.21
  6.2 0.1 copy.44
  6.3 0.4 fusion.20
  6.7 7.6 %scatter_custom_fusion = bf16[2048,896]{1,0:T(8,128)(2,1)} fusion(s32[1024]{0:T(1024)S(1)} %bitcast.57, bf16[1024,128]{1,0:T(8,128)(2,1)S(1)} %copy.45, bf16[]{:T(256)} %constant.171, bf16[1024,768]{1,0:T(8,128)(2,1)S(1)} %copy-done.2, bf16[]{:T(256)} %constant.124.clone.1), kind=kCustom, calls=%fused_computation.12 | custom fusion | flops 3670016 | bytes 5505028 | tf_op jit(solution)/shard_map/scatter | solution.py:194
  14.3 11.1 %all-to-all-start = ((bf16[128,16,896]{2,1,0:T(8,128)(2,1)}), bf16[128,16,896]{2,1,0:T(8,128)(2,1)}, u32[]{:S(2)}, u32[]{:S(2)}) async-start(bf16[128,16,896]{2,1,0:T(8,128)(2,1)} %bitcast.51), calls=%async_computation | async-start | bytes 7340032 | tf_op jit(solution)/shard_map/all_to_all | solution.py:195
  25.4 0.5 iota_multiply_fusion.1.picks_ref
  26.0 43.4 %all-to-all-done = bf16[128,16,896]{2,1,0:T(8,128)(2,1)} async-done(((bf16[128,16,896]{2,1,0:T(8,128)(2,1)}), bf16[128,16,896]{2,1,0:T(8,128)(2,1)}, u32[]{:S(2)}, u32[]{:S(2)}) %all-to-all-start) | async-done | bytes 3670048 | tf_op jit(solution)/shard_map/all_to_all | solution.py:195
  69.3 2.9 %select_reduce_fusion = s32[2048]{0:T(1024)} fusion(bf16[2048,896]{1,0:T(8,128)(2,1)} %bitcast.8.docs_ref), kind=kLoop, calls=%fused_computation.28 | loop fusion | flops 12288 | bytes 20480 | tf_op jit(solution)/shard_map/jit(_where)/select_n | solution.py:204
  72.3 8.7 %shard_map.82 = (f32[64,64,768]{2,1,0:T(8,128)}, f32[64,64,128]{2,1,0:T(8,128)}) custom-call(s32[2]{0:T(128)} %iota_multiply_fusion.1.picks_ref, s32[1,2048]{1,0:T(1,128)} %bitcast.52, bf16[2048,896]{1,0:T(8,128)(2,1)} %bitcast.8.docs_ref), custom_call_target="tpu_custom_call" | custom-call | tf_op jit(solution)/shard_map/pallas_call | solution.py:53
  81.0 2.1 fusion.39
  83.1 1.1 fusion.40
  84.1 1.4 pad_maximum_fusion
  85.5 5.0 %collective-permute-start = (f32[64,8,896]{2,1,0:T(8,128)}, f32[64,8,896]{2,1,0:T(8,128)S(1)}, u32[]{:S(2)}, u32[]{:S(2)}) collective-permute-start(f32[64,8,896]{2,1,0:T(8,128)} %pad_maximum_fusion), channel_id=1, source_target_pairs={{0,1},{1,2},{2,3},{3,4},{4,5},{5,6},{6,7},{8,9},{9,10},{10,11},{11... | collective-permute-start | bytes 5505032 | tf_op jit(solution)/shard_map/ppermute | solution.py:169
  90.6 1.3 pad_maximum_fusion.1
  91.9 2.1 collective-permute-start.1
  94.0 18.2 %shard_map.83 = (f32[64,64,768]{2,1,0:T(8,128)}, f32[64,64,128]{2,1,0:T(8,128)}) custom-call(s32[6]{0:T(128)} %constant.142.clone.picks_ref, s32[1,2048]{1,0:T(1,128)} %bitcast.53, bf16[2048,896]{1,0:T(8,128)(2,1)} %bitcast.8.docs_ref, f32[64,64,768]{2,1,0:T(8,128)} %get-tuple-element.45.refs_0_, ...), custom_call_target="tpu_custom_call", output_to_operand_aliasing={{0}: (3, {}), {1}: (4, {})} | custom-call | tf_op jit(solution)/shard_map/pallas_call | solution.py:53
  112.2 2.8 %slice_reduce_fusion = f32[64,64]{1,0:T(8,128)S(1)} fusion(f32[64,64,128]{2,1,0:T(8,128)} %get-tuple-element.48), kind=kLoop, calls=%fused_computation.8 | loop fusion | bytes 32768 | tf_op jit(solution)/shard_map/slice | solution.py:215
  115.0 0.2 fusion.41
  115.2 14.0 %collective-permute-done = f32[64,8,896]{2,1,0:T(8,128)S(1)} collective-permute-done((f32[64,8,896]{2,1,0:T(8,128)}, f32[64,8,896]{2,1,0:T(8,128)S(1)}, u32[]{:S(2)}, u32[]{:S(2)}) %collective-permute-start) | collective-permute-done | bytes 1835040 | tf_op jit(solution)/shard_map/ppermute | solution.py:169
  129.2 0.1 slice.159
  129.3 0.1 copy.46
  129.5 8.5 %collective-permute-done.1 = f32[64,8,896]{2,1,0:T(8,128)} collective-permute-done((f32[64,8,896]{2,1,0:T(8,128)}, f32[64,8,896]{2,1,0:T(8,128)}, u32[]{:S(2)}, u32[]{:S(2)}) %collective-permute-start.1) | collective-permute-done | bytes 1835040 | tf_op jit(solution)/shard_map/ppermute | solution.py:169
  138.0 1.1 slice.160
  139.0 0.1 copy.47
  139.2 0.1 slice.156
  139.3 0.0 copy-start.7
  139.3 1.5 slice.157
  140.9 8.6 %fusion.6.mid_ref = f32[64,64,768]{2,1,0:T(8,128)S(1)} fusion(f32[64,80,1]{1,0,2:T(8,128)S(1)} %copy-done.7, f32[64,8,768]{2,1,0:T(8,128)S(1)} %slice.157, f32[64,64,768]{2,1,0:T(8,128)} %get-tuple-element.47, f32[64,8,768]{2,1,0:T(8,128)S(1)} %slice.156), kind=kOutput, calls=%fused_computation.7 | convolution fusion | flops 1517813760 | bytes 28332032 | tf_op jit(solution)/shard_map/ck,rke->rce/dot_general | solution.py:221
  149.5 4.6 %copy-done = f32[64,64,768]{2,1,0:T(8,128)} copy-done((f32[64,64,768]{2,1,0:T(8,128)}, f32[64,64,768]{2,1,0:T(8,128)S(1)}, u32[]{:S(2)}) %copy-start) | copy-done | bytes 12582936
  154.0 0.3 fusion.38
  154.3 0.5 copy-done.5
  154.8 0.2 fusion.30
  155.0 0.2 fusion.14
  155.3 0.1 copy.48
  155.4 1.4 select_maximum_fusion.1
  156.8 5.0 %collective-permute-start.2 = (f32[8,64,896]{2,1,0:T(8,128)}, f32[8,64,896]{2,1,0:T(8,128)S(1)}, u32[]{:S(2)}, u32[]{:S(2)}) collective-permute-start(f32[8,64,896]{2,1,0:T(8,128)} %select_maximum_fusion.1), channel_id=1, source_target_pairs={{0,8},{8,16},{16,24},{24,32},{32,40},{40,48},{48,56},{56,64},{64,7... | collective-permute-start | bytes 5505032 | tf_op jit(solution)/shard_map/ppermute | solution.py:169
  161.9 0.9 copy.49
  162.7 2.4 %select_maximum_fusion = f32[8,64,896]{2,1,0:T(8,128)} fusion(f32[8,64,1]{2,1,0:T(8,128)} %copy.49, f32[8,64,768]{2,1,0:T(8,128)S(1)} %get-tuple-element.49), kind=kLoop, calls=%fused_computation.9 | loop fusion | flops 1376256 | bytes 3409920 | tf_op jit(solution)/shard_map/concatenate | solution.py:226
  165.1 1.9 collective-permute-start.3
  167.0 0.1 fusion.16
  167.2 2.1 copy.52.inv_ref
  169.2 15.6 %shard_map.84.prev_ref = bf16[64,64,768]{2,1,0:T(8,128)(2,1)} custom-call(f32[64,64,768]{2,1,0:T(8,128)} %copy-done, bf16[64,64,768]{2,1,0:T(8,128)(2,1)} %cb_ref.3, f32[64,64,1]{2,1,0:T(8,128)} %copy.52.inv_ref), custom_call_target="tpu_custom_call" | custom-call | tf_op jit(solution)/shard_map/pallas_call | solution.py:104
  184.9 0.1 fusion.26
  185.0 0.1 fusion.24
  185.1 16.9 %collective-permute-done.2.above_ref = f32[8,64,896]{2,1,0:T(8,128)S(1)} collective-permute-done((f32[8,64,896]{2,1,0:T(8,128)}, f32[8,64,896]{2,1,0:T(8,128)S(1)}, u32[]{:S(2)}, u32[]{:S(2)}) %collective-permute-start.2) | collective-permute-done | bytes 1835040 | tf_op jit(solution)/shard_map/ppermute | solution.py:169
  202.0 0.1 slice_reduce_fusion.2
  202.1 0.0 copy-done.9
  202.1 0.1 fusion.18
  202.3 1.5 collective-permute-done.3.below_ref
  203.7 1.1 slice_reduce_fusion.1
  204.8 0.1 fusion.17
  204.9 0.2 copy.51
  205.2 0.9 broadcast_divide_fusion.inv_ref
  206.1 7.9 %shard_map.85 = bf16[64,64,768]{2,1,0:T(8,128)(2,1)} custom-call(f32[8,64,896]{2,1,0:T(8,128)} %copy-done.1, f32[64,64,768]{2,1,0:T(8,128)} %copy-done, f32[8,64,896]{2,1,0:T(8,128)} %collective-permute-done.3.below_ref, bf16[64,64,768]{2,1,0:T(8,128)(2,1)} %cb_ref.3, f32[16,64,1]{2,1,0:T(8,128)} %broadcast_divide_fusion.inv_ref, ...), custom_call_target="tpu_custom_call", output_to_operand_aliasing={{}: (5, {})} | custom-call | tf_op jit(solution)/shard_map/pallas_call | solution.py:147
  (33 shorter events, 0.2 us)
Async XLA Ops:
  0.0 6.3 %copy-start.3 = (s32[1024,1]{0,1:T(1,128)S(1)}, s32[1024,1]{0,1:T(1,128)}, u32[]{:S(2)}) copy-start(s32[1024,1]{0,1:T(1,128)} %param.15) | copy-start | bytes 12292
  4.8 1.9 copy-start.2
  14.3 55.0 %all-to-all-start = ((bf16[128,16,896]{2,1,0:T(8,128)(2,1)}), bf16[128,16,896]{2,1,0:T(8,128)(2,1)}, u32[]{:S(2)}, u32[]{:S(2)}) async-start(bf16[128,16,896]{2,1,0:T(8,128)(2,1)} %bitcast.51), calls=%async_computation | async-start | bytes 7340032 | tf_op jit(solution)/shard_map/all_to_all | solution.py:195
  85.5 43.7 %collective-permute-start = (f32[64,8,896]{2,1,0:T(8,128)}, f32[64,8,896]{2,1,0:T(8,128)S(1)}, u32[]{:S(2)}, u32[]{:S(2)}) collective-permute-start(f32[64,8,896]{2,1,0:T(8,128)} %pad_maximum_fusion), channel_id=1, source_target_pairs={{0,1},{1,2},{2,3},{3,4},{4,5},{5,6},{6,7},{8,9},{9,10},{10,11},{11... | collective-permute-start | bytes 5505032 | tf_op jit(solution)/shard_map/ppermute | solution.py:169
  91.9 46.1 %collective-permute-start.1 = (f32[64,8,896]{2,1,0:T(8,128)}, f32[64,8,896]{2,1,0:T(8,128)}, u32[]{:S(2)}, u32[]{:S(2)}) collective-permute-start(f32[64,8,896]{2,1,0:T(8,128)} %pad_maximum_fusion.1), channel_id=1, source_target_pairs={{1,0},{2,1},{3,2},{4,3},{5,4},{6,5},{7,6},{9,8},{10,9},{11,10},{12... | collective-permute-start | bytes 5505032 | tf_op jit(solution)/shard_map/ppermute | solution.py:169
  112.2 2.8 %copy-start.4 = (f32[64,64]{1,0:T(8,128)S(1)}, f32[64,64]{1,0:T(8,128)}, u32[]{:S(2)}) copy-start(f32[64,64]{1,0:T(8,128)} %constant.151) | copy-start | bytes 49156
  139.3 1.5 copy-start.7
  149.5 4.6 %copy-start = (f32[64,64,768]{2,1,0:T(8,128)}, f32[64,64,768]{2,1,0:T(8,128)S(1)}, u32[]{:S(2)}) copy-start(f32[64,64,768]{2,1,0:T(8,128)S(1)} %fusion.6.mid_ref) | copy-start | bytes 37748740
  154.0 0.8 copy-start.5
  154.0 1.0 copy-start.6
  156.8 45.2 %collective-permute-start.2 = (f32[8,64,896]{2,1,0:T(8,128)}, f32[8,64,896]{2,1,0:T(8,128)S(1)}, u32[]{:S(2)}, u32[]{:S(2)}) collective-permute-start(f32[8,64,896]{2,1,0:T(8,128)} %select_maximum_fusion.1), channel_id=1, source_target_pairs={{0,8},{8,16},{16,24},{24,32},{32,40},{40,48},{48,56},{56,64},{64,7... | collective-permute-start | bytes 5505032 | tf_op jit(solution)/shard_map/ppermute | solution.py:169
  162.7 4.3 %copy-start.12 = (f32[48,64]{1,0:T(8,128)S(1)}, f32[48,64]{1,0:T(8,128)}, u32[]{:S(2)}) copy-start(f32[48,64]{1,0:T(8,128)} %constant.154) | copy-start | bytes 36868
  165.1 38.6 %collective-permute-start.3 = (f32[8,64,896]{2,1,0:T(8,128)}, f32[8,64,896]{2,1,0:T(8,128)}, u32[]{:S(2)}, u32[]{:S(2)}) collective-permute-start(f32[8,64,896]{2,1,0:T(8,128)} %select_maximum_fusion), channel_id=1, source_target_pairs={{8,0},{16,8},{24,16},{32,24},{40,32},{48,40},{56,48},{64,56},{72,6... | collective-permute-start | bytes 5505032 | tf_op jit(solution)/shard_map/ppermute | solution.py:169
  169.2 15.6 %copy-start.11 = (f32[8,16]{1,0:T(8,128)S(1)}, f32[8,16]{1,0:T(8,128)}, u32[]{:S(2)}) copy-start(f32[8,16]{1,0:T(8,128)} %constant.156) | copy-start | bytes 1540
  169.2 15.8 %copy-start.10 = (f32[8,16]{1,0:T(8,128)S(1)}, f32[8,16]{1,0:T(8,128)}, u32[]{:S(2)}) copy-start(f32[8,16]{1,0:T(8,128)} %constant.157) | copy-start | bytes 1540
  169.2 32.9 %copy-start.9 = (f32[8,8]{1,0:T(8,128)S(1)}, f32[8,8]{1,0:T(8,128)}, u32[]{:S(2)}) copy-start(f32[8,8]{1,0:T(8,128)} %constant.155) | copy-start | bytes 772
  169.2 35.6 %copy-start.8 = (f32[8,8]{1,0:T(8,128)S(1)}, f32[8,8]{1,0:T(8,128)}, u32[]{:S(2)}) copy-start(f32[8,8]{1,0:T(8,128)} %constant.158) | copy-start | bytes 772
  202.0 4.1 %copy-start.1 = (f32[8,64,896]{2,1,0:T(8,128)}, f32[8,64,896]{2,1,0:T(8,128)S(1)}, u32[]{:S(2)}) copy-start(f32[8,64,896]{2,1,0:T(8,128)S(1)} %collective-permute-done.2.above_ref) | copy-start | bytes 5505028

commit v9 on v8

--- a/solution.py
+++ b/solution.py
@@ -84,50 +84,64 @@
             out_ref[r, pl.ds(c0, 8), lanes] = upd.astype(out_ref.dtype)
 
 
-def finish_inner(middle, codebook, inv):
-    rows, cols, feature = middle.shape
+def finish_inner(top, middle, bottom, codebook, inv):
+    inner, cols, feature = middle.shape
+    rows = inner + 2 * RADIUS
     lanes = 128
 
-    def kernel(mid_ref, cb_ref, inv_ref, out_ref):
-        def body(i, carry):
-            first = RADIUS + i * GROUP
-
-            def read(j, c0, part):
-                return mid_ref[first + j - RADIUS, pl.ds(c0, 8), part]
+    def kernel(top_ref, mid_ref, bot_ref, cb_ref, inv_ref, out_ref):
+        def read_row(rr, c0):
+            if rr < RADIUS:
+                return top_ref[rr, pl.ds(c0, 8), :]
+            if rr < RADIUS + inner:
+                return mid_ref[rr - RADIUS, pl.ds(c0, 8), :]
+            return bot_ref[rr - RADIUS - inner, pl.ds(c0, 8), :]
+
+        for first in range(RADIUS, rows - RADIUS, GROUP):
+
+            def read(j, c0, part, first=first):
+                return read_row(first + j - RADIUS, c0)
 
             row_group(read, cb_ref, inv_ref, out_ref, first, cols, slice(None))
-            return carry
-
-        lax.fori_loop(0, (rows - 2 * RADIUS) // GROUP, body, 0)
-
+
+    band_spec = pl.BlockSpec((RADIUS, cols, lanes), lambda j: (0, 0, j))
     slab_spec = pl.BlockSpec((rows, cols, lanes), lambda j: (0, 0, j))
     return pl.pallas_call(
         kernel,
         grid=(feature // lanes,),
-        in_specs=[slab_spec, slab_spec, pl.BlockSpec((rows, cols, 1), lambda j: (0, 0, 0))],
+        in_specs=[
+            band_spec,
+            pl.BlockSpec((inner, cols, lanes), lambda j: (0, 0, j)),
+            band_spec,
+            slab_spec,
+            pl.BlockSpec((rows, cols, 1), lambda j: (0, 0, 0)),
+        ],
         out_specs=slab_spec,
         out_shape=jax.ShapeDtypeStruct(codebook.shape, codebook.dtype),
-    )(middle, codebook, inv)
-
-
-def finish_edges(above, middle, below, codebook, inv, partial):
-    rows, cols, feature = middle.shape
+    )(top, middle, bottom, codebook, inv)
+
+
+def finish_edges(above, top, middle, bottom, below, codebook, inv, partial):
+    rows, cols, feature = codebook.shape
     lanes = 128
     near = 2 * RADIUS
     last_edge = rows // RADIUS - 1
-
-    def kernel(above_ref, mid_ref, below_ref, cb_ref, inv_ref, prev_ref, out_ref, ext_ref):
+    mid_last = middle.shape[0] // RADIUS - 1
+
+    def kernel(above_ref, top_ref, mid_ref, bot_ref, below_ref, cb_ref, inv_ref, prev_ref, out_ref, ext_ref):
         del prev_ref
         side = pl.program_id(0)
 
         @pl.when(side == 0)
         def _():
             ext_ref[0:RADIUS] = above_ref[...]
-            ext_ref[RADIUS:] = mid_ref[...]
+            ext_ref[RADIUS:near] = top_ref[...]
+            ext_ref[near:] = mid_ref[...]
 
         @pl.when(side == 1)
         def _():
-            ext_ref[0:near] = mid_ref[...]
+            ext_ref[0:RADIUS] = mid_ref[...]
+            ext_ref[RADIUS:near] = bot_ref[...]
             ext_ref[near:] = below_ref[...]
 
         def body(i, carry):
@@ -142,15 +156,17 @@
 
         lax.fori_loop(0, RADIUS // GROUP, body, 0)
 
-    halo_spec = pl.BlockSpec((RADIUS, cols, feature), lambda i: (0, 0, 0))
+    band_spec = pl.BlockSpec((RADIUS, cols, feature), lambda i: (0, 0, 0))
     edge_spec = pl.BlockSpec((RADIUS, cols, feature), lambda i: (i * last_edge, 0, 0))
     return pl.pallas_call(
         kernel,
         grid=(2,),
         in_specs=[
-            halo_spec,
-            pl.BlockSpec((near, cols, feature), lambda i: (i * (rows // near - 1), 0, 0)),
-            halo_spec,
+            band_spec,
+            band_spec,
+            pl.BlockSpec((RADIUS, cols, feature), lambda i: (i * mid_last, 0, 0)),
+            band_spec,
+            band_spec,
             edge_spec,
             pl.BlockSpec((RADIUS, cols, 1), lambda i: (i, 0, 0)),
             pl.BlockSpec(memory_space=pl.ANY),
@@ -158,8 +174,8 @@
         out_specs=edge_spec,
         out_shape=jax.ShapeDtypeStruct(codebook.shape, codebook.dtype),
         scratch_shapes=[pltpu.VMEM((near + RADIUS, cols, feature), jnp.float32)],
-        input_output_aliases={5: 0},
-    )(above, middle, below, codebook, inv, partial)
+        input_output_aliases={7: 0},
+    )(above, top, middle, bottom, below, codebook, inv, partial)
 
 
 def exchange(lead, last, axis):
@@ -216,17 +232,27 @@
 
     g_rows = jnp.asarray(band_matrix(rows_tile))
     g_cols = jnp.asarray(band_matrix(cols_tile))
-    ext_num = jnp.concatenate([from_left, numerator, from_right], axis=1)
     ext_hits = jnp.concatenate([hits_left, counter, hits_right], axis=1)
-    col_num = jnp.einsum("ck,rke->rce", g_cols, ext_num, precision=HI)
     col_hits = jnp.einsum("ck,rk->rc", g_cols, ext_hits, precision=HI)
     last = rows_tile - RADIUS
-    def with_hits(rows):
+
+    def col_pass(lo, hi):
+        pieces = [from_left[lo:hi], numerator[lo:hi], from_right[lo:hi]]
+        return jnp.einsum("ck,rke->rce", g_cols, jnp.concatenate(pieces, axis=1), precision=HI)
+
+    col_top, col_bottom = col_pass(0, RADIUS), col_pass(last, rows_tile)
+
+    def with_hits(part, rows):
         hit_lanes = jnp.pad(col_hits[rows][:, :, None], ((0, 0), (0, 0), (0, 127)))
-        return jnp.concatenate([col_num[rows], hit_lanes], axis=2)
-
-    above, below = exchange(with_hits(slice(0, RADIUS)), with_hits(slice(last, rows_tile)), "mx")
+        return jnp.concatenate([part, hit_lanes], axis=2)
+
+    above, below = exchange(
+        with_hits(col_top, slice(0, RADIUS)),
+        with_hits(col_bottom, slice(last, rows_tile)),
+        "mx",
+    )
     hits_above, hits_below = above[:, :, feature], below[:, :, feature]
+    col_mid = col_pass(RADIUS, last)
     inner_hits = jnp.einsum("rk,kc->rc", g_rows[RADIUS:last, RADIUS : RADIUS + rows_tile], col_hits, precision=HI)
     inv_inner = 1.0 / (inner_hits + 8.0)
     inv = jnp.concatenate([jnp.zeros_like(inv_inner[:RADIUS]), inv_inner, jnp.zeros_like(inv_inner[:RADIUS])])
@@ -237,8 +263,8 @@
     top_hits = jnp.einsum("rk,kc->rc", g_edge, edge_top, precision=HI)
     bottom_hits = jnp.einsum("rk,kc->rc", g_edge, edge_bottom, precision=HI)
     inv_edges = (1.0 / (jnp.concatenate([top_hits, bottom_hits], axis=0) + 8.0))[:, :, None]
-    partial = finish_inner(col_num, codebook, inv)
-    return finish_edges(above, col_num, below, codebook, inv_edges, partial)
+    partial = finish_inner(col_top, col_mid, col_bottom, codebook, inv)
+    return finish_edges(above, col_top, col_mid, col_bottom, below, codebook, inv_edges, partial)
 
 
 def solution(mesh):

time: 215 us -> 206 us (0.958); the launches traced: 214 us -> 202 us
  waiting for transfers between devices: 84.2 us -> 57.4 us
  local copies, waits for them, and re-layouts: 20.3 us -> 29.4 us
  matrix products: 9.81 us -> 14.3 us
  starting transfers between devices: 25.1 us -> 27.5 us
    ppermute x4, waiting for transfers between devices: 40.8 us -> 14.1 us  [exchange(): return (lax.ppermute(last, axis, up), lax.ppermute(lead, axis, down))]
    slice x3 -> x6, local copies, waits for them, and re-layouts: 1.93 us -> 15.3 us  [col_pass(): pieces = [from_left[lo:hi], numerator[lo:hi], from_right[lo:hi]]]
    dot_general x1 -> x3, matrix products: 8.6 us -> 13 us  [col_pass(): jnp.einsum('ck,rke->rce', g_cols, jnp.concatenate(pieces, axis=1), precis...]
    unnamed x26 -> x28, local copies, waits for them, and re-layouts: 5.08 us -> 0.7 us
    ppermute x4, starting transfers between devices: 14.1 us -> 16.4 us  [exchange(): return (lax.ppermute(last, axis, up), lax.ppermute(lead, axis, down))]
  transfers between devices with their start and end apart: 5 -> 5, of which waited for: 5 -> 3; matrix products, arithmetic and copies ran while one was open for 5% -> 18% of each run, Pallas kernels for 16% -> 16%
where the time goes in v9:
time: 206 us; the launch traced here: 202 us
  waiting for transfers between devices  57.4 us (28%)
  Pallas kernels  50.4 us (24%)
  local copies, waits for them, and re-layouts  29.4 us (14%)
  starting transfers between devices  27.5 us (13%)
  other arithmetic  23.1 us (11%)
  matrix products  14.3 us (7%)
    all_to_all x1, waiting for transfers between devices, on_device(): lax.all_to_all(outgoing.reshape(tile_total, capacity, width), ('mx', 'my'...  43.4 us
    pallas_call x2, Pallas kernels, accumulate(): pl.pallas_call(kernel, grid_spec=pltpu.PrefetchScalarGridSpec(num_scalar_...  26.9 us
    ppermute x4, starting transfers between devices, exchange(): return (lax.ppermute(last, axis, up), lax.ppermute(lead, axis, down))  16.4 us
    slice x6, local copies, waits for them, and re-layouts, col_pass(): pieces = [from_left[lo:hi], numerator[lo:hi], from_right[lo:hi]]  15.3 us
    pallas_call x1, Pallas kernels, finish_inner(): pl.pallas_call(kernel, grid=(feature // lanes,), in_specs=[band_spec, pl....  15 us
    ppermute x4, waiting for transfers between devices, exchange(): return (lax.ppermute(last, axis, up), lax.ppermute(lead, axis, down))  14.1 us
    dot_general x3, matrix products, col_pass(): jnp.einsum('ck,rke->rce', g_cols, jnp.concatenate(pieces, axis=1), precis...  13 us
    all_to_all x1, starting transfers between devices, on_device(): lax.all_to_all(outgoing.reshape(tile_total, capacity, width), ('mx', 'my'...  11.1 us
  transfers between devices with their start and end apart: 5, of which 3 were waited for; matrix products, arithmetic and copies ran while one was open for 18% of the time, Pallas kernels for 16%

profile of v9, /device:TPU:15, one launch (start us, length us, event | category | flops | bytes accessed | tf_op | source)
XLA Modules:
  0.0 202.5 jit_solution(11341487750785373346)
XLA Ops:
  0.0 0.7 compare_reduce_fusion.2
  0.7 0.6 compare_reduce_fusion.1
  1.4 0.6 compare_reduce_fusion
  2.0 2.0 %fusion.53 = (bf16[1024]{0:T(1024)(128)(2,1)S(1)}, bf16[1024]{0:T(1024)(128)(2,1)S(1)}) fusion(s32[1024]{0:T(1024)} %param.16, pred[]{:T(512)} %compare_reduce_fusion.1, pred[]{:T(512)} %compare_reduce_fusion.2), kind=kLoop, calls=%fused_computation.79 | loop fusion | flops 23552 | bytes 8194 | tf_op jit(solution)/shard_map/select.14
  4.1 0.8 copy.43
  4.9 0.1 scatter.19
  4.9 0.6 broadcast_select_fusion
  5.5 0.1 scatter.24
  5.6 0.2 copy.45
  5.8 0.2 fusion.39
  6.1 0.1 copy.44
  6.2 0.4 fusion.38
  6.6 0.4 copy-done.3
  7.0 7.6 %scatter_custom_fusion = bf16[2048,896]{1,0:T(8,128)(2,1)} fusion(s32[1024]{0:T(1024)S(1)} %bitcast.64, bf16[1024,128]{1,0:T(8,128)(2,1)S(1)} %copy.45, bf16[]{:T(256)} %constant.173, bf16[1024,768]{1,0:T(8,128)(2,1)S(1)} %copy-done.3, bf16[]{:T(256)} %constant.124.clone.1), kind=kCustom, calls=%fused_computation.24 | custom fusion | flops 3670016 | bytes 5505028 | tf_op jit(solution)/shard_map/scatter | solution.py:210
  14.7 11.1 %all-to-all-start = ((bf16[128,16,896]{2,1,0:T(8,128)(2,1)}), bf16[128,16,896]{2,1,0:T(8,128)(2,1)}, u32[]{:S(2)}, u32[]{:S(2)}) async-start(bf16[128,16,896]{2,1,0:T(8,128)(2,1)} %bitcast.58), calls=%async_computation | async-start | bytes 7340032 | tf_op jit(solution)/shard_map/all_to_all | solution.py:211
  25.7 0.5 iota_multiply_fusion.1.picks_ref
  26.3 43.4 %all-to-all-done = bf16[128,16,896]{2,1,0:T(8,128)(2,1)} async-done(((bf16[128,16,896]{2,1,0:T(8,128)(2,1)}), bf16[128,16,896]{2,1,0:T(8,128)(2,1)}, u32[]{:S(2)}, u32[]{:S(2)}) %all-to-all-start) | async-done | bytes 3670048 | tf_op jit(solution)/shard_map/all_to_all | solution.py:211
  69.6 2.9 %select_reduce_fusion = s32[2048]{0:T(1024)} fusion(bf16[2048,896]{1,0:T(8,128)(2,1)} %bitcast.8.docs_ref), kind=kLoop, calls=%fused_computation.42 | loop fusion | flops 12288 | bytes 20480 | tf_op jit(solution)/shard_map/jit(_where)/select_n | solution.py:220
  72.6 8.7 %shard_map.82 = (f32[64,64,768]{2,1,0:T(8,128)}, f32[64,64,128]{2,1,0:T(8,128)}) custom-call(s32[2]{0:T(128)} %iota_multiply_fusion.1.picks_ref, s32[1,2048]{1,0:T(1,128)} %bitcast.59, bf16[2048,896]{1,0:T(8,128)(2,1)} %bitcast.8.docs_ref), custom_call_target="tpu_custom_call" | custom-call | tf_op jit(solution)/shard_map/pallas_call | solution.py:53
  81.3 1.1 fusion.60
  82.4 2.1 %fusion.59 = (f32[64,8,768]{2,1,0:T(8,128)S(1)}, f32[64,8,768]{2,1,0:T(8,128)S(1)}) fusion(f32[64,64,768]{2,1,0:T(8,128)} %get-tuple-element.45.refs_0_), kind=kLoop, calls=%fused_computation.90 | loop fusion | bytes 6291456 | tf_op jit(solution)/shard_map/slice | solution.py:225
  84.5 1.3 pad_maximum_fusion.1
  85.8 2.7 %collective-permute-start.1 = (f32[64,8,896]{2,1,0:T(8,128)}, f32[64,8,896]{2,1,0:T(8,128)}, u32[]{:S(2)}, u32[]{:S(2)}) collective-permute-start(f32[64,8,896]{2,1,0:T(8,128)} %pad_maximum_fusion.1), channel_id=1, source_target_pairs={{1,0},{2,1},{3,2},{4,3},{5,4},{6,5},{7,6},{9,8},{10,9},{11,10},{12... | collective-permute-start | bytes 5505032 | tf_op jit(solution)/shard_map/ppermute | solution.py:185
  88.5 1.4 pad_maximum_fusion
  89.9 6.3 %collective-permute-start = (f32[64,8,896]{2,1,0:T(8,128)}, f32[64,8,896]{2,1,0:T(8,128)}, u32[]{:S(2)}, u32[]{:S(2)}) collective-permute-start(f32[64,8,896]{2,1,0:T(8,128)} %pad_maximum_fusion), channel_id=1, source_target_pairs={{0,1},{1,2},{2,3},{3,4},{4,5},{5,6},{6,7},{8,9},{9,10},{10,11},{11... | collective-permute-start | bytes 5505032 | tf_op jit(solution)/shard_map/ppermute | solution.py:185
  96.2 18.2 %shard_map.83 = (f32[64,64,768]{2,1,0:T(8,128)}, f32[64,64,128]{2,1,0:T(8,128)}) custom-call(s32[6]{0:T(128)} %constant.142.clone.picks_ref, s32[1,2048]{1,0:T(1,128)} %bitcast.60, bf16[2048,896]{1,0:T(8,128)(2,1)} %bitcast.8.docs_ref, f32[64,64,768]{2,1,0:T(8,128)} %get-tuple-element.45.refs_0_, ...), custom_call_target="tpu_custom_call", output_to_operand_aliasing={{0}: (3, {}), {1}: (4, {})} | custom-call | tf_op jit(solution)/shard_map/pallas_call | solution.py:53
  114.5 2.8 %slice_reduce_fusion = f32[64,64]{1,0:T(8,128)S(1)} fusion(f32[64,64,128]{2,1,0:T(8,128)} %get-tuple-element.48), kind=kLoop, calls=%fused_computation.8 | loop fusion | bytes 32768 | tf_op jit(solution)/shard_map/slice | solution.py:231
  117.3 0.2 fusion.63
  117.5 2.2 %fusion.58 = (f32[8,64,768]{2,1,0:T(8,128)S(1)}, f32[8,64,768]{2,1,0:T(8,128)S(1)}) fusion(f32[64,64,768]{2,1,0:T(8,128)} %get-tuple-element.47), kind=kLoop, calls=%fused_computation.89 | loop fusion | bytes 6291456 | tf_op jit(solution)/shard_map/slice | solution.py:240
  119.7 13.0 %collective-permute-done.1 = f32[64,8,896]{2,1,0:T(8,128)} collective-permute-done((f32[64,8,896]{2,1,0:T(8,128)}, f32[64,8,896]{2,1,0:T(8,128)}, u32[]{:S(2)}, u32[]{:S(2)}) %collective-permute-start.1) | collective-permute-done | bytes 1835040 | tf_op jit(solution)/shard_map/ppermute | solution.py:185
  132.7 1.1 slice.187
  133.8 0.1 copy.47
  134.0 1.0 collective-permute-done
  135.0 1.1 slice.186
  136.1 0.1 copy.46
  136.2 0.2 fusion.48
  136.5 0.2 fusion.32
  136.7 0.1 copy.49
  136.8 1.1 fusion.62
  137.9 1.1 fusion.61
  139.0 0.8 fusion.26.top_ref
  139.8 1.5 select_maximum_fusion
  141.3 0.2 copy-done
  141.5 3.5 %collective-permute-start.3 = (f32[8,64,896]{2,1,0:T(8,128)}, f32[8,64,896]{2,1,0:T(8,128)}, u32[]{:S(2)}, u32[]{:S(2)}) collective-permute-start(f32[8,64,896]{2,1,0:T(8,128)} %select_maximum_fusion), channel_id=1, source_target_pairs={{8,0},{16,8},{24,16},{32,24},{40,32},{48,40},{56,48},{64,56},{72,6... | collective-permute-start | bytes 5505032 | tf_op jit(solution)/shard_map/ppermute | solution.py:185
  145.0 0.8 fusion.29.bot_ref
  145.8 0.1 copy.48
  145.9 1.6 select_maximum_fusion.1
  147.6 3.8 %collective-permute-start.2 = (f32[8,64,896]{2,1,0:T(8,128)}, f32[8,64,896]{2,1,0:T(8,128)S(1)}, u32[]{:S(2)}, u32[]{:S(2)}) collective-permute-start(f32[8,64,896]{2,1,0:T(8,128)} %select_maximum_fusion.1), channel_id=1, source_target_pairs={{0,8},{8,16},{16,24},{24,32},{32,40},{40,48},{48,56},{56,64},{64,7... | collective-permute-start | bytes 5505032 | tf_op jit(solution)/shard_map/ppermute | solution.py:185
  151.4 8.3 %slice.162 = f32[48,64,768]{2,1,0:T(8,128)} slice(f32[64,64,768]{2,1,0:T(8,128)} %get-tuple-element.47), slice={[8:56], [0:64], [0:768]} | slice | bytes 18874368 | tf_op jit(solution)/shard_map/slice | solution.py:240
  159.7 0.1 fusion.34
  159.9 2.0 copy.52.inv_ref
  161.9 1.3 slice.192
  163.2 1.3 slice.191
  164.6 11.5 %fusion.6.mid_ref = f32[48,64,768]{2,1,0:T(8,128)} fusion(f32[64,80,1]{1,0,2:T(8,128)S(1)} %copy-done.4, f32[48,8,768]{2,1,0:T(8,128)S(1)} %slice.192, f32[48,64,768]{2,1,0:T(8,128)} %slice.162, f32[48,8,768]{2,1,0:T(8,128)S(1)} %slice.191), kind=kOutput, calls=%fused_computation.7 | convolution fusion | flops 1138360320 | bytes 21254144 | tf_op jit(solution)/shard_map/ck,rke->rce/dot_general | solution.py:241
  176.1 15.0 %shard_map.84.prev_ref = bf16[64,64,768]{2,1,0:T(8,128)(2,1)} custom-call(f32[8,64,768]{2,1,0:T(8,128)} %copy-done, f32[48,64,768]{2,1,0:T(8,128)} %fusion.6.mid_ref, f32[8,64,768]{2,1,0:T(8,128)} %copy-done.1, bf16[64,64,768]{2,1,0:T(8,128)(2,1)} %cb_ref.3, f32[64,64,1]{2,1,0:T(8,128)} %copy.52.inv_ref), custom_call_target="tpu_custom_call" | custom-call | tf_op jit(solution)/shard_map/pallas_call | solution.py:109
  191.1 0.1 fusion.42
  191.2 0.1 fusion.44
  191.4 1.1 slice_reduce_fusion.1
  192.5 0.1 fusion.35
  192.6 0.2 slice_reduce_fusion.2
  192.8 0.1 fusion.36
  192.9 0.2 copy.51
  193.2 0.9 broadcast_divide_fusion.inv_ref
  194.1 8.4 %shard_map.85 = bf16[64,64,768]{2,1,0:T(8,128)(2,1)} custom-call(f32[8,64,896]{2,1,0:T(8,128)} %copy-done.2, f32[8,64,768]{2,1,0:T(8,128)} %copy-done, f32[48,64,768]{2,1,0:T(8,128)} %fusion.6.mid_ref, f32[8,64,768]{2,1,0:T(8,128)} %copy-done.1, f32[8,64,896]{2,1,0:T(8,128)} %collective-permute-done.3.below_ref, ...), custom_call_target="tpu_custom_call", output_to_operand_aliasing={{}: (7, {})} | custom-call | tf_op jit(solution)/shard_map/pallas_call | solution.py:161
  (40 shorter events, 0.2 us)
Async XLA Ops:
  0.0 6.2 %copy-start.5 = (s32[1024,1]{0,1:T(1,128)S(1)}, s32[1024,1]{0,1:T(1,128)}, u32[]{:S(2)}) copy-start(s32[1024,1]{0,1:T(1,128)} %param.15) | copy-start | bytes 12292
  5.6 1.4 copy-start.3
  14.7 55.0 %all-to-all-start = ((bf16[128,16,896]{2,1,0:T(8,128)(2,1)}), bf16[128,16,896]{2,1,0:T(8,128)(2,1)}, u32[]{:S(2)}, u32[]{:S(2)}) async-start(bf16[128,16,896]{2,1,0:T(8,128)(2,1)} %bitcast.58), calls=%async_computation | async-start | bytes 7340032 | tf_op jit(solution)/shard_map/all_to_all | solution.py:211
  85.8 46.9 %collective-permute-start.1 = (f32[64,8,896]{2,1,0:T(8,128)}, f32[64,8,896]{2,1,0:T(8,128)}, u32[]{:S(2)}, u32[]{:S(2)}) collective-permute-start(f32[64,8,896]{2,1,0:T(8,128)} %pad_maximum_fusion.1), channel_id=1, source_target_pairs={{1,0},{2,1},{3,2},{4,3},{5,4},{6,5},{7,6},{9,8},{10,9},{11,10},{12... | collective-permute-start | bytes 5505032 | tf_op jit(solution)/shard_map/ppermute | solution.py:185
  89.9 45.1 %collective-permute-start = (f32[64,8,896]{2,1,0:T(8,128)}, f32[64,8,896]{2,1,0:T(8,128)}, u32[]{:S(2)}, u32[]{:S(2)}) collective-permute-start(f32[64,8,896]{2,1,0:T(8,128)} %pad_maximum_fusion), channel_id=1, source_target_pairs={{0,1},{1,2},{2,3},{3,4},{4,5},{5,6},{6,7},{8,9},{9,10},{10,11},{11... | collective-permute-start | bytes 5505032 | tf_op jit(solution)/shard_map/ppermute | solution.py:185
  114.5 2.8 %copy-start.6 = (f32[64,64]{1,0:T(8,128)S(1)}, f32[64,64]{1,0:T(8,128)}, u32[]{:S(2)}) copy-start(f32[64,64]{1,0:T(8,128)} %constant.151) | copy-start | bytes 49156
  117.5 18.8 %copy-start.7 = (f32[64,8]{1,0:T(8,128)S(1)}, f32[64,8]{1,0:T(8,128)}, u32[]{:S(2)}) copy-start(f32[64,8]{1,0:T(8,128)} %constant.152) | copy-start | bytes 6148
  117.5 19.0 %copy-start.8 = (f32[64,8]{1,0:T(8,128)S(1)}, f32[64,8]{1,0:T(8,128)}, u32[]{:S(2)}) copy-start(f32[64,8]{1,0:T(8,128)} %constant.150) | copy-start | bytes 6148
  119.7 19.3 %copy-start.4 = (f32[64,80,1]{1,0,2:T(8,128)S(1)}, f32[64,80,1]{1,0,2:T(8,128)}, u32[]{:S(2)}) copy-start(f32[64,80,1]{1,0,2:T(8,128)} %constant.159) | copy-start | bytes 61444
  139.8 1.7 copy-start
  141.5 49.9 %collective-permute-start.3 = (f32[8,64,896]{2,1,0:T(8,128)}, f32[8,64,896]{2,1,0:T(8,128)}, u32[]{:S(2)}, u32[]{:S(2)}) collective-permute-start(f32[8,64,896]{2,1,0:T(8,128)} %select_maximum_fusion), channel_id=1, source_target_pairs={{8,0},{16,8},{24,16},{32,24},{40,32},{48,40},{56,48},{64,56},{72,6... | collective-permute-start | bytes 5505032 | tf_op jit(solution)/shard_map/ppermute | solution.py:185
  145.8 1.8 copy-start.1
  147.6 12.1 %copy-start.13 = (f32[48,64]{1,0:T(8,128)S(1)}, f32[48,64]{1,0:T(8,128)}, u32[]{:S(2)}) copy-start(f32[48,64]{1,0:T(8,128)} %constant.154) | copy-start | bytes 36868
  147.6 45.0 %collective-permute-start.2 = (f32[8,64,896]{2,1,0:T(8,128)}, f32[8,64,896]{2,1,0:T(8,128)S(1)}, u32[]{:S(2)}, u32[]{:S(2)}) collective-permute-start(f32[8,64,896]{2,1,0:T(8,128)} %select_maximum_fusion.1), channel_id=1, source_target_pairs={{0,8},{8,16},{16,24},{24,32},{32,40},{40,48},{48,56},{56,64},{64,7... | collective-permute-start | bytes 5505032 | tf_op jit(solution)/shard_map/ppermute | solution.py:185
  176.1 15.1 %copy-start.12 = (f32[8,16]{1,0:T(8,128)S(1)}, f32[8,16]{1,0:T(8,128)}, u32[]{:S(2)}) copy-start(f32[8,16]{1,0:T(8,128)} %constant.157) | copy-start | bytes 1540
  176.1 15.2 %copy-start.11 = (f32[8,16]{1,0:T(8,128)S(1)}, f32[8,16]{1,0:T(8,128)}, u32[]{:S(2)}) copy-start(f32[8,16]{1,0:T(8,128)} %constant.156) | copy-start | bytes 1540
  176.1 16.4 %copy-start.10 = (f32[8,8]{1,0:T(8,128)S(1)}, f32[8,8]{1,0:T(8,128)}, u32[]{:S(2)}) copy-start(f32[8,8]{1,0:T(8,128)} %constant.158) | copy-start | bytes 772
  176.1 16.7 %copy-start.9 = (f32[8,8]{1,0:T(8,128)S(1)}, f32[8,8]{1,0:T(8,128)}, u32[]{:S(2)}) copy-start(f32[8,8]{1,0:T(8,128)} %constant.155) | copy-start | bytes 772
  192.6 1.5 copy-start.2

commit v10 on v8

--- a/solution.py
+++ b/solution.py
@@ -216,17 +216,27 @@
 
     g_rows = jnp.asarray(band_matrix(rows_tile))
     g_cols = jnp.asarray(band_matrix(cols_tile))
-    ext_num = jnp.concatenate([from_left, numerator, from_right], axis=1)
     ext_hits = jnp.concatenate([hits_left, counter, hits_right], axis=1)
-    col_num = jnp.einsum("ck,rke->rce", g_cols, ext_num, precision=HI)
     col_hits = jnp.einsum("ck,rk->rc", g_cols, ext_hits, precision=HI)
     last = rows_tile - RADIUS
-    def with_hits(rows):
+
+    def col_pass(lo, hi):
+        pieces = [from_left[lo:hi], numerator[lo:hi], from_right[lo:hi]]
+        return jnp.einsum("ck,rke->rce", g_cols, jnp.concatenate(pieces, axis=1), precision=HI)
+
+    col_top, col_bottom = col_pass(0, RADIUS), col_pass(last, rows_tile)
+
+    def with_hits(part, rows):
         hit_lanes = jnp.pad(col_hits[rows][:, :, None], ((0, 0), (0, 0), (0, 127)))
-        return jnp.concatenate([col_num[rows], hit_lanes], axis=2)
-
-    above, below = exchange(with_hits(slice(0, RADIUS)), with_hits(slice(last, rows_tile)), "mx")
+        return jnp.concatenate([part, hit_lanes], axis=2)
+
+    above, below = exchange(
+        with_hits(col_top, slice(0, RADIUS)),
+        with_hits(col_bottom, slice(last, rows_tile)),
+        "mx",
+    )
     hits_above, hits_below = above[:, :, feature], below[:, :, feature]
+    col_num = col_pass(0, rows_tile)
     inner_hits = jnp.einsum("rk,kc->rc", g_rows[RADIUS:last, RADIUS : RADIUS + rows_tile], col_hits, precision=HI)
     inv_inner = 1.0 / (inner_hits + 8.0)
     inv = jnp.concatenate([jnp.zeros_like(inv_inner[:RADIUS]), inv_inner, jnp.zeros_like(inv_inner[:RADIUS])])

time: 215 us -> 201 us (0.935); the launches traced: 214 us -> 198 us
  waiting for transfers between devices: 84.2 us -> 61.6 us
  matrix products: 9.81 us -> 14.1 us
    ppermute x4, waiting for transfers between devices: 40.8 us -> 18.2 us  [exchange(): return (lax.ppermute(last, axis, up), lax.ppermute(lead, axis, down))]
    unnamed x26 -> x24, local copies, waits for them, and re-layouts: 5.08 us -> 0.47 us
    dot_general x1 -> x3, matrix products: 8.6 us -> 12.8 us  [col_pass(): jnp.einsum('ck,rke->rce', g_cols, jnp.concatenate(pieces, axis=1), precis...]
    slice x1 -> x3, local copies, waits for them, and re-layouts: 0.28 us -> 4.3 us  [col_pass(): pieces = [from_left[lo:hi], numerator[lo:hi], from_right[lo:hi]]]
  transfers between devices with their start and end apart: 5 -> 5, of which waited for: 5 -> 4; matrix products, arithmetic and copies ran while one was open for 5% -> 14% of each run, Pallas kernels for 16% -> 17%
where the time goes in v10:
time: 201 us; the launch traced here: 198 us
  waiting for transfers between devices  61.6 us (31%)
  Pallas kernels  50.5 us (25%)
  starting transfers between devices  27.1 us (13%)
  other arithmetic  22.9 us (11%)
  local copies, waits for them, and re-layouts  21.3 us (11%)
  matrix products  14.1 us (7%)
    all_to_all x1, waiting for transfers between devices, on_device(): lax.all_to_all(outgoing.reshape(tile_total, capacity, width), ('mx', 'my'...  43.4 us
    pallas_call x2, Pallas kernels, accumulate(): pl.pallas_call(kernel, grid_spec=pltpu.PrefetchScalarGridSpec(num_scalar_...  27 us
    ppermute x4, waiting for transfers between devices, exchange(): return (lax.ppermute(last, axis, up), lax.ppermute(lead, axis, down))  18.2 us
    ppermute x4, starting transfers between devices, exchange(): return (lax.ppermute(last, axis, up), lax.ppermute(lead, axis, down))  16 us
    pallas_call x1, Pallas kernels, finish_inner(): pl.pallas_call(kernel, grid=(feature // lanes,), in_specs=[slab_spec, sla...  15.6 us
    dot_general x3, matrix products, col_pass(): jnp.einsum('ck,rke->rce', g_cols, jnp.concatenate(pieces, axis=1), precis...  12.8 us
    all_to_all x1, starting transfers between devices, on_device(): lax.all_to_all(outgoing.reshape(tile_total, capacity, width), ('mx', 'my'...  11.1 us
    pallas_call x1, Pallas kernels, finish_edges(): pl.pallas_call(kernel, grid=(2,), in_specs=[halo_spec, pl.BlockSpec((near...  7.93 us
  transfers between devices with their start and end apart: 5, of which 4 were waited for; matrix products, arithmetic and copies ran while one was open for 14% of the time, Pallas kernels for 17%

profile of v10, /device:TPU:15, one launch (start us, length us, event | category | flops | bytes accessed | tf_op | source)
XLA Modules:
  0.0 197.8 jit_solution(15161831091674582186)
XLA Ops:
  0.0 0.7 compare_reduce_fusion.2
  0.7 0.6 compare_reduce_fusion.1
  1.4 0.6 compare_reduce_fusion
  2.0 2.0 %fusion.53 = (bf16[1024]{0:T(1024)(128)(2,1)S(1)}, bf16[1024]{0:T(1024)(128)(2,1)S(1)}) fusion(s32[1024]{0:T(1024)} %param.16, pred[]{:T(512)} %compare_reduce_fusion.1, pred[]{:T(512)} %compare_reduce_fusion.2), kind=kLoop, calls=%fused_computation.79 | loop fusion | flops 23552 | bytes 8194 | tf_op jit(solution)/shard_map/select.14
  4.1 0.8 copy.43
  4.9 0.1 scatter.19
  4.9 0.6 broadcast_select_fusion
  5.5 0.1 scatter.24
  5.6 0.2 copy.45
  5.8 0.2 fusion.39
  6.1 0.1 copy.44
  6.2 0.4 fusion.38
  6.6 0.4 copy-done.1
  7.0 7.6 %scatter_custom_fusion = bf16[2048,896]{1,0:T(8,128)(2,1)} fusion(s32[1024]{0:T(1024)S(1)} %bitcast.64, bf16[1024,128]{1,0:T(8,128)(2,1)S(1)} %copy.45, bf16[]{:T(256)} %constant.173, bf16[1024,768]{1,0:T(8,128)(2,1)S(1)} %copy-done.1, bf16[]{:T(256)} %constant.124.clone.1), kind=kCustom, calls=%fused_computation.24 | custom fusion | flops 3670016 | bytes 5505028 | tf_op jit(solution)/shard_map/scatter | solution.py:194
  14.7 11.1 %all-to-all-start = ((bf16[128,16,896]{2,1,0:T(8,128)(2,1)}), bf16[128,16,896]{2,1,0:T(8,128)(2,1)}, u32[]{:S(2)}, u32[]{:S(2)}) async-start(bf16[128,16,896]{2,1,0:T(8,128)(2,1)} %bitcast.58), calls=%async_computation | async-start | bytes 7340032 | tf_op jit(solution)/shard_map/all_to_all | solution.py:195
  25.7 0.5 iota_multiply_fusion.1.picks_ref
  26.3 43.4 %all-to-all-done = bf16[128,16,896]{2,1,0:T(8,128)(2,1)} async-done(((bf16[128,16,896]{2,1,0:T(8,128)(2,1)}), bf16[128,16,896]{2,1,0:T(8,128)(2,1)}, u32[]{:S(2)}, u32[]{:S(2)}) %all-to-all-start) | async-done | bytes 3670048 | tf_op jit(solution)/shard_map/all_to_all | solution.py:195
  69.6 3.0 %select_reduce_fusion = s32[2048]{0:T(1024)} fusion(bf16[2048,896]{1,0:T(8,128)(2,1)} %bitcast.8.docs_ref), kind=kLoop, calls=%fused_computation.42 | loop fusion | flops 12288 | bytes 20480 | tf_op jit(solution)/shard_map/jit(_where)/select_n | solution.py:204
  72.6 8.7 %shard_map.82 = (f32[64,64,768]{2,1,0:T(8,128)}, f32[64,64,128]{2,1,0:T(8,128)}) custom-call(s32[2]{0:T(128)} %iota_multiply_fusion.1.picks_ref, s32[1,2048]{1,0:T(1,128)} %bitcast.59, bf16[2048,896]{1,0:T(8,128)(2,1)} %bitcast.8.docs_ref), custom_call_target="tpu_custom_call" | custom-call | tf_op jit(solution)/shard_map/pallas_call | solution.py:53
  81.3 1.1 fusion.60
  82.4 2.1 %fusion.59 = (f32[64,8,768]{2,1,0:T(8,128)S(1)}, f32[64,8,768]{2,1,0:T(8,128)S(1)}) fusion(f32[64,64,768]{2,1,0:T(8,128)} %get-tuple-element.45.refs_0_), kind=kLoop, calls=%fused_computation.90 | loop fusion | bytes 6291456 | tf_op jit(solution)/shard_map/slice | solution.py:209
  84.5 1.4 pad_maximum_fusion.1
  85.8 2.7 %collective-permute-start.1 = (f32[64,8,896]{2,1,0:T(8,128)}, f32[64,8,896]{2,1,0:T(8,128)}, u32[]{:S(2)}, u32[]{:S(2)}) collective-permute-start(f32[64,8,896]{2,1,0:T(8,128)} %pad_maximum_fusion.1), channel_id=1, source_target_pairs={{1,0},{2,1},{3,2},{4,3},{5,4},{6,5},{7,6},{9,8},{10,9},{11,10},{12... | collective-permute-start | bytes 5505032 | tf_op jit(solution)/shard_map/ppermute | solution.py:169
  88.6 1.4 pad_maximum_fusion
  90.0 6.3 %collective-permute-start = (f32[64,8,896]{2,1,0:T(8,128)}, f32[64,8,896]{2,1,0:T(8,128)}, u32[]{:S(2)}, u32[]{:S(2)}) collective-permute-start(f32[64,8,896]{2,1,0:T(8,128)} %pad_maximum_fusion), channel_id=1, source_target_pairs={{0,1},{1,2},{2,3},{3,4},{4,5},{5,6},{6,7},{8,9},{9,10},{10,11},{11... | collective-permute-start | bytes 5505032 | tf_op jit(solution)/shard_map/ppermute | solution.py:169
  96.3 18.2 %shard_map.83 = (f32[64,64,768]{2,1,0:T(8,128)}, f32[64,64,128]{2,1,0:T(8,128)}) custom-call(s32[6]{0:T(128)} %constant.142.clone.picks_ref, s32[1,2048]{1,0:T(1,128)} %bitcast.60, bf16[2048,896]{1,0:T(8,128)(2,1)} %bitcast.8.docs_ref, f32[64,64,768]{2,1,0:T(8,128)} %get-tuple-element.45.refs_0_, ...), custom_call_target="tpu_custom_call", output_to_operand_aliasing={{0}: (3, {}), {1}: (4, {})} | custom-call | tf_op jit(solution)/shard_map/pallas_call | solution.py:53
  114.6 2.8 %slice_reduce_fusion = f32[64,64]{1,0:T(8,128)S(1)} fusion(f32[64,64,128]{2,1,0:T(8,128)} %get-tuple-element.48), kind=kLoop, calls=%fused_computation.8 | loop fusion | bytes 32768 | tf_op jit(solution)/shard_map/slice | solution.py:215
  117.3 0.2 fusion.63
  117.5 0.0 copy-start.6
  117.5 2.2 %fusion.58 = (f32[8,64,768]{2,1,0:T(8,128)S(1)}, f32[8,64,768]{2,1,0:T(8,128)S(1)}) fusion(f32[64,64,768]{2,1,0:T(8,128)} %get-tuple-element.47), kind=kLoop, calls=%fused_computation.89 | loop fusion | bytes 6291456 | tf_op jit(solution)/shard_map/slice | solution.py:224
  119.8 13.0 %collective-permute-done.1 = f32[64,8,896]{2,1,0:T(8,128)} collective-permute-done((f32[64,8,896]{2,1,0:T(8,128)}, f32[64,8,896]{2,1,0:T(8,128)}, u32[]{:S(2)}, u32[]{:S(2)}) %collective-permute-start.1) | collective-permute-done | bytes 1835040 | tf_op jit(solution)/shard_map/ppermute | solution.py:169
  132.8 1.1 slice.179
  133.9 0.1 copy.47
  134.0 1.0 collective-permute-done
  135.0 1.1 slice.178
  136.1 0.1 copy.46
  136.3 0.2 fusion.48
  136.5 0.2 fusion.32
  136.8 0.1 copy.49
  136.9 1.1 fusion.62
  138.0 1.1 fusion.61
  139.0 0.8 fusion.26
  139.8 1.5 select_maximum_fusion
  141.3 3.5 %collective-permute-start.3 = (f32[8,64,896]{2,1,0:T(8,128)}, f32[8,64,896]{2,1,0:T(8,128)}, u32[]{:S(2)}, u32[]{:S(2)}) collective-permute-start(f32[8,64,896]{2,1,0:T(8,128)} %select_maximum_fusion), channel_id=1, source_target_pairs={{8,0},{16,8},{24,16},{32,24},{40,32},{48,40},{56,48},{64,56},{72,6... | collective-permute-start | bytes 5505032 | tf_op jit(solution)/shard_map/ppermute | solution.py:169
  144.8 0.8 fusion.29
  145.6 0.1 copy.48
  145.7 1.4 select_maximum_fusion.1
  147.1 3.5 %collective-permute-start.2 = (f32[8,64,896]{2,1,0:T(8,128)}, f32[8,64,896]{2,1,0:T(8,128)S(1)}, u32[]{:S(2)}, u32[]{:S(2)}) collective-permute-start(f32[8,64,896]{2,1,0:T(8,128)} %select_maximum_fusion.1), channel_id=1, source_target_pairs={{0,8},{8,16},{16,24},{24,32},{32,40},{40,48},{48,56},{56,64},{64,7... | collective-permute-start | bytes 5505032 | tf_op jit(solution)/shard_map/ppermute | solution.py:169
  150.6 0.1 fusion.34
  150.8 2.1 %copy.52.inv_ref = f32[64,64,1]{2,1,0:T(8,128)} copy(f32[64,64,1]{1,0,2:T(8,128)S(1)} %maximum_bitcast_fusion) | data formatting | bytes 32768 | tf_op jit(solution)/shard_map/broadcast_in_dim | solution.py:243
  152.9 1.5 slice.182
  154.4 1.5 slice.181
  155.9 11.3 %fusion.6.mid_ref = f32[64,64,768]{2,1,0:T(8,128)} fusion(f32[64,80,1]{1,0,2:T(8,128)S(1)} %copy-done.2, f32[64,8,768]{2,1,0:T(8,128)S(1)} %slice.182, f32[64,64,768]{2,1,0:T(8,128)} %get-tuple-element.47, f32[64,8,768]{2,1,0:T(8,128)S(1)} %slice.181), kind=kOutput, calls=%fused_computation.7 | convolution fusion | flops 1517813760 | bytes 28332032 | tf_op jit(solution)/shard_map/ck,rke->rce/dot_general | solution.py:225
  167.2 15.6 %shard_map.84.prev_ref = bf16[64,64,768]{2,1,0:T(8,128)(2,1)} custom-call(f32[64,64,768]{2,1,0:T(8,128)} %fusion.6.mid_ref, bf16[64,64,768]{2,1,0:T(8,128)(2,1)} %cb_ref.3, f32[64,64,1]{2,1,0:T(8,128)} %copy.52.inv_ref), custom_call_target="tpu_custom_call" | custom-call | tf_op jit(solution)/shard_map/pallas_call | solution.py:104
  182.8 0.1 fusion.42
  182.9 0.1 fusion.44
  183.1 4.2 %collective-permute-done.3.below_ref = f32[8,64,896]{2,1,0:T(8,128)} collective-permute-done((f32[8,64,896]{2,1,0:T(8,128)}, f32[8,64,896]{2,1,0:T(8,128)}, u32[]{:S(2)}, u32[]{:S(2)}) %collective-permute-start.3) | collective-permute-done | bytes 1835040 | tf_op jit(solution)/shard_map/ppermute | solution.py:169
  187.2 1.1 slice_reduce_fusion.1
  188.3 0.1 fusion.35
  188.4 0.2 slice_reduce_fusion.2
  188.6 0.1 fusion.36
  188.7 0.2 copy.51
  189.0 0.9 broadcast_divide_fusion.inv_ref
  189.9 7.9 %shard_map.85 = bf16[64,64,768]{2,1,0:T(8,128)(2,1)} custom-call(f32[8,64,896]{2,1,0:T(8,128)} %copy-done, f32[64,64,768]{2,1,0:T(8,128)} %fusion.6.mid_ref, f32[8,64,896]{2,1,0:T(8,128)} %collective-permute-done.3.below_ref, bf16[64,64,768]{2,1,0:T(8,128)(2,1)} %cb_ref.3, ...), custom_call_target="tpu_custom_call", output_to_operand_aliasing={{}: (5, {})} | custom-call | tf_op jit(solution)/shard_map/pallas_call | solution.py:147
  (35 shorter events, 0.2 us)
Async XLA Ops:
  0.0 6.2 %copy-start.3 = (s32[1024,1]{0,1:T(1,128)S(1)}, s32[1024,1]{0,1:T(1,128)}, u32[]{:S(2)}) copy-start(s32[1024,1]{0,1:T(1,128)} %param.15) | copy-start | bytes 12292
  5.6 1.4 copy-start.1
  14.7 55.0 %all-to-all-start = ((bf16[128,16,896]{2,1,0:T(8,128)(2,1)}), bf16[128,16,896]{2,1,0:T(8,128)(2,1)}, u32[]{:S(2)}, u32[]{:S(2)}) async-start(bf16[128,16,896]{2,1,0:T(8,128)(2,1)} %bitcast.58), calls=%async_computation | async-start | bytes 7340032 | tf_op jit(solution)/shard_map/all_to_all | solution.py:195
  85.8 46.9 %collective-permute-start.1 = (f32[64,8,896]{2,1,0:T(8,128)}, f32[64,8,896]{2,1,0:T(8,128)}, u32[]{:S(2)}, u32[]{:S(2)}) collective-permute-start(f32[64,8,896]{2,1,0:T(8,128)} %pad_maximum_fusion.1), channel_id=1, source_target_pairs={{1,0},{2,1},{3,2},{4,3},{5,4},{6,5},{7,6},{9,8},{10,9},{11,10},{12... | collective-permute-start | bytes 5505032 | tf_op jit(solution)/shard_map/ppermute | solution.py:169
  90.0 45.1 %collective-permute-start = (f32[64,8,896]{2,1,0:T(8,128)}, f32[64,8,896]{2,1,0:T(8,128)}, u32[]{:S(2)}, u32[]{:S(2)}) collective-permute-start(f32[64,8,896]{2,1,0:T(8,128)} %pad_maximum_fusion), channel_id=1, source_target_pairs={{0,1},{1,2},{2,3},{3,4},{4,5},{5,6},{6,7},{8,9},{9,10},{10,11},{11... | collective-permute-start | bytes 5505032 | tf_op jit(solution)/shard_map/ppermute | solution.py:169
  114.6 2.8 %copy-start.4 = (f32[64,64]{1,0:T(8,128)S(1)}, f32[64,64]{1,0:T(8,128)}, u32[]{:S(2)}) copy-start(f32[64,64]{1,0:T(8,128)} %constant.151) | copy-start | bytes 49156
  117.5 18.7 %copy-start.5 = (f32[64,8]{1,0:T(8,128)S(1)}, f32[64,8]{1,0:T(8,128)}, u32[]{:S(2)}) copy-start(f32[64,8]{1,0:T(8,128)} %constant.152) | copy-start | bytes 6148
  117.5 19.0 %copy-start.6 = (f32[64,8]{1,0:T(8,128)S(1)}, f32[64,8]{1,0:T(8,128)}, u32[]{:S(2)}) copy-start(f32[64,8]{1,0:T(8,128)} %constant.150) | copy-start | bytes 6148
  119.7 19.3 %copy-start.2 = (f32[64,80,1]{1,0,2:T(8,128)S(1)}, f32[64,80,1]{1,0,2:T(8,128)}, u32[]{:S(2)}) copy-start(f32[64,80,1]{1,0,2:T(8,128)} %constant.159) | copy-start | bytes 61444
  141.3 45.9 %collective-permute-start.3 = (f32[8,64,896]{2,1,0:T(8,128)}, f32[8,64,896]{2,1,0:T(8,128)}, u32[]{:S(2)}, u32[]{:S(2)}) collective-permute-start(f32[8,64,896]{2,1,0:T(8,128)} %select_maximum_fusion), channel_id=1, source_target_pairs={{8,0},{16,8},{24,16},{32,24},{40,32},{48,40},{56,48},{64,56},{72,6... | collective-permute-start | bytes 5505032 | tf_op jit(solution)/shard_map/ppermute | solution.py:169
  145.7 4.9 %copy-start.11 = (f32[48,64]{1,0:T(8,128)S(1)}, f32[48,64]{1,0:T(8,128)}, u32[]{:S(2)}) copy-start(f32[48,64]{1,0:T(8,128)} %constant.154) | copy-start | bytes 36868
  147.1 41.3 %collective-permute-start.2 = (f32[8,64,896]{2,1,0:T(8,128)}, f32[8,64,896]{2,1,0:T(8,128)S(1)}, u32[]{:S(2)}, u32[]{:S(2)}) collective-permute-start(f32[8,64,896]{2,1,0:T(8,128)} %select_maximum_fusion.1), channel_id=1, source_target_pairs={{0,8},{8,16},{16,24},{24,32},{32,40},{40,48},{48,56},{56,64},{64,7... | collective-permute-start | bytes 5505032 | tf_op jit(solution)/shard_map/ppermute | solution.py:169
  167.2 15.6 %copy-start.10 = (f32[8,16]{1,0:T(8,128)S(1)}, f32[8,16]{1,0:T(8,128)}, u32[]{:S(2)}) copy-start(f32[8,16]{1,0:T(8,128)} %constant.157) | copy-start | bytes 1540
  167.2 15.8 %copy-start.9 = (f32[8,16]{1,0:T(8,128)S(1)}, f32[8,16]{1,0:T(8,128)}, u32[]{:S(2)}) copy-start(f32[8,16]{1,0:T(8,128)} %constant.156) | copy-start | bytes 1540
  167.2 21.1 %copy-start.8 = (f32[8,8]{1,0:T(8,128)S(1)}, f32[8,8]{1,0:T(8,128)}, u32[]{:S(2)}) copy-start(f32[8,8]{1,0:T(8,128)} %constant.158) | copy-start | bytes 772
  167.2 21.4 %copy-start.7 = (f32[8,8]{1,0:T(8,128)S(1)}, f32[8,8]{1,0:T(8,128)}, u32[]{:S(2)}) copy-start(f32[8,8]{1,0:T(8,128)} %constant.155) | copy-start | bytes 772
  188.4 1.5 copy-start

commit v11 on v10

--- a/solution.py
+++ b/solution.py
@@ -27,19 +27,15 @@
     picks = jnp.asarray(col_blocks, jnp.int32)
 
     def kernel(picks_ref, ids_ref, docs_ref, *refs):
-        num_ref, hits_ref = refs[-2:]
+        num_ref = refs[-1]
         place = lax.broadcasted_iota(jnp.int32, (band, rows), 0)
         first_col = picks_ref[pl.program_id(0)] * RADIUS
         units = (place // RADIUS) * cols_tile + first_col + place % RADIUS
         one_hot = (units == ids_ref[...]).astype(jnp.bfloat16)
         sums = jnp.dot(one_hot, docs_ref[...], preferred_element_type=jnp.float32)
-        num_ref[...] = sums[:, :feature].reshape(rows_tile, RADIUS, feature)
-        hits_ref[...] = sums[:, feature:].reshape(rows_tile, RADIUS, width - feature)
-
-    out_specs = [
-        pl.BlockSpec((rows_tile, RADIUS, feature), lambda j, p: (0, p[j], 0)),
-        pl.BlockSpec((rows_tile, RADIUS, width - feature), lambda j, p: (0, p[j], 0)),
-    ]
+        num_ref[...] = sums.reshape(rows_tile, RADIUS, width)
+
+    out_specs = pl.BlockSpec((rows_tile, RADIUS, width), lambda j, p: (0, p[j], 0))
     in_specs = [
         pl.BlockSpec((1, rows), lambda j, p: (0, 0)),
         pl.BlockSpec((rows, width), lambda j, p: (0, 0)),
@@ -47,9 +43,9 @@
     operands = [ids.reshape(1, rows), docs]
     aliases = {}
     if prior is not None:
-        in_specs += [pl.BlockSpec(memory_space=pl.ANY)] * 2
-        operands += list(prior)
-        aliases = {3: 0, 4: 1}
+        in_specs += [pl.BlockSpec(memory_space=pl.ANY)]
+        operands += [prior]
+        aliases = {3: 0}
     return pl.pallas_call(
         kernel,
         grid_spec=pltpu.PrefetchScalarGridSpec(
@@ -58,10 +54,7 @@
             in_specs=in_specs,
             out_specs=out_specs,
         ),
-        out_shape=[
-            jax.ShapeDtypeStruct((rows_tile, cols_tile, feature), jnp.float32),
-            jax.ShapeDtypeStruct((rows_tile, cols_tile, width - feature), jnp.float32),
-        ],
+        out_shape=jax.ShapeDtypeStruct((rows_tile, cols_tile, width), jnp.float32),
         input_output_aliases=aliases,
     )(picks, *operands)
 
@@ -85,7 +78,7 @@
 
 
 def finish_inner(middle, codebook, inv):
-    rows, cols, feature = middle.shape
+    rows, cols, feature = codebook.shape
     lanes = 128
 
     def kernel(mid_ref, cb_ref, inv_ref, out_ref):
@@ -111,7 +104,7 @@
 
 
 def finish_edges(above, middle, below, codebook, inv, partial):
-    rows, cols, feature = middle.shape
+    rows, cols, feature = codebook.shape
     lanes = 128
     near = 2 * RADIUS
     last_edge = rows // RADIUS - 1
@@ -205,19 +198,12 @@
     col_total = cols_tile // RADIUS
     bands = accumulate(unit_ids, got, rows_tile, cols_tile, feature, [0, col_total - 1])
     last = cols_tile - RADIUS
-    lead = jnp.concatenate([bands[0][:, :RADIUS], bands[1][:, :RADIUS]], axis=2)
-    tail = jnp.concatenate([bands[0][:, last:], bands[1][:, last:]], axis=2)
-    from_left, from_right = exchange(lead, tail, "my")
-    hits_left, hits_right = from_left[:, :, feature + 2], from_right[:, :, feature + 2]
-    from_left, from_right = from_left[:, :, :feature], from_right[:, :, :feature]
+    from_left, from_right = exchange(bands[:, :RADIUS], bands[:, last:], "my")
     inner = list(range(1, col_total - 1))
-    numerator, counter = accumulate(unit_ids, got, rows_tile, cols_tile, feature, inner, bands)
-    counter = counter[:, :, 2]
+    numerator = accumulate(unit_ids, got, rows_tile, cols_tile, feature, inner, bands)
 
     g_rows = jnp.asarray(band_matrix(rows_tile))
     g_cols = jnp.asarray(band_matrix(cols_tile))
-    ext_hits = jnp.concatenate([hits_left, counter, hits_right], axis=1)
-    col_hits = jnp.einsum("ck,rk->rc", g_cols, ext_hits, precision=HI)
     last = rows_tile - RADIUS
 
     def col_pass(lo, hi):
@@ -226,17 +212,10 @@
 
     col_top, col_bottom = col_pass(0, RADIUS), col_pass(last, rows_tile)
 
-    def with_hits(part, rows):
-        hit_lanes = jnp.pad(col_hits[rows][:, :, None], ((0, 0), (0, 0), (0, 127)))
-        return jnp.concatenate([part, hit_lanes], axis=2)
-
-    above, below = exchange(
-        with_hits(col_top, slice(0, RADIUS)),
-        with_hits(col_bottom, slice(last, rows_tile)),
-        "mx",
-    )
-    hits_above, hits_below = above[:, :, feature], below[:, :, feature]
+    above, below = exchange(col_top, col_bottom, "mx")
+    hits_above, hits_below = above[:, :, feature + 2], below[:, :, feature + 2]
     col_num = col_pass(0, rows_tile)
+    col_hits = col_num[:, :, feature + 2]
     inner_hits = jnp.einsum("rk,kc->rc", g_rows[RADIUS:last, RADIUS : RADIUS + rows_tile], col_hits, precision=HI)
     inv_inner = 1.0 / (inner_hits + 8.0)
     inv = jnp.concatenate([jnp.zeros_like(inv_inner[:RADIUS]), inv_inner, jnp.zeros_like(inv_inner[:RADIUS])])

time: 201 us -> 197 us (0.980)
  other arithmetic: 22.9 us -> 16.6 us
  matrix products: 14.1 us -> 17.7 us
  local copies, waits for them, and re-layouts: 21.3 us -> 18.2 us
    concatenate x4 -> x0, other arithmetic: 5.64 us -> none  [the longest x2 2.86 us: with_hits(): return jnp.concatenate([part, hit_lanes], axis=2)]
    dot_general x3, matrix products: 12.8 us -> 17.1 us  [col_pass(): jnp.einsum('ck,rke->rce', g_cols, jnp.concatenate(pieces, axis=1), precis...]
    slice x11 -> x5, local copies, waits for them, and re-layouts: 12.6 us -> 11.2 us  [the longest x1 4.15 us: on_device(): from_left, from_right = exchange(bands[:, :RADIUS], bands[:, last:], 'my')]
where the time goes in v11:
time: 197 us; the launch traced here: 193 us
  waiting for transfers between devices  62.8 us (32%)
  Pallas kernels  50.3 us (26%)
  starting transfers between devices  27.3 us (14%)
  local copies, waits for them, and re-layouts  18.2 us (9%)
  matrix products  17.7 us (9%)
  other arithmetic  16.6 us (8%)
    all_to_all x1, waiting for transfers between devices, on_device(): lax.all_to_all(outgoing.reshape(tile_total, capacity, width), ('mx', 'my'...  43.4 us
    pallas_call x2, Pallas kernels, accumulate(): pl.pallas_call(kernel, grid_spec=pltpu.PrefetchScalarGridSpec(num_scalar_...  26.7 us
    ppermute x4, waiting for transfers between devices, exchange(): return (lax.ppermute(last, axis, up), lax.ppermute(lead, axis, down))  19.4 us
    dot_general x3, matrix products, col_pass(): jnp.einsum('ck,rke->rce', g_cols, jnp.concatenate(pieces, axis=1), precis...  17.1 us
    ppermute x4, starting transfers between devices, exchange(): return (lax.ppermute(last, axis, up), lax.ppermute(lead, axis, down))  16.2 us
    pallas_call x1, Pallas kernels, finish_inner(): pl.pallas_call(kernel, grid=(feature // lanes,), in_specs=[slab_spec, sla...  15.6 us
    all_to_all x1, starting transfers between devices, on_device(): lax.all_to_all(outgoing.reshape(tile_total, capacity, width), ('mx', 'my'...  11.1 us
    pallas_call x1, Pallas kernels, finish_edges(): pl.pallas_call(kernel, grid=(2,), in_specs=[halo_spec, pl.BlockSpec((near...  7.92 us
  transfers between devices with their start and end apart: 5, of which 4 were waited for; matrix products, arithmetic and copies ran while one was open for 14% of the time, Pallas kernels for 17%

profile of v11, /device:TPU:15, one launch (start us, length us, event | category | flops | bytes accessed | tf_op | source)
XLA Modules:
  0.0 193.1 jit_solution(2152746646845434462)
XLA Ops:
  0.0 0.0 copy-start.2
  0.0 0.0 copy-start.3
  0.0 0.0 copy-start
  0.0 0.6 compare_reduce_fusion.1
  0.6 0.7 compare_reduce_fusion.2
  1.4 0.6 compare_reduce_fusion
  2.0 0.8 copy.24
  2.8 0.2 fusion.38
  3.1 0.1 copy.25
  3.2 0.0 copy-done.2
  3.2 0.4 fusion.37
  3.6 0.0 copy-done.3
  3.6 1.3 fusion.45
  5.0 0.1 scatter.19
  5.1 0.6 broadcast_select_fusion
  5.7 0.1 scatter.24
  5.7 0.2 copy.26
  5.9 0.0 copy-done
  5.9 7.6 %scatter_custom_fusion = bf16[2048,896]{1,0:T(8,128)(2,1)} fusion(s32[1024]{0:T(1024)S(1)} %bitcast.51, bf16[1024,128]{1,0:T(8,128)(2,1)S(1)} %copy.26, bf16[]{:T(256)} %constant.163, bf16[1024,768]{1,0:T(8,128)(2,1)S(1)} %copy-done, bf16[]{:T(256)} %constant.123.clone.1), kind=kCustom, calls=%fused_computation.21 | custom fusion | flops 3670016 | bytes 5505028 | tf_op jit(solution)/shard_map/scatter | solution.py:187
  13.6 11.1 %all-to-all-start = ((bf16[128,16,896]{2,1,0:T(8,128)(2,1)}), bf16[128,16,896]{2,1,0:T(8,128)(2,1)}, u32[]{:S(2)}, u32[]{:S(2)}) async-start(bf16[128,16,896]{2,1,0:T(8,128)(2,1)} %bitcast.45), calls=%async_computation | async-start | bytes 7340032 | tf_op jit(solution)/shard_map/all_to_all | solution.py:188
  24.7 0.5 iota_multiply_fusion.1.picks_ref
  25.2 43.4 %all-to-all-done = bf16[128,16,896]{2,1,0:T(8,128)(2,1)} async-done(((bf16[128,16,896]{2,1,0:T(8,128)(2,1)}), bf16[128,16,896]{2,1,0:T(8,128)(2,1)}, u32[]{:S(2)}, u32[]{:S(2)}) %all-to-all-start) | async-done | bytes 3670048 | tf_op jit(solution)/shard_map/all_to_all | solution.py:188
  68.5 3.0 %select_reduce_fusion = s32[2048]{0:T(1024)} fusion(bf16[2048,896]{1,0:T(8,128)(2,1)} %bitcast.8.docs_ref), kind=kLoop, calls=%fused_computation.35 | loop fusion | flops 12288 | bytes 20480 | tf_op jit(solution)/shard_map/jit(_where)/select_n | solution.py:197
  71.5 8.7 %shard_map.82.refs_0_ = f32[64,64,896]{2,1,0:T(8,128)} custom-call(s32[2]{0:T(128)} %iota_multiply_fusion.1.picks_ref, s32[1,2048]{1,0:T(1,128)} %bitcast.46, bf16[2048,896]{1,0:T(8,128)(2,1)} %bitcast.8.docs_ref), custom_call_target="tpu_custom_call" | custom-call | tf_op jit(solution)/shard_map/pallas_call | solution.py:49
  80.2 4.2 %fusion.51 = (f32[64,8,896]{2,1,0:T(8,128)}, f32[64,8,896]{2,1,0:T(8,128)}) fusion(f32[64,64,896]{2,1,0:T(8,128)} %shard_map.82.refs_0_), kind=kLoop, calls=%fused_computation.76 | loop fusion | bytes 7340032 | tf_op jit(solution)/shard_map/slice | solution.py:201
  84.3 2.7 %collective-permute-start.1 = (f32[64,8,896]{2,1,0:T(8,128)}, f32[64,8,896]{2,1,0:T(8,128)S(1)}, u32[]{:S(2)}, u32[]{:S(2)}) collective-permute-start(f32[64,8,896]{2,1,0:T(8,128)} %get-tuple-element.46), channel_id=1, source_target_pairs={{1,0},{2,1},{3,2},{4,3},{5,4},{6,5},{7,6},{9,8},{10,9},{11,10},{12... | collective-permute-start | bytes 5505032 | tf_op jit(solution)/shard_map/ppermute | solution.py:162
  87.1 6.2 %collective-permute-start = (f32[64,8,896]{2,1,0:T(8,128)}, f32[64,8,896]{2,1,0:T(8,128)}, u32[]{:S(2)}, u32[]{:S(2)}) collective-permute-start(f32[64,8,896]{2,1,0:T(8,128)} %get-tuple-element.45), channel_id=1, source_target_pairs={{0,1},{1,2},{2,3},{3,4},{4,5},{5,6},{6,7},{8,9},{9,10},{10,11},{11... | collective-permute-start | bytes 5505032 | tf_op jit(solution)/shard_map/ppermute | solution.py:162
  93.2 18.1 %shard_map.83 = f32[64,64,896]{2,1,0:T(8,128)} custom-call(s32[6]{0:T(128)} %constant.141.clone.picks_ref, s32[1,2048]{1,0:T(1,128)} %bitcast.47, bf16[2048,896]{1,0:T(8,128)(2,1)} %bitcast.8.docs_ref, f32[64,64,896]{2,1,0:T(8,128)} %shard_map.82.refs_0_), custom_call_target="tpu_custom_call", output_to_operand_aliasing={{}: (3, {})} | custom-call | tf_op jit(solution)/shard_map/pallas_call | solution.py:49
  111.3 0.0 copy-start.1
  111.3 2.3 %fusion.50 = (f32[8,64,896]{2,1,0:T(8,128)S(1)}, f32[8,64,896]{2,1,0:T(8,128)S(1)}) fusion(f32[64,64,896]{2,1,0:T(8,128)} %shard_map.83), kind=kLoop, calls=%fused_computation.75 | loop fusion | bytes 7340032 | tf_op jit(solution)/shard_map/slice | solution.py:210
  113.7 17.5 %collective-permute-done.1 = f32[64,8,896]{2,1,0:T(8,128)S(1)} collective-permute-done((f32[64,8,896]{2,1,0:T(8,128)}, f32[64,8,896]{2,1,0:T(8,128)S(1)}, u32[]{:S(2)}, u32[]{:S(2)}) %collective-permute-start.1) | collective-permute-done | bytes 1835040 | tf_op jit(solution)/shard_map/ppermute | solution.py:162
  131.2 0.9 collective-permute-done
  132.1 1.1 fusion.52
  133.2 0.0 copy-done.1
  133.2 2.1 %fusion.26 = f32[8,64,896]{2,1,0:T(8,128)} fusion(f32[64,80,1]{1,0,2:T(8,128)S(1)} %copy-done.1, f32[8,8,896]{2,1,0:T(8,128)S(1)} %get-tuple-element.49, f32[8,64,896]{2,1,0:T(8,128)S(1)} %get-tuple-element.43, f32[8,8,896]{2,1,0:T(8,128)S(1)} %get-tuple-element.47), kind=kOutput, calls=%fused_computation.26 | convolution fusion | flops 221347840 | bytes 4149248 | tf_op jit(solution)/shard_map/ck,rke->rce/dot_general | solution.py:211
  135.4 3.7 %collective-permute-start.3 = (f32[8,64,896]{2,1,0:T(8,128)}, f32[8,64,896]{2,1,0:T(8,128)}, u32[]{:S(2)}, u32[]{:S(2)}) collective-permute-start(f32[8,64,896]{2,1,0:T(8,128)} %fusion.26), channel_id=1, source_target_pairs={{8,0},{16,8},{24,16},{32,24},{40,32},{48,40},{56,48},{64,56},{72,6... | collective-permute-start | bytes 5505032 | tf_op jit(solution)/shard_map/ppermute | solution.py:162
  139.1 2.2 %fusion.29 = f32[8,64,896]{2,1,0:T(8,128)} fusion(f32[64,80,1]{1,0,2:T(8,128)S(1)} %copy-done.1, f32[8,8,896]{2,1,0:T(8,128)S(1)} %get-tuple-element.50, f32[8,64,896]{2,1,0:T(8,128)S(1)} %get-tuple-element.44, f32[8,8,896]{2,1,0:T(8,128)S(1)} %get-tuple-element.48), kind=kOutput, calls=%fused_computation.27 | convolution fusion | flops 221347840 | bytes 4149248 | tf_op jit(solution)/shard_map/ck,rke->rce/dot_general | solution.py:211
  141.2 0.0 copy-start.8
  141.2 3.6 %collective-permute-start.2 = (f32[8,64,896]{2,1,0:T(8,128)}, f32[8,64,896]{2,1,0:T(8,128)}, u32[]{:S(2)}, u32[]{:S(2)}) collective-permute-start(f32[8,64,896]{2,1,0:T(8,128)} %fusion.29), channel_id=1, source_target_pairs={{0,8},{8,16},{16,24},{24,32},{32,40},{40,48},{48,56},{56,64},{64,7... | collective-permute-start | bytes 5505032 | tf_op jit(solution)/shard_map/ppermute | solution.py:162
  144.8 12.8 %fusion.6.mid_ref = f32[64,64,896]{2,1,0:T(8,128)} fusion(f32[64,80,1]{1,0,2:T(8,128)S(1)} %copy-done.1, f32[64,8,896]{2,1,0:T(8,128)S(1)} %collective-permute-done.1, f32[64,64,896]{2,1,0:T(8,128)} %shard_map.83, f32[64,8,896]{2,1,0:T(8,128)} %collective-permute-done), kind=kOutput, calls=%fused_computation.7 | convolution fusion | flops 1770782720 | bytes 33050624 | tf_op jit(solution)/shard_map/ck,rke->rce/dot_general | solution.py:211
  157.6 2.8 %slice_reduce_fusion = f32[64,64]{1,0:T(8,128)S(1)} fusion(f32[64,64,896]{2,1,0:T(8,128)} %fusion.6.mid_ref), kind=kLoop, calls=%fused_computation.20 | loop fusion | bytes 32768 | tf_op jit(solution)/shard_map/slice | solution.py:218
  160.4 0.0 copy-done.8
  160.4 0.1 fusion.33
  160.6 2.0 %copy.29.inv_ref = f32[64,64,1]{2,1,0:T(8,128)} copy(f32[64,64,1]{1,0,2:T(8,128)S(1)} %maximum_bitcast_fusion) | data formatting | bytes 32768 | tf_op jit(solution)/shard_map/broadcast_in_dim | solution.py:222
  162.6 0.0 copy-start.7
  162.6 0.0 copy-start.6
  162.6 0.0 copy-start.5
  162.6 15.6 %shard_map.84.prev_ref = bf16[64,64,768]{2,1,0:T(8,128)(2,1)} custom-call(f32[64,64,896]{2,1,0:T(8,128)} %fusion.6.mid_ref, bf16[64,64,768]{2,1,0:T(8,128)(2,1)} %cb_ref.3, f32[64,64,1]{2,1,0:T(8,128)} %copy.29.inv_ref), custom_call_target="tpu_custom_call" | custom-call | tf_op jit(solution)/shard_map/pallas_call | solution.py:97
  178.2 1.9 slice_reduce_fusion.2
  180.1 0.0 copy-done.7
  180.1 0.1 fusion.55
  180.2 0.0 copy-done.6
  180.2 0.1 fusion.54
  180.3 1.0 collective-permute-done.3.below_ref
  181.3 1.2 slice_reduce_fusion.3
  182.6 0.0 copy-done.5
  182.6 0.1 fusion.34
  182.7 0.0 collective-permute-done.2.above_ref
  182.7 1.2 slice_reduce_fusion.4
  183.9 0.0 copy-done.4
  183.9 0.1 fusion.35
  184.1 0.2 copy.28
  184.3 0.9 broadcast_divide_fusion.inv_ref
  185.2 7.9 %shard_map.85 = bf16[64,64,768]{2,1,0:T(8,128)(2,1)} custom-call(f32[8,64,896]{2,1,0:T(8,128)} %collective-permute-done.2.above_ref, f32[64,64,896]{2,1,0:T(8,128)} %fusion.6.mid_ref, f32[8,64,896]{2,1,0:T(8,128)} %collective-permute-done.3.below_ref, bf16[64,64,768]{2,1,0:T(8,128)(2,1)} %cb_ref.3, ...), custom_call_target="tpu_custom_call", output_to_operand_aliasing={{}: (5, {})} | custom-call | tf_op jit(solution)/shard_map/pallas_call | solution.py:140
  (13 shorter events, 0.2 us)
Async XLA Ops:
  0.0 3.2 %copy-start.2 = (s32[1024,1]{0,1:T(1,128)S(1)}, s32[1024,1]{0,1:T(1,128)}, u32[]{:S(2)}) copy-start(s32[1024,1]{0,1:T(1,128)} %param.15) | copy-start | bytes 12292
  0.0 3.6 %copy-start.3 = (s32[1024]{0:T(1024)S(1)}, s32[1024]{0:T(1024)}, u32[]{:S(2)}) copy-start(s32[1024]{0:T(1024)} %param.16) | copy-start | bytes 12292
  0.0 5.9 %copy-start = (bf16[1024,768]{1,0:T(8,128)(2,1)S(1)}, bf16[1024,768]{1,0:T(8,128)(2,1)}, u32[]{:S(2)}) copy-start(bf16[1024,768]{1,0:T(8,128)(2,1)} %param.14) | copy-start | bytes 4718596
  13.6 55.0 %all-to-all-start = ((bf16[128,16,896]{2,1,0:T(8,128)(2,1)}), bf16[128,16,896]{2,1,0:T(8,128)(2,1)}, u32[]{:S(2)}, u32[]{:S(2)}) async-start(bf16[128,16,896]{2,1,0:T(8,128)(2,1)} %bitcast.45), calls=%async_computation | async-start | bytes 7340032 | tf_op jit(solution)/shard_map/all_to_all | solution.py:188
  84.3 46.8 %collective-permute-start.1 = (f32[64,8,896]{2,1,0:T(8,128)}, f32[64,8,896]{2,1,0:T(8,128)S(1)}, u32[]{:S(2)}, u32[]{:S(2)}) collective-permute-start(f32[64,8,896]{2,1,0:T(8,128)} %get-tuple-element.46), channel_id=1, source_target_pairs={{1,0},{2,1},{3,2},{4,3},{5,4},{6,5},{7,6},{9,8},{10,9},{11,10},{12... | collective-permute-start | bytes 5505032 | tf_op jit(solution)/shard_map/ppermute | solution.py:162
  87.1 45.1 %collective-permute-start = (f32[64,8,896]{2,1,0:T(8,128)}, f32[64,8,896]{2,1,0:T(8,128)}, u32[]{:S(2)}, u32[]{:S(2)}) collective-permute-start(f32[64,8,896]{2,1,0:T(8,128)} %get-tuple-element.45), channel_id=1, source_target_pairs={{0,1},{1,2},{2,3},{3,4},{4,5},{5,6},{6,7},{8,9},{9,10},{10,11},{11... | collective-permute-start | bytes 5505032 | tf_op jit(solution)/shard_map/ppermute | solution.py:162
  111.3 21.9 %copy-start.1 = (f32[64,80,1]{1,0,2:T(8,128)S(1)}, f32[64,80,1]{1,0,2:T(8,128)}, u32[]{:S(2)}) copy-start(f32[64,80,1]{1,0,2:T(8,128)} %constant.151) | copy-start | bytes 61444
  135.4 45.9 %collective-permute-start.3 = (f32[8,64,896]{2,1,0:T(8,128)}, f32[8,64,896]{2,1,0:T(8,128)}, u32[]{:S(2)}, u32[]{:S(2)}) collective-permute-start(f32[8,64,896]{2,1,0:T(8,128)} %fusion.26), channel_id=1, source_target_pairs={{8,0},{16,8},{24,16},{32,24},{40,32},{48,40},{56,48},{64,56},{72,6... | collective-permute-start | bytes 5505032 | tf_op jit(solution)/shard_map/ppermute | solution.py:162
  141.2 19.1 %copy-start.8 = (f32[48,64]{1,0:T(8,128)S(1)}, f32[48,64]{1,0:T(8,128)}, u32[]{:S(2)}) copy-start(f32[48,64]{1,0:T(8,128)} %constant.146) | copy-start | bytes 36868
  141.2 41.4 %collective-permute-start.2 = (f32[8,64,896]{2,1,0:T(8,128)}, f32[8,64,896]{2,1,0:T(8,128)}, u32[]{:S(2)}, u32[]{:S(2)}) collective-permute-start(f32[8,64,896]{2,1,0:T(8,128)} %fusion.29), channel_id=1, source_target_pairs={{0,8},{8,16},{16,24},{24,32},{32,40},{40,48},{48,56},{56,64},{64,7... | collective-permute-start | bytes 5505032 | tf_op jit(solution)/shard_map/ppermute | solution.py:162
  162.6 17.5 %copy-start.7 = (f32[8,16]{1,0:T(8,128)S(1)}, f32[8,16]{1,0:T(8,128)}, u32[]{:S(2)}) copy-start(f32[8,16]{1,0:T(8,128)} %constant.149) | copy-start | bytes 1540
  162.6 17.6 %copy-start.6 = (f32[8,16]{1,0:T(8,128)S(1)}, f32[8,16]{1,0:T(8,128)}, u32[]{:S(2)}) copy-start(f32[8,16]{1,0:T(8,128)} %constant.148) | copy-start | bytes 1540
  162.6 20.0 %copy-start.5 = (f32[8,8]{1,0:T(8,128)S(1)}, f32[8,8]{1,0:T(8,128)}, u32[]{:S(2)}) copy-start(f32[8,8]{1,0:T(8,128)} %constant.150) | copy-start | bytes 772
  162.6 21.3 %copy-start.4 = (f32[8,8]{1,0:T(8,128)S(1)}, f32[8,8]{1,0:T(8,128)}, u32[]{:S(2)}) copy-start(f32[8,8]{1,0:T(8,128)} %constant.147) | copy-start | bytes 772

commit v12 on v11

--- a/solution.py
+++ b/solution.py
@@ -27,15 +27,25 @@
     picks = jnp.asarray(col_blocks, jnp.int32)
 
     def kernel(picks_ref, ids_ref, docs_ref, *refs):
-        num_ref = refs[-1]
+        num_ref = refs[-1] if prior is not None else refs[-3]
         place = lax.broadcasted_iota(jnp.int32, (band, rows), 0)
         first_col = picks_ref[pl.program_id(0)] * RADIUS
         units = (place // RADIUS) * cols_tile + first_col + place % RADIUS
         one_hot = (units == ids_ref[...]).astype(jnp.bfloat16)
         sums = jnp.dot(one_hot, docs_ref[...], preferred_element_type=jnp.float32)
         num_ref[...] = sums.reshape(rows_tile, RADIUS, width)
-
-    out_specs = pl.BlockSpec((rows_tile, RADIUS, width), lambda j, p: (0, p[j], 0))
+        if prior is None:
+            for side in range(2):
+
+                @pl.when(pl.program_id(0) == side)
+                def _():
+                    refs[side - 2][...] = sums.reshape(rows_tile, RADIUS, width)
+
+    out_specs = [pl.BlockSpec((rows_tile, RADIUS, width), lambda j, p: (0, p[j], 0))]
+    out_shape = [jax.ShapeDtypeStruct((rows_tile, cols_tile, width), jnp.float32)]
+    if prior is None:
+        out_specs += [pl.BlockSpec((rows_tile, RADIUS, width), lambda j, p: (0, 0, 0))] * 2
+        out_shape += [jax.ShapeDtypeStruct((rows_tile, RADIUS, width), jnp.float32)] * 2
     in_specs = [
         pl.BlockSpec((1, rows), lambda j, p: (0, 0)),
         pl.BlockSpec((rows, width), lambda j, p: (0, 0)),
@@ -54,7 +64,7 @@
             in_specs=in_specs,
             out_specs=out_specs,
         ),
-        out_shape=jax.ShapeDtypeStruct((rows_tile, cols_tile, width), jnp.float32),
+        out_shape=out_shape,
         input_output_aliases=aliases,
     )(picks, *operands)
 
@@ -198,9 +208,10 @@
     col_total = cols_tile // RADIUS
     bands = accumulate(unit_ids, got, rows_tile, cols_tile, feature, [0, col_total - 1])
     last = cols_tile - RADIUS
-    from_left, from_right = exchange(bands[:, :RADIUS], bands[:, last:], "my")
+    bands, lead, tail = bands
+    from_left, from_right = exchange(lead, tail, "my")
     inner = list(range(1, col_total - 1))
-    numerator = accumulate(unit_ids, got, rows_tile, cols_tile, feature, inner, bands)
+    (numerator,) = accumulate(unit_ids, got, rows_tile, cols_tile, feature, inner, bands)
 
     g_rows = jnp.asarray(band_matrix(rows_tile))
     g_cols = jnp.asarray(band_matrix(cols_tile))

time: 197 us -> 194 us (0.985)
  local copies, waits for them, and re-layouts: 18.2 us -> 14.1 us
    slice x1 -> x0, local copies, waits for them, and re-layouts: 4.15 us -> none  [on_device(): from_left, from_right = exchange(bands[:, :RADIUS], bands[:, last:], 'my')]
  transfers between devices with their start and end apart: 5 -> 5, of which waited for: 4 -> 4; matrix products, arithmetic and copies ran while one was open for 14% -> 14% of each run, Pallas kernels for 17% -> 18%
where the time goes in v12:
time: 194 us; the launch traced here: 190 us
  waiting for transfers between devices  62.7 us (32%)
  Pallas kernels  51.8 us (27%)
  starting transfers between devices  27.2 us (14%)
  matrix products  17.7 us (9%)
  other arithmetic  16.6 us (9%)
  local copies, waits for them, and re-layouts  14.1 us (7%)
    all_to_all x1, waiting for transfers between devices, on_device(): lax.all_to_all(outgoing.reshape(tile_total, capacity, width), ('mx', 'my'...  43.3 us
    pallas_call x2, Pallas kernels, accumulate(): pl.pallas_call(kernel, grid_spec=pltpu.PrefetchScalarGridSpec(num_scalar_...  28.2 us
    ppermute x4, waiting for transfers between devices, exchange(): return (lax.ppermute(last, axis, up), lax.ppermute(lead, axis, down))  19.4 us
    dot_general x3, matrix products, col_pass(): jnp.einsum('ck,rke->rce', g_cols, jnp.concatenate(pieces, axis=1), precis...  17 us
    ppermute x4, starting transfers between devices, exchange(): return (lax.ppermute(last, axis, up), lax.ppermute(lead, axis, down))  16.2 us
    pallas_call x1, Pallas kernels, finish_inner(): pl.pallas_call(kernel, grid=(feature // lanes,), in_specs=[slab_spec, sla...  15.6 us
    all_to_all x1, starting transfers between devices, on_device(): lax.all_to_all(outgoing.reshape(tile_total, capacity, width), ('mx', 'my'...  11.1 us
    pallas_call x1, Pallas kernels, finish_edges(): pl.pallas_call(kernel, grid=(2,), in_specs=[halo_spec, pl.BlockSpec((near...  7.92 us
  transfers between devices with their start and end apart: 5, of which 4 were waited for; matrix products, arithmetic and copies ran while one was open for 14% of the time, Pallas kernels for 18%

profile of v12, /device:TPU:15, one launch (start us, length us, event | category | flops | bytes accessed | tf_op | source)
XLA Modules:
  0.0 190.4 jit_solution(12403516784362456922)
XLA Ops:
  0.0 0.0 copy-start.2
  0.0 0.0 copy-start.3
  0.0 0.0 copy-start
  0.0 0.6 compare_reduce_fusion.1
  0.6 0.7 compare_reduce_fusion.2
  1.4 0.6 compare_reduce_fusion
  2.0 0.8 copy.24
  2.8 0.2 fusion.38
  3.1 0.1 copy.25
  3.2 0.0 copy-done.2
  3.2 0.4 fusion.37
  3.6 0.0 copy-done.3
  3.6 1.3 fusion.45
  5.0 0.1 scatter.19
  5.1 0.6 broadcast_select_fusion
  5.7 0.1 scatter.24
  5.7 0.2 copy.26
  5.9 0.0 copy-done
  5.9 7.6 %scatter_custom_fusion = bf16[2048,896]{1,0:T(8,128)(2,1)} fusion(s32[1024]{0:T(1024)S(1)} %bitcast.51, bf16[1024,128]{1,0:T(8,128)(2,1)S(1)} %copy.26, bf16[]{:T(256)} %constant.163, bf16[1024,768]{1,0:T(8,128)(2,1)S(1)} %copy-done, bf16[]{:T(256)} %constant.123.clone.1), kind=kCustom, calls=%fused_computation.21 | custom fusion | flops 3670016 | bytes 5505028 | tf_op jit(solution)/shard_map/scatter | solution.py:197
  13.6 11.1 %all-to-all-start = ((bf16[128,16,896]{2,1,0:T(8,128)(2,1)}), bf16[128,16,896]{2,1,0:T(8,128)(2,1)}, u32[]{:S(2)}, u32[]{:S(2)}) async-start(bf16[128,16,896]{2,1,0:T(8,128)(2,1)} %bitcast.45), calls=%async_computation | async-start | bytes 7340032 | tf_op jit(solution)/shard_map/all_to_all | solution.py:198
  24.7 0.6 iota_multiply_fusion.1.picks_ref
  25.2 43.3 %all-to-all-done = bf16[128,16,896]{2,1,0:T(8,128)(2,1)} async-done(((bf16[128,16,896]{2,1,0:T(8,128)(2,1)}), bf16[128,16,896]{2,1,0:T(8,128)(2,1)}, u32[]{:S(2)}, u32[]{:S(2)}) %all-to-all-start) | async-done | bytes 3670048 | tf_op jit(solution)/shard_map/all_to_all | solution.py:198
  68.5 3.0 %select_reduce_fusion = s32[2048]{0:T(1024)} fusion(bf16[2048,896]{1,0:T(8,128)(2,1)} %bitcast.8.docs_ref), kind=kLoop, calls=%fused_computation.35 | loop fusion | flops 12288 | bytes 20480 | tf_op jit(solution)/shard_map/jit(_where)/select_n | solution.py:207
  71.5 10.2 %shard_map.82 = (f32[64,64,896]{2,1,0:T(8,128)}, f32[64,8,896]{2,1,0:T(8,128)}, f32[64,8,896]{2,1,0:T(8,128)}) custom-call(s32[2]{0:T(128)} %iota_multiply_fusion.1.picks_ref, s32[1,2048]{1,0:T(1,128)} %bitcast.46, bf16[2048,896]{1,0:T(8,128)(2,1)} %bitcast.8.docs_ref), custom_call_target="tpu_custom_call" | custom-call | tf_op jit(solution)/shard_map/pallas_call | solution.py:59
  81.7 2.7 %collective-permute-start.1 = (f32[64,8,896]{2,1,0:T(8,128)}, f32[64,8,896]{2,1,0:T(8,128)S(1)}, u32[]{:S(2)}, u32[]{:S(2)}) collective-permute-start(f32[64,8,896]{2,1,0:T(8,128)} %get-tuple-element.46), channel_id=1, source_target_pairs={{1,0},{2,1},{3,2},{4,3},{5,4},{6,5},{7,6},{9,8},{10,9},{11,10},{12... | collective-permute-start | bytes 5505032 | tf_op jit(solution)/shard_map/ppermute | solution.py:172
  84.4 6.2 %collective-permute-start = (f32[64,8,896]{2,1,0:T(8,128)}, f32[64,8,896]{2,1,0:T(8,128)}, u32[]{:S(2)}, u32[]{:S(2)}) collective-permute-start(f32[64,8,896]{2,1,0:T(8,128)} %get-tuple-element.44), channel_id=1, source_target_pairs={{0,1},{1,2},{2,3},{3,4},{4,5},{5,6},{6,7},{8,9},{9,10},{10,11},{11... | collective-permute-start | bytes 5505032 | tf_op jit(solution)/shard_map/ppermute | solution.py:172
  90.6 18.1 %shard_map.83 = f32[64,64,896]{2,1,0:T(8,128)} custom-call(s32[6]{0:T(128)} %constant.141.clone.picks_ref, s32[1,2048]{1,0:T(1,128)} %bitcast.47, bf16[2048,896]{1,0:T(8,128)(2,1)} %bitcast.8.docs_ref, f32[64,64,896]{2,1,0:T(8,128)} %get-tuple-element.45.refs_0_), custom_call_target="tpu_custom_call", output_to_operand_aliasing={{}: (3, {})} | custom-call | tf_op jit(solution)/shard_map/pallas_call | solution.py:59
  108.6 0.0 copy-start.1
  108.6 2.4 %fusion.50 = (f32[8,64,896]{2,1,0:T(8,128)S(1)}, f32[8,64,896]{2,1,0:T(8,128)S(1)}) fusion(f32[64,64,896]{2,1,0:T(8,128)} %shard_map.83), kind=kLoop, calls=%fused_computation.75 | loop fusion | bytes 7340032 | tf_op jit(solution)/shard_map/slice | solution.py:221
  111.0 17.4 %collective-permute-done.1 = f32[64,8,896]{2,1,0:T(8,128)S(1)} collective-permute-done((f32[64,8,896]{2,1,0:T(8,128)}, f32[64,8,896]{2,1,0:T(8,128)S(1)}, u32[]{:S(2)}, u32[]{:S(2)}) %collective-permute-start.1) | collective-permute-done | bytes 1835040 | tf_op jit(solution)/shard_map/ppermute | solution.py:172
  128.5 0.9 collective-permute-done
  129.5 1.1 fusion.51
  130.5 0.0 copy-done.1
  130.6 2.1 %fusion.26 = f32[8,64,896]{2,1,0:T(8,128)} fusion(f32[64,80,1]{1,0,2:T(8,128)S(1)} %copy-done.1, f32[8,8,896]{2,1,0:T(8,128)S(1)} %get-tuple-element.53, f32[8,64,896]{2,1,0:T(8,128)S(1)} %get-tuple-element.49, f32[8,8,896]{2,1,0:T(8,128)S(1)} %get-tuple-element.51), kind=kOutput, calls=%fused_computation.26 | convolution fusion | flops 221347840 | bytes 4149248 | tf_op jit(solution)/shard_map/ck,rke->rce/dot_general | solution.py:222
  132.7 3.7 %collective-permute-start.3 = (f32[8,64,896]{2,1,0:T(8,128)}, f32[8,64,896]{2,1,0:T(8,128)}, u32[]{:S(2)}, u32[]{:S(2)}) collective-permute-start(f32[8,64,896]{2,1,0:T(8,128)} %fusion.26), channel_id=1, source_target_pairs={{8,0},{16,8},{24,16},{32,24},{40,32},{48,40},{56,48},{64,56},{72,6... | collective-permute-start | bytes 5505032 | tf_op jit(solution)/shard_map/ppermute | solution.py:172
  136.4 2.2 %fusion.29 = f32[8,64,896]{2,1,0:T(8,128)} fusion(f32[64,80,1]{1,0,2:T(8,128)S(1)} %copy-done.1, f32[8,8,896]{2,1,0:T(8,128)S(1)} %get-tuple-element.54, f32[8,64,896]{2,1,0:T(8,128)S(1)} %get-tuple-element.50, f32[8,8,896]{2,1,0:T(8,128)S(1)} %get-tuple-element.52), kind=kOutput, calls=%fused_computation.27 | convolution fusion | flops 221347840 | bytes 4149248 | tf_op jit(solution)/shard_map/ck,rke->rce/dot_general | solution.py:222
  138.5 0.0 copy-start.8
  138.5 3.6 %collective-permute-start.2 = (f32[8,64,896]{2,1,0:T(8,128)}, f32[8,64,896]{2,1,0:T(8,128)}, u32[]{:S(2)}, u32[]{:S(2)}) collective-permute-start(f32[8,64,896]{2,1,0:T(8,128)} %fusion.29), channel_id=1, source_target_pairs={{0,8},{8,16},{16,24},{24,32},{32,40},{40,48},{48,56},{56,64},{64,7... | collective-permute-start | bytes 5505032 | tf_op jit(solution)/shard_map/ppermute | solution.py:172
  142.1 12.8 %fusion.6.mid_ref = f32[64,64,896]{2,1,0:T(8,128)} fusion(f32[64,80,1]{1,0,2:T(8,128)S(1)} %copy-done.1, f32[64,8,896]{2,1,0:T(8,128)S(1)} %collective-permute-done.1, f32[64,64,896]{2,1,0:T(8,128)} %shard_map.83, f32[64,8,896]{2,1,0:T(8,128)} %collective-permute-done), kind=kOutput, calls=%fused_computation.7 | convolution fusion | flops 1770782720 | bytes 33050624 | tf_op jit(solution)/shard_map/ck,rke->rce/dot_general | solution.py:222
  154.9 2.8 %slice_reduce_fusion = f32[64,64]{1,0:T(8,128)S(1)} fusion(f32[64,64,896]{2,1,0:T(8,128)} %fusion.6.mid_ref), kind=kLoop, calls=%fused_computation.20 | loop fusion | bytes 32768 | tf_op jit(solution)/shard_map/slice | solution.py:229
  157.7 0.0 copy-done.8
  157.7 0.1 fusion.33
  157.9 2.0 %copy.29.inv_ref = f32[64,64,1]{2,1,0:T(8,128)} copy(f32[64,64,1]{1,0,2:T(8,128)S(1)} %maximum_bitcast_fusion) | data formatting | bytes 32768 | tf_op jit(solution)/shard_map/broadcast_in_dim | solution.py:233
  159.9 0.0 copy-start.7
  159.9 0.0 copy-start.6
  159.9 0.0 copy-start.5
  159.9 0.0 copy-start.4
  159.9 15.6 %shard_map.84.prev_ref = bf16[64,64,768]{2,1,0:T(8,128)(2,1)} custom-call(f32[64,64,896]{2,1,0:T(8,128)} %fusion.6.mid_ref, bf16[64,64,768]{2,1,0:T(8,128)(2,1)} %cb_ref.3, f32[64,64,1]{2,1,0:T(8,128)} %copy.29.inv_ref), custom_call_target="tpu_custom_call" | custom-call | tf_op jit(solution)/shard_map/pallas_call | solution.py:107
  175.5 1.9 slice_reduce_fusion.2
  177.4 0.0 copy-done.7
  177.4 0.1 fusion.54
  177.5 0.0 copy-done.6
  177.5 0.1 fusion.53
  177.6 1.0 collective-permute-done.3.below_ref
  178.6 1.2 slice_reduce_fusion.3
  179.9 0.0 copy-done.5
  179.9 0.1 fusion.34
  180.0 0.0 collective-permute-done.2.above_ref
  180.0 1.2 slice_reduce_fusion.4
  181.2 0.0 copy-done.4
  181.2 0.1 fusion.35
  181.4 0.2 copy.28
  181.6 0.9 broadcast_divide_fusion.inv_ref
  182.5 7.9 %shard_map.85 = bf16[64,64,768]{2,1,0:T(8,128)(2,1)} custom-call(f32[8,64,896]{2,1,0:T(8,128)} %collective-permute-done.2.above_ref, f32[64,64,896]{2,1,0:T(8,128)} %fusion.6.mid_ref, f32[8,64,896]{2,1,0:T(8,128)} %collective-permute-done.3.below_ref, bf16[64,64,768]{2,1,0:T(8,128)(2,1)} %cb_ref.3, ...), custom_call_target="tpu_custom_call", output_to_operand_aliasing={{}: (5, {})} | custom-call | tf_op jit(solution)/shard_map/pallas_call | solution.py:150
  (12 shorter events, 0.2 us)
Async XLA Ops:
  0.0 3.2 %copy-start.2 = (s32[1024,1]{0,1:T(1,128)S(1)}, s32[1024,1]{0,1:T(1,128)}, u32[]{:S(2)}) copy-start(s32[1024,1]{0,1:T(1,128)} %param.15) | copy-start | bytes 12292
  0.0 3.6 %copy-start.3 = (s32[1024]{0:T(1024)S(1)}, s32[1024]{0:T(1024)}, u32[]{:S(2)}) copy-start(s32[1024]{0:T(1024)} %param.16) | copy-start | bytes 12292
  0.0 5.9 %copy-start = (bf16[1024,768]{1,0:T(8,128)(2,1)S(1)}, bf16[1024,768]{1,0:T(8,128)(2,1)}, u32[]{:S(2)}) copy-start(bf16[1024,768]{1,0:T(8,128)(2,1)} %param.14) | copy-start | bytes 4718596
  13.6 55.0 %all-to-all-start = ((bf16[128,16,896]{2,1,0:T(8,128)(2,1)}), bf16[128,16,896]{2,1,0:T(8,128)(2,1)}, u32[]{:S(2)}, u32[]{:S(2)}) async-start(bf16[128,16,896]{2,1,0:T(8,128)(2,1)} %bitcast.45), calls=%async_computation | async-start | bytes 7340032 | tf_op jit(solution)/shard_map/all_to_all | solution.py:198
  81.7 46.8 %collective-permute-start.1 = (f32[64,8,896]{2,1,0:T(8,128)}, f32[64,8,896]{2,1,0:T(8,128)S(1)}, u32[]{:S(2)}, u32[]{:S(2)}) collective-permute-start(f32[64,8,896]{2,1,0:T(8,128)} %get-tuple-element.46), channel_id=1, source_target_pairs={{1,0},{2,1},{3,2},{4,3},{5,4},{6,5},{7,6},{9,8},{10,9},{11,10},{12... | collective-permute-start | bytes 5505032 | tf_op jit(solution)/shard_map/ppermute | solution.py:172
  84.4 45.1 %collective-permute-start = (f32[64,8,896]{2,1,0:T(8,128)}, f32[64,8,896]{2,1,0:T(8,128)}, u32[]{:S(2)}, u32[]{:S(2)}) collective-permute-start(f32[64,8,896]{2,1,0:T(8,128)} %get-tuple-element.44), channel_id=1, source_target_pairs={{0,1},{1,2},{2,3},{3,4},{4,5},{5,6},{6,7},{8,9},{9,10},{10,11},{11... | collective-permute-start | bytes 5505032 | tf_op jit(solution)/shard_map/ppermute | solution.py:172
  108.6 21.9 %copy-start.1 = (f32[64,80,1]{1,0,2:T(8,128)S(1)}, f32[64,80,1]{1,0,2:T(8,128)}, u32[]{:S(2)}) copy-start(f32[64,80,1]{1,0,2:T(8,128)} %constant.151) | copy-start | bytes 61444
  132.7 45.9 %collective-permute-start.3 = (f32[8,64,896]{2,1,0:T(8,128)}, f32[8,64,896]{2,1,0:T(8,128)}, u32[]{:S(2)}, u32[]{:S(2)}) collective-permute-start(f32[8,64,896]{2,1,0:T(8,128)} %fusion.26), channel_id=1, source_target_pairs={{8,0},{16,8},{24,16},{32,24},{40,32},{48,40},{56,48},{64,56},{72,6... | collective-permute-start | bytes 5505032 | tf_op jit(solution)/shard_map/ppermute | solution.py:172
  138.5 19.1 %copy-start.8 = (f32[48,64]{1,0:T(8,128)S(1)}, f32[48,64]{1,0:T(8,128)}, u32[]{:S(2)}) copy-start(f32[48,64]{1,0:T(8,128)} %constant.146) | copy-start | bytes 36868
  138.5 41.5 %collective-permute-start.2 = (f32[8,64,896]{2,1,0:T(8,128)}, f32[8,64,896]{2,1,0:T(8,128)}, u32[]{:S(2)}, u32[]{:S(2)}) collective-permute-start(f32[8,64,896]{2,1,0:T(8,128)} %fusion.29), channel_id=1, source_target_pairs={{0,8},{8,16},{16,24},{24,32},{32,40},{40,48},{48,56},{56,64},{64,7... | collective-permute-start | bytes 5505032 | tf_op jit(solution)/shard_map/ppermute | solution.py:172
  159.9 17.5 %copy-start.7 = (f32[8,16]{1,0:T(8,128)S(1)}, f32[8,16]{1,0:T(8,128)}, u32[]{:S(2)}) copy-start(f32[8,16]{1,0:T(8,128)} %constant.149) | copy-start | bytes 1540
  159.9 17.6 %copy-start.6 = (f32[8,16]{1,0:T(8,128)S(1)}, f32[8,16]{1,0:T(8,128)}, u32[]{:S(2)}) copy-start(f32[8,16]{1,0:T(8,128)} %constant.148) | copy-start | bytes 1540
  159.9 20.0 %copy-start.5 = (f32[8,8]{1,0:T(8,128)S(1)}, f32[8,8]{1,0:T(8,128)}, u32[]{:S(2)}) copy-start(f32[8,8]{1,0:T(8,128)} %constant.150) | copy-start | bytes 772
  159.9 21.3 %copy-start.4 = (f32[8,8]{1,0:T(8,128)S(1)}, f32[8,8]{1,0:T(8,128)}, u32[]{:S(2)}) copy-start(f32[8,8]{1,0:T(8,128)} %constant.147) | copy-start | bytes 772

commit v13 on v12

--- a/solution.py
+++ b/solution.py
@@ -73,7 +73,7 @@
 GROUP = 4
 
 
-def row_group(read, cb_ref, inv_ref, out_ref, first, cols, lanes):
+def row_group(read, first, cols, lanes, emit):
     for c0 in range(0, cols, 8):
         window = [read(j, c0, lanes) for j in range(GROUP + 2 * RADIUS)]
         for q in range(GROUP):
@@ -81,45 +81,75 @@
             acc = TAPS[0] * window[centre]
             for k in range(1, RADIUS + 1):
                 acc = acc + TAPS[k] * (window[centre - k] + window[centre + k])
-            r = first + q
-            base = cb_ref[r, pl.ds(c0, 8), lanes].astype(jnp.float32)
-            upd = (acc + 8.0 * base) * inv_ref[r, pl.ds(c0, 8), :]
-            out_ref[r, pl.ds(c0, 8), lanes] = upd.astype(out_ref.dtype)
-
-
-def finish_inner(middle, codebook, inv):
+            emit(first + q, c0, acc)
+
+
+def updater(cb_ref, inv_ref, out_ref, lanes):
+    def emit(r, c0, acc):
+        base = cb_ref[r, pl.ds(c0, 8), lanes].astype(jnp.float32)
+        upd = (acc + 8.0 * base) * inv_ref[r, pl.ds(c0, 8), :]
+        out_ref[r, pl.ds(c0, 8), lanes] = upd.astype(out_ref.dtype)
+
+    return emit
+
+
+def inverter(inv_ref):
+    def emit(r, c0, acc):
+        inv_ref[r, pl.ds(c0, 8), :] = 1.0 / (acc[:, 2:3] + 8.0)
+
+    return emit
+
+
+def finish_inner(middle, codebook):
     rows, cols, feature = codebook.shape
     lanes = 128
-
-    def kernel(mid_ref, cb_ref, inv_ref, out_ref):
-        def body(i, carry):
-            first = RADIUS + i * GROUP
-
-            def read(j, c0, part):
-                return mid_ref[first + j - RADIUS, pl.ds(c0, 8), part]
-
-            row_group(read, cb_ref, inv_ref, out_ref, first, cols, slice(None))
-            return carry
-
-        lax.fori_loop(0, (rows - 2 * RADIUS) // GROUP, body, 0)
-
-    slab_spec = pl.BlockSpec((rows, cols, lanes), lambda j: (0, 0, j))
+    blocks = feature // lanes
+
+    def kernel(mid_ref, cb_ref, out_ref, inv_ref):
+        step = pl.program_id(0)
+
+        def rows_pass(emit):
+            def body(i, carry):
+                first = RADIUS + i * GROUP
+
+                def read(j, c0, part):
+                    return mid_ref[first + j - RADIUS, pl.ds(c0, 8), part]
+
+                row_group(read, first, cols, slice(None), emit)
+                return carry
+
+            lax.fori_loop(0, (rows - 2 * RADIUS) // GROUP, body, 0)
+
+        @pl.when(step == 0)
+        def _():
+            rows_pass(inverter(inv_ref))
+
+        @pl.when(step > 0)
+        def _():
+            rows_pass(updater(cb_ref, inv_ref, out_ref, slice(None)))
+
+    out_spec = pl.BlockSpec((rows, cols, lanes), lambda j: (0, 0, jnp.maximum(j - 1, 0)))
     return pl.pallas_call(
         kernel,
-        grid=(feature // lanes,),
-        in_specs=[slab_spec, slab_spec, pl.BlockSpec((rows, cols, 1), lambda j: (0, 0, 0))],
-        out_specs=slab_spec,
+        grid=(blocks + 1,),
+        in_specs=[
+            pl.BlockSpec((rows, cols, lanes), lambda j: (0, 0, (j + blocks) % (blocks + 1))),
+            out_spec,
+        ],
+        out_specs=out_spec,
         out_shape=jax.ShapeDtypeStruct(codebook.shape, codebook.dtype),
-    )(middle, codebook, inv)
-
-
-def finish_edges(above, middle, below, codebook, inv, partial):
+        scratch_shapes=[pltpu.VMEM((rows, cols, 1), jnp.float32)],
+    )(middle, codebook)
+
+
+def finish_edges(above, middle, below, codebook, partial):
     rows, cols, feature = codebook.shape
+    width = middle.shape[2]
     lanes = 128
     near = 2 * RADIUS
     last_edge = rows // RADIUS - 1
 
-    def kernel(above_ref, mid_ref, below_ref, cb_ref, inv_ref, prev_ref, out_ref, ext_ref):
+    def kernel(above_ref, mid_ref, below_ref, cb_ref, prev_ref, out_ref, ext_ref, inv_ref):
         del prev_ref
         side = pl.program_id(0)
 
@@ -139,30 +169,34 @@
             def read(j, c0, part):
                 return ext_ref[first + j, pl.ds(c0, 8), part]
 
+            row_group(read, first, cols, pl.ds(feature, lanes), inverter(inv_ref))
             for lane in range(0, feature, lanes):
-                row_group(read, cb_ref, inv_ref, out_ref, first, cols, pl.ds(lane, lanes))
+                part = pl.ds(lane, lanes)
+                row_group(read, first, cols, part, updater(cb_ref, inv_ref, out_ref, part))
             return carry
 
         lax.fori_loop(0, RADIUS // GROUP, body, 0)
 
-    halo_spec = pl.BlockSpec((RADIUS, cols, feature), lambda i: (0, 0, 0))
+    halo_spec = pl.BlockSpec((RADIUS, cols, width), lambda i: (0, 0, 0))
     edge_spec = pl.BlockSpec((RADIUS, cols, feature), lambda i: (i * last_edge, 0, 0))
     return pl.pallas_call(
         kernel,
         grid=(2,),
         in_specs=[
             halo_spec,
-            pl.BlockSpec((near, cols, feature), lambda i: (i * (rows // near - 1), 0, 0)),
+            pl.BlockSpec((near, cols, width), lambda i: (i * (rows // near - 1), 0, 0)),
             halo_spec,
             edge_spec,
-            pl.BlockSpec((RADIUS, cols, 1), lambda i: (i, 0, 0)),
             pl.BlockSpec(memory_space=pl.ANY),
         ],
         out_specs=edge_spec,
         out_shape=jax.ShapeDtypeStruct(codebook.shape, codebook.dtype),
-        scratch_shapes=[pltpu.VMEM((near + RADIUS, cols, feature), jnp.float32)],
-        input_output_aliases={5: 0},
-    )(above, middle, below, codebook, inv, partial)
+        scratch_shapes=[
+            pltpu.VMEM((near + RADIUS, cols, width), jnp.float32),
+            pltpu.VMEM((RADIUS, cols, 1), jnp.float32),
+        ],
+        input_output_aliases={4: 0},
+    )(above, middle, below, codebook, partial)
 
 
 def exchange(lead, last, axis):
@@ -224,21 +258,9 @@
     col_top, col_bottom = col_pass(0, RADIUS), col_pass(last, rows_tile)
 
     above, below = exchange(col_top, col_bottom, "mx")
-    hits_above, hits_below = above[:, :, feature + 2], below[:, :, feature + 2]
     col_num = col_pass(0, rows_tile)
-    col_hits = col_num[:, :, feature + 2]
-    inner_hits = jnp.einsum("rk,kc->rc", g_rows[RADIUS:last, RADIUS : RADIUS + rows_tile], col_hits, precision=HI)
-    inv_inner = 1.0 / (inner_hits + 8.0)
-    inv = jnp.concatenate([jnp.zeros_like(inv_inner[:RADIUS]), inv_inner, jnp.zeros_like(inv_inner[:RADIUS])])
-    inv = inv[:, :, None]
-    edge_top = jnp.concatenate([hits_above, col_hits[: 2 * RADIUS]], axis=0)
-    edge_bottom = jnp.concatenate([col_hits[last - RADIUS :], hits_below], axis=0)
-    g_edge = g_rows[:RADIUS, : 3 * RADIUS]
-    top_hits = jnp.einsum("rk,kc->rc", g_edge, edge_top, precision=HI)
-    bottom_hits = jnp.einsum("rk,kc->rc", g_edge, edge_bottom, precision=HI)
-    inv_edges = (1.0 / (jnp.concatenate([top_hits, bottom_hits], axis=0) + 8.0))[:, :, None]
-    partial = finish_inner(col_num, codebook, inv)
-    return finish_edges(above, col_num, below, codebook, inv_edges, partial)
+    partial = finish_inner(col_num, codebook)
+    return finish_edges(above, col_num, below, codebook, partial)
 
 
 def solution(mesh):

time: 194 us -> 191 us (0.985)
  local copies, waits for them, and re-layouts: 14.1 us -> 4.77 us
  waiting for transfers between devices: 62.7 us -> 69.3 us
    slice x4 -> x0, local copies, waits for them, and re-layouts: 7.07 us -> none  [the longest x1 2.76 us: on_device(): col_hits = col_num[:, :, feature + 2]]
    ppermute x4, waiting for transfers between devices: 19.4 us -> 25.9 us  [exchange(): return (lax.ppermute(last, axis, up), lax.ppermute(lead, axis, down))]
    broadcast_in_dim x1 -> x0, local copies, waits for them, and re-layouts: 2.03 us -> none  [on_device(): inv = inv[:, :, None]]
  transfers between devices with their start and end apart: 5 -> 5, of which waited for: 4 -> 5; matrix products, arithmetic and copies ran while one was open for 14% -> 10% of each run, Pallas kernels for 18% -> 19%
where the time goes in v13:
time: 191 us; the launch traced here: 188 us
  waiting for transfers between devices  69.3 us (36%)
  Pallas kernels  53.7 us (28%)
  starting transfers between devices  27.1 us (14%)
  matrix products  17 us (9%)
  other arithmetic  15.7 us (8%)
  local copies, waits for them, and re-layouts  4.77 us (2%)
    all_to_all x1, waiting for transfers between devices, on_device(): lax.all_to_all(outgoing.reshape(tile_total, capacity, width), ('mx', 'my'...  43.4 us
    pallas_call x2, Pallas kernels, accumulate(): pl.pallas_call(kernel, grid_spec=pltpu.PrefetchScalarGridSpec(num_scalar_...  28.2 us
    ppermute x4, waiting for transfers between devices, exchange(): return (lax.ppermute(last, axis, up), lax.ppermute(lead, axis, down))  25.9 us
    dot_general x3, matrix products, col_pass(): jnp.einsum('ck,rke->rce', g_cols, jnp.concatenate(pieces, axis=1), precis...  17 us
    pallas_call x1, Pallas kernels, finish_inner(): pl.pallas_call(kernel, grid=(blocks + 1,), in_specs=[pl.BlockSpec((rows,...  16.7 us
    ppermute x4, starting transfers between devices, exchange(): return (lax.ppermute(last, axis, up), lax.ppermute(lead, axis, down))  16 us
    all_to_all x1, starting transfers between devices, on_device(): lax.all_to_all(outgoing.reshape(tile_total, capacity, width), ('mx', 'my'...  11.1 us
    pallas_call x1, Pallas kernels, finish_edges(): pl.pallas_call(kernel, grid=(2,), in_specs=[halo_spec, pl.BlockSpec((near...  8.7 us
  transfers between devices with their start and end apart: 5, of which 5 were waited for; matrix products, arithmetic and copies ran while one was open for 10% of the time, Pallas kernels for 19%

profile of v13, /device:TPU:15, one launch (start us, length us, event | category | flops | bytes accessed | tf_op | source)
XLA Modules:
  0.0 187.7 jit_solution(16530724173189709725)
XLA Ops:
  0.0 0.0 copy-start.2
  0.0 0.0 copy-start.3
  0.0 0.0 copy-start
  0.0 0.6 compare_reduce_fusion.1
  0.6 0.7 compare_reduce_fusion.2
  1.4 0.6 compare_reduce_fusion
  2.0 0.8 copy.11
  2.8 0.2 fusion.34
  3.1 0.1 copy.12
  3.2 0.0 copy-done.2
  3.2 0.4 fusion.33
  3.6 0.0 copy-done.3
  3.6 1.3 fusion.41
  5.0 0.1 scatter.19
  5.1 0.6 broadcast_select_fusion
  5.7 0.1 scatter.24
  5.7 0.2 copy.13
  5.9 0.0 copy-done
  5.9 7.6 %scatter_custom_fusion = bf16[2048,896]{1,0:T(8,128)(2,1)} fusion(s32[1024]{0:T(1024)S(1)} %bitcast.33, bf16[1024,128]{1,0:T(8,128)(2,1)S(1)} %copy.13, bf16[]{:T(256)} %constant.142, bf16[1024,768]{1,0:T(8,128)(2,1)S(1)} %copy-done, bf16[]{:T(256)} %constant.118.clone.1), kind=kCustom, calls=%fused_computation.20 | custom fusion | flops 3670016 | bytes 5505028 | tf_op jit(solution)/shard_map/scatter | solution.py:231
  13.6 11.1 %all-to-all-start = ((bf16[128,16,896]{2,1,0:T(8,128)(2,1)}), bf16[128,16,896]{2,1,0:T(8,128)(2,1)}, u32[]{:S(2)}, u32[]{:S(2)}) async-start(bf16[128,16,896]{2,1,0:T(8,128)(2,1)} %bitcast.27), calls=%async_computation | async-start | bytes 7340032 | tf_op jit(solution)/shard_map/all_to_all | solution.py:232
  24.7 0.5 iota_multiply_fusion.1.picks_ref
  25.2 43.4 %all-to-all-done = bf16[128,16,896]{2,1,0:T(8,128)(2,1)} async-done(((bf16[128,16,896]{2,1,0:T(8,128)(2,1)}), bf16[128,16,896]{2,1,0:T(8,128)(2,1)}, u32[]{:S(2)}, u32[]{:S(2)}) %all-to-all-start) | async-done | bytes 3670048 | tf_op jit(solution)/shard_map/all_to_all | solution.py:232
  68.5 3.0 %select_reduce_fusion = s32[2048]{0:T(1024)} fusion(bf16[2048,896]{1,0:T(8,128)(2,1)} %bitcast.8.docs_ref), kind=kLoop, calls=%fused_computation.27 | loop fusion | flops 12288 | bytes 20480 | tf_op jit(solution)/shard_map/jit(_where)/select_n | solution.py:241
  71.5 10.2 %shard_map.73 = (f32[64,64,896]{2,1,0:T(8,128)}, f32[64,8,896]{2,1,0:T(8,128)}, f32[64,8,896]{2,1,0:T(8,128)}) custom-call(s32[2]{0:T(128)} %iota_multiply_fusion.1.picks_ref, s32[1,2048]{1,0:T(1,128)} %bitcast.28, bf16[2048,896]{1,0:T(8,128)(2,1)} %bitcast.8.docs_ref), custom_call_target="tpu_custom_call" | custom-call | tf_op jit(solution)/shard_map/pallas_call | solution.py:59
  81.7 2.7 %collective-permute-start.1 = (f32[64,8,896]{2,1,0:T(8,128)}, f32[64,8,896]{2,1,0:T(8,128)S(1)}, u32[]{:S(2)}, u32[]{:S(2)}) collective-permute-start(f32[64,8,896]{2,1,0:T(8,128)} %get-tuple-element.46), channel_id=1, source_target_pairs={{1,0},{2,1},{3,2},{4,3},{5,4},{6,5},{7,6},{9,8},{10,9},{11,10},{12... | collective-permute-start | bytes 5505032 | tf_op jit(solution)/shard_map/ppermute | solution.py:206
  84.4 6.1 %collective-permute-start = (f32[64,8,896]{2,1,0:T(8,128)}, f32[64,8,896]{2,1,0:T(8,128)}, u32[]{:S(2)}, u32[]{:S(2)}) collective-permute-start(f32[64,8,896]{2,1,0:T(8,128)} %get-tuple-element.44), channel_id=1, source_target_pairs={{0,1},{1,2},{2,3},{3,4},{4,5},{5,6},{6,7},{8,9},{9,10},{10,11},{11... | collective-permute-start | bytes 5505032 | tf_op jit(solution)/shard_map/ppermute | solution.py:206
  90.6 18.1 %shard_map.74 = f32[64,64,896]{2,1,0:T(8,128)} custom-call(s32[6]{0:T(128)} %constant.133.clone.picks_ref, s32[1,2048]{1,0:T(1,128)} %bitcast.29, bf16[2048,896]{1,0:T(8,128)(2,1)} %bitcast.8.docs_ref, f32[64,64,896]{2,1,0:T(8,128)} %get-tuple-element.45.refs_0_), custom_call_target="tpu_custom_call", output_to_operand_aliasing={{}: (3, {})} | custom-call | tf_op jit(solution)/shard_map/pallas_call | solution.py:59
  108.6 0.0 copy-start.1
  108.6 2.4 %fusion.46 = (f32[8,64,896]{2,1,0:T(8,128)S(1)}, f32[8,64,896]{2,1,0:T(8,128)S(1)}) fusion(f32[64,64,896]{2,1,0:T(8,128)} %shard_map.74), kind=kLoop, calls=%fused_computation.60 | loop fusion | bytes 7340032 | tf_op jit(solution)/shard_map/slice | solution.py:255
  111.1 17.4 %collective-permute-done.1 = f32[64,8,896]{2,1,0:T(8,128)S(1)} collective-permute-done((f32[64,8,896]{2,1,0:T(8,128)}, f32[64,8,896]{2,1,0:T(8,128)S(1)}, u32[]{:S(2)}, u32[]{:S(2)}) %collective-permute-start.1) | collective-permute-done | bytes 1835040 | tf_op jit(solution)/shard_map/ppermute | solution.py:206
  128.5 0.9 collective-permute-done
  129.5 1.1 fusion.47
  130.5 0.0 copy-done.1
  130.6 2.1 %fusion.29 = f32[8,64,896]{2,1,0:T(8,128)} fusion(f32[64,80,1]{1,0,2:T(8,128)S(1)} %copy-done.1, f32[8,8,896]{2,1,0:T(8,128)S(1)} %get-tuple-element.52, f32[8,64,896]{2,1,0:T(8,128)S(1)} %get-tuple-element.48, f32[8,8,896]{2,1,0:T(8,128)S(1)} %get-tuple-element.50), kind=kOutput, calls=%fused_computation.26 | convolution fusion | flops 221347840 | bytes 4149248 | tf_op jit(solution)/shard_map/ck,rke->rce/dot_general | solution.py:256
  132.7 5.2 %collective-permute-start.2 = (f32[8,64,896]{2,1,0:T(8,128)}, f32[8,64,896]{2,1,0:T(8,128)}, u32[]{:S(2)}, u32[]{:S(2)}) collective-permute-start(f32[8,64,896]{2,1,0:T(8,128)} %fusion.29), channel_id=1, source_target_pairs={{0,8},{8,16},{16,24},{24,32},{32,40},{40,48},{48,56},{56,64},{64,7... | collective-permute-start | bytes 5505032 | tf_op jit(solution)/shard_map/ppermute | solution.py:206
  137.9 2.2 %fusion.26 = f32[8,64,896]{2,1,0:T(8,128)} fusion(f32[64,80,1]{1,0,2:T(8,128)S(1)} %copy-done.1, f32[8,8,896]{2,1,0:T(8,128)S(1)} %get-tuple-element.51, f32[8,64,896]{2,1,0:T(8,128)S(1)} %get-tuple-element.47, f32[8,8,896]{2,1,0:T(8,128)S(1)} %get-tuple-element.49), kind=kOutput, calls=%fused_computation.25 | convolution fusion | flops 221347840 | bytes 4149248 | tf_op jit(solution)/shard_map/ck,rke->rce/dot_general | solution.py:256
  140.1 1.9 %collective-permute-start.3 = (f32[8,64,896]{2,1,0:T(8,128)}, f32[8,64,896]{2,1,0:T(8,128)}, u32[]{:S(2)}, u32[]{:S(2)}) collective-permute-start(f32[8,64,896]{2,1,0:T(8,128)} %fusion.26), channel_id=1, source_target_pairs={{8,0},{16,8},{24,16},{32,24},{40,32},{48,40},{56,48},{64,56},{72,6... | collective-permute-start | bytes 5505032 | tf_op jit(solution)/shard_map/ppermute | solution.py:206
  142.0 12.7 %fusion.6.mid_ref = f32[64,64,896]{2,1,0:T(8,128)} fusion(f32[64,80,1]{1,0,2:T(8,128)S(1)} %copy-done.1, f32[64,8,896]{2,1,0:T(8,128)S(1)} %collective-permute-done.1, f32[64,64,896]{2,1,0:T(8,128)} %shard_map.74, f32[64,8,896]{2,1,0:T(8,128)} %collective-permute-done), kind=kOutput, calls=%fused_computation.7 | convolution fusion | flops 1770782720 | bytes 33050624 | tf_op jit(solution)/shard_map/ck,rke->rce/dot_general | solution.py:256
  154.7 16.7 %shard_map.75.prev_ref = bf16[64,64,768]{2,1,0:T(8,128)(2,1)} custom-call(f32[64,64,896]{2,1,0:T(8,128)} %fusion.6.mid_ref, bf16[64,64,768]{2,1,0:T(8,128)(2,1)} %cb_ref.3), custom_call_target="tpu_custom_call" | custom-call | tf_op jit(solution)/shard_map/pallas_call | solution.py:132
  171.4 6.4 %collective-permute-done.2.above_ref = f32[8,64,896]{2,1,0:T(8,128)} collective-permute-done((f32[8,64,896]{2,1,0:T(8,128)}, f32[8,64,896]{2,1,0:T(8,128)}, u32[]{:S(2)}, u32[]{:S(2)}) %collective-permute-start.2) | collective-permute-done | bytes 1835040 | tf_op jit(solution)/shard_map/ppermute | solution.py:206
  177.9 1.1 collective-permute-done.3.below_ref
  179.0 8.7 %shard_map.76 = bf16[64,64,768]{2,1,0:T(8,128)(2,1)} custom-call(f32[8,64,896]{2,1,0:T(8,128)} %collective-permute-done.2.above_ref, f32[64,64,896]{2,1,0:T(8,128)} %fusion.6.mid_ref, f32[8,64,896]{2,1,0:T(8,128)} %collective-permute-done.3.below_ref, bf16[64,64,768]{2,1,0:T(8,128)(2,1)} %cb_ref.3, ...), custom_call_target="tpu_custom_call", output_to_operand_aliasing={{}: (4, {})} | custom-call | tf_op jit(solution)/shard_map/pallas_call | solution.py:182
  (9 shorter events, 0.1 us)
Async XLA Ops:
  0.0 3.2 %copy-start.2 = (s32[1024,1]{0,1:T(1,128)S(1)}, s32[1024,1]{0,1:T(1,128)}, u32[]{:S(2)}) copy-start(s32[1024,1]{0,1:T(1,128)} %param.14) | copy-start | bytes 12292
  0.0 3.6 %copy-start.3 = (s32[1024]{0:T(1024)S(1)}, s32[1024]{0:T(1024)}, u32[]{:S(2)}) copy-start(s32[1024]{0:T(1024)} %param.15) | copy-start | bytes 12292
  0.0 5.9 %copy-start = (bf16[1024,768]{1,0:T(8,128)(2,1)S(1)}, bf16[1024,768]{1,0:T(8,128)(2,1)}, u32[]{:S(2)}) copy-start(bf16[1024,768]{1,0:T(8,128)(2,1)} %param.13) | copy-start | bytes 4718596
  13.6 55.0 %all-to-all-start = ((bf16[128,16,896]{2,1,0:T(8,128)(2,1)}), bf16[128,16,896]{2,1,0:T(8,128)(2,1)}, u32[]{:S(2)}, u32[]{:S(2)}) async-start(bf16[128,16,896]{2,1,0:T(8,128)(2,1)} %bitcast.27), calls=%async_computation | async-start | bytes 7340032 | tf_op jit(solution)/shard_map/all_to_all | solution.py:232
  81.7 46.8 %collective-permute-start.1 = (f32[64,8,896]{2,1,0:T(8,128)}, f32[64,8,896]{2,1,0:T(8,128)S(1)}, u32[]{:S(2)}, u32[]{:S(2)}) collective-permute-start(f32[64,8,896]{2,1,0:T(8,128)} %get-tuple-element.46), channel_id=1, source_target_pairs={{1,0},{2,1},{3,2},{4,3},{5,4},{6,5},{7,6},{9,8},{10,9},{11,10},{12... | collective-permute-start | bytes 5505032 | tf_op jit(solution)/shard_map/ppermute | solution.py:206
  84.4 45.1 %collective-permute-start = (f32[64,8,896]{2,1,0:T(8,128)}, f32[64,8,896]{2,1,0:T(8,128)}, u32[]{:S(2)}, u32[]{:S(2)}) collective-permute-start(f32[64,8,896]{2,1,0:T(8,128)} %get-tuple-element.44), channel_id=1, source_target_pairs={{0,1},{1,2},{2,3},{3,4},{4,5},{5,6},{6,7},{8,9},{9,10},{10,11},{11... | collective-permute-start | bytes 5505032 | tf_op jit(solution)/shard_map/ppermute | solution.py:206
  108.6 21.9 %copy-start.1 = (f32[64,80,1]{1,0,2:T(8,128)S(1)}, f32[64,80,1]{1,0,2:T(8,128)}, u32[]{:S(2)}) copy-start(f32[64,80,1]{1,0,2:T(8,128)} %constant.137) | copy-start | bytes 61444
  132.7 45.2 %collective-permute-start.2 = (f32[8,64,896]{2,1,0:T(8,128)}, f32[8,64,896]{2,1,0:T(8,128)}, u32[]{:S(2)}, u32[]{:S(2)}) collective-permute-start(f32[8,64,896]{2,1,0:T(8,128)} %fusion.29), channel_id=1, source_target_pairs={{0,8},{8,16},{16,24},{24,32},{32,40},{40,48},{48,56},{56,64},{64,7... | collective-permute-start | bytes 5505032 | tf_op jit(solution)/shard_map/ppermute | solution.py:206
  140.1 38.9 %collective-permute-start.3 = (f32[8,64,896]{2,1,0:T(8,128)}, f32[8,64,896]{2,1,0:T(8,128)}, u32[]{:S(2)}, u32[]{:S(2)}) collective-permute-start(f32[8,64,896]{2,1,0:T(8,128)} %fusion.26), channel_id=1, source_target_pairs={{8,0},{16,8},{24,16},{32,24},{40,32},{48,40},{56,48},{64,56},{72,6... | collective-permute-start | bytes 5505032 | tf_op jit(solution)/shard_map/ppermute | solution.py:206

commit v14 on v13

--- a/solution.py
+++ b/solution.py
@@ -100,21 +100,33 @@
     return emit
 
 
-def finish_inner(middle, codebook):
+def piece_reader(refs, row_of):
+    left_ref, inner_ref, right_ref = refs
+    span = inner_ref.shape[1]
+
+    def read(j, c0, part):
+        row = row_of(j)
+        if c0 < RADIUS:
+            return left_ref[row, pl.ds(c0, 8), part]
+        if c0 < RADIUS + span:
+            return inner_ref[row, pl.ds(c0 - RADIUS, 8), part]
+        return right_ref[row, pl.ds(c0 - RADIUS - span, 8), part]
+
+    return read
+
+
+def finish_inner(pieces, codebook):
     rows, cols, feature = codebook.shape
     lanes = 128
     blocks = feature // lanes
 
-    def kernel(mid_ref, cb_ref, out_ref, inv_ref):
+    def kernel(left_ref, inner_ref, right_ref, cb_ref, out_ref, inv_ref):
         step = pl.program_id(0)
 
         def rows_pass(emit):
             def body(i, carry):
                 first = RADIUS + i * GROUP
-
-                def read(j, c0, part):
-                    return mid_ref[first + j - RADIUS, pl.ds(c0, 8), part]
-
+                read = piece_reader((left_ref, inner_ref, right_ref), lambda j: first + j - RADIUS)
                 row_group(read, first, cols, slice(None), emit)
                 return carry
 
@@ -127,40 +139,46 @@
         @pl.when(step > 0)
         def _():
             rows_pass(updater(cb_ref, inv_ref, out_ref, slice(None)))
+
+    def piece_spec(piece):
+        return pl.BlockSpec((rows, piece.shape[1], lanes), lambda j: (0, 0, (j + blocks) % (blocks + 1)))
 
     out_spec = pl.BlockSpec((rows, cols, lanes), lambda j: (0, 0, jnp.maximum(j - 1, 0)))
     return pl.pallas_call(
         kernel,
         grid=(blocks + 1,),
-        in_specs=[
-            pl.BlockSpec((rows, cols, lanes), lambda j: (0, 0, (j + blocks) % (blocks + 1))),
-            out_spec,
-        ],
+        in_specs=[piece_spec(p) for p in pieces] + [out_spec],
         out_specs=out_spec,
         out_shape=jax.ShapeDtypeStruct(codebook.shape, codebook.dtype),
         scratch_shapes=[pltpu.VMEM((rows, cols, 1), jnp.float32)],
-    )(middle, codebook)
-
-
-def finish_edges(above, middle, below, codebook, partial):
+    )(*pieces, codebook)
+
+
+def finish_edges(above, pieces, below, codebook, partial):
     rows, cols, feature = codebook.shape
-    width = middle.shape[2]
+    width = above.shape[2]
     lanes = 128
     near = 2 * RADIUS
     last_edge = rows // RADIUS - 1
-
-    def kernel(above_ref, mid_ref, below_ref, cb_ref, prev_ref, out_ref, ext_ref, inv_ref):
+    span = pieces[1].shape[1]
+
+    def kernel(above_ref, left_ref, inner_ref, right_ref, below_ref, cb_ref, prev_ref, out_ref, ext_ref, inv_ref):
         del prev_ref
         side = pl.program_id(0)
+
+        def fill(lo):
+            ext_ref[lo : lo + near, 0:RADIUS] = left_ref[...]
+            ext_ref[lo : lo + near, RADIUS : RADIUS + span] = inner_ref[...]
+            ext_ref[lo : lo + near, RADIUS + span :] = right_ref[...]
 
         @pl.when(side == 0)
         def _():
             ext_ref[0:RADIUS] = above_ref[...]
-            ext_ref[RADIUS:] = mid_ref[...]
+            fill(RADIUS)
 
         @pl.when(side == 1)
         def _():
-            ext_ref[0:near] = mid_ref[...]
+            fill(0)
             ext_ref[near:] = below_ref[...]
 
         def body(i, carry):
@@ -179,12 +197,14 @@
 
     halo_spec = pl.BlockSpec((RADIUS, cols, width), lambda i: (0, 0, 0))
     edge_spec = pl.BlockSpec((RADIUS, cols, feature), lambda i: (i * last_edge, 0, 0))
+
+    def piece_spec(piece):
+        return pl.BlockSpec((near, piece.shape[1], width), lambda i: (i * (rows // near - 1), 0, 0))
+
     return pl.pallas_call(
         kernel,
         grid=(2,),
-        in_specs=[
-            halo_spec,
-            pl.BlockSpec((near, cols, width), lambda i: (i * (rows // near - 1), 0, 0)),
+        in_specs=[halo_spec] + [piece_spec(p) for p in pieces] + [
             halo_spec,
             edge_spec,
             pl.BlockSpec(memory_space=pl.ANY),
@@ -195,8 +215,8 @@
             pltpu.VMEM((near + RADIUS, cols, width), jnp.float32),
             pltpu.VMEM((RADIUS, cols, 1), jnp.float32),
         ],
-        input_output_aliases={4: 0},
-    )(above, middle, below, codebook, partial)
+        input_output_aliases={6: 0},
+    )(above, *pieces, below, codebook, partial)
 
 
 def exchange(lead, last, axis):
@@ -247,8 +267,12 @@
     inner = list(range(1, col_total - 1))
     (numerator,) = accumulate(unit_ids, got, rows_tile, cols_tile, feature, inner, bands)
 
-    g_rows = jnp.asarray(band_matrix(rows_tile))
     g_cols = jnp.asarray(band_matrix(cols_tile))
+    inner_piece = jnp.einsum(
+        "ck,rke->rce", g_cols[RADIUS : cols_tile - RADIUS, RADIUS : RADIUS + cols_tile], numerator,
+        precision=HI,
+    )
+    from_left, from_right, inner_piece = lax.optimization_barrier((from_left, from_right, inner_piece))
     last = rows_tile - RADIUS
 
     def col_pass(lo, hi):
@@ -258,9 +282,22 @@
     col_top, col_bottom = col_pass(0, RADIUS), col_pass(last, rows_tile)
 
     above, below = exchange(col_top, col_bottom, "mx")
-    col_num = col_pass(0, rows_tile)
-    partial = finish_inner(col_num, codebook)
-    return finish_edges(above, col_num, below, codebook, partial)
+    right_start = cols_tile - 2 * RADIUS
+    left_piece = jnp.einsum(
+        "ck,rke->rce",
+        g_cols[:RADIUS, : 3 * RADIUS],
+        jnp.concatenate([from_left, numerator[:, : 2 * RADIUS]], axis=1),
+        precision=HI,
+    )
+    right_piece = jnp.einsum(
+        "ck,rke->rce",
+        g_cols[:RADIUS, : 3 * RADIUS],
+        jnp.concatenate([numerator[:, right_start:], from_right], axis=1),
+        precision=HI,
+    )
+    pieces = (left_piece, inner_piece, right_piece)
+    partial = finish_inner(pieces, codebook)
+    return finish_edges(above, pieces, below, codebook, partial)
 
 
 def solution(mesh):

time: 191 us -> 193 us (1.010); the launches traced: 188 us -> 192 us
  matrix products: 17 us -> 22.4 us
    dot_general x0 -> x3, matrix products: none -> 18.2 us  [the longest x1 11.2 us: on_device(): jnp.einsum('ck,rke->rce', g_cols[RADIUS:cols_tile - RADIUS, RADIUS:RADIUS...]
    dot_general x3 -> x2, matrix products: 17 us -> 4.23 us  [col_pass(): jnp.einsum('ck,rke->rce', g_cols, jnp.concatenate(pieces, axis=1), precis...]
  transfers between devices with their start and end apart: 5 -> 5, of which waited for: 5 -> 4; matrix products, arithmetic and copies ran while one was open for 10% -> 12% of each run, Pallas kernels for 19% -> 18%
where the time goes in v14:
time: 193 us; the launch traced here: 192 us
  waiting for transfers between devices  67.8 us (35%)
  Pallas kernels  54.4 us (28%)
  starting transfers between devices  25.5 us (13%)
  matrix products  22.4 us (12%)
  other arithmetic  16.5 us (9%)
  local copies, waits for them, and re-layouts  5.29 us (3%)
    all_to_all x1, waiting for transfers between devices, on_device(): lax.all_to_all(outgoing.reshape(tile_total, capacity, width), ('mx', 'my'...  43.4 us
    pallas_call x2, Pallas kernels, accumulate(): pl.pallas_call(kernel, grid_spec=pltpu.PrefetchScalarGridSpec(num_scalar_...  28.2 us
    ppermute x4, waiting for transfers between devices, exchange(): return (lax.ppermute(last, axis, up), lax.ppermute(lead, axis, down))  24.5 us
    pallas_call x1, Pallas kernels, finish_inner(): pl.pallas_call(kernel, grid=(blocks + 1,), in_specs=[piece_spec(p) for p...  16.7 us
    ppermute x4, starting transfers between devices, exchange(): return (lax.ppermute(last, axis, up), lax.ppermute(lead, axis, down))  14.4 us
    dot_general x1, matrix products, on_device(): jnp.einsum('ck,rke->rce', g_cols[RADIUS:cols_tile - RADIUS, RADIUS:RADIUS...  11.2 us
    all_to_all x1, starting transfers between devices, on_device(): lax.all_to_all(outgoing.reshape(tile_total, capacity, width), ('mx', 'my'...  11.1 us
    pallas_call x1, Pallas kernels, finish_edges(): pl.pallas_call(kernel, grid=(2,), in_specs=[halo_spec] + [piece_spec(p) f...  9.5 us
  transfers between devices with their start and end apart: 5, of which 4 were waited for; matrix products, arithmetic and copies ran while one was open for 12% of the time, Pallas kernels for 18%

profile of v14, /device:TPU:15, one launch (start us, length us, event | category | flops | bytes accessed | tf_op | source)
XLA Modules:
  0.0 192.2 jit_solution(785523480150155602)
XLA Ops:
  0.0 0.0 copy-start.2
  0.0 0.0 copy-start
  0.0 0.6 compare_reduce_fusion.1
  0.6 0.7 compare_reduce_fusion.2
  1.3 0.7 compare_reduce_fusion
  2.0 2.0 %fusion.46 = (bf16[1024]{0:T(1024)(128)(2,1)S(1)}, bf16[1024]{0:T(1024)(128)(2,1)S(1)}) fusion(s32[1024]{0:T(1024)} %param.15, pred[]{:T(512)} %compare_reduce_fusion.1, pred[]{:T(512)} %compare_reduce_fusion.2), kind=kLoop, calls=%fused_computation.54 | loop fusion | flops 23552 | bytes 8194 | tf_op jit(solution)/shard_map/select.14
  4.0 0.1 scatter.19
  4.1 0.6 broadcast_select_fusion
  4.8 0.1 scatter.24
  4.8 0.2 copy.13
  5.0 0.8 copy.11
  5.8 0.2 fusion.39
  6.1 0.1 copy.12
  6.2 0.0 copy-done.2
  6.2 0.4 fusion.38
  6.6 0.0 copy-done
  6.6 7.6 %scatter_custom_fusion = bf16[2048,896]{1,0:T(8,128)(2,1)} fusion(s32[1024]{0:T(1024)S(1)} %bitcast.44, bf16[1024,128]{1,0:T(8,128)(2,1)S(1)} %copy.13, bf16[]{:T(256)} %constant.147, bf16[1024,768]{1,0:T(8,128)(2,1)S(1)} %copy-done, bf16[]{:T(256)} %constant.118.clone.1), kind=kCustom, calls=%fused_computation.22 | custom fusion | flops 3670016 | bytes 5505028 | tf_op jit(solution)/shard_map/scatter | solution.py:251
  14.3 11.1 %all-to-all-start = ((bf16[128,16,896]{2,1,0:T(8,128)(2,1)}), bf16[128,16,896]{2,1,0:T(8,128)(2,1)}, u32[]{:S(2)}, u32[]{:S(2)}) async-start(bf16[128,16,896]{2,1,0:T(8,128)(2,1)} %bitcast.38), calls=%async_computation | async-start | bytes 7340032 | tf_op jit(solution)/shard_map/all_to_all | solution.py:252
  25.4 0.5 iota_multiply_fusion.1.picks_ref
  25.9 43.4 %all-to-all-done = bf16[128,16,896]{2,1,0:T(8,128)(2,1)} async-done(((bf16[128,16,896]{2,1,0:T(8,128)(2,1)}), bf16[128,16,896]{2,1,0:T(8,128)(2,1)}, u32[]{:S(2)}, u32[]{:S(2)}) %all-to-all-start) | async-done | bytes 3670048 | tf_op jit(solution)/shard_map/all_to_all | solution.py:252
  69.3 3.1 %select_reduce_fusion = s32[2048]{0:T(1024)} fusion(bf16[2048,896]{1,0:T(8,128)(2,1)} %bitcast.8.docs_ref), kind=kLoop, calls=%fused_computation.31 | loop fusion | flops 12288 | bytes 20480 | tf_op jit(solution)/shard_map/jit(_where)/select_n | solution.py:261
  72.3 10.1 %shard_map.73 = (f32[64,64,896]{2,1,0:T(8,128)}, f32[64,8,896]{2,1,0:T(8,128)}, f32[64,8,896]{2,1,0:T(8,128)}) custom-call(s32[2]{0:T(128)} %iota_multiply_fusion.1.picks_ref, s32[1,2048]{1,0:T(1,128)} %bitcast.39, bf16[2048,896]{1,0:T(8,128)(2,1)} %bitcast.8.docs_ref), custom_call_target="tpu_custom_call" | custom-call | tf_op jit(solution)/shard_map/pallas_call | solution.py:59
  82.4 5.0 %collective-permute-start = (f32[64,8,896]{2,1,0:T(8,128)}, f32[64,8,896]{2,1,0:T(8,128)S(1)}, u32[]{:S(2)}, u32[]{:S(2)}) collective-permute-start(f32[64,8,896]{2,1,0:T(8,128)} %get-tuple-element.47), channel_id=1, source_target_pairs={{0,1},{1,2},{2,3},{3,4},{4,5},{5,6},{6,7},{8,9},{9,10},{10,11},{11... | collective-permute-start | bytes 5505032 | tf_op jit(solution)/shard_map/ppermute | solution.py:226
  87.5 2.1 %collective-permute-start.1 = (f32[64,8,896]{2,1,0:T(8,128)}, f32[64,8,896]{2,1,0:T(8,128)}, u32[]{:S(2)}, u32[]{:S(2)}) collective-permute-start(f32[64,8,896]{2,1,0:T(8,128)} %get-tuple-element.48), channel_id=1, source_target_pairs={{1,0},{2,1},{3,2},{4,3},{5,4},{6,5},{7,6},{9,8},{10,9},{11,10},{12... | collective-permute-start | bytes 5505032 | tf_op jit(solution)/shard_map/ppermute | solution.py:226
  89.6 18.1 %shard_map.74 = f32[64,64,896]{2,1,0:T(8,128)} custom-call(s32[6]{0:T(128)} %constant.133.clone.picks_ref, s32[1,2048]{1,0:T(1,128)} %bitcast.40, bf16[2048,896]{1,0:T(8,128)(2,1)} %bitcast.8.docs_ref, f32[64,64,896]{2,1,0:T(8,128)} %get-tuple-element.49.refs_0_), custom_call_target="tpu_custom_call", output_to_operand_aliasing={{}: (3, {})} | custom-call | tf_op jit(solution)/shard_map/pallas_call | solution.py:59
  107.7 0.0 copy-start.3
  107.7 2.4 %fusion.52 = (f32[8,64,896]{2,1,0:T(8,128)S(1)}, f32[8,64,896]{2,1,0:T(8,128)S(1)}) fusion(f32[64,64,896]{2,1,0:T(8,128)} %shard_map.74), kind=kLoop, calls=%fused_computation.65 | loop fusion | bytes 7340032 | tf_op jit(solution)/shard_map/slice | solution.py:279
  110.1 0.0 copy-done.3
  110.1 0.0 copy-start.1
  110.1 0.0 slice-start
  110.1 0.0 slice-start.1
  110.2 0.0 slice-start.2
  110.2 11.2 %convolution_bitcast_fusion.inner_ref = f32[64,48,896]{2,1,0:T(8,128)} fusion(f32[64,64,896]{2,1,0:T(8,128)} %shard_map.74, f32[48,64,1]{1,0,2:T(8,128)S(1)} %copy-done.3), kind=kOutput, calls=%fused_computation.9 | convolution fusion | flops 1056964608 | bytes 25702400 | tf_op jit(solution)/shard_map/ck,rke->rce/dot_general | solution.py:271
  121.3 0.0 slice-start.3
  121.3 4.8 %collective-permute-done = f32[64,8,896]{2,1,0:T(8,128)S(1)} collective-permute-done((f32[64,8,896]{2,1,0:T(8,128)}, f32[64,8,896]{2,1,0:T(8,128)S(1)}, u32[]{:S(2)}, u32[]{:S(2)}) %collective-permute-start) | collective-permute-done | bytes 1835040 | tf_op jit(solution)/shard_map/ppermute | solution.py:226
  126.1 7.4 %collective-permute-done.1 = f32[64,8,896]{2,1,0:T(8,128)} collective-permute-done((f32[64,8,896]{2,1,0:T(8,128)}, f32[64,8,896]{2,1,0:T(8,128)}, u32[]{:S(2)}, u32[]{:S(2)}) %collective-permute-start.1) | collective-permute-done | bytes 1835040 | tf_op jit(solution)/shard_map/ppermute | solution.py:226
  133.6 1.1 fusion.54
  134.7 0.0 copy-done.1
  134.7 2.1 %fusion.25 = f32[8,64,896]{2,1,0:T(8,128)} fusion(f32[64,80,1]{1,0,2:T(8,128)S(1)} %copy-done.1, f32[8,8,896]{2,1,0:T(8,128)S(1)} %get-tuple-element.64, f32[8,64,896]{2,1,0:T(8,128)S(1)} %get-tuple-element.53, f32[8,8,896]{2,1,0:T(8,128)S(1)} %get-tuple-element.57), kind=kOutput, calls=%fused_computation.27 | convolution fusion | flops 221347840 | bytes 4149248 | tf_op jit(solution)/shard_map/ck,rke->rce/dot_general | solution.py:280
  136.8 4.1 %collective-permute-start.3 = (f32[8,64,896]{2,1,0:T(8,128)}, f32[8,64,896]{2,1,0:T(8,128)}, u32[]{:S(2)}, u32[]{:S(2)}) collective-permute-start(f32[8,64,896]{2,1,0:T(8,128)} %fusion.25), channel_id=1, source_target_pairs={{8,0},{16,8},{24,16},{32,24},{40,32},{48,40},{56,48},{64,56},{72,6... | collective-permute-start | bytes 5505032 | tf_op jit(solution)/shard_map/ppermute | solution.py:226
  140.9 2.1 %fusion.28 = f32[8,64,896]{2,1,0:T(8,128)} fusion(f32[64,80,1]{1,0,2:T(8,128)S(1)} %copy-done.1, f32[8,8,896]{2,1,0:T(8,128)S(1)} %get-tuple-element.63, f32[8,64,896]{2,1,0:T(8,128)S(1)} %get-tuple-element.54, f32[8,8,896]{2,1,0:T(8,128)S(1)} %get-tuple-element.58), kind=kOutput, calls=%fused_computation.28 | convolution fusion | flops 221347840 | bytes 4149248 | tf_op jit(solution)/shard_map/ck,rke->rce/dot_general | solution.py:280
  143.0 0.0 copy-start.4
  143.0 3.2 %collective-permute-start.2 = (f32[8,64,896]{2,1,0:T(8,128)}, f32[8,64,896]{2,1,0:T(8,128)}, u32[]{:S(2)}, u32[]{:S(2)}) collective-permute-start(f32[8,64,896]{2,1,0:T(8,128)} %fusion.28), channel_id=1, source_target_pairs={{0,8},{8,16},{16,24},{24,32},{32,40},{40,48},{48,56},{56,64},{64,7... | collective-permute-start | bytes 5505032 | tf_op jit(solution)/shard_map/ppermute | solution.py:226
  146.2 0.0 slice-done
  146.2 0.0 slice-done.1
  146.3 0.0 slice-done.2
  146.3 0.0 slice-done.3
  146.3 0.5 fusion.53
  146.8 0.0 copy-done.4
  146.8 4.2 %fusion.31.right_ref = f32[64,8,896]{2,1,0:T(8,128)} fusion(f32[8,24,1]{1,0,2:T(8,128)S(1)} %copy-done.4, f32[64,8,896]{2,1,0:T(8,128)} %collective-permute-done.1, f32[64,16,896]{2,1,0:T(8,128)S(1)} %get-tuple-element.55), kind=kOutput, calls=%fused_computation.29 | convolution fusion | flops 67436544 | bytes 7340800 | tf_op jit(solution)/shard_map/ck,rke->rce/dot_general | solution.py:292
  151.0 2.8 %fusion.34.left_ref = f32[64,8,896]{2,1,0:T(8,128)} fusion(f32[8,24,1]{1,0,2:T(8,128)S(1)} %copy-done.4, f32[64,16,896]{2,1,0:T(8,128)S(1)} %get-tuple-element.56, f32[64,8,896]{2,1,0:T(8,128)S(1)} %collective-permute-done), kind=kOutput, calls=%fused_computation.30 | convolution fusion | flops 67436544 | bytes 7340800 | tf_op jit(solution)/shard_map/ck,rke->rce/dot_general | solution.py:286
  153.8 16.7 %shard_map.75.prev_ref = bf16[64,64,768]{2,1,0:T(8,128)(2,1)} custom-call(f32[64,8,896]{2,1,0:T(8,128)} %fusion.34.left_ref, f32[64,48,896]{2,1,0:T(8,128)} %convolution_bitcast_fusion.inner_ref, f32[64,8,896]{2,1,0:T(8,128)} %fusion.31.right_ref, bf16[64,64,768]{2,1,0:T(8,128)(2,1)} %cb_ref.3), custom_call_target="tpu_custom_call" | custom-call | tf_op jit(solution)/shard_map/pallas_call | solution.py:147
  170.5 12.2 %collective-permute-done.3.below_ref = f32[8,64,896]{2,1,0:T(8,128)} collective-permute-done((f32[8,64,896]{2,1,0:T(8,128)}, f32[8,64,896]{2,1,0:T(8,128)}, u32[]{:S(2)}, u32[]{:S(2)}) %collective-permute-start.3) | collective-permute-done | bytes 1835040 | tf_op jit(solution)/shard_map/ppermute | solution.py:226
  182.7 0.0 collective-permute-done.2.above_ref
  182.7 9.5 %shard_map.76 = bf16[64,64,768]{2,1,0:T(8,128)(2,1)} custom-call(f32[8,64,896]{2,1,0:T(8,128)} %collective-permute-done.2.above_ref, f32[64,8,896]{2,1,0:T(8,128)} %fusion.34.left_ref, f32[64,48,896]{2,1,0:T(8,128)} %convolution_bitcast_fusion.inner_ref, f32[64,8,896]{2,1,0:T(8,128)} %fusion.31.right_ref, ...), custom_call_target="tpu_custom_call", output_to_operand_aliasing={{}: (6, {})} | custom-call | tf_op jit(solution)/shard_map/pallas_call | solution.py:204
  (9 shorter events, 0.1 us)
Async XLA Ops:
  0.0 6.2 %copy-start.2 = (s32[1024,1]{0,1:T(1,128)S(1)}, s32[1024,1]{0,1:T(1,128)}, u32[]{:S(2)}) copy-start(s32[1024,1]{0,1:T(1,128)} %param.14) | copy-start | bytes 12292
  0.0 6.6 %copy-start = (bf16[1024,768]{1,0:T(8,128)(2,1)S(1)}, bf16[1024,768]{1,0:T(8,128)(2,1)}, u32[]{:S(2)}) copy-start(bf16[1024,768]{1,0:T(8,128)(2,1)} %param.13) | copy-start | bytes 4718596
  14.3 55.0 %all-to-all-start = ((bf16[128,16,896]{2,1,0:T(8,128)(2,1)}), bf16[128,16,896]{2,1,0:T(8,128)(2,1)}, u32[]{:S(2)}, u32[]{:S(2)}) async-start(bf16[128,16,896]{2,1,0:T(8,128)(2,1)} %bitcast.38), calls=%async_computation | async-start | bytes 7340032 | tf_op jit(solution)/shard_map/all_to_all | solution.py:252
  82.4 43.7 %collective-permute-start = (f32[64,8,896]{2,1,0:T(8,128)}, f32[64,8,896]{2,1,0:T(8,128)S(1)}, u32[]{:S(2)}, u32[]{:S(2)}) collective-permute-start(f32[64,8,896]{2,1,0:T(8,128)} %get-tuple-element.47), channel_id=1, source_target_pairs={{0,1},{1,2},{2,3},{3,4},{4,5},{5,6},{6,7},{8,9},{9,10},{10,11},{11... | collective-permute-start | bytes 5505032 | tf_op jit(solution)/shard_map/ppermute | solution.py:226
  87.5 46.1 %collective-permute-start.1 = (f32[64,8,896]{2,1,0:T(8,128)}, f32[64,8,896]{2,1,0:T(8,128)}, u32[]{:S(2)}, u32[]{:S(2)}) collective-permute-start(f32[64,8,896]{2,1,0:T(8,128)} %get-tuple-element.48), channel_id=1, source_target_pairs={{1,0},{2,1},{3,2},{4,3},{5,4},{6,5},{7,6},{9,8},{10,9},{11,10},{12... | collective-permute-start | bytes 5505032 | tf_op jit(solution)/shard_map/ppermute | solution.py:226
  107.7 2.4 %copy-start.3 = (f32[48,64,1]{1,0,2:T(8,128)S(1)}, f32[48,64,1]{1,0,2:T(8,128)}, u32[]{:S(2)}) copy-start(f32[48,64,1]{1,0,2:T(8,128)} %constant.139) | copy-start | bytes 36868
  110.1 24.6 %copy-start.1 = (f32[64,80,1]{1,0,2:T(8,128)S(1)}, f32[64,80,1]{1,0,2:T(8,128)}, u32[]{:S(2)}) copy-start(f32[64,80,1]{1,0,2:T(8,128)} %constant.140) | copy-start | bytes 61444
  110.1 36.1 %slice-start = ((s8[14680064]{0:T(1024)(128)(4,1)}), s8[4194304]{0:T(1024)(128)(4,1)S(1)}, s32[]{:S(2)}) async-start(s8[14680064]{0:T(1024)(128)(4,1)} %bitcast.36), calls=%async_computation.1 | async-start | bytes 8388608
  110.1 36.1 %slice-start.1 = ((s8[14680064]{0:T(1024)(128)(4,1)}), s8[4194304]{0:T(1024)(128)(4,1)S(1)}, s32[]{:S(2)}) async-start(s8[14680064]{0:T(1024)(128)(4,1)} %bitcast.36), calls=%async_computation.2 | async-start | bytes 8388608
  110.2 36.1 %slice-start.2 = ((s8[14680064]{0:T(1024)(128)(4,1)}), s8[2097152]{0:T(1024)(128)(4,1)S(1)}, s32[]{:S(2)}) async-start(s8[14680064]{0:T(1024)(128)(4,1)} %bitcast.36), calls=%async_computation.3 | async-start | bytes 4194304
  121.3 24.9 %slice-start.3 = ((s8[14680064]{0:T(1024)(128)(4,1)}), s8[4194304]{0:T(1024)(128)(4,1)S(1)}, s32[]{:S(2)}) async-start(s8[14680064]{0:T(1024)(128)(4,1)} %bitcast.36), calls=%async_computation.4 | async-start | bytes 8388608
  136.8 45.9 %collective-permute-start.3 = (f32[8,64,896]{2,1,0:T(8,128)}, f32[8,64,896]{2,1,0:T(8,128)}, u32[]{:S(2)}, u32[]{:S(2)}) collective-permute-start(f32[8,64,896]{2,1,0:T(8,128)} %fusion.25), channel_id=1, source_target_pairs={{8,0},{16,8},{24,16},{32,24},{40,32},{48,40},{56,48},{64,56},{72,6... | collective-permute-start | bytes 5505032 | tf_op jit(solution)/shard_map/ppermute | solution.py:226
  143.0 3.8 %copy-start.4 = (f32[8,24,1]{1,0,2:T(8,128)S(1)}, f32[8,24,1]{1,0,2:T(8,128)}, u32[]{:S(2)}) copy-start(f32[8,24,1]{1,0,2:T(8,128)} %constant.141) | copy-start | bytes 2308
  143.0 39.7 %collective-permute-start.2 = (f32[8,64,896]{2,1,0:T(8,128)}, f32[8,64,896]{2,1,0:T(8,128)}, u32[]{:S(2)}, u32[]{:S(2)}) collective-permute-start(f32[8,64,896]{2,1,0:T(8,128)} %fusion.28), channel_id=1, source_target_pairs={{0,8},{8,16},{16,24},{24,32},{32,40},{40,48},{48,56},{56,64},{64,7... | collective-permute-start | bytes 5505032 | tf_op jit(solution)/shard_map/ppermute | solution.py:226

commit v15 on v13

--- a/solution.py
+++ b/solution.py
@@ -70,7 +70,7 @@
 
 
 TAPS = [math.exp(-2.0 * k * k / RADIUS**2) for k in range(RADIUS + 1)]
-GROUP = 4
+GROUP = 8
 
 
 def row_group(read, first, cols, lanes, emit):

time: 191 us -> 190 us (level)
  transfers between devices with their start and end apart: 5 -> 5, of which waited for: 5 -> 5; matrix products, arithmetic and copies ran while one was open for 10% -> 10% of each run, Pallas kernels for 19% -> 18%
where the time goes in v15:
time: 190 us; the launch traced here: 188 us
  waiting for transfers between devices  69.9 us (37%)
  Pallas kernels  53 us (28%)
  starting transfers between devices  27.1 us (14%)
  matrix products  17 us (9%)
  other arithmetic  15.7 us (8%)
  local copies, waits for them, and re-layouts  4.77 us (3%)
    all_to_all x1, waiting for transfers between devices, on_device(): lax.all_to_all(outgoing.reshape(tile_total, capacity, width), ('mx', 'my'...  43.4 us
    pallas_call x2, Pallas kernels, accumulate(): pl.pallas_call(kernel, grid_spec=pltpu.PrefetchScalarGridSpec(num_scalar_...  28.2 us
    ppermute x4, waiting for transfers between devices, exchange(): return (lax.ppermute(last, axis, up), lax.ppermute(lead, axis, down))  26.5 us
    dot_general x3, matrix products, col_pass(): jnp.einsum('ck,rke->rce', g_cols, jnp.concatenate(pieces, axis=1), precis...  17 us
    pallas_call x1, Pallas kernels, finish_inner(): pl.pallas_call(kernel, grid=(blocks + 1,), in_specs=[pl.BlockSpec((rows,...  16.1 us
    ppermute x4, starting transfers between devices, exchange(): return (lax.ppermute(last, axis, up), lax.ppermute(lead, axis, down))  16 us
    all_to_all x1, starting transfers between devices, on_device(): lax.all_to_all(outgoing.reshape(tile_total, capacity, width), ('mx', 'my'...  11.1 us
    pallas_call x1, Pallas kernels, finish_edges(): pl.pallas_call(kernel, grid=(2,), in_specs=[halo_spec, pl.BlockSpec((near...  8.6 us
  transfers between devices with their start and end apart: 5, of which 5 were waited for; matrix products, arithmetic and copies ran while one was open for 10% of the time, Pallas kernels for 18%

profile of v15, /device:TPU:15, one launch (start us, length us, event | category | flops | bytes accessed | tf_op | source)
XLA Modules:
  0.0 187.6 jit_solution(5015222513643934513)
XLA Ops:
  0.0 0.0 copy-start.2
  0.0 0.0 copy-start.3
  0.0 0.0 copy-start
  0.0 0.6 compare_reduce_fusion.1
  0.6 0.7 compare_reduce_fusion.2
  1.4 0.6 compare_reduce_fusion
  2.0 0.8 copy.11
  2.8 0.2 fusion.34
  3.1 0.1 copy.12
  3.2 0.0 copy-done.2
  3.2 0.4 fusion.33
  3.6 0.0 copy-done.3
  3.6 1.3 fusion.41
  5.0 0.1 scatter.19
  5.1 0.6 broadcast_select_fusion
  5.7 0.1 scatter.24
  5.7 0.2 copy.13
  5.9 0.0 copy-done
  5.9 7.6 %scatter_custom_fusion = bf16[2048,896]{1,0:T(8,128)(2,1)} fusion(s32[1024]{0:T(1024)S(1)} %bitcast.33, bf16[1024,128]{1,0:T(8,128)(2,1)S(1)} %copy.13, bf16[]{:T(256)} %constant.142, bf16[1024,768]{1,0:T(8,128)(2,1)S(1)} %copy-done, bf16[]{:T(256)} %constant.118.clone.1), kind=kCustom, calls=%fused_computation.20 | custom fusion | flops 3670016 | bytes 5505028 | tf_op jit(solution)/shard_map/scatter | solution.py:231
  13.6 11.1 %all-to-all-start = ((bf16[128,16,896]{2,1,0:T(8,128)(2,1)}), bf16[128,16,896]{2,1,0:T(8,128)(2,1)}, u32[]{:S(2)}, u32[]{:S(2)}) async-start(bf16[128,16,896]{2,1,0:T(8,128)(2,1)} %bitcast.27), calls=%async_computation | async-start | bytes 7340032 | tf_op jit(solution)/shard_map/all_to_all | solution.py:232
  24.7 0.5 iota_multiply_fusion.1.picks_ref
  25.2 43.4 %all-to-all-done = bf16[128,16,896]{2,1,0:T(8,128)(2,1)} async-done(((bf16[128,16,896]{2,1,0:T(8,128)(2,1)}), bf16[128,16,896]{2,1,0:T(8,128)(2,1)}, u32[]{:S(2)}, u32[]{:S(2)}) %all-to-all-start) | async-done | bytes 3670048 | tf_op jit(solution)/shard_map/all_to_all | solution.py:232
  68.5 3.0 %select_reduce_fusion = s32[2048]{0:T(1024)} fusion(bf16[2048,896]{1,0:T(8,128)(2,1)} %bitcast.8.docs_ref), kind=kLoop, calls=%fused_computation.27 | loop fusion | flops 12288 | bytes 20480 | tf_op jit(solution)/shard_map/jit(_where)/select_n | solution.py:241
  71.5 10.2 %shard_map.73 = (f32[64,64,896]{2,1,0:T(8,128)}, f32[64,8,896]{2,1,0:T(8,128)}, f32[64,8,896]{2,1,0:T(8,128)}) custom-call(s32[2]{0:T(128)} %iota_multiply_fusion.1.picks_ref, s32[1,2048]{1,0:T(1,128)} %bitcast.28, bf16[2048,896]{1,0:T(8,128)(2,1)} %bitcast.8.docs_ref), custom_call_target="tpu_custom_call" | custom-call | tf_op jit(solution)/shard_map/pallas_call | solution.py:59
  81.7 2.7 %collective-permute-start.1 = (f32[64,8,896]{2,1,0:T(8,128)}, f32[64,8,896]{2,1,0:T(8,128)S(1)}, u32[]{:S(2)}, u32[]{:S(2)}) collective-permute-start(f32[64,8,896]{2,1,0:T(8,128)} %get-tuple-element.46), channel_id=1, source_target_pairs={{1,0},{2,1},{3,2},{4,3},{5,4},{6,5},{7,6},{9,8},{10,9},{11,10},{12... | collective-permute-start | bytes 5505032 | tf_op jit(solution)/shard_map/ppermute | solution.py:206
  84.4 6.1 %collective-permute-start = (f32[64,8,896]{2,1,0:T(8,128)}, f32[64,8,896]{2,1,0:T(8,128)}, u32[]{:S(2)}, u32[]{:S(2)}) collective-permute-start(f32[64,8,896]{2,1,0:T(8,128)} %get-tuple-element.44), channel_id=1, source_target_pairs={{0,1},{1,2},{2,3},{3,4},{4,5},{5,6},{6,7},{8,9},{9,10},{10,11},{11... | collective-permute-start | bytes 5505032 | tf_op jit(solution)/shard_map/ppermute | solution.py:206
  90.6 18.1 %shard_map.74 = f32[64,64,896]{2,1,0:T(8,128)} custom-call(s32[6]{0:T(128)} %constant.133.clone.picks_ref, s32[1,2048]{1,0:T(1,128)} %bitcast.29, bf16[2048,896]{1,0:T(8,128)(2,1)} %bitcast.8.docs_ref, f32[64,64,896]{2,1,0:T(8,128)} %get-tuple-element.45.refs_0_), custom_call_target="tpu_custom_call", output_to_operand_aliasing={{}: (3, {})} | custom-call | tf_op jit(solution)/shard_map/pallas_call | solution.py:59
  108.6 0.0 copy-start.1
  108.6 2.4 %fusion.46 = (f32[8,64,896]{2,1,0:T(8,128)S(1)}, f32[8,64,896]{2,1,0:T(8,128)S(1)}) fusion(f32[64,64,896]{2,1,0:T(8,128)} %shard_map.74), kind=kLoop, calls=%fused_computation.60 | loop fusion | bytes 7340032 | tf_op jit(solution)/shard_map/slice | solution.py:255
  111.1 17.4 %collective-permute-done.1 = f32[64,8,896]{2,1,0:T(8,128)S(1)} collective-permute-done((f32[64,8,896]{2,1,0:T(8,128)}, f32[64,8,896]{2,1,0:T(8,128)S(1)}, u32[]{:S(2)}, u32[]{:S(2)}) %collective-permute-start.1) | collective-permute-done | bytes 1835040 | tf_op jit(solution)/shard_map/ppermute | solution.py:206
  128.5 0.9 collective-permute-done
  129.5 1.1 fusion.47
  130.5 0.0 copy-done.1
  130.6 2.1 %fusion.29 = f32[8,64,896]{2,1,0:T(8,128)} fusion(f32[64,80,1]{1,0,2:T(8,128)S(1)} %copy-done.1, f32[8,8,896]{2,1,0:T(8,128)S(1)} %get-tuple-element.52, f32[8,64,896]{2,1,0:T(8,128)S(1)} %get-tuple-element.48, f32[8,8,896]{2,1,0:T(8,128)S(1)} %get-tuple-element.50), kind=kOutput, calls=%fused_computation.26 | convolution fusion | flops 221347840 | bytes 4149248 | tf_op jit(solution)/shard_map/ck,rke->rce/dot_general | solution.py:256
  132.7 5.2 %collective-permute-start.2 = (f32[8,64,896]{2,1,0:T(8,128)}, f32[8,64,896]{2,1,0:T(8,128)}, u32[]{:S(2)}, u32[]{:S(2)}) collective-permute-start(f32[8,64,896]{2,1,0:T(8,128)} %fusion.29), channel_id=1, source_target_pairs={{0,8},{8,16},{16,24},{24,32},{32,40},{40,48},{48,56},{56,64},{64,7... | collective-permute-start | bytes 5505032 | tf_op jit(solution)/shard_map/ppermute | solution.py:206
  137.9 2.2 %fusion.26 = f32[8,64,896]{2,1,0:T(8,128)} fusion(f32[64,80,1]{1,0,2:T(8,128)S(1)} %copy-done.1, f32[8,8,896]{2,1,0:T(8,128)S(1)} %get-tuple-element.51, f32[8,64,896]{2,1,0:T(8,128)S(1)} %get-tuple-element.47, f32[8,8,896]{2,1,0:T(8,128)S(1)} %get-tuple-element.49), kind=kOutput, calls=%fused_computation.25 | convolution fusion | flops 221347840 | bytes 4149248 | tf_op jit(solution)/shard_map/ck,rke->rce/dot_general | solution.py:256
  140.1 1.9 %collective-permute-start.3 = (f32[8,64,896]{2,1,0:T(8,128)}, f32[8,64,896]{2,1,0:T(8,128)}, u32[]{:S(2)}, u32[]{:S(2)}) collective-permute-start(f32[8,64,896]{2,1,0:T(8,128)} %fusion.26), channel_id=1, source_target_pairs={{8,0},{16,8},{24,16},{32,24},{40,32},{48,40},{56,48},{64,56},{72,6... | collective-permute-start | bytes 5505032 | tf_op jit(solution)/shard_map/ppermute | solution.py:206
  142.0 12.7 %fusion.6.mid_ref = f32[64,64,896]{2,1,0:T(8,128)} fusion(f32[64,80,1]{1,0,2:T(8,128)S(1)} %copy-done.1, f32[64,8,896]{2,1,0:T(8,128)S(1)} %collective-permute-done.1, f32[64,64,896]{2,1,0:T(8,128)} %shard_map.74, f32[64,8,896]{2,1,0:T(8,128)} %collective-permute-done), kind=kOutput, calls=%fused_computation.7 | convolution fusion | flops 1770782720 | bytes 33050624 | tf_op jit(solution)/shard_map/ck,rke->rce/dot_general | solution.py:256
  154.7 16.1 %shard_map.75.prev_ref = bf16[64,64,768]{2,1,0:T(8,128)(2,1)} custom-call(f32[64,64,896]{2,1,0:T(8,128)} %fusion.6.mid_ref, bf16[64,64,768]{2,1,0:T(8,128)(2,1)} %cb_ref.3), custom_call_target="tpu_custom_call" | custom-call | tf_op jit(solution)/shard_map/pallas_call | solution.py:132
  170.8 7.0 %collective-permute-done.2.above_ref = f32[8,64,896]{2,1,0:T(8,128)} collective-permute-done((f32[8,64,896]{2,1,0:T(8,128)}, f32[8,64,896]{2,1,0:T(8,128)}, u32[]{:S(2)}, u32[]{:S(2)}) %collective-permute-start.2) | collective-permute-done | bytes 1835040 | tf_op jit(solution)/shard_map/ppermute | solution.py:206
  177.9 1.1 collective-permute-done.3.below_ref
  179.0 8.6 %shard_map.76 = bf16[64,64,768]{2,1,0:T(8,128)(2,1)} custom-call(f32[8,64,896]{2,1,0:T(8,128)} %collective-permute-done.2.above_ref, f32[64,64,896]{2,1,0:T(8,128)} %fusion.6.mid_ref, f32[8,64,896]{2,1,0:T(8,128)} %collective-permute-done.3.below_ref, bf16[64,64,768]{2,1,0:T(8,128)(2,1)} %cb_ref.3, ...), custom_call_target="tpu_custom_call", output_to_operand_aliasing={{}: (4, {})} | custom-call | tf_op jit(solution)/shard_map/pallas_call | solution.py:182
  (9 shorter events, 0.1 us)
Async XLA Ops:
  0.0 3.2 %copy-start.2 = (s32[1024,1]{0,1:T(1,128)S(1)}, s32[1024,1]{0,1:T(1,128)}, u32[]{:S(2)}) copy-start(s32[1024,1]{0,1:T(1,128)} %param.14) | copy-start | bytes 12292
  0.0 3.6 %copy-start.3 = (s32[1024]{0:T(1024)S(1)}, s32[1024]{0:T(1024)}, u32[]{:S(2)}) copy-start(s32[1024]{0:T(1024)} %param.15) | copy-start | bytes 12292
  0.0 5.9 %copy-start = (bf16[1024,768]{1,0:T(8,128)(2,1)S(1)}, bf16[1024,768]{1,0:T(8,128)(2,1)}, u32[]{:S(2)}) copy-start(bf16[1024,768]{1,0:T(8,128)(2,1)} %param.13) | copy-start | bytes 4718596
  13.6 55.0 %all-to-all-start = ((bf16[128,16,896]{2,1,0:T(8,128)(2,1)}), bf16[128,16,896]{2,1,0:T(8,128)(2,1)}, u32[]{:S(2)}, u32[]{:S(2)}) async-start(bf16[128,16,896]{2,1,0:T(8,128)(2,1)} %bitcast.27), calls=%async_computation | async-start | bytes 7340032 | tf_op jit(solution)/shard_map/all_to_all | solution.py:232
  81.7 46.8 %collective-permute-start.1 = (f32[64,8,896]{2,1,0:T(8,128)}, f32[64,8,896]{2,1,0:T(8,128)S(1)}, u32[]{:S(2)}, u32[]{:S(2)}) collective-permute-start(f32[64,8,896]{2,1,0:T(8,128)} %get-tuple-element.46), channel_id=1, source_target_pairs={{1,0},{2,1},{3,2},{4,3},{5,4},{6,5},{7,6},{9,8},{10,9},{11,10},{12... | collective-permute-start | bytes 5505032 | tf_op jit(solution)/shard_map/ppermute | solution.py:206
  84.4 45.1 %collective-permute-start = (f32[64,8,896]{2,1,0:T(8,128)}, f32[64,8,896]{2,1,0:T(8,128)}, u32[]{:S(2)}, u32[]{:S(2)}) collective-permute-start(f32[64,8,896]{2,1,0:T(8,128)} %get-tuple-element.44), channel_id=1, source_target_pairs={{0,1},{1,2},{2,3},{3,4},{4,5},{5,6},{6,7},{8,9},{9,10},{10,11},{11... | collective-permute-start | bytes 5505032 | tf_op jit(solution)/shard_map/ppermute | solution.py:206
  108.6 21.9 %copy-start.1 = (f32[64,80,1]{1,0,2:T(8,128)S(1)}, f32[64,80,1]{1,0,2:T(8,128)}, u32[]{:S(2)}) copy-start(f32[64,80,1]{1,0,2:T(8,128)} %constant.137) | copy-start | bytes 61444
  132.7 45.2 %collective-permute-start.2 = (f32[8,64,896]{2,1,0:T(8,128)}, f32[8,64,896]{2,1,0:T(8,128)}, u32[]{:S(2)}, u32[]{:S(2)}) collective-permute-start(f32[8,64,896]{2,1,0:T(8,128)} %fusion.29), channel_id=1, source_target_pairs={{0,8},{8,16},{16,24},{24,32},{32,40},{40,48},{48,56},{56,64},{64,7... | collective-permute-start | bytes 5505032 | tf_op jit(solution)/shard_map/ppermute | solution.py:206
  140.1 38.9 %collective-permute-start.3 = (f32[8,64,896]{2,1,0:T(8,128)}, f32[8,64,896]{2,1,0:T(8,128)}, u32[]{:S(2)}, u32[]{:S(2)}) collective-permute-start(f32[8,64,896]{2,1,0:T(8,128)} %fusion.26), channel_id=1, source_target_pairs={{8,0},{16,8},{24,16},{32,24},{40,32},{48,40},{56,48},{64,56},{72,6... | collective-permute-start | bytes 5505032 | tf_op jit(solution)/shard_map/ppermute | solution.py:206

commit v16 on v13

--- a/solution.py
+++ b/solution.py
@@ -21,52 +21,61 @@
     return mat
 
 
-def accumulate(ids, docs, rows_tile, cols_tile, feature, col_blocks, prior=None):
+def accumulate_bands(ids, docs, rows_tile, cols_tile):
     rows, width = docs.shape
     band = rows_tile * RADIUS
-    picks = jnp.asarray(col_blocks, jnp.int32)
-
-    def kernel(picks_ref, ids_ref, docs_ref, *refs):
-        num_ref = refs[-1] if prior is not None else refs[-3]
-        place = lax.broadcasted_iota(jnp.int32, (band, rows), 0)
-        first_col = picks_ref[pl.program_id(0)] * RADIUS
-        units = (place // RADIUS) * cols_tile + first_col + place % RADIUS
+
+    def kernel(ids_ref, docs_ref, lead_ref, tail_ref):
+        place = lax.broadcasted_iota(jnp.int32, (2 * band, rows), 0)
+        side = place // band
+        within = place % band
+        units = (within // RADIUS) * cols_tile + side * (cols_tile - RADIUS) + within % RADIUS
         one_hot = (units == ids_ref[...]).astype(jnp.bfloat16)
         sums = jnp.dot(one_hot, docs_ref[...], preferred_element_type=jnp.float32)
-        num_ref[...] = sums.reshape(rows_tile, RADIUS, width)
-        if prior is None:
-            for side in range(2):
-
-                @pl.when(pl.program_id(0) == side)
-                def _():
-                    refs[side - 2][...] = sums.reshape(rows_tile, RADIUS, width)
-
-    out_specs = [pl.BlockSpec((rows_tile, RADIUS, width), lambda j, p: (0, p[j], 0))]
-    out_shape = [jax.ShapeDtypeStruct((rows_tile, cols_tile, width), jnp.float32)]
-    if prior is None:
-        out_specs += [pl.BlockSpec((rows_tile, RADIUS, width), lambda j, p: (0, 0, 0))] * 2
-        out_shape += [jax.ShapeDtypeStruct((rows_tile, RADIUS, width), jnp.float32)] * 2
-    in_specs = [
-        pl.BlockSpec((1, rows), lambda j, p: (0, 0)),
-        pl.BlockSpec((rows, width), lambda j, p: (0, 0)),
-    ]
-    operands = [ids.reshape(1, rows), docs]
-    aliases = {}
-    if prior is not None:
-        in_specs += [pl.BlockSpec(memory_space=pl.ANY)]
-        operands += [prior]
-        aliases = {3: 0}
+        lead_ref[...] = sums[:band].reshape(rows_tile, RADIUS, width)
+        tail_ref[...] = sums[band:].reshape(rows_tile, RADIUS, width)
+
+    band_shape = jax.ShapeDtypeStruct((rows_tile, RADIUS, width), jnp.float32)
+    return pl.pallas_call(kernel, out_shape=[band_shape, band_shape])(ids.reshape(1, rows), docs)
+
+
+def accumulate(ids, docs, rows_tile, cols_tile, lead, tail):
+    rows, width = docs.shape
+    band = rows_tile * RADIUS
+    blocks = cols_tile // RADIUS
+
+    def kernel(ids_ref, docs_ref, lead_ref, tail_ref, num_ref):
+        step = pl.program_id(0)
+
+        @pl.when(step == 0)
+        def _():
+            num_ref[...] = lead_ref[...]
+
+        @pl.when(step == blocks - 1)
+        def _():
+            num_ref[...] = tail_ref[...]
+
+        @pl.when((step > 0) & (step < blocks - 1))
+        def _():
+            place = lax.broadcasted_iota(jnp.int32, (band, rows), 0)
+            units = (place // RADIUS) * cols_tile + step * RADIUS + place % RADIUS
+            one_hot = (units == ids_ref[...]).astype(jnp.bfloat16)
+            sums = jnp.dot(one_hot, docs_ref[...], preferred_element_type=jnp.float32)
+            num_ref[...] = sums.reshape(rows_tile, RADIUS, width)
+
+    band_spec = pl.BlockSpec((rows_tile, RADIUS, width), lambda j: (0, 0, 0))
     return pl.pallas_call(
         kernel,
-        grid_spec=pltpu.PrefetchScalarGridSpec(
-            num_scalar_prefetch=1,
-            grid=(len(col_blocks),),
-            in_specs=in_specs,
-            out_specs=out_specs,
-        ),
-        out_shape=out_shape,
-        input_output_aliases=aliases,
-    )(picks, *operands)
+        grid=(blocks,),
+        in_specs=[
+            pl.BlockSpec((1, rows), lambda j: (0, 0)),
+            pl.BlockSpec((rows, width), lambda j: (0, 0)),
+            band_spec,
+            band_spec,
+        ],
+        out_specs=pl.BlockSpec((rows_tile, RADIUS, width), lambda j: (0, j, 0)),
+        out_shape=jax.ShapeDtypeStruct((rows_tile, cols_tile, width), jnp.float32),
+    )(ids.reshape(1, rows), docs, lead, tail)
 
 
 TAPS = [math.exp(-2.0 * k * k / RADIUS**2) for k in range(RADIUS + 1)]
@@ -240,12 +249,10 @@
     mark_col = got[:, feature + 1].astype(jnp.int32)
     unit_ids = jnp.where(got[:, feature + 2] > 0.5, mark_row * cols_tile + mark_col, -1)
     col_total = cols_tile // RADIUS
-    bands = accumulate(unit_ids, got, rows_tile, cols_tile, feature, [0, col_total - 1])
     last = cols_tile - RADIUS
-    bands, lead, tail = bands
+    lead, tail = accumulate_bands(unit_ids, got, rows_tile, cols_tile)
     from_left, from_right = exchange(lead, tail, "my")
-    inner = list(range(1, col_total - 1))
-    (numerator,) = accumulate(unit_ids, got, rows_tile, cols_tile, feature, inner, bands)
+    numerator = accumulate(unit_ids, got, rows_tile, cols_tile, lead, tail)
 
     g_rows = jnp.asarray(band_matrix(rows_tile))
     g_cols = jnp.asarray(band_matrix(cols_tile))

time: 191 us -> 189 us (0.990)
  blocking collectives: 0 us -> 54.9 us
  waiting for transfers between devices: 69.3 us -> 24.6 us
  starting transfers between devices: 27.1 us -> 16.1 us
  other arithmetic: 15.7 us -> 13.6 us
    all_to_all x0 -> x1, blocking collectives: none -> 54.9 us  [on_device(): lax.all_to_all(outgoing.reshape(tile_total, capacity, width), ('mx', 'my'...]
    all_to_all x1 -> x0, waiting for transfers between devices: 43.4 us -> none  [on_device(): lax.all_to_all(outgoing.reshape(tile_total, capacity, width), ('mx', 'my'...]
    all_to_all x1 -> x0, starting transfers between devices: 11.1 us -> none  [on_device(): lax.all_to_all(outgoing.reshape(tile_total, capacity, width), ('mx', 'my'...]
    another operation x9 -> x8, other arithmetic: 4.69 us -> 4.17 us
  transfers between devices with their start and end apart: 5 -> 4, of which waited for: 5 -> 4; matrix products, arithmetic and copies ran while one was open for 10% -> 9% of each run, Pallas kernels for 19% -> 19%
where the time goes in v16:
time: 189 us; the launch traced here: 186 us
  blocking collectives  54.9 us (29%)
  Pallas kernels  53.1 us (28%)
  waiting for transfers between devices  24.6 us (13%)
  matrix products  17 us (9%)
  starting transfers between devices  16.1 us (9%)
  other arithmetic  13.6 us (7%)
  local copies, waits for them, and re-layouts  6.54 us (3%)
    all_to_all x1, blocking collectives, on_device(): lax.all_to_all(outgoing.reshape(tile_total, capacity, width), ('mx', 'my'...  54.9 us
    ppermute x4, waiting for transfers between devices, exchange(): return (lax.ppermute(last, axis, up), lax.ppermute(lead, axis, down))  24.6 us
    pallas_call x1, Pallas kernels, accumulate(): pl.pallas_call(kernel, grid=(blocks,), in_specs=[pl.BlockSpec((1, rows),...  19.5 us
    dot_general x3, matrix products, col_pass(): jnp.einsum('ck,rke->rce', g_cols, jnp.concatenate(pieces, axis=1), precis...  17 us
    pallas_call x1, Pallas kernels, finish_inner(): pl.pallas_call(kernel, grid=(blocks + 1,), in_specs=[pl.BlockSpec((rows,...  16.7 us
    ppermute x4, starting transfers between devices, exchange(): return (lax.ppermute(last, axis, up), lax.ppermute(lead, axis, down))  16.1 us
    pallas_call x1, Pallas kernels, finish_edges(): pl.pallas_call(kernel, grid=(2,), in_specs=[halo_spec, pl.BlockSpec((near...  8.7 us
    pallas_call x1, Pallas kernels, accumulate_bands(): pl.pallas_call(kernel, out_shape=[band_shape, band_shape])  8.21 us
  transfers between devices with their start and end apart: 4, of which 4 were waited for; matrix products, arithmetic and copies ran while one was open for 9% of the time, Pallas kernels for 19%

profile of v16, /device:TPU:15, one launch (start us, length us, event | category | flops | bytes accessed | tf_op | source)
XLA Modules:
  0.0 186.0 jit_solution(8353205644978971017)
XLA Ops:
  0.0 0.0 copy-start.3
  0.0 0.0 copy-start.4
  0.0 0.0 copy-start.1
  0.0 0.6 compare_reduce_fusion.1
  0.6 0.7 compare_reduce_fusion.2
  1.4 0.6 compare_reduce_fusion
  2.0 0.8 copy.8
  2.8 0.2 fusion.34
  3.1 0.1 copy.9
  3.2 0.0 copy-done.3
  3.2 0.4 fusion.33
  3.6 0.0 copy-done.4
  3.6 1.3 fusion.41
  5.0 0.1 scatter.19
  5.1 0.6 broadcast_select_fusion
  5.7 0.1 scatter.24
  5.7 0.2 copy.10
  5.9 0.0 copy-done.1
  5.9 7.6 %scatter_custom_fusion = bf16[2048,896]{1,0:T(8,128)(2,1)} fusion(s32[1024]{0:T(1024)S(1)} %bitcast.36, bf16[1024,128]{1,0:T(8,128)(2,1)S(1)} %copy.10, bf16[]{:T(256)} %constant.135, bf16[1024,768]{1,0:T(8,128)(2,1)S(1)} %copy-done.1, bf16[]{:T(256)} %constant.113.clone.1), kind=kCustom, calls=%fused_computation.20 | custom fusion | flops 3670016 | bytes 5505028 | tf_op jit(solution)/shard_map/scatter | solution.py:240
  13.6 54.9 %all_to_all.5 = bf16[128,16,896]{2,1,0:T(8,128)(2,1)S(1)} all-to-all(bf16[128,16,896]{2,1,0:T(8,128)(2,1)} %bitcast.30), channel_id=1, replica_groups=mesh['mx'=16,'my'=8] {'mx','my'}, dimensions={0} | all-to-all | bytes 7340032 | tf_op jit(solution)/shard_map/all_to_all | solution.py:241
  68.4 0.0 copy-start
  68.4 1.8 copy-done
  70.3 1.4 select_reduce_fusion
  71.7 8.2 %shard_map.55 = (f32[64,8,896]{2,1,0:T(8,128)}, f32[64,8,896]{2,1,0:T(8,128)}) custom-call(s32[1,2048]{1,0:T(1,128)} %bitcast.31, bf16[2048,896]{1,0:T(8,128)(2,1)} %bitcast.28), custom_call_target="tpu_custom_call" | custom-call | tf_op jit(solution)/shard_map/pallas_call | solution.py:39
  79.9 2.7 %collective-permute-start.1 = (f32[64,8,896]{2,1,0:T(8,128)}, f32[64,8,896]{2,1,0:T(8,128)S(1)}, u32[]{:S(2)}, u32[]{:S(2)}) collective-permute-start(f32[64,8,896]{2,1,0:T(8,128)} %get-tuple-element.44.lead_ref), channel_id=1, source_target_pairs={{1,0},{2,1},{3,2},{4,3},{5,4},{6,5},{7,6},{9,8},{10,9},{11,10},{12... | collective-permute-start | bytes 5505032 | tf_op jit(solution)/shard_map/ppermute | solution.py:215
  82.6 6.4 %collective-permute-start = (f32[64,8,896]{2,1,0:T(8,128)}, f32[64,8,896]{2,1,0:T(8,128)}, u32[]{:S(2)}, u32[]{:S(2)}) collective-permute-start(f32[64,8,896]{2,1,0:T(8,128)} %get-tuple-element.43.tail_ref), channel_id=1, source_target_pairs={{0,1},{1,2},{2,3},{3,4},{4,5},{5,6},{6,7},{8,9},{9,10},{10,11},{11... | collective-permute-start | bytes 5505032 | tf_op jit(solution)/shard_map/ppermute | solution.py:215
  89.0 19.5 %shard_map.56 = f32[64,64,896]{2,1,0:T(8,128)} custom-call(s32[1,2048]{1,0:T(1,128)} %bitcast.32, bf16[2048,896]{1,0:T(8,128)(2,1)} %bitcast.29, f32[64,8,896]{2,1,0:T(8,128)} %get-tuple-element.44.lead_ref, f32[64,8,896]{2,1,0:T(8,128)} %get-tuple-element.43.tail_ref), custom_call_target="tpu_custom_call" | custom-call | tf_op jit(solution)/shard_map/pallas_call | solution.py:67
  108.5 0.0 copy-start.2
  108.5 2.3 %fusion.46 = (f32[8,64,896]{2,1,0:T(8,128)S(1)}, f32[8,64,896]{2,1,0:T(8,128)S(1)}) fusion(f32[64,64,896]{2,1,0:T(8,128)} %shard_map.56), kind=kLoop, calls=%fused_computation.59 | loop fusion | bytes 7340032 | tf_op jit(solution)/shard_map/slice | solution.py:262
  110.8 15.9 %collective-permute-done.1 = f32[64,8,896]{2,1,0:T(8,128)S(1)} collective-permute-done((f32[64,8,896]{2,1,0:T(8,128)}, f32[64,8,896]{2,1,0:T(8,128)S(1)}, u32[]{:S(2)}, u32[]{:S(2)}) %collective-permute-start.1) | collective-permute-done | bytes 1835040 | tf_op jit(solution)/shard_map/ppermute | solution.py:215
  126.8 0.9 collective-permute-done
  127.7 1.1 fusion.47
  128.8 0.0 copy-done.2
  128.8 2.1 %fusion.29 = f32[8,64,896]{2,1,0:T(8,128)} fusion(f32[64,80,1]{1,0,2:T(8,128)S(1)} %copy-done.2, f32[8,8,896]{2,1,0:T(8,128)S(1)} %get-tuple-element.50, f32[8,64,896]{2,1,0:T(8,128)S(1)} %get-tuple-element.46, f32[8,8,896]{2,1,0:T(8,128)S(1)} %get-tuple-element.48), kind=kOutput, calls=%fused_computation.26 | convolution fusion | flops 221347840 | bytes 4149248 | tf_op jit(solution)/shard_map/ck,rke->rce/dot_general | solution.py:263
  130.9 5.1 %collective-permute-start.2 = (f32[8,64,896]{2,1,0:T(8,128)}, f32[8,64,896]{2,1,0:T(8,128)}, u32[]{:S(2)}, u32[]{:S(2)}) collective-permute-start(f32[8,64,896]{2,1,0:T(8,128)} %fusion.29), channel_id=1, source_target_pairs={{0,8},{8,16},{16,24},{24,32},{32,40},{40,48},{48,56},{56,64},{64,7... | collective-permute-start | bytes 5505032 | tf_op jit(solution)/shard_map/ppermute | solution.py:215
  136.0 2.2 %fusion.26 = f32[8,64,896]{2,1,0:T(8,128)} fusion(f32[64,80,1]{1,0,2:T(8,128)S(1)} %copy-done.2, f32[8,8,896]{2,1,0:T(8,128)S(1)} %get-tuple-element.49, f32[8,64,896]{2,1,0:T(8,128)S(1)} %get-tuple-element.45, f32[8,8,896]{2,1,0:T(8,128)S(1)} %get-tuple-element.47), kind=kOutput, calls=%fused_computation.25 | convolution fusion | flops 221347840 | bytes 4149248 | tf_op jit(solution)/shard_map/ck,rke->rce/dot_general | solution.py:263
  138.2 1.9 %collective-permute-start.3 = (f32[8,64,896]{2,1,0:T(8,128)}, f32[8,64,896]{2,1,0:T(8,128)}, u32[]{:S(2)}, u32[]{:S(2)}) collective-permute-start(f32[8,64,896]{2,1,0:T(8,128)} %fusion.26), channel_id=1, source_target_pairs={{8,0},{16,8},{24,16},{32,24},{40,32},{48,40},{56,48},{64,56},{72,6... | collective-permute-start | bytes 5505032 | tf_op jit(solution)/shard_map/ppermute | solution.py:215
  140.1 12.7 %fusion.6.mid_ref = f32[64,64,896]{2,1,0:T(8,128)} fusion(f32[64,80,1]{1,0,2:T(8,128)S(1)} %copy-done.2, f32[64,8,896]{2,1,0:T(8,128)S(1)} %collective-permute-done.1, f32[64,64,896]{2,1,0:T(8,128)} %shard_map.56, f32[64,8,896]{2,1,0:T(8,128)} %collective-permute-done), kind=kOutput, calls=%fused_computation.7 | convolution fusion | flops 1770782720 | bytes 33050624 | tf_op jit(solution)/shard_map/ck,rke->rce/dot_general | solution.py:263
  152.8 16.7 %shard_map.57.prev_ref = bf16[64,64,768]{2,1,0:T(8,128)(2,1)} custom-call(f32[64,64,896]{2,1,0:T(8,128)} %fusion.6.mid_ref, bf16[64,64,768]{2,1,0:T(8,128)(2,1)} %cb_ref.3), custom_call_target="tpu_custom_call" | custom-call | tf_op jit(solution)/shard_map/pallas_call | solution.py:141
  169.5 6.6 %collective-permute-done.2.above_ref = f32[8,64,896]{2,1,0:T(8,128)} collective-permute-done((f32[8,64,896]{2,1,0:T(8,128)}, f32[8,64,896]{2,1,0:T(8,128)}, u32[]{:S(2)}, u32[]{:S(2)}) %collective-permute-start.2) | collective-permute-done | bytes 1835040 | tf_op jit(solution)/shard_map/ppermute | solution.py:215
  176.1 1.1 collective-permute-done.3.below_ref
  177.2 8.7 %shard_map.58 = bf16[64,64,768]{2,1,0:T(8,128)(2,1)} custom-call(f32[8,64,896]{2,1,0:T(8,128)} %collective-permute-done.2.above_ref, f32[64,64,896]{2,1,0:T(8,128)} %fusion.6.mid_ref, f32[8,64,896]{2,1,0:T(8,128)} %collective-permute-done.3.below_ref, bf16[64,64,768]{2,1,0:T(8,128)(2,1)} %cb_ref.3, ...), custom_call_target="tpu_custom_call", output_to_operand_aliasing={{}: (4, {})} | custom-call | tf_op jit(solution)/shard_map/pallas_call | solution.py:191
  (9 shorter events, 0.1 us)
Async XLA Ops:
  0.0 3.2 %copy-start.3 = (s32[1024,1]{0,1:T(1,128)S(1)}, s32[1024,1]{0,1:T(1,128)}, u32[]{:S(2)}) copy-start(s32[1024,1]{0,1:T(1,128)} %param.12) | copy-start | bytes 12292
  0.0 3.6 %copy-start.4 = (s32[1024]{0:T(1024)S(1)}, s32[1024]{0:T(1024)}, u32[]{:S(2)}) copy-start(s32[1024]{0:T(1024)} %param.13) | copy-start | bytes 12292
  0.0 5.9 %copy-start.1 = (bf16[1024,768]{1,0:T(8,128)(2,1)S(1)}, bf16[1024,768]{1,0:T(8,128)(2,1)}, u32[]{:S(2)}) copy-start(bf16[1024,768]{1,0:T(8,128)(2,1)} %param.11) | copy-start | bytes 4718596
  68.4 1.8 copy-start
  79.9 46.8 %collective-permute-start.1 = (f32[64,8,896]{2,1,0:T(8,128)}, f32[64,8,896]{2,1,0:T(8,128)S(1)}, u32[]{:S(2)}, u32[]{:S(2)}) collective-permute-start(f32[64,8,896]{2,1,0:T(8,128)} %get-tuple-element.44.lead_ref), channel_id=1, source_target_pairs={{1,0},{2,1},{3,2},{4,3},{5,4},{6,5},{7,6},{9,8},{10,9},{11,10},{12... | collective-permute-start | bytes 5505032 | tf_op jit(solution)/shard_map/ppermute | solution.py:215
  82.6 45.1 %collective-permute-start = (f32[64,8,896]{2,1,0:T(8,128)}, f32[64,8,896]{2,1,0:T(8,128)}, u32[]{:S(2)}, u32[]{:S(2)}) collective-permute-start(f32[64,8,896]{2,1,0:T(8,128)} %get-tuple-element.43.tail_ref), channel_id=1, source_target_pairs={{0,1},{1,2},{2,3},{3,4},{4,5},{5,6},{6,7},{8,9},{9,10},{10,11},{11... | collective-permute-start | bytes 5505032 | tf_op jit(solution)/shard_map/ppermute | solution.py:215
  108.5 20.3 %copy-start.2 = (f32[64,80,1]{1,0,2:T(8,128)S(1)}, f32[64,80,1]{1,0,2:T(8,128)}, u32[]{:S(2)}) copy-start(f32[64,80,1]{1,0,2:T(8,128)} %constant.130) | copy-start | bytes 61444
  130.9 45.2 %collective-permute-start.2 = (f32[8,64,896]{2,1,0:T(8,128)}, f32[8,64,896]{2,1,0:T(8,128)}, u32[]{:S(2)}, u32[]{:S(2)}) collective-permute-start(f32[8,64,896]{2,1,0:T(8,128)} %fusion.29), channel_id=1, source_target_pairs={{0,8},{8,16},{16,24},{24,32},{32,40},{40,48},{48,56},{56,64},{64,7... | collective-permute-start | bytes 5505032 | tf_op jit(solution)/shard_map/ppermute | solution.py:215
  138.2 39.1 %collective-permute-start.3 = (f32[8,64,896]{2,1,0:T(8,128)}, f32[8,64,896]{2,1,0:T(8,128)}, u32[]{:S(2)}, u32[]{:S(2)}) collective-permute-start(f32[8,64,896]{2,1,0:T(8,128)} %fusion.26), channel_id=1, source_target_pairs={{8,0},{16,8},{24,16},{32,24},{40,32},{48,40},{56,48},{64,56},{72,6... | collective-permute-start | bytes 5505032 | tf_op jit(solution)/shard_map/ppermute | solution.py:215

commit v17 on v16

--- a/solution.py
+++ b/solution.py
@@ -41,27 +41,32 @@
 
 def accumulate(ids, docs, rows_tile, cols_tile, lead, tail):
     rows, width = docs.shape
-    band = rows_tile * RADIUS
-    blocks = cols_tile // RADIUS
+    span = 2 * RADIUS
+    blocks = cols_tile // span
 
     def kernel(ids_ref, docs_ref, lead_ref, tail_ref, num_ref):
         step = pl.program_id(0)
 
-        @pl.when(step == 0)
-        def _():
-            num_ref[...] = lead_ref[...]
-
-        @pl.when(step == blocks - 1)
-        def _():
-            num_ref[...] = tail_ref[...]
-
-        @pl.when((step > 0) & (step < blocks - 1))
-        def _():
-            place = lax.broadcasted_iota(jnp.int32, (band, rows), 0)
-            units = (place // RADIUS) * cols_tile + step * RADIUS + place % RADIUS
+        def sums_for(first_col, count):
+            place = lax.broadcasted_iota(jnp.int32, (rows_tile * count, rows), 0)
+            units = (place // count) * cols_tile + first_col + place % count
             one_hot = (units == ids_ref[...]).astype(jnp.bfloat16)
             sums = jnp.dot(one_hot, docs_ref[...], preferred_element_type=jnp.float32)
-            num_ref[...] = sums.reshape(rows_tile, RADIUS, width)
+            return sums.reshape(rows_tile, count, width)
+
+        @pl.when(step == 0)
+        def _():
+            num_ref[:, :RADIUS] = lead_ref[...]
+            num_ref[:, RADIUS:] = sums_for(RADIUS, RADIUS)
+
+        @pl.when(step == blocks - 1)
+        def _():
+            num_ref[:, :RADIUS] = sums_for(cols_tile - span, RADIUS)
+            num_ref[:, RADIUS:] = tail_ref[...]
+
+        @pl.when((step > 0) & (step < blocks - 1))
+        def _():
+            num_ref[...] = sums_for(step * span, span)
 
     band_spec = pl.BlockSpec((rows_tile, RADIUS, width), lambda j: (0, 0, 0))
     return pl.pallas_call(
@@ -73,7 +78,7 @@
             band_spec,
             band_spec,
         ],
-        out_specs=pl.BlockSpec((rows_tile, RADIUS, width), lambda j: (0, j, 0)),
+        out_specs=pl.BlockSpec((rows_tile, span, width), lambda j: (0, j, 0)),
         out_shape=jax.ShapeDtypeStruct((rows_tile, cols_tile, width), jnp.float32),
     )(ids.reshape(1, rows), docs, lead, tail)
 

time: 189 us -> 189 us (level)
  no operation moved by 1% of the time
where the time goes in v17:
time: 189 us; the launch traced here: 186 us
  blocking collectives  54.9 us (29%)
  Pallas kernels  52.7 us (28%)
  waiting for transfers between devices  24.8 us (13%)
  matrix products  17 us (9%)
  starting transfers between devices  16.3 us (9%)
  other arithmetic  13.6 us (7%)
  local copies, waits for them, and re-layouts  6.54 us (3%)
    all_to_all x1, blocking collectives, on_device(): lax.all_to_all(outgoing.reshape(tile_total, capacity, width), ('mx', 'my'...  54.9 us
    ppermute x4, waiting for transfers between devices, exchange(): return (lax.ppermute(last, axis, up), lax.ppermute(lead, axis, down))  24.8 us
    pallas_call x1, Pallas kernels, accumulate(): pl.pallas_call(kernel, grid=(blocks,), in_specs=[pl.BlockSpec((1, rows),...  19.1 us
    dot_general x3, matrix products, col_pass(): jnp.einsum('ck,rke->rce', g_cols, jnp.concatenate(pieces, axis=1), precis...  17 us
    pallas_call x1, Pallas kernels, finish_inner(): pl.pallas_call(kernel, grid=(blocks + 1,), in_specs=[pl.BlockSpec((rows,...  16.7 us
    ppermute x4, starting transfers between devices, exchange(): return (lax.ppermute(last, axis, up), lax.ppermute(lead, axis, down))  16.3 us
    pallas_call x1, Pallas kernels, finish_edges(): pl.pallas_call(kernel, grid=(2,), in_specs=[halo_spec, pl.BlockSpec((near...  8.7 us
    pallas_call x1, Pallas kernels, accumulate_bands(): pl.pallas_call(kernel, out_shape=[band_shape, band_shape])  8.21 us
  transfers between devices with their start and end apart: 4, of which 4 were waited for; matrix products, arithmetic and copies ran while one was open for 9% of the time, Pallas kernels for 19%

profile of v17, /device:TPU:15, one launch (start us, length us, event | category | flops | bytes accessed | tf_op | source)
XLA Modules:
  0.0 186.0 jit_solution(13080113116787259616)
XLA Ops:
  0.0 0.0 copy-start.3
  0.0 0.0 copy-start.4
  0.0 0.0 copy-start.1
  0.0 0.6 compare_reduce_fusion.1
  0.6 0.7 compare_reduce_fusion.2
  1.4 0.6 compare_reduce_fusion
  2.0 0.8 copy.8
  2.8 0.2 fusion.34
  3.1 0.1 copy.9
  3.2 0.0 copy-done.3
  3.2 0.4 fusion.33
  3.6 0.0 copy-done.4
  3.6 1.3 fusion.41
  5.0 0.1 scatter.19
  5.1 0.6 broadcast_select_fusion
  5.7 0.1 scatter.24
  5.7 0.2 copy.10
  5.9 0.0 copy-done.1
  5.9 7.6 %scatter_custom_fusion = bf16[2048,896]{1,0:T(8,128)(2,1)} fusion(s32[1024]{0:T(1024)S(1)} %bitcast.36, bf16[1024,128]{1,0:T(8,128)(2,1)S(1)} %copy.10, bf16[]{:T(256)} %constant.135, bf16[1024,768]{1,0:T(8,128)(2,1)S(1)} %copy-done.1, bf16[]{:T(256)} %constant.113.clone.1), kind=kCustom, calls=%fused_computation.20 | custom fusion | flops 3670016 | bytes 5505028 | tf_op jit(solution)/shard_map/scatter | solution.py:245
  13.6 54.9 %all_to_all.5 = bf16[128,16,896]{2,1,0:T(8,128)(2,1)S(1)} all-to-all(bf16[128,16,896]{2,1,0:T(8,128)(2,1)} %bitcast.30), channel_id=1, replica_groups=mesh['mx'=16,'my'=8] {'mx','my'}, dimensions={0} | all-to-all | bytes 7340032 | tf_op jit(solution)/shard_map/all_to_all | solution.py:246
  68.4 0.0 copy-start
  68.4 1.8 copy-done
  70.3 1.4 select_reduce_fusion
  71.7 8.2 %shard_map.55 = (f32[64,8,896]{2,1,0:T(8,128)}, f32[64,8,896]{2,1,0:T(8,128)}) custom-call(s32[1,2048]{1,0:T(1,128)} %bitcast.31, bf16[2048,896]{1,0:T(8,128)(2,1)} %bitcast.28), custom_call_target="tpu_custom_call" | custom-call | tf_op jit(solution)/shard_map/pallas_call | solution.py:39
  79.9 2.7 %collective-permute-start.1 = (f32[64,8,896]{2,1,0:T(8,128)}, f32[64,8,896]{2,1,0:T(8,128)S(1)}, u32[]{:S(2)}, u32[]{:S(2)}) collective-permute-start(f32[64,8,896]{2,1,0:T(8,128)} %get-tuple-element.44.lead_ref), channel_id=1, source_target_pairs={{1,0},{2,1},{3,2},{4,3},{5,4},{6,5},{7,6},{9,8},{10,9},{11,10},{12... | collective-permute-start | bytes 5505032 | tf_op jit(solution)/shard_map/ppermute | solution.py:220
  82.6 6.4 %collective-permute-start = (f32[64,8,896]{2,1,0:T(8,128)}, f32[64,8,896]{2,1,0:T(8,128)}, u32[]{:S(2)}, u32[]{:S(2)}) collective-permute-start(f32[64,8,896]{2,1,0:T(8,128)} %get-tuple-element.43.tail_ref), channel_id=1, source_target_pairs={{0,1},{1,2},{2,3},{3,4},{4,5},{5,6},{6,7},{8,9},{9,10},{10,11},{11... | collective-permute-start | bytes 5505032 | tf_op jit(solution)/shard_map/ppermute | solution.py:220
  89.0 19.1 %shard_map.56 = f32[64,64,896]{2,1,0:T(8,128)} custom-call(s32[1,2048]{1,0:T(1,128)} %bitcast.32, bf16[2048,896]{1,0:T(8,128)(2,1)} %bitcast.29, f32[64,8,896]{2,1,0:T(8,128)} %get-tuple-element.44.lead_ref, f32[64,8,896]{2,1,0:T(8,128)} %get-tuple-element.43.tail_ref), custom_call_target="tpu_custom_call" | custom-call | tf_op jit(solution)/shard_map/pallas_call | solution.py:72
  108.0 0.0 copy-start.2
  108.0 2.3 %fusion.46 = (f32[8,64,896]{2,1,0:T(8,128)S(1)}, f32[8,64,896]{2,1,0:T(8,128)S(1)}) fusion(f32[64,64,896]{2,1,0:T(8,128)} %shard_map.56), kind=kLoop, calls=%fused_computation.59 | loop fusion | bytes 7340032 | tf_op jit(solution)/shard_map/slice | solution.py:267
  110.4 16.3 %collective-permute-done.1 = f32[64,8,896]{2,1,0:T(8,128)S(1)} collective-permute-done((f32[64,8,896]{2,1,0:T(8,128)}, f32[64,8,896]{2,1,0:T(8,128)S(1)}, u32[]{:S(2)}, u32[]{:S(2)}) %collective-permute-start.1) | collective-permute-done | bytes 1835040 | tf_op jit(solution)/shard_map/ppermute | solution.py:220
  126.8 0.9 collective-permute-done
  127.7 1.1 fusion.47
  128.8 0.0 copy-done.2
  128.8 2.1 %fusion.29 = f32[8,64,896]{2,1,0:T(8,128)} fusion(f32[64,80,1]{1,0,2:T(8,128)S(1)} %copy-done.2, f32[8,8,896]{2,1,0:T(8,128)S(1)} %get-tuple-element.50, f32[8,64,896]{2,1,0:T(8,128)S(1)} %get-tuple-element.46, f32[8,8,896]{2,1,0:T(8,128)S(1)} %get-tuple-element.48), kind=kOutput, calls=%fused_computation.26 | convolution fusion | flops 221347840 | bytes 4149248 | tf_op jit(solution)/shard_map/ck,rke->rce/dot_general | solution.py:268
  130.9 5.1 %collective-permute-start.2 = (f32[8,64,896]{2,1,0:T(8,128)}, f32[8,64,896]{2,1,0:T(8,128)}, u32[]{:S(2)}, u32[]{:S(2)}) collective-permute-start(f32[8,64,896]{2,1,0:T(8,128)} %fusion.29), channel_id=1, source_target_pairs={{0,8},{8,16},{16,24},{24,32},{32,40},{40,48},{48,56},{56,64},{64,7... | collective-permute-start | bytes 5505032 | tf_op jit(solution)/shard_map/ppermute | solution.py:220
  136.0 2.2 %fusion.26 = f32[8,64,896]{2,1,0:T(8,128)} fusion(f32[64,80,1]{1,0,2:T(8,128)S(1)} %copy-done.2, f32[8,8,896]{2,1,0:T(8,128)S(1)} %get-tuple-element.49, f32[8,64,896]{2,1,0:T(8,128)S(1)} %get-tuple-element.45, f32[8,8,896]{2,1,0:T(8,128)S(1)} %get-tuple-element.47), kind=kOutput, calls=%fused_computation.25 | convolution fusion | flops 221347840 | bytes 4149248 | tf_op jit(solution)/shard_map/ck,rke->rce/dot_general | solution.py:268
  138.2 2.1 %collective-permute-start.3 = (f32[8,64,896]{2,1,0:T(8,128)}, f32[8,64,896]{2,1,0:T(8,128)}, u32[]{:S(2)}, u32[]{:S(2)}) collective-permute-start(f32[8,64,896]{2,1,0:T(8,128)} %fusion.26), channel_id=1, source_target_pairs={{8,0},{16,8},{24,16},{32,24},{40,32},{48,40},{56,48},{64,56},{72,6... | collective-permute-start | bytes 5505032 | tf_op jit(solution)/shard_map/ppermute | solution.py:220
  140.3 12.7 %fusion.6.mid_ref = f32[64,64,896]{2,1,0:T(8,128)} fusion(f32[64,80,1]{1,0,2:T(8,128)S(1)} %copy-done.2, f32[64,8,896]{2,1,0:T(8,128)S(1)} %collective-permute-done.1, f32[64,64,896]{2,1,0:T(8,128)} %shard_map.56, f32[64,8,896]{2,1,0:T(8,128)} %collective-permute-done), kind=kOutput, calls=%fused_computation.7 | convolution fusion | flops 1770782720 | bytes 33050624 | tf_op jit(solution)/shard_map/ck,rke->rce/dot_general | solution.py:268
  153.0 16.7 %shard_map.57.prev_ref = bf16[64,64,768]{2,1,0:T(8,128)(2,1)} custom-call(f32[64,64,896]{2,1,0:T(8,128)} %fusion.6.mid_ref, bf16[64,64,768]{2,1,0:T(8,128)(2,1)} %cb_ref.3), custom_call_target="tpu_custom_call" | custom-call | tf_op jit(solution)/shard_map/pallas_call | solution.py:146
  169.7 6.4 %collective-permute-done.2.above_ref = f32[8,64,896]{2,1,0:T(8,128)} collective-permute-done((f32[8,64,896]{2,1,0:T(8,128)}, f32[8,64,896]{2,1,0:T(8,128)}, u32[]{:S(2)}, u32[]{:S(2)}) %collective-permute-start.2) | collective-permute-done | bytes 1835040 | tf_op jit(solution)/shard_map/ppermute | solution.py:220
  176.1 1.1 collective-permute-done.3.below_ref
  177.2 8.7 %shard_map.58 = bf16[64,64,768]{2,1,0:T(8,128)(2,1)} custom-call(f32[8,64,896]{2,1,0:T(8,128)} %collective-permute-done.2.above_ref, f32[64,64,896]{2,1,0:T(8,128)} %fusion.6.mid_ref, f32[8,64,896]{2,1,0:T(8,128)} %collective-permute-done.3.below_ref, bf16[64,64,768]{2,1,0:T(8,128)(2,1)} %cb_ref.3, ...), custom_call_target="tpu_custom_call", output_to_operand_aliasing={{}: (4, {})} | custom-call | tf_op jit(solution)/shard_map/pallas_call | solution.py:196
  (9 shorter events, 0.1 us)
Async XLA Ops:
  0.0 3.2 %copy-start.3 = (s32[1024,1]{0,1:T(1,128)S(1)}, s32[1024,1]{0,1:T(1,128)}, u32[]{:S(2)}) copy-start(s32[1024,1]{0,1:T(1,128)} %param.12) | copy-start | bytes 12292
  0.0 3.6 %copy-start.4 = (s32[1024]{0:T(1024)S(1)}, s32[1024]{0:T(1024)}, u32[]{:S(2)}) copy-start(s32[1024]{0:T(1024)} %param.13) | copy-start | bytes 12292
  0.0 5.9 %copy-start.1 = (bf16[1024,768]{1,0:T(8,128)(2,1)S(1)}, bf16[1024,768]{1,0:T(8,128)(2,1)}, u32[]{:S(2)}) copy-start(bf16[1024,768]{1,0:T(8,128)(2,1)} %param.11) | copy-start | bytes 4718596
  68.4 1.8 copy-start
  79.9 46.8 %collective-permute-start.1 = (f32[64,8,896]{2,1,0:T(8,128)}, f32[64,8,896]{2,1,0:T(8,128)S(1)}, u32[]{:S(2)}, u32[]{:S(2)}) collective-permute-start(f32[64,8,896]{2,1,0:T(8,128)} %get-tuple-element.44.lead_ref), channel_id=1, source_target_pairs={{1,0},{2,1},{3,2},{4,3},{5,4},{6,5},{7,6},{9,8},{10,9},{11,10},{12... | collective-permute-start | bytes 5505032 | tf_op jit(solution)/shard_map/ppermute | solution.py:220
  82.6 45.1 %collective-permute-start = (f32[64,8,896]{2,1,0:T(8,128)}, f32[64,8,896]{2,1,0:T(8,128)}, u32[]{:S(2)}, u32[]{:S(2)}) collective-permute-start(f32[64,8,896]{2,1,0:T(8,128)} %get-tuple-element.43.tail_ref), channel_id=1, source_target_pairs={{0,1},{1,2},{2,3},{3,4},{4,5},{5,6},{6,7},{8,9},{9,10},{10,11},{11... | collective-permute-start | bytes 5505032 | tf_op jit(solution)/shard_map/ppermute | solution.py:220
  108.0 20.7 %copy-start.2 = (f32[64,80,1]{1,0,2:T(8,128)S(1)}, f32[64,80,1]{1,0,2:T(8,128)}, u32[]{:S(2)}) copy-start(f32[64,80,1]{1,0,2:T(8,128)} %constant.130) | copy-start | bytes 61444
  130.9 45.2 %collective-permute-start.2 = (f32[8,64,896]{2,1,0:T(8,128)}, f32[8,64,896]{2,1,0:T(8,128)}, u32[]{:S(2)}, u32[]{:S(2)}) collective-permute-start(f32[8,64,896]{2,1,0:T(8,128)} %fusion.29), channel_id=1, source_target_pairs={{0,8},{8,16},{16,24},{24,32},{32,40},{40,48},{48,56},{56,64},{64,7... | collective-permute-start | bytes 5505032 | tf_op jit(solution)/shard_map/ppermute | solution.py:220
  138.2 39.1 %collective-permute-start.3 = (f32[8,64,896]{2,1,0:T(8,128)}, f32[8,64,896]{2,1,0:T(8,128)}, u32[]{:S(2)}, u32[]{:S(2)}) collective-permute-start(f32[8,64,896]{2,1,0:T(8,128)} %fusion.26), channel_id=1, source_target_pairs={{8,0},{16,8},{24,16},{32,24},{40,32},{48,40},{56,48},{64,56},{72,6... | collective-permute-start | bytes 5505032 | tf_op jit(solution)/shard_map/ppermute | solution.py:220
